TPU v7x, 512 devices: a whole 4x8x8 slice. The times are simulated.
512 devices in a mesh: ctx: 64 (over y_lo, z, core), tp: 8 (over y_hi, x).
Axes of the slice: x: 4, y: 8 (y_hi: 2, y_lo: 4; y = y_hi * 4 + y_lo), z: 8, core: 2. Of those that a mesh axis runs over, the one named last changes fastest.
Arguments:
- tokens: bfloat16 [16384, 2048], P('ctx', 'tp'), may hold values from -6 to 6
- w_in: bfloat16 [2048, 4096], P('ctx', 'tp'), may hold values from -0.125 to 0.125
- w_bc: bfloat16 [2048, 2048], P('ctx', 'tp'), may hold values from -0.01171875 to 0.01171875
- w_dt: bfloat16 [2048, 64], P('ctx', 'tp'), may hold values from -0.125 to 0.125
- dt_bias: float32 [64], P('tp'), may hold values from -2 to 0
- decay_rate: float32 [64], P('tp'), may hold values from 1e-05 to 0.1
- skip_gain: float32 [64], P('tp'), may hold values from 0.5 to 1.5
- w_out: bfloat16 [4096, 2048], P('tp', 'ctx'), may hold values from -0.09375 to 0.09375
- cotangent: bfloat16 [16384, 2048], P('ctx', 'tp'), may hold values from -6 to 6
Outputs:
- output: bfloat16 [16384, 2048], P('ctx', 'tp')
- grad: bfloat16 [16384, 2048], P('ctx', 'tp')
All inputs are finite; a program needn't handle non-finite values.
Results may differ from a plain program's by a relative error of at most 0.0061.
Values may be sent and summed in bfloat16 or wider, within the bound.
No kernel may reach another device: no remote copies, remote signals or barrier semaphores. Data moves between devices by JAX's collectives and lax.ppermute only.
A program may use at most 128 MiB of HBM per device.

v0:
```python
import jax
import jax.numpy as jnp
from jax import lax
from jax.sharding import PartitionSpec as P

HEADDIM = 64
STATE = 128
SPAN = 256


HIGH = lax.Precision.HIGHEST


def carried_in(value, axis, combine, identity, reverse):
    devices, position = (lax.axis_size(axis), lax.axis_index(axis))
    everything = jax.tree.map(lambda part: lax.all_gather(part, axis), value)
    start = jax.tree.map(
        lambda part, zero: jnp.broadcast_to(jnp.asarray(zero, part.dtype), part.shape),
        value,
        identity,
    )

    def step(k, before):
        at = devices - 1 - k if reverse else k
        reached = at > position if reverse else at < position
        new = combine(before, jax.tree.map(lambda part: part[at], everything))
        return jax.tree.map(lambda a, b: jnp.where(reached, a, b), new, before)

    return lax.fori_loop(0, devices, step, start)


def ssd_core(values, b_rows, c_rows, step_size, decay_rate, state):
    length, heads, head_dim = values.shape
    groups = b_rows.shape[1]
    per_group = heads // groups
    blocks = length // SPAN
    lower_mask = (jnp.arange(SPAN)[:, None] >= jnp.arange(SPAN)[None, :])[None]

    def blocked(array):
        return array.reshape((blocks, SPAN) + array.shape[1:])

    def ssd_advance(carry, item):
        value_blk, b_blk, c_blk, step_blk = item
        cums = jnp.cumsum(-step_blk * decay_rate[None, :], axis=0)
        diff = cums.T[:, :, None] - cums.T[:, None, :]
        weight = jnp.where(lower_mask, jnp.exp(jnp.where(lower_mask, diff, 0.0)), 0.0)
        scores = jnp.einsum("tgn,sgn->gts", c_blk, b_blk, precision=HIGH)
        scores = jnp.repeat(scores, per_group, axis=0)
        inputs = step_blk[:, :, None] * value_blk
        inside = jnp.einsum("hts,shp->thp", scores * weight, inputs, precision=HIGH)
        c_head = jnp.repeat(c_blk, per_group, axis=1)
        b_head = jnp.repeat(b_blk, per_group, axis=1)
        carried = jnp.exp(cums)[:, :, None] * jnp.einsum(
            "thn,hpn->thp", c_head, carry, precision=HIGH
        )
        tail = jnp.exp(cums[-1][None, :] - cums)
        fresh = jnp.einsum("shp,shn->hpn", tail[:, :, None] * inputs, b_head, precision=HIGH)
        carry = jnp.exp(cums[-1])[:, None, None] * carry + fresh
        return (carry, inside + carried)

    final, outputs = lax.scan(
        jax.checkpoint(ssd_advance),
        state,
        (blocked(values), blocked(b_rows), blocked(c_rows), blocked(step_size)),
    )
    return (outputs.reshape(length, heads, head_dim), final)


def local_states(values, b_rows, step_size, decay_rate):
    length, heads, head_dim = values.shape
    groups = b_rows.shape[1]
    per_group = heads // groups
    blocks = length // SPAN

    def blocked(array):
        return array.reshape((blocks, SPAN) + array.shape[1:])

    def local_advance(carry, item):
        value_blk, b_blk, step_blk = item
        cums = jnp.cumsum(-step_blk * decay_rate[None, :], axis=0)
        tail = jnp.exp(cums[-1][None, :] - cums)
        b_head = jnp.repeat(b_blk, per_group, axis=1)
        inputs = (tail * step_blk)[:, :, None] * value_blk
        fresh = jnp.einsum("shp,shn->hpn", inputs, b_head, precision=HIGH)
        return (jnp.exp(cums[-1])[:, None, None] * carry + fresh, None)

    start = jnp.zeros((heads, head_dim, STATE), jnp.float32)
    final, unused = lax.scan(
        local_advance, start, (blocked(values), blocked(b_rows), blocked(step_size))
    )
    return final


def local_adjoint(d_mixed, c_rows, step_size, decay_rate):
    length, heads, head_dim = d_mixed.shape
    groups = c_rows.shape[1]
    per_group = heads // groups
    blocks = length // SPAN

    def blocked(array):
        return array.reshape((blocks, SPAN) + array.shape[1:])

    def retreat(carry, item):
        grad_blk, c_blk, step_blk = item
        cums = jnp.cumsum(-step_blk * decay_rate[None, :], axis=0)
        c_head = jnp.repeat(c_blk, per_group, axis=1)
        weighted = jnp.exp(cums)[:, :, None] * grad_blk
        term = jnp.einsum("thp,thn->hpn", weighted, c_head, precision=HIGH)
        return (term + jnp.exp(cums[-1])[:, None, None] * carry, None)

    start = jnp.zeros((heads, head_dim, STATE), jnp.float32)
    final, unused = lax.scan(
        retreat, start, (blocked(d_mixed), blocked(c_rows), blocked(step_size)), reverse=True
    )
    return final


def chain_combine(earlier, later):
    return (earlier[0] * later[0], later[0][:, None, None] * earlier[1] + later[1])


def per_device(tokens, w_in, w_bc, w_dt, dt_bias, decay_rate, skip_gain, w_out, cotangent):
    full_tokens = lax.all_gather(tokens, "tp", axis=1, tiled=True)
    rows = full_tokens.shape[0]
    heads = decay_rate.shape[0]
    inner = w_in.shape[1]
    pair_cols = w_bc.shape[1]
    groups = pair_cols // (2 * STATE)
    w_cat = jnp.concatenate([w_in, w_bc, w_dt], axis=1)
    whole_in, whole_out = (
        lax.all_gather(w_cat, "ctx", axis=0, tiled=True),
        lax.all_gather(w_out, "ctx", axis=1, tiled=True),
    )
    projected = jnp.dot(full_tokens, whole_in, preferred_element_type=jnp.float32)
    values = projected[:, :inner].astype(jnp.bfloat16)
    pairs = projected[:, inner : inner + pair_cols].astype(jnp.bfloat16)
    pre_step = projected[:, inner + pair_cols :] + dt_bias[None, :]
    step_size = jax.nn.softplus(pre_step)
    value_f = values.astype(jnp.float32).reshape(rows, heads, HEADDIM)
    paired = pairs.astype(jnp.float32).reshape(rows, groups, 2, STATE)
    b_rows = paired[:, :, 0]
    c_rows = paired[:, :, 1]
    zero_state = jnp.zeros((heads, HEADDIM, STATE), jnp.float32)
    end_state = local_states(value_f, b_rows, step_size, decay_rate)
    decay_total = jnp.exp(-jnp.sum(step_size * decay_rate[None, :], axis=0))
    unit_decay = jnp.ones_like(decay_total)
    state_in = carried_in(
        (decay_total, end_state), "ctx", chain_combine, (unit_decay, zero_state), False
    )[1]

    def with_state(vals, brows, crows, steps):
        return ssd_core(vals, brows, crows, steps, decay_rate, state_in)

    (core_out, core_end), pullback = jax.vjp(with_state, value_f, b_rows, c_rows, step_size)
    mixed = (
        (core_out + skip_gain[None, :, None] * value_f).reshape(rows, inner).astype(jnp.bfloat16)
    )
    partial_out = jnp.dot(mixed, whole_out, preferred_element_type=jnp.float32)
    output = lax.psum_scatter(partial_out, "tp", scatter_dimension=1, tiled=True).astype(
        jnp.bfloat16
    )
    full_cotangent = lax.all_gather(cotangent, "tp", axis=1, tiled=True)
    d_flat = lax.dot_general(
        full_cotangent, whole_out, (((1,), (1,)), ((), ())), preferred_element_type=jnp.float32
    )
    d_mixed = d_flat.reshape(rows, heads, HEADDIM)
    own_adjoint = local_adjoint(d_mixed, c_rows, step_size, decay_rate)
    adjoint = carried_in(
        (decay_total, own_adjoint), "ctx", chain_combine, (unit_decay, zero_state), True
    )[1]
    grads = pullback((d_mixed, adjoint))
    d_values = grads[0] + skip_gain[None, :, None] * d_mixed
    d_pre = grads[3] * jax.nn.sigmoid(pre_step)
    d_pairs = jnp.stack([grads[1], grads[2]], axis=2).reshape(rows, pair_cols)
    d_cat = jnp.concatenate(
        [
            d_values.reshape(rows, inner).astype(jnp.bfloat16),
            d_pairs.astype(jnp.bfloat16),
            d_pre.astype(jnp.bfloat16),
        ],
        axis=1,
    )
    partial_grad = lax.dot_general(
        d_cat, whole_in, (((1,), (1,)), ((), ())), preferred_element_type=jnp.float32
    )
    grad = lax.psum_scatter(partial_grad, "tp", scatter_dimension=1, tiled=True).astype(
        jnp.bfloat16
    )
    return (output, grad)


def solution(mesh):
    placed = (
        P("ctx", "tp"),
        P("ctx", "tp"),
        P("ctx", "tp"),
        P("ctx", "tp"),
        P("tp"),
        P("tp"),
        P("tp"),
        P("tp", "ctx"),
        P("ctx", "tp"),
    )
    return jax.shard_map(
        per_device,
        mesh=mesh,
        in_specs=placed,
        out_specs=(P("ctx", "tp"), P("ctx", "tp")),
        check_vma=False,
    )
```

profile of v0, /device:TPU:1, one launch (start us, length us, event | category | flops | bytes accessed | tf_op | source)
XLA Modules:
  0.0 956.4 jit_solution(10502070990085466387)
XLA Ops:
  8.7 1.4 pad_maximum_fusion.1
  11.5 68.9 %all-gather.12.cloned.1.call-done = bf16[256,2048]{1,0:T(8,128)(2,1)} async-done(((bf16[256,256]{1,0:T(8,128)(2,1)}), bf16[256,2048]{1,0:T(8,128)(2,1)}) %all-gather.12.cloned.1.call-update) | async-done | bytes 1048592 | tf_op jit(solution)/shard_map/all_gather | solution.py:123
  80.4 121.3 %all-gather.10.cloned.1.call-done = bf16[2048,776]{1,0:T(8,128)(2,1)} async-done(((bf16[32,776]{1,0:T(8,128)(2,1)}), bf16[2048,776]{1,0:T(8,128)(2,1)}) %all-gather.10.cloned.1.call-update) | async-done | bytes 3178512 | tf_op jit(solution)/shard_map/all_gather | solution.py:131
  201.8 3.5 fusion.87
  207.5 1.3 convolution_add_fusion.1
  209.0 58.5 %all-gather.16.cloned.1.call-done = bf16[256,2048]{1,0:T(8,128)(2,1)} async-done(((bf16[256,256]{1,0:T(8,128)(2,1)}), bf16[256,2048]{1,0:T(8,128)(2,1)}) %all-gather.16.cloned.1.call-update) | async-done | bytes 1048592 | tf_op jit(solution)/shard_map/all_gather | solution.py:162
  267.4 118.6 %all-gather.14.cloned.1.call-done = bf16[512,2048]{0,1:T(8,128)(2,1)} async-done(((bf16[512,32]{0,1:T(8,128)(2,1)}), bf16[512,2048]{0,1:T(8,128)(2,1)}) %all-gather.14.cloned.1.call-update) | async-done | bytes 2097168 | tf_op jit(solution)/shard_map/all_gather | solution.py:132
  386.1 2.8 fusion.89
  389.0 1.4 convolution_add_fusion
  391.3 1.3 dynamic-slice.2
  393.4 135.9 %all-reduce.2 = f32[512]{0:T(512)S(1)} all-reduce(f32[512]{0:T(512)S(1)} %exponential_dynamic-update-slice_fusion), channel_id=2, replica_groups=mesh['ctx'=64,'tp'=8] {'ctx'}, use_global_device_ids=true, to_apply=%add.2 | all-reduce | flops 512 | bytes 4096
  529.7 2.5 fusion.12
  532.2 70.2 %while.22 = (s32[]{:T(128)}, f32[8,64,128]{2,1,0:T(8,128)S(1)}, s32[]{:T(128)}, f32[64,8]{1,0:T(8,128)S(1)}, f32[64,8,64,128]{3,2,1,0:T(8,128)}, /*index=5*/s32[]{:T(128)}, s32[]{:T(128)}) while((s32[]{:T(128)}, f32[8,64,128]{2,1,0:T(8,128)S(1)}, s32[]{:T(128)}, f32[64,8]{1,0:T(8,128)S(1)}, f32[64,8,64,128]{3,2,1,0:T(8,128)}, ...), condition=%wide.region_4.5_spmd.clone, body=%wide.region_3.4_spmd.clone.sunk | while | flops 262148 | bytes 786633 | solution.py:29
  536.6 1.1 fusion.106
  541.0 1.1 fusion.106
  543.2 1.1 fusion.106
  545.4 1.1 fusion.106
  549.8 1.1 fusion.106
  550.9 1.1 fusion.106
  555.3 1.1 fusion.106
  556.4 1.1 fusion.106
  559.7 1.1 fusion.106
  563.0 1.1 fusion.106
  566.3 1.1 fusion.106
  568.5 1.1 fusion.106
  569.6 1.1 fusion.106
  570.7 1.1 fusion.106
  572.9 1.1 fusion.106
  574.0 1.1 fusion.106
  577.3 1.1 fusion.106
  580.5 1.1 fusion.106
  581.6 1.1 fusion.106
  582.7 1.1 fusion.106
  588.2 1.1 fusion.106
  591.5 1.1 fusion.106
  594.8 1.1 fusion.106
  595.9 1.1 fusion.106
  598.1 1.1 fusion.106
  599.2 1.1 fusion.106
  602.5 55.5 %all-gather.20.cloned.1.call-done = f32[512,64,128]{2,1,0:T(8,128)} async-done(((f32[8,64,128]{2,1,0:T(8,128)}), f32[512,64,128]{2,1,0:T(8,128)}) %all-gather.20.cloned.1.call-update) | async-done | bytes 16777232 | tf_op jit(solution)/shard_map/all_gather | solution.py:16
  658.0 70.8 %while.23 = (s32[]{:T(128)}, f32[8,64,128]{2,1,0:T(8,128)S(1)}, s32[]{:T(128)}, f32[64,8]{1,0:T(8,128)S(1)}, f32[64,8,64,128]{3,2,1,0:T(8,128)}, /*index=5*/s32[]{:T(128)}, s32[]{:T(128)}, s32[]{:T(128)}, s32[]{:T(128)}) while((s32[]{:T(128)}, f32[8,64,128]{2,1,0:T(8,128)S(1)}, s32[]{:T(128)}, f32[64,8]{1,0:T(8,128)S(1)}, ...), condition=%wide.region_7.8_spmd.clone, body=%wide.region_6.7_spmd.clone.sunk | while | flops 262152 | bytes 786695 | solution.py:29
  659.1 1.1 fusion.107
  664.6 1.1 fusion.107
  672.4 1.1 fusion.107
  680.1 1.1 fusion.107
  685.7 1.1 fusion.107
  693.4 1.1 fusion.107
  701.2 1.1 fusion.107
  706.7 1.1 fusion.107
  714.4 1.1 fusion.107
  722.2 1.1 fusion.107
  732.0 3.1 fusion.22
  735.9 1.2 convolution_bitcast_fusion.2
  737.0 3.4 multiply_reduce_fusion.1
  740.8 1.2 fusion.26
  742.1 2.7 reduce-window.44
  744.9 1.2 fusion.20
  747.2 2.7 fusion.59
  749.9 1.5 copy-done.1
  751.4 2.1 fusion.88
  753.5 93.4 %reduce-scatter.5.cloned.1.call-done = f32[256,256]{1,0:T(8,128)} async-done(((f32[256,2048]{1,0:T(8,128)}), f32[256,256]{1,0:T(8,128)}) %reduce-scatter.5.cloned.1.call-update) | async-done | bytes 262160 | tf_op jit(solution)/shard_map/reduce_scatter | solution.py:186
  846.9 1.6 convert_element_type.31
  848.5 99.5 %reduce-scatter.3.cloned.1.call-done = f32[256,256]{1,0:T(8,128)} async-done(((f32[256,2048]{1,0:T(8,128)}), f32[256,256]{1,0:T(8,128)}) %reduce-scatter.3.cloned.1.call-update) | async-done | bytes 262160 | tf_op jit(solution)/shard_map/reduce_scatter | solution.py:159
  948.0 1.6 convert_element_type.27
  (311 shorter events, 110.3 us)
Async XLA Ops:
  7.2 73.3 %all-gather.12.cloned.1.call-start = ((), (), s32[]{:S(2)}) async-start(), calls=%async_computation.3 | async-start | bytes 1179648 | tf_op jit(solution)/shard_map/all_gather | solution.py:123
  7.9 193.9 %all-gather.10.cloned.1.call-start = ((), (), s32[]{:S(2)}) async-start(), calls=%async_computation.2 | async-start | bytes 3727360 | tf_op jit(solution)/shard_map/all_gather | solution.py:131
  10.1 257.3 %all-gather.16.cloned.1.call-start = ((), (), s32[]{:S(2)}) async-start(), calls=%async_computation.6 | async-start | bytes 1179648 | tf_op jit(solution)/shard_map/all_gather | solution.py:162
  10.9 375.2 %all-gather.14.cloned.1.call-start = ((), (), s32[]{:S(2)}) async-start(), calls=%async_computation.4 | async-start | bytes 2129920 | tf_op jit(solution)/shard_map/all_gather | solution.py:132
  11.5 193.8 %copy-start.3 = (f32[8]{0:T(128)S(1)}, f32[8]{0:T(128)}, u32[]{:S(2)}) copy-start(f32[8]{0:T(128)} %param.18) | copy-start | bytes 100
  11.5 193.8 %copy-start.6 = (f32[8]{0:T(128)S(1)}, f32[8]{0:T(128)}, u32[]{:S(2)}) copy-start(f32[8]{0:T(128)} %param.17) | copy-start | bytes 100
  11.5 520.7 %all-gather.18.cloned.1.call-start = ((), (), s32[]{:S(2)}) async-start(), calls=%async_computation.8 | async-start | bytes 17039360 | tf_op jit(solution)/shard_map/all_gather | solution.py:16
  205.2 0.9 copy-start.9
  208.9 181.6 %copy-start.8 = (f32[8]{0:T(128)S(1)}, f32[8]{0:T(128)}, u32[]{:S(2)}) copy-start(f32[8]{0:T(128)} %param.19) | copy-start | bytes 100
  208.9 449.1 %all-gather.20.cloned.1.call-start = ((), (), s32[]{:S(2)}) async-start(), calls=%async_computation.9 | async-start | bytes 17039360 | tf_op jit(solution)/shard_map/all_gather | solution.py:16
  390.4 456.4 %reduce-scatter.5.cloned.1.call-start = ((), (), s32[]{:S(2)}) async-start(), calls=%async_computation.7 | async-start | bytes 2359296 | tf_op jit(solution)/shard_map/reduce_scatter | solution.py:186
  740.4 5.7 copy-start.4
  740.4 5.7 copy-start.7
  740.4 6.5 copy-start.5
  740.8 6.2 copy-start.2
  744.9 2.2 copy-start
  749.8 1.6 copy-start.1
  749.9 198.1 %reduce-scatter.3.cloned.1.call-start = ((), (), s32[]{:S(2)}) async-start(), calls=%async_computation.5 | async-start | bytes 2359296 | tf_op jit(solution)/shard_map/reduce_scatter | solution.py:159
Sparse Core Ops, SparseCore 0:
  11.1 69.3 all-gather.11
  83.2 118.5 all-gather.9
  204.8 62.5 all-gather.15
  269.5 116.5 all-gather.13
  388.1 133.5 all-gather.17
  523.7 134.2 all-gather.19
  750.0 96.8 reduce-scatter.4
  852.2 95.7 reduce-scatter.2
where the time goes:
time: 961 us; the launch traced here: 956 us
  waiting for transfers between devices  618 us (64%)
  other arithmetic  146 us (15%)
  blocking collectives  136 us (14%)
  matrix products  28.8 us (3%)
  between operations  15.2 us (2%)
    unnamed x1, blocking collectives  136 us
    select_n x128, other arithmetic, step(): return jax.tree.map(lambda a, b: jnp.where(reached, a, b), new, before)  135 us
    all_gather x1, waiting for transfers between devices, per_device(): lax.all_gather(w_cat, 'ctx', axis=0, tiled=True)  121 us
    all_gather x1, waiting for transfers between devices, per_device(): lax.all_gather(w_out, 'ctx', axis=1, tiled=True)  119 us
    reduce_scatter x1, waiting for transfers between devices, per_device(): lax.psum_scatter(partial_out, 'tp', scatter_dimension=1, tiled=True)  99.5 us
    reduce_scatter x1, waiting for transfers between devices, per_device(): lax.psum_scatter(partial_grad, 'tp', scatter_dimension=1, tiled=True)  93.4 us
    all_gather x1, waiting for transfers between devices, per_device(): full_tokens = lax.all_gather(tokens, 'tp', axis=1, tiled=True)  68.9 us
    all_gather x1, waiting for transfers between devices, per_device(): full_cotangent = lax.all_gather(cotangent, 'tp', axis=1, tiled=True)  58.5 us
  transfers between devices with their start and end apart: 8, of which 7 were waited for; matrix products, arithmetic and copies ran while one was open for 9% of the time, Pallas kernels for 0%

commit v1 on v0

--- a/solution.py
+++ b/solution.py
@@ -11,22 +11,31 @@
 HIGH = lax.Precision.HIGHEST
 
 
-def carried_in(value, axis, combine, identity, reverse):
+def carried_in(decay, state, axis, reverse):
     devices, position = (lax.axis_size(axis), lax.axis_index(axis))
-    everything = jax.tree.map(lambda part: lax.all_gather(part, axis), value)
-    start = jax.tree.map(
-        lambda part, zero: jnp.broadcast_to(jnp.asarray(zero, part.dtype), part.shape),
-        value,
-        identity,
-    )
-
-    def step(k, before):
-        at = devices - 1 - k if reverse else k
-        reached = at > position if reverse else at < position
-        new = combine(before, jax.tree.map(lambda part: part[at], everything))
-        return jax.tree.map(lambda a, b: jnp.where(reached, a, b), new, before)
-
-    return lax.fori_loop(0, devices, step, start)
+    heads = decay.shape[0]
+    packed = jnp.concatenate(
+        [state.reshape(heads, -1), jnp.broadcast_to(decay[:, None], (heads, 128))], axis=1
+    )
+
+    def shifted(x, shift):
+        if reverse:
+            perm = [(i + shift, i) for i in range(devices - shift)]
+        else:
+            perm = [(i, i + shift) for i in range(devices - shift)]
+        return lax.ppermute(x, axis, perm)
+
+    shift = 1
+    while shift < devices:
+        got = shifted(packed, shift)
+        own = packed[:, -128:]
+        reached = position < devices - shift if reverse else position >= shift
+        mixed_s = own[:, :1] * got[:, :-128] + packed[:, :-128]
+        mixed_a = jnp.where(reached, own * got[:, -128:], own)
+        packed = jnp.concatenate([mixed_s, mixed_a], axis=1)
+        shift *= 2
+    before = shifted(packed[:, :-128], 1)
+    return before.reshape(state.shape)
 
 
 def ssd_core(values, b_rows, c_rows, step_size, decay_rate, state):
@@ -115,10 +124,6 @@
     return final
 
 
-def chain_combine(earlier, later):
-    return (earlier[0] * later[0], later[0][:, None, None] * earlier[1] + later[1])
-
-
 def per_device(tokens, w_in, w_bc, w_dt, dt_bias, decay_rate, skip_gain, w_out, cotangent):
     full_tokens = lax.all_gather(tokens, "tp", axis=1, tiled=True)
     rows = full_tokens.shape[0]
@@ -143,10 +148,7 @@
     zero_state = jnp.zeros((heads, HEADDIM, STATE), jnp.float32)
     end_state = local_states(value_f, b_rows, step_size, decay_rate)
     decay_total = jnp.exp(-jnp.sum(step_size * decay_rate[None, :], axis=0))
-    unit_decay = jnp.ones_like(decay_total)
-    state_in = carried_in(
-        (decay_total, end_state), "ctx", chain_combine, (unit_decay, zero_state), False
-    )[1]
+    state_in = carried_in(decay_total, end_state, "ctx", False)
 
     def with_state(vals, brows, crows, steps):
         return ssd_core(vals, brows, crows, steps, decay_rate, state_in)
@@ -165,9 +167,7 @@
     )
     d_mixed = d_flat.reshape(rows, heads, HEADDIM)
     own_adjoint = local_adjoint(d_mixed, c_rows, step_size, decay_rate)
-    adjoint = carried_in(
-        (decay_total, own_adjoint), "ctx", chain_combine, (unit_decay, zero_state), True
-    )[1]
+    adjoint = carried_in(decay_total, own_adjoint, "ctx", True)
     grads = pullback((d_mixed, adjoint))
     d_values = grads[0] + skip_gain[None, :, None] * d_mixed
     d_pre = grads[3] * jax.nn.sigmoid(pre_step)

time: 961 us -> 737 us (0.77)
  blocking collectives: 136 us -> 0 us
  other arithmetic: 146 us -> 16.8 us
  starting transfers between devices: 0.32 us -> 51.4 us
    unnamed x1 -> x0, blocking collectives: 136 us -> none
    select_n x128 -> x9, other arithmetic: 135 us -> 0.78 us  [carried_in(): mixed_a = jnp.where(reached, own * got[:, -128:], own)]
    all_gather x2 -> x0, waiting for transfers between devices: 55.5 us -> none  [carried_in(): everything = jax.tree.map(lambda part: lax.all_gather(part, axis), value)]
    ppermute x0 -> x14, starting transfers between devices: none -> 51.1 us  [shifted(): return lax.ppermute(x, axis, perm)]
    ppermute x0 -> x14, waiting for transfers between devices: none -> 43 us  [shifted(): return lax.ppermute(x, axis, perm)]
    all_gather x1, waiting for transfers between devices: 58.5 us -> 68.1 us  [per_device(): full_cotangent = lax.all_gather(cotangent, 'tp', axis=1, tiled=True)]
  transfers between devices with their start and end apart: 8 -> 20, of which waited for: 7 -> 16; matrix products, arithmetic and copies ran while one was open for 9% -> 2% of each run, Pallas kernels for 0% -> 0%
where the time goes in v1:
time: 737 us; the launch traced here: 736 us
  waiting for transfers between devices  613 us (83%)
  starting transfers between devices  51.4 us (7%)
  matrix products  32.5 us (4%)
  other arithmetic  16.8 us (2%)
  between operations  14.8 us (2%)
    all_gather x1, waiting for transfers between devices, per_device(): lax.all_gather(w_cat, 'ctx', axis=0, tiled=True)  121 us
    all_gather x1, waiting for transfers between devices, per_device(): lax.all_gather(w_out, 'ctx', axis=1, tiled=True)  119 us
    reduce_scatter x1, waiting for transfers between devices, per_device(): lax.psum_scatter(partial_out, 'tp', scatter_dimension=1, tiled=True)  99.1 us
    reduce_scatter x1, waiting for transfers between devices, per_device(): lax.psum_scatter(partial_grad, 'tp', scatter_dimension=1, tiled=True)  98 us
    all_gather x1, waiting for transfers between devices, per_device(): full_cotangent = lax.all_gather(cotangent, 'tp', axis=1, tiled=True)  68.1 us
    all_gather x1, waiting for transfers between devices, per_device(): full_tokens = lax.all_gather(tokens, 'tp', axis=1, tiled=True)  62.7 us
    ppermute x14, starting transfers between devices, shifted(): return lax.ppermute(x, axis, perm)  51.1 us
    ppermute x14, waiting for transfers between devices, shifted(): return lax.ppermute(x, axis, perm)  43 us
  transfers between devices with their start and end apart: 20, of which 16 were waited for; matrix products, arithmetic and copies ran while one was open for 2% of the time, Pallas kernels for 0%

profile of v1, /device:TPU:1, one launch (start us, length us, event | category | flops | bytes accessed | tf_op | source)
XLA Modules:
  0.0 735.8 jit_solution(6299721520931784923)
XLA Ops:
  7.2 0.7 all-gather.11.cloned.1.call-update
  7.9 0.7 all-gather.9.cloned.1.call-update
  8.7 0.7 all-gather.7.cloned.1.call-update
  9.4 0.8 copy.68
  10.2 1.4 pad_maximum_fusion.13
  11.7 0.7 iota_compare_fusion
  12.3 68.1 %all-gather.11.cloned.1.call-done = bf16[256,2048]{1,0:T(8,128)(2,1)} async-done(((bf16[256,256]{1,0:T(8,128)(2,1)}), bf16[256,2048]{1,0:T(8,128)(2,1)}) %all-gather.11.cloned.1.call-update) | async-done | bytes 1048592 | tf_op jit(solution)/shard_map/all_gather | solution.py:164
  80.4 118.8 %all-gather.9.cloned.1.call-done = bf16[512,2048]{0,1:T(8,128)(2,1)} async-done(((bf16[512,32]{0,1:T(8,128)(2,1)}), bf16[512,2048]{0,1:T(8,128)(2,1)}) %all-gather.9.cloned.1.call-update) | async-done | bytes 2097168 | tf_op jit(solution)/shard_map/all_gather | solution.py:137
  199.2 2.8 fusion.103
  202.1 62.7 %all-gather.7.cloned.1.call-done = bf16[256,2048]{1,0:T(8,128)(2,1)} async-done(((bf16[256,256]{1,0:T(8,128)(2,1)}), bf16[256,2048]{1,0:T(8,128)(2,1)}) %all-gather.7.cloned.1.call-update) | async-done | bytes 1048592 | tf_op jit(solution)/shard_map/all_gather | solution.py:128
  264.8 121.1 %all-gather.5.cloned.1.call-done = bf16[2048,776]{1,0:T(8,128)(2,1)} async-done(((bf16[32,776]{1,0:T(8,128)(2,1)}), bf16[2048,776]{1,0:T(8,128)(2,1)}) %all-gather.5.cloned.1.call-update) | async-done | bytes 3178512 | tf_op jit(solution)/shard_map/all_gather | solution.py:136
  385.9 3.5 fusion.101
  391.2 0.6 fusion.25
  391.8 0.6 fusion.26
  392.9 3.3 collective-permute-start
  396.2 1.9 collective-permute-start.7
  398.2 0.7 mul.496
  399.5 4.5 collective-permute-done.7
  404.0 1.3 fusion.70
  405.3 0.7 fusion.89
  406.0 1.3 collective-permute-start.8
  407.4 4.0 collective-permute-start.1
  411.6 3.0 collective-permute-done.8
  414.8 1.3 collective-permute-start.9
  416.6 5.4 collective-permute-start.2
  422.2 9.2 %collective-permute-done.9 = f32[8,8320]{1,0:T(8,128)S(1)} collective-permute-done((f32[8,8320]{1,0:T(8,128)S(1)}, f32[8,8320]{1,0:T(8,128)S(1)}, u32[]{:S(2)}, u32[]{:S(2)}) %collective-permute-start.9) | collective-permute-done | bytes 266272 | tf_op jit(solution)/shard_map/ppermute | solution.py:26
  431.6 1.3 collective-permute-start.10
  433.0 9.6 %collective-permute-start.3 = (f32[8,8320]{1,0:T(8,128)S(1)}, f32[8,8320]{1,0:T(8,128)S(1)}, u32[]{:S(2)}, u32[]{:S(2)}) collective-permute-start(f32[8,8320]{1,0:T(8,128)S(1)} %pad_maximum_fusion.4), channel_id=1, source_target_pairs={{0,64},{8,72},{16,80},{24,88},{32,96},{40,104},{48,112},{56,120},{... | collective-permute-start | bytes 798728 | tf_op jit(solution)/shard_map/ppermute | solution.py:26
  442.9 2.7 collective-permute-done.10
  445.7 1.3 collective-permute-start.11
  447.0 9.5 %collective-permute-done.3 = f32[8,8320]{1,0:T(8,128)S(1)} collective-permute-done((f32[8,8320]{1,0:T(8,128)S(1)}, f32[8,8320]{1,0:T(8,128)S(1)}, u32[]{:S(2)}, u32[]{:S(2)}) %collective-permute-start.3) | collective-permute-done | bytes 266272 | tf_op jit(solution)/shard_map/ppermute | solution.py:26
  456.6 9.7 %collective-permute-start.4 = (f32[8,8320]{1,0:T(8,128)S(1)}, f32[8,8320]{1,0:T(8,128)S(1)}, u32[]{:S(2)}, u32[]{:S(2)}) collective-permute-start(f32[8,8320]{1,0:T(8,128)S(1)} %pad_maximum_fusion.5), channel_id=1, source_target_pairs={{0,128},{8,136},{16,144},{24,152},{32,160},{40,168},{48,176},{56,1... | collective-permute-start | bytes 798728 | tf_op jit(solution)/shard_map/ppermute | solution.py:26
  466.6 1.3 collective-permute-start.12
  467.9 3.6 collective-permute-done.4
  471.6 2.0 collective-permute-start.5
  473.9 9.1 %collective-permute-done.12 = f32[8,8320]{1,0:T(8,128)S(1)} collective-permute-done((f32[8,8320]{1,0:T(8,128)S(1)}, f32[8,8320]{1,0:T(8,128)S(1)}, u32[]{:S(2)}, u32[]{:S(2)}) %collective-permute-start.12) | collective-permute-done | bytes 266272 | tf_op jit(solution)/shard_map/ppermute | solution.py:26
  483.0 2.9 collective-permute-start.13
  486.1 5.9 collective-permute-start.6
  492.1 2.5 fusion.10
  494.7 0.6 collective-permute-done.6
  495.4 0.7 reduce-window.42
  496.3 0.7 fusion.99
  497.0 0.7 add_bitcast_fusion.1
  498.1 0.6 copy-done.12
  498.8 0.6 copy-done.8
  499.4 0.6 convolution_bitcast_fusion.5
  500.4 1.3 convolution_bitcast_fusion.4
  501.7 4.6 fusion.20
  506.3 0.9 fusion.30
  507.2 1.0 fusion.29
  508.3 1.2 convolution_bitcast_fusion.2
  509.5 4.3 multiply_reduce_fusion.1
  514.5 1.2 fusion.24
  515.7 0.8 fusion.88
  516.5 2.5 reduce-window.44
  519.2 2.0 fusion.18
  521.3 0.8 fusion.86
  522.3 2.7 fusion.59
  525.0 1.5 copy-done.1
  526.5 2.1 fusion.102
  528.6 98.0 %reduce-scatter.5.cloned.1.call-done = f32[256,256]{1,0:T(8,128)} async-done(((f32[256,2048]{1,0:T(8,128)}), f32[256,256]{1,0:T(8,128)}) %reduce-scatter.5.cloned.1.call-update) | async-done | bytes 262160 | tf_op jit(solution)/shard_map/reduce_scatter | solution.py:186
  626.6 1.6 convert_element_type.31
  628.2 99.1 %reduce-scatter.3.cloned.1.call-done = f32[256,256]{1,0:T(8,128)} async-done(((f32[256,2048]{1,0:T(8,128)}), f32[256,256]{1,0:T(8,128)}) %reduce-scatter.3.cloned.1.call-update) | async-done | bytes 262160 | tf_op jit(solution)/shard_map/reduce_scatter | solution.py:161
  727.3 1.6 convert_element_type.27
  (136 shorter events, 8.2 us)
Async XLA Ops:
  7.2 73.3 %all-gather.11.cloned.1.call-start = ((), (), s32[]{:S(2)}) async-start(), calls=%async_computation.6 | async-start | bytes 1179648 | tf_op jit(solution)/shard_map/all_gather | solution.py:164
  7.9 191.3 %all-gather.9.cloned.1.call-start = ((), (), s32[]{:S(2)}) async-start(), calls=%async_computation.4 | async-start | bytes 2129920 | tf_op jit(solution)/shard_map/all_gather | solution.py:137
  8.6 256.1 %all-gather.7.cloned.1.call-start = ((), (), s32[]{:S(2)}) async-start(), calls=%async_computation.3 | async-start | bytes 1179648 | tf_op jit(solution)/shard_map/all_gather | solution.py:128
  9.4 376.5 %all-gather.5.cloned.1.call-start = ((), (), s32[]{:S(2)}) async-start(), calls=%async_computation.2 | async-start | bytes 3727360 | tf_op jit(solution)/shard_map/all_gather | solution.py:136
  11.6 615.0 %reduce-scatter.5.cloned.1.call-start = ((), (), s32[]{:S(2)}) async-start(), calls=%async_computation.7 | async-start | bytes 2359296 | tf_op jit(solution)/shard_map/reduce_scatter | solution.py:186
  202.1 187.3 %copy-start.10 = (f32[8]{0:T(128)S(1)}, f32[8]{0:T(128)}, u32[]{:S(2)}) copy-start(f32[8]{0:T(128)} %param.14) | copy-start | bytes 100
  202.1 187.3 %copy-start.17 = (f32[8]{0:T(128)S(1)}, f32[8]{0:T(128)}, u32[]{:S(2)}) copy-start(f32[8]{0:T(128)} %param.13) | copy-start | bytes 100
  389.4 3.1 copy-start.20
  390.5 1.9 copy-start.7
  391.1 7.0 copy-start.19
  392.9 6.6 collective-permute-start
  396.2 7.8 %collective-permute-start.7 = (f32[8,8320]{1,0:T(8,128)S(1)}, f32[8,8320]{1,0:T(8,128)}, u32[]{:S(2)}, u32[]{:S(2)}) collective-permute-start(f32[8,8320]{1,0:T(8,128)S(1)} %get-tuple-element.208), channel_id=1, source_target_pairs={{8,0},{16,8},{24,16},{32,24},{40,32},{48,40},{56,48},{64,56},{72,6... | collective-permute-start | bytes 798728 | tf_op jit(solution)/shard_map/ppermute | solution.py:26
  406.0 8.6 %collective-permute-start.8 = (f32[8,8320]{1,0:T(8,128)S(1)}, f32[8,8320]{1,0:T(8,128)S(1)}, u32[]{:S(2)}, u32[]{:S(2)}) collective-permute-start(f32[8,8320]{1,0:T(8,128)S(1)} %pad_maximum_fusion.7), channel_id=1, source_target_pairs={{16,0},{24,8},{32,16},{40,24},{48,32},{56,40},{64,48},{72,56},{80,... | collective-permute-start | bytes 798728 | tf_op jit(solution)/shard_map/ppermute | solution.py:26
  407.4 9.0 %collective-permute-start.1 = (f32[8,8320]{1,0:T(8,128)S(1)}, f32[8,8320]{1,0:T(8,128)S(1)}, u32[]{:S(2)}, u32[]{:S(2)}) collective-permute-start(f32[8,8320]{1,0:T(8,128)S(1)} %pad_maximum_fusion.2), channel_id=1, source_target_pairs={{0,16},{8,24},{16,32},{24,40},{32,48},{40,56},{48,64},{56,72},{64,... | collective-permute-start | bytes 798728 | tf_op jit(solution)/shard_map/ppermute | solution.py:26
  414.8 16.7 %collective-permute-start.9 = (f32[8,8320]{1,0:T(8,128)S(1)}, f32[8,8320]{1,0:T(8,128)S(1)}, u32[]{:S(2)}, u32[]{:S(2)}) collective-permute-start(f32[8,8320]{1,0:T(8,128)S(1)} %pad_maximum_fusion.8), channel_id=1, source_target_pairs={{32,0},{40,8},{48,16},{56,24},{64,32},{72,40},{80,48},{88,56},{96,... | collective-permute-start | bytes 798728 | tf_op jit(solution)/shard_map/ppermute | solution.py:26
  416.6 16.3 %collective-permute-start.2 = (f32[8,8320]{1,0:T(8,128)S(1)}, f32[8,8320]{1,0:T(8,128)S(1)}, u32[]{:S(2)}, u32[]{:S(2)}) collective-permute-start(f32[8,8320]{1,0:T(8,128)S(1)} %pad_maximum_fusion.3), channel_id=1, source_target_pairs={{0,32},{8,40},{16,48},{24,56},{32,64},{40,72},{48,80},{56,88},{64,... | collective-permute-start | bytes 798728 | tf_op jit(solution)/shard_map/ppermute | solution.py:26
  431.6 14.0 %collective-permute-start.10 = (f32[8,8320]{1,0:T(8,128)S(1)}, f32[8,8320]{1,0:T(8,128)S(1)}, u32[]{:S(2)}, u32[]{:S(2)}) collective-permute-start(f32[8,8320]{1,0:T(8,128)S(1)} %pad_maximum_fusion.9), channel_id=1, source_target_pairs={{64,0},{72,8},{80,16},{88,24},{96,32},{104,40},{112,48},{120,56},{... | collective-permute-start | bytes 798728 | tf_op jit(solution)/shard_map/ppermute | solution.py:26
  433.0 23.4 %collective-permute-start.3 = (f32[8,8320]{1,0:T(8,128)S(1)}, f32[8,8320]{1,0:T(8,128)S(1)}, u32[]{:S(2)}, u32[]{:S(2)}) collective-permute-start(f32[8,8320]{1,0:T(8,128)S(1)} %pad_maximum_fusion.4), channel_id=1, source_target_pairs={{0,64},{8,72},{16,80},{24,88},{32,96},{40,104},{48,112},{56,120},{... | collective-permute-start | bytes 798728 | tf_op jit(solution)/shard_map/ppermute | solution.py:26
  445.7 20.8 %collective-permute-start.11 = (f32[8,8320]{1,0:T(8,128)S(1)}, f32[8,8320]{1,0:T(8,128)S(1)}, u32[]{:S(2)}, u32[]{:S(2)}) collective-permute-start(f32[8,8320]{1,0:T(8,128)S(1)} %pad_maximum_fusion.10), channel_id=1, source_target_pairs={{128,0},{136,8},{144,16},{152,24},{160,32},{168,40},{176,48},{184,... | collective-permute-start | bytes 798728 | tf_op jit(solution)/shard_map/ppermute | solution.py:26
  456.6 14.9 %collective-permute-start.4 = (f32[8,8320]{1,0:T(8,128)S(1)}, f32[8,8320]{1,0:T(8,128)S(1)}, u32[]{:S(2)}, u32[]{:S(2)}) collective-permute-start(f32[8,8320]{1,0:T(8,128)S(1)} %pad_maximum_fusion.5), channel_id=1, source_target_pairs={{0,128},{8,136},{16,144},{24,152},{32,160},{40,168},{48,176},{56,1... | collective-permute-start | bytes 798728 | tf_op jit(solution)/shard_map/ppermute | solution.py:26
  466.6 16.3 %collective-permute-start.12 = (f32[8,8320]{1,0:T(8,128)S(1)}, f32[8,8320]{1,0:T(8,128)S(1)}, u32[]{:S(2)}, u32[]{:S(2)}) collective-permute-start(f32[8,8320]{1,0:T(8,128)S(1)} %pad_maximum_fusion.11), channel_id=1, source_target_pairs={{256,0},{264,8},{272,16},{280,24},{288,32},{296,40},{304,48},{312,... | collective-permute-start | bytes 798728 | tf_op jit(solution)/shard_map/ppermute | solution.py:26
  471.6 14.3 %collective-permute-start.5 = (f32[8,8320]{1,0:T(8,128)S(1)}, f32[8,8320]{1,0:T(8,128)S(1)}, u32[]{:S(2)}, u32[]{:S(2)}) collective-permute-start(f32[8,8320]{1,0:T(8,128)S(1)} %pad_maximum_fusion.6), channel_id=1, source_target_pairs={{0,256},{8,264},{16,272},{24,280},{32,288},{40,296},{48,304},{56,3... | collective-permute-start | bytes 798728 | tf_op jit(solution)/shard_map/ppermute | solution.py:26
  483.0 11.6 %collective-permute-start.13 = (f32[8,8192]{1,0:T(8,128)S(1)}, f32[8,8192]{1,0:T(8,128)S(1)}, u32[]{:S(2)}, u32[]{:S(2)}) collective-permute-start(f32[8,8192]{1,0:T(8,128)S(1)} %fusion.65), channel_id=1, source_target_pairs={{8,0},{16,8},{24,16},{32,24},{40,32},{48,40},{56,48},{64,56},{72,6... | collective-permute-start | bytes 786440 | tf_op jit(solution)/shard_map/ppermute | solution.py:26
  486.1 9.2 %collective-permute-start.6 = (f32[8,8192]{1,0:T(8,128)S(1)}, f32[8,8192]{1,0:T(8,128)S(1)}, u32[]{:S(2)}, u32[]{:S(2)}) collective-permute-start(f32[8,8192]{1,0:T(8,128)S(1)} %fusion.71), channel_id=1, source_target_pairs={{0,8},{8,16},{16,24},{24,32},{32,40},{40,48},{48,56},{56,64},{64,7... | collective-permute-start | bytes 786440 | tf_op jit(solution)/shard_map/ppermute | solution.py:26
  497.0 1.1 copy-start.5
  497.9 3.8 copy-start.14
  498.1 0.6 copy-start.12
  498.8 0.6 copy-start.8
  509.5 4.3 copy-start.6
  509.5 4.3 copy-start.13
  513.8 0.6 copy-start.9
  513.8 7.4 %copy-start.3 = (bf16[256,1,1,128]{0,3,2,1:T(8,128)(2,1)S(1)}, bf16[256,1,1,128]{0,3,2,1:T(8,128)(2,1)}, u32[]{:S(2)}) copy-start(bf16[256,1,1,128]{0,3,2,1:T(8,128)(2,1)} %fusion.30) | copy-start | bytes 196612
  513.8 7.4 %copy-start.4 = (bf16[256,1,1,128]{0,3,2,1:T(8,128)(2,1)S(1)}, bf16[256,1,1,128]{0,3,2,1:T(8,128)(2,1)}, u32[]{:S(2)}) copy-start(bf16[256,1,1,128]{0,3,2,1:T(8,128)(2,1)} %fusion.29) | copy-start | bytes 196612
  513.8 7.4 %copy-start.11 = (f32[8]{0:T(128)S(1)}, f32[8]{0:T(128)}, u32[]{:S(2)}) copy-start(f32[8]{0:T(128)} %param.14) | copy-start | bytes 100
  513.8 7.4 %copy-start.15 = (f32[256,8]{0,1:T(8,128)S(1)}, f32[256,8]{0,1:T(8,128)}, u32[]{:S(2)}) copy-start(f32[256,8]{0,1:T(8,128)} %get-tuple-element.194) | copy-start | bytes 24580
  513.8 7.4 %copy-start.18 = (f32[8]{0:T(128)S(1)}, f32[8]{0:T(128)}, u32[]{:S(2)}) copy-start(f32[8]{0:T(128)} %param.13) | copy-start | bytes 100
  513.8 8.2 %copy-start.16 = (f32[512]{0:T(512)S(1)}, f32[512]{0:T(512)}, u32[]{:S(2)}) copy-start(f32[512]{0:T(512)} %mul.496) | copy-start | bytes 6148
  514.5 7.6 %copy-start.2 = (f32[256,8,64]{0,2,1:T(8,128)S(1)}, f32[256,8,64]{0,2,1:T(8,128)}, u32[]{:S(2)}) copy-start(f32[256,8,64]{0,2,1:T(8,128)} %get-tuple-element.201) | copy-start | bytes 1572868
  519.2 3.1 copy-start
  524.9 1.6 copy-start.1
  525.0 202.4 %reduce-scatter.3.cloned.1.call-start = ((), (), s32[]{:S(2)}) async-start(), calls=%async_computation.5 | async-start | bytes 2359296 | tf_op jit(solution)/shard_map/reduce_scatter | solution.py:161
Sparse Core Ops, SparseCore 0:
  11.1 69.3 all-gather.10
  82.6 116.5 all-gather.8
  202.3 62.4 all-gather.6
  267.3 118.5 all-gather.4
  525.1 101.4 reduce-scatter.4
  631.8 95.5 reduce-scatter.2

commit v2 on v1

--- a/solution.py
+++ b/solution.py
@@ -124,19 +124,49 @@
     return final
 
 
+def from_each(x, axis):
+    devices = lax.axis_size(axis)
+    got = [x]
+    for k in range(1, devices):
+        got.append(lax.ppermute(x, axis, [(i, (i + k) % devices) for i in range(devices)]))
+    return got
+
+
+def summed_over(part_for, axis):
+    devices, position = (lax.axis_size(axis), lax.axis_index(axis))
+    total = part_for(position)
+    for k in range(1, devices):
+        part = part_for((position + k) % devices)
+        total = total + lax.ppermute(
+            part, axis, [(i, (i + k) % devices) for i in range(devices)]
+        )
+    return total
+
+
+def row_block(w, index, size):
+    return lax.dynamic_slice_in_dim(w, index * size, size, axis=0)
+
+
 def per_device(tokens, w_in, w_bc, w_dt, dt_bias, decay_rate, skip_gain, w_out, cotangent):
-    full_tokens = lax.all_gather(tokens, "tp", axis=1, tiled=True)
-    rows = full_tokens.shape[0]
+    devices, position = (lax.axis_size("tp"), lax.axis_index("tp"))
+    rows, width = tokens.shape
     heads = decay_rate.shape[0]
     inner = w_in.shape[1]
     pair_cols = w_bc.shape[1]
     groups = pair_cols // (2 * STATE)
-    w_cat = jnp.concatenate([w_in, w_bc, w_dt], axis=1)
-    whole_in, whole_out = (
-        lax.all_gather(w_cat, "ctx", axis=0, tiled=True),
-        lax.all_gather(w_out, "ctx", axis=1, tiled=True),
-    )
-    projected = jnp.dot(full_tokens, whole_in, preferred_element_type=jnp.float32)
+    out_cols = w_out.shape[0]
+    w_all = lax.all_gather(
+        jnp.concatenate([w_out.T, w_in, w_bc, w_dt], axis=1), "ctx", axis=0, tiled=True
+    )
+    pieces = from_each(jnp.concatenate([tokens, cotangent], axis=1), "tp")
+    projected = None
+    d_flat = None
+    for k in range(devices):
+        block = row_block(w_all, (position - k) % devices, width)
+        term = jnp.dot(pieces[k][:, :width], block[:, out_cols:], preferred_element_type=jnp.float32)
+        projected = term if projected is None else projected + term
+        term = jnp.dot(pieces[k][:, width:], block[:, :out_cols], preferred_element_type=jnp.float32)
+        d_flat = term if d_flat is None else d_flat + term
     values = projected[:, :inner].astype(jnp.bfloat16)
     pairs = projected[:, inner : inner + pair_cols].astype(jnp.bfloat16)
     pre_step = projected[:, inner + pair_cols :] + dt_bias[None, :]
@@ -145,7 +175,6 @@
     paired = pairs.astype(jnp.float32).reshape(rows, groups, 2, STATE)
     b_rows = paired[:, :, 0]
     c_rows = paired[:, :, 1]
-    zero_state = jnp.zeros((heads, HEADDIM, STATE), jnp.float32)
     end_state = local_states(value_f, b_rows, step_size, decay_rate)
     decay_total = jnp.exp(-jnp.sum(step_size * decay_rate[None, :], axis=0))
     state_in = carried_in(decay_total, end_state, "ctx", False)
@@ -157,14 +186,14 @@
     mixed = (
         (core_out + skip_gain[None, :, None] * value_f).reshape(rows, inner).astype(jnp.bfloat16)
     )
-    partial_out = jnp.dot(mixed, whole_out, preferred_element_type=jnp.float32)
-    output = lax.psum_scatter(partial_out, "tp", scatter_dimension=1, tiled=True).astype(
-        jnp.bfloat16
-    )
-    full_cotangent = lax.all_gather(cotangent, "tp", axis=1, tiled=True)
-    d_flat = lax.dot_general(
-        full_cotangent, whole_out, (((1,), (1,)), ((), ())), preferred_element_type=jnp.float32
-    )
+
+    def out_part(dest):
+        block = row_block(w_all, dest, width)[:, :out_cols]
+        return lax.dot_general(
+            mixed, block, (((1,), (1,)), ((), ())), preferred_element_type=jnp.float32
+        )
+
+    output = summed_over(out_part, "tp").astype(jnp.bfloat16)
     d_mixed = d_flat.reshape(rows, heads, HEADDIM)
     own_adjoint = local_adjoint(d_mixed, c_rows, step_size, decay_rate)
     adjoint = carried_in(decay_total, own_adjoint, "ctx", True)
@@ -180,12 +209,14 @@
         ],
         axis=1,
     )
-    partial_grad = lax.dot_general(
-        d_cat, whole_in, (((1,), (1,)), ((), ())), preferred_element_type=jnp.float32
-    )
-    grad = lax.psum_scatter(partial_grad, "tp", scatter_dimension=1, tiled=True).astype(
-        jnp.bfloat16
-    )
+
+    def grad_part(dest):
+        block = row_block(w_all, dest, width)[:, out_cols:]
+        return lax.dot_general(
+            d_cat, block, (((1,), (1,)), ((), ())), preferred_element_type=jnp.float32
+        )
+
+    grad = summed_over(grad_part, "tp").astype(jnp.bfloat16)
     return (output, grad)
 
 

time: 737 us -> 493 us (0.67)
  waiting for transfers between devices: 613 us -> 228 us
  starting transfers between devices: 51.4 us -> 166 us
  matrix products: 32.5 us -> 58.8 us
    all_gather x4 -> x1, waiting for transfers between devices: 371 us -> 131 us  [per_device(): lax.all_gather(jnp.concatenate([w_out.T, w_in, w_bc, w_dt], axis=1), 'ctx...]
    reduce_scatter x2 -> x0, waiting for transfers between devices: 197 us -> none  [the longest x1 99.1 us: per_device(): lax.psum_scatter(partial_out, 'tp', scatter_dimension=1, tiled=True)]
    ppermute x0 -> x21, starting transfers between devices: none -> 88.9 us  [the longest x14 55.6 us: summed_over(): lax.ppermute(part, axis, [(i, (i + k) % devices) for i in range(devices)])]
    ppermute x0 -> x21, waiting for transfers between devices: none -> 74 us  [the longest x14 63.5 us: summed_over(): lax.ppermute(part, axis, [(i, (i + k) % devices) for i in range(devices)])]
    ppermute x14, starting transfers between devices: 51.1 us -> 76.6 us  [shifted(): return lax.ppermute(x, axis, perm)]
    dot_general x4 -> x32, matrix products: 11 us -> 35.5 us  [the longest x8 11.1 us: per_device(): jnp.dot(pieces[k][:, :width], block[:, out_cols:], preferred_element_type...]
    ppermute x14, waiting for transfers between devices: 43 us -> 22.9 us  [shifted(): return lax.ppermute(x, axis, perm)]
  transfers between devices with their start and end apart: 20 -> 36, of which waited for: 16 -> 21; matrix products, arithmetic and copies ran while one was open for 2% -> 7% of each run, Pallas kernels for 0% -> 0%
where the time goes in v2:
time: 493 us; the launch traced here: 491 us
  waiting for transfers between devices  228 us (46%)
  starting transfers between devices  166 us (34%)
  matrix products  58.8 us (12%)
  other arithmetic  15.7 us (3%)
  between operations  15.2 us (3%)
  local copies, waits for them, and re-layouts  7.83 us (2%)
    all_gather x1, waiting for transfers between devices, per_device(): lax.all_gather(jnp.concatenate([w_out.T, w_in, w_bc, w_dt], axis=1), 'ctx...  131 us
    ppermute x14, starting transfers between devices, shifted(): return lax.ppermute(x, axis, perm)  76.6 us
    ppermute x14, waiting for transfers between devices, summed_over(): lax.ppermute(part, axis, [(i, (i + k) % devices) for i in range(devices)])  63.5 us
    ppermute x14, starting transfers between devices, summed_over(): lax.ppermute(part, axis, [(i, (i + k) % devices) for i in range(devices)])  55.6 us
    ppermute x7, starting transfers between devices, from_each(): lax.ppermute(x, axis, [(i, (i + k) % devices) for i in range(devices)])  33.3 us
    ppermute x14, waiting for transfers between devices, shifted(): return lax.ppermute(x, axis, perm)  22.9 us
    dot_general x3, matrix products, ssd_advance(): inside = jnp.einsum('hts,shp->thp', scores * weight, inputs, precision=HIGH)  11.6 us
    dot_general x8, matrix products, per_device(): jnp.dot(pieces[k][:, :width], block[:, out_cols:], preferred_element_type...  11.1 us
  transfers between devices with their start and end apart: 36, of which 21 were waited for; matrix products, arithmetic and copies ran while one was open for 7% of the time, Pallas kernels for 0%

profile of v2, /device:TPU:1, one launch (start us, length us, event | category | flops | bytes accessed | tf_op | source)
XLA Modules:
  0.0 490.9 jit_solution(12874036346795955105)
XLA Ops:
  8.0 1.4 pad_maximum_fusion.14
  11.3 10.5 %collective-permute-start.6 = (bf16[256,512]{1,0:T(8,128)(2,1)S(1)}, bf16[256,512]{1,0:T(8,128)(2,1)S(1)}, u32[]{:S(2)}, u32[]{:S(2)}) collective-permute-start(bf16[256,512]{1,0:T(8,128)(2,1)S(1)} %constant_dynamic-update-slice_fusion), channel_id=1, source_target_pairs={{0,7},{1,0},{2,1},{3,2},{4,3},{5,4},{6,5},{7,6},{8,15},{9,8},{10,9... | collective-permute-start | bytes 786440 | tf_op jit(solution)/shard_map/ppermute | solution.py:131
  21.8 2.4 collective-permute-start.5
  24.2 2.1 collective-permute-start.4
  26.3 7.5 %collective-permute-start.3 = (bf16[256,512]{1,0:T(8,128)(2,1)S(1)}, bf16[256,512]{1,0:T(8,128)(2,1)S(1)}, u32[]{:S(2)}, u32[]{:S(2)}) collective-permute-start(bf16[256,512]{1,0:T(8,128)(2,1)S(1)} %constant_dynamic-update-slice_fusion), channel_id=1, source_target_pairs={{0,4},{1,5},{2,6},{3,7},{4,0},{5,1},{6,2},{7,3},{8,12},{9,13},{10,... | collective-permute-start | bytes 786440 | tf_op jit(solution)/shard_map/ppermute | solution.py:131
  33.7 1.9 collective-permute-start.2
  36.3 130.9 %all-gather.2.cloned.1.call-done = bf16[2048,1288]{1,0:T(8,128)(2,1)} async-done(((bf16[32,1288]{1,0:T(8,128)(2,1)}), bf16[2048,1288]{1,0:T(8,128)(2,1)}) %all-gather.2.cloned.1.call-update) | async-done | bytes 5275664 | tf_op jit(solution)/shard_map/all_gather | solution.py:158
  167.2 1.4 convolution_bitcast_fusion
  168.6 1.9 collective-permute-start.1
  171.9 7.1 %collective-permute-start = (bf16[256,512]{1,0:T(8,128)(2,1)S(1)}, bf16[256,512]{1,0:T(8,128)(2,1)S(1)}, u32[]{:S(2)}, u32[]{:S(2)}) collective-permute-start(bf16[256,512]{1,0:T(8,128)(2,1)S(1)} %constant_dynamic-update-slice_fusion), channel_id=1, source_target_pairs={{0,1},{1,2},{2,3},{3,4},{4,5},{5,6},{6,7},{7,0},{8,9},{9,10},{10,1... | collective-permute-start | bytes 786440 | tf_op jit(solution)/shard_map/ppermute | solution.py:131
  184.3 3.4 collective-permute-done.1
  187.8 1.4 fusion.110
  189.2 7.1 %collective-permute-done = bf16[256,512]{1,0:T(8,128)(2,1)S(1)} collective-permute-done((bf16[256,512]{1,0:T(8,128)(2,1)S(1)}, bf16[256,512]{1,0:T(8,128)(2,1)S(1)}, u32[]{:S(2)}, u32[]{:S(2)}) %collective-permute-start) | collective-permute-done | bytes 262176 | tf_op jit(solution)/shard_map/ppermute | solution.py:131
  196.3 1.6 fusion.208
  213.6 1.3 fusion.44
  216.1 12.6 %collective-permute-start.21 = (f32[8,8320]{1,0:T(8,128)S(1)}, f32[8,8320]{1,0:T(8,128)S(1)}, u32[]{:S(2)}, u32[]{:S(2)}) collective-permute-start(f32[8,8320]{1,0:T(8,128)S(1)} %get-tuple-element.208), channel_id=1, source_target_pairs={{8,0},{16,8},{24,16},{32,24},{40,32},{48,40},{56,48},{64,56},{72,6... | collective-permute-start | bytes 798728 | tf_op jit(solution)/shard_map/ppermute | solution.py:26
  228.7 2.5 collective-permute-start.7
  235.0 3.6 collective-permute-start.8
  240.1 3.2 collective-permute-done.8
  243.5 4.3 collective-permute-start.9
  249.5 2.0 collective-permute-done.9
  251.6 7.4 %collective-permute-start.10 = (f32[8,8320]{1,0:T(8,128)S(1)}, f32[8,8320]{1,0:T(8,128)S(1)}, u32[]{:S(2)}, u32[]{:S(2)}) collective-permute-start(f32[8,8320]{1,0:T(8,128)S(1)} %pad_maximum_fusion.5), channel_id=1, source_target_pairs={{0,64},{8,72},{16,80},{24,88},{32,96},{40,104},{48,112},{56,120},{... | collective-permute-start | bytes 798728 | tf_op jit(solution)/shard_map/ppermute | solution.py:26
  259.0 3.2 collective-permute-done.23
  264.0 15.7 %collective-permute-start.11 = (f32[8,8320]{1,0:T(8,128)S(1)}, f32[8,8320]{1,0:T(8,128)S(1)}, u32[]{:S(2)}, u32[]{:S(2)}) collective-permute-start(f32[8,8320]{1,0:T(8,128)S(1)} %pad_maximum_fusion.6), channel_id=1, source_target_pairs={{0,128},{8,136},{16,144},{24,152},{32,160},{40,168},{48,176},{56,1... | collective-permute-start | bytes 798728 | tf_op jit(solution)/shard_map/ppermute | solution.py:26
  279.7 1.9 collective-permute-done.24
  281.7 1.4 collective-permute-start.25
  283.5 14.7 %collective-permute-start.12 = (f32[8,8320]{1,0:T(8,128)S(1)}, f32[8,8320]{1,0:T(8,128)S(1)}, u32[]{:S(2)}, u32[]{:S(2)}) collective-permute-start(f32[8,8320]{1,0:T(8,128)S(1)} %pad_maximum_fusion.7), channel_id=1, source_target_pairs={{0,256},{8,264},{16,272},{24,280},{32,288},{40,296},{48,304},{56,3... | collective-permute-start | bytes 798728 | tf_op jit(solution)/shard_map/ppermute | solution.py:26
  298.3 2.1 collective-permute-done.25
  300.5 1.4 collective-permute-start.26
  302.8 5.1 %collective-permute-start.13 = (f32[8,8192]{1,0:T(8,128)S(1)}, f32[8,8192]{1,0:T(8,128)S(1)}, u32[]{:S(2)}, u32[]{:S(2)}) collective-permute-start(f32[8,8192]{1,0:T(8,128)S(1)} %fusion.149), channel_id=1, source_target_pairs={{0,8},{8,16},{16,24},{24,32},{32,40},{40,48},{48,56},{56,64},{64,7... | collective-permute-start | bytes 786440 | tf_op jit(solution)/shard_map/ppermute | solution.py:26
  307.9 8.0 %collective-permute-done.26 = f32[8,8320]{1,0:T(8,128)S(1)} collective-permute-done((f32[8,8320]{1,0:T(8,128)S(1)}, f32[8,8320]{1,0:T(8,128)S(1)}, u32[]{:S(2)}, u32[]{:S(2)}) %collective-permute-start.26) | collective-permute-done | bytes 266272 | tf_op jit(solution)/shard_map/ppermute | solution.py:26
  316.1 3.9 collective-permute-start.27
  320.1 3.3 fusion.16
  325.0 2.2 fusion.24
  329.1 1.8 fusion.36
  333.3 3.8 fusion.32
  337.1 4.5 multiply_reduce_fusion.1
  344.7 2.5 reduce-window.44
  348.6 1.4 fusion.134
  350.0 2.7 collective-permute-start.20
  354.4 1.4 fusion.85
  355.8 1.9 collective-permute-start.34
  359.0 10.1 %collective-permute-start.19 = (f32[256,256]{1,0:T(8,128)S(1)}, f32[256,256]{1,0:T(8,128)S(1)}, u32[]{:S(2)}, u32[]{:S(2)}) collective-permute-start(f32[256,256]{1,0:T(8,128)S(1)} %fusion.136), channel_id=1, source_target_pairs={{0,6},{1,7},{2,0},{3,1},{4,2},{5,3},{6,4},{7,5},{8,14},{9,15},{10,... | collective-permute-start | bytes 786440 | tf_op jit(solution)/shard_map/ppermute | solution.py:140
  369.1 1.4 fusion.87
  370.5 2.1 collective-permute-start.33
  373.9 2.9 collective-permute-start.18
  376.8 1.4 fusion.97
  381.6 7.2 %collective-permute-start.17 = (f32[256,256]{1,0:T(8,128)S(1)}, f32[256,256]{1,0:T(8,128)S(1)}, u32[]{:S(2)}, u32[]{:S(2)}) collective-permute-start(f32[256,256]{1,0:T(8,128)S(1)} %fusion.140), channel_id=1, source_target_pairs={{0,4},{1,5},{2,6},{3,7},{4,0},{5,1},{6,2},{7,3},{8,12},{9,13},{10,... | collective-permute-start | bytes 786440 | tf_op jit(solution)/shard_map/ppermute | solution.py:140
  388.8 8.9 %collective-permute-done.34 = f32[256,256]{1,0:T(8,128)S(1)} collective-permute-done((f32[256,256]{1,0:T(8,128)S(1)}, f32[256,256]{1,0:T(8,128)S(1)}, u32[]{:S(2)}, u32[]{:S(2)}) %collective-permute-start.34) | collective-permute-done | bytes 262176 | tf_op jit(solution)/shard_map/ppermute | solution.py:140
  397.7 1.9 collective-permute-start.16
  399.6 14.1 %collective-permute-done.19 = f32[256,256]{1,0:T(8,128)S(1)} collective-permute-done((f32[256,256]{1,0:T(8,128)S(1)}, f32[256,256]{1,0:T(8,128)S(1)}, u32[]{:S(2)}, u32[]{:S(2)}) %collective-permute-start.19) | collective-permute-done | bytes 262176 | tf_op jit(solution)/shard_map/ppermute | solution.py:140
  413.7 1.9 collective-permute-start.15
  415.6 7.2 %collective-permute-done.33 = f32[256,256]{1,0:T(8,128)S(1)} collective-permute-done((f32[256,256]{1,0:T(8,128)S(1)}, f32[256,256]{1,0:T(8,128)S(1)}, u32[]{:S(2)}, u32[]{:S(2)}) %collective-permute-start.33) | collective-permute-done | bytes 262176 | tf_op jit(solution)/shard_map/ppermute | solution.py:140
  422.9 1.9 collective-permute-start.14
  425.9 6.1 %collective-permute-done.18 = f32[256,256]{1,0:T(8,128)S(1)} collective-permute-done((f32[256,256]{1,0:T(8,128)S(1)}, f32[256,256]{1,0:T(8,128)S(1)}, u32[]{:S(2)}, u32[]{:S(2)}) %collective-permute-start.18) | collective-permute-done | bytes 262176 | tf_op jit(solution)/shard_map/ppermute | solution.py:140
  432.0 9.0 %collective-permute-start.32 = (f32[256,256]{1,0:T(8,128)S(1)}, f32[256,256]{1,0:T(8,128)S(1)}, u32[]{:S(2)}, u32[]{:S(2)}) collective-permute-start(f32[256,256]{1,0:T(8,128)S(1)} %fusion.89), channel_id=1, source_target_pairs={{0,5},{1,6},{2,7},{3,0},{4,1},{5,2},{6,3},{7,4},{8,13},{9,14},{10,... | collective-permute-start | bytes 786440 | tf_op jit(solution)/shard_map/ppermute | solution.py:140
  441.1 4.7 collective-permute-start.31
  445.8 1.9 collective-permute-start.30
  447.8 3.6 collective-permute-done.15
  451.4 5.3 %collective-permute-start.29 = (f32[256,256]{1,0:T(8,128)S(1)}, f32[256,256]{1,0:T(8,128)S(1)}, u32[]{:S(2)}, u32[]{:S(2)}) collective-permute-start(f32[256,256]{1,0:T(8,128)S(1)} %fusion.95), channel_id=1, source_target_pairs={{0,2},{1,3},{2,4},{3,5},{4,6},{5,7},{6,0},{7,1},{8,10},{9,11},{10,... | collective-permute-start | bytes 786440 | tf_op jit(solution)/shard_map/ppermute | solution.py:140
  456.7 6.6 %collective-permute-done.14 = f32[256,256]{1,0:T(8,128)S(1)} collective-permute-done((f32[256,256]{1,0:T(8,128)S(1)}, f32[256,256]{1,0:T(8,128)S(1)}, u32[]{:S(2)}, u32[]{:S(2)}) %collective-permute-start.14) | collective-permute-done | bytes 262176 | tf_op jit(solution)/shard_map/ppermute | solution.py:140
  463.3 1.9 collective-permute-start.28
  466.2 7.7 %collective-permute-done.29 = f32[256,256]{1,0:T(8,128)S(1)} collective-permute-done((f32[256,256]{1,0:T(8,128)S(1)}, f32[256,256]{1,0:T(8,128)S(1)}, u32[]{:S(2)}, u32[]{:S(2)}) %collective-permute-start.29) | collective-permute-done | bytes 262176 | tf_op jit(solution)/shard_map/ppermute | solution.py:140
  473.9 9.2 %collective-permute-done.28 = f32[256,256]{1,0:T(8,128)S(1)} collective-permute-done((f32[256,256]{1,0:T(8,128)S(1)}, f32[256,256]{1,0:T(8,128)S(1)}, u32[]{:S(2)}, u32[]{:S(2)}) %collective-permute-start.28) | collective-permute-done | bytes 262176 | tf_op jit(solution)/shard_map/ppermute | solution.py:140
  (214 shorter events, 58.1 us)
Async XLA Ops:
  7.2 160.0 %all-gather.2.cloned.1.call-start = ((), (), s32[]{:S(2)}) async-start(), calls=%async_computation | async-start | bytes 5857280 | tf_op jit(solution)/shard_map/all_gather | solution.py:158
  11.3 157.3 %collective-permute-start.6 = (bf16[256,512]{1,0:T(8,128)(2,1)S(1)}, bf16[256,512]{1,0:T(8,128)(2,1)S(1)}, u32[]{:S(2)}, u32[]{:S(2)}) collective-permute-start(bf16[256,512]{1,0:T(8,128)(2,1)S(1)} %constant_dynamic-update-slice_fusion), channel_id=1, source_target_pairs={{0,7},{1,0},{2,1},{3,2},{4,3},{5,4},{6,5},{7,6},{8,15},{9,8},{10,9... | collective-permute-start | bytes 786440 | tf_op jit(solution)/shard_map/ppermute | solution.py:131
  21.8 150.1 %collective-permute-start.5 = (bf16[256,512]{1,0:T(8,128)(2,1)S(1)}, bf16[256,512]{1,0:T(8,128)(2,1)S(1)}, u32[]{:S(2)}, u32[]{:S(2)}) collective-permute-start(bf16[256,512]{1,0:T(8,128)(2,1)S(1)} %constant_dynamic-update-slice_fusion), channel_id=1, source_target_pairs={{0,6},{1,7},{2,0},{3,1},{4,2},{5,3},{6,4},{7,5},{8,14},{9,15},{10,... | collective-permute-start | bytes 786440 | tf_op jit(solution)/shard_map/ppermute | solution.py:131
  24.2 156.1 %collective-permute-start.4 = (bf16[256,512]{1,0:T(8,128)(2,1)S(1)}, bf16[256,512]{1,0:T(8,128)(2,1)S(1)}, u32[]{:S(2)}, u32[]{:S(2)}) collective-permute-start(bf16[256,512]{1,0:T(8,128)(2,1)S(1)} %constant_dynamic-update-slice_fusion), channel_id=1, source_target_pairs={{0,5},{1,6},{2,7},{3,0},{4,1},{5,2},{6,3},{7,4},{8,13},{9,14},{10,... | collective-permute-start | bytes 786440 | tf_op jit(solution)/shard_map/ppermute | solution.py:131
  26.3 155.4 %collective-permute-start.3 = (bf16[256,512]{1,0:T(8,128)(2,1)S(1)}, bf16[256,512]{1,0:T(8,128)(2,1)S(1)}, u32[]{:S(2)}, u32[]{:S(2)}) collective-permute-start(bf16[256,512]{1,0:T(8,128)(2,1)S(1)} %constant_dynamic-update-slice_fusion), channel_id=1, source_target_pairs={{0,4},{1,5},{2,6},{3,7},{4,0},{5,1},{6,2},{7,3},{8,12},{9,13},{10,... | collective-permute-start | bytes 786440 | tf_op jit(solution)/shard_map/ppermute | solution.py:131
  33.7 149.3 %collective-permute-start.2 = (bf16[256,512]{1,0:T(8,128)(2,1)S(1)}, bf16[256,512]{1,0:T(8,128)(2,1)S(1)}, u32[]{:S(2)}, u32[]{:S(2)}) collective-permute-start(bf16[256,512]{1,0:T(8,128)(2,1)S(1)} %constant_dynamic-update-slice_fusion), channel_id=1, source_target_pairs={{0,3},{1,4},{2,5},{3,6},{4,7},{5,0},{6,1},{7,2},{8,11},{9,12},{10,... | collective-permute-start | bytes 786440 | tf_op jit(solution)/shard_map/ppermute | solution.py:131
  168.6 19.2 %collective-permute-start.1 = (bf16[256,512]{1,0:T(8,128)(2,1)S(1)}, bf16[256,512]{1,0:T(8,128)(2,1)S(1)}, u32[]{:S(2)}, u32[]{:S(2)}) collective-permute-start(bf16[256,512]{1,0:T(8,128)(2,1)S(1)} %constant_dynamic-update-slice_fusion), channel_id=1, source_target_pairs={{0,2},{1,3},{2,4},{3,5},{4,6},{5,7},{6,0},{7,1},{8,10},{9,11},{10,... | collective-permute-start | bytes 786440 | tf_op jit(solution)/shard_map/ppermute | solution.py:131
  171.9 24.4 %collective-permute-start = (bf16[256,512]{1,0:T(8,128)(2,1)S(1)}, bf16[256,512]{1,0:T(8,128)(2,1)S(1)}, u32[]{:S(2)}, u32[]{:S(2)}) collective-permute-start(bf16[256,512]{1,0:T(8,128)(2,1)S(1)} %constant_dynamic-update-slice_fusion), channel_id=1, source_target_pairs={{0,1},{1,2},{2,3},{3,4},{4,5},{5,6},{6,7},{7,0},{8,9},{9,10},{10,1... | collective-permute-start | bytes 786440 | tf_op jit(solution)/shard_map/ppermute | solution.py:131
  181.6 17.2 %copy-start.21 = (f32[8]{0:T(128)S(1)}, f32[8]{0:T(128)}, u32[]{:S(2)}) copy-start(f32[8]{0:T(128)} %param.14) | copy-start | bytes 100
  181.6 17.2 %copy-start.28 = (f32[8]{0:T(128)S(1)}, f32[8]{0:T(128)}, u32[]{:S(2)}) copy-start(f32[8]{0:T(128)} %param.13) | copy-start | bytes 100
  197.9 13.1 %copy-start.7 = (bf16[256,256]{1,0:T(8,128)(2,1)S(1)}, bf16[256,256]{1,0:T(8,128)(2,1)}, u32[]{:S(2)}) copy-start(bf16[256,256]{1,0:T(8,128)(2,1)} %param.17) | copy-start | bytes 393220
  199.6 11.4 %copy-start.13 = (f32[8,2,128]{2,0,1:T(8,128)}, f32[8,2,128]{2,0,1:T(8,128)S(1)}, u32[]{:S(2)}) copy-start(f32[8,2,128]{2,0,1:T(8,128)S(1)} %reduce-window.40) | copy-start | bytes 24580
  203.4 11.6 %copy-start.4 = (f32[256,128]{1,0:T(8,128)}, f32[256,128]{1,0:T(8,128)S(1)}, u32[]{:S(2)}) copy-start(f32[256,128]{1,0:T(8,128)S(1)} %copy.90) | copy-start | bytes 393220
  203.5 11.5 %copy-start.18 = (f32[256,8]{0,1:T(8,128)S(1)}, f32[256,8]{0,1:T(8,128)}, u32[]{:S(2)}) copy-start(f32[256,8]{0,1:T(8,128)} %exponential_multiply_fusion) | copy-start | bytes 24580
  203.5 11.5 %copy-start.27 = (f32[8]{0:T(128)S(1)}, f32[8]{0:T(128)}, u32[]{:S(2)}) copy-start(f32[8]{0:T(128)} %exponential_multiply_fusion.2) | copy-start | bytes 100
  207.3 8.7 %copy-start.26 = (f32[8]{0:T(128)S(1)}, f32[8]{0:T(128)}, u32[]{:S(2)}) copy-start(f32[8]{0:T(128)} %negate_exponential_fusion) | copy-start | bytes 100
  208.5 23.3 %copy-start.29 = (f32[8]{0:T(128)S(1)}, f32[8]{0:T(128)}, u32[]{:S(2)}) copy-start(f32[8]{0:T(128)} %param.15) | copy-start | bytes 100
  216.1 17.3 %collective-permute-start.21 = (f32[8,8320]{1,0:T(8,128)S(1)}, f32[8,8320]{1,0:T(8,128)S(1)}, u32[]{:S(2)}, u32[]{:S(2)}) collective-permute-start(f32[8,8320]{1,0:T(8,128)S(1)} %get-tuple-element.208), channel_id=1, source_target_pairs={{8,0},{16,8},{24,16},{32,24},{40,32},{48,40},{56,48},{64,56},{72,6... | collective-permute-start | bytes 798728 | tf_op jit(solution)/shard_map/ppermute | solution.py:26
  228.7 5.9 %collective-permute-start.7 = (f32[8,8320]{1,0:T(8,128)S(1)}, f32[8,8320]{1,0:T(8,128)S(1)}, u32[]{:S(2)}, u32[]{:S(2)}) collective-permute-start(f32[8,8320]{1,0:T(8,128)S(1)} %get-tuple-element.209), channel_id=1, source_target_pairs={{0,8},{8,16},{16,24},{24,32},{32,40},{40,48},{48,56},{56,64},{64,7... | collective-permute-start | bytes 798728 | tf_op jit(solution)/shard_map/ppermute | solution.py:26
  235.0 8.4 %collective-permute-start.8 = (f32[8,8320]{1,0:T(8,128)S(1)}, f32[8,8320]{1,0:T(8,128)S(1)}, u32[]{:S(2)}, u32[]{:S(2)}) collective-permute-start(f32[8,8320]{1,0:T(8,128)S(1)} %pad_maximum_fusion.3), channel_id=1, source_target_pairs={{0,16},{8,24},{16,32},{24,40},{32,48},{40,56},{48,64},{56,72},{64,... | collective-permute-start | bytes 798728 | tf_op jit(solution)/shard_map/ppermute | solution.py:26
  238.6 9.2 %collective-permute-start.22 = (f32[8,8320]{1,0:T(8,128)S(1)}, f32[8,8320]{1,0:T(8,128)S(1)}, u32[]{:S(2)}, u32[]{:S(2)}) collective-permute-start(f32[8,8320]{1,0:T(8,128)S(1)} %pad_maximum_fusion.8), channel_id=1, source_target_pairs={{16,0},{24,8},{32,16},{40,24},{48,32},{56,40},{64,48},{72,56},{80,... | collective-permute-start | bytes 798728 | tf_op jit(solution)/shard_map/ppermute | solution.py:26
  243.4 76.5 %copy-start.14 = (f32[8,2,128]{2,0,1:T(8,128)S(1)}, f32[8,2,128]{2,0,1:T(8,128)}, u32[]{:S(2)}) copy-start(f32[8,2,128]{2,0,1:T(8,128)} %copy-done.13) | copy-start | bytes 24580
  243.5 76.6 %copy-start.16 = (pred[256,256]{1,0:T(8,128)(4,1)S(1)}, pred[256,256]{1,0:T(8,128)(4,1)}, u32[]{:S(2)}) copy-start(pred[256,256]{1,0:T(8,128)(4,1)} %iota_compare_fusion.1) | copy-start | bytes 196612
  243.5 8.0 %collective-permute-start.9 = (f32[8,8320]{1,0:T(8,128)S(1)}, f32[8,8320]{1,0:T(8,128)S(1)}, u32[]{:S(2)}, u32[]{:S(2)}) collective-permute-start(f32[8,8320]{1,0:T(8,128)S(1)} %pad_maximum_fusion.4), channel_id=1, source_target_pairs={{0,32},{8,40},{16,48},{24,56},{32,64},{40,72},{48,80},{56,88},{64,... | collective-permute-start | bytes 798728 | tf_op jit(solution)/shard_map/ppermute | solution.py:26
  248.0 14.2 %collective-permute-start.23 = (f32[8,8320]{1,0:T(8,128)S(1)}, f32[8,8320]{1,0:T(8,128)S(1)}, u32[]{:S(2)}, u32[]{:S(2)}) collective-permute-start(f32[8,8320]{1,0:T(8,128)S(1)} %pad_maximum_fusion.9), channel_id=1, source_target_pairs={{32,0},{40,8},{48,16},{56,24},{64,32},{72,40},{80,48},{88,56},{96,... | collective-permute-start | bytes 798728 | tf_op jit(solution)/shard_map/ppermute | solution.py:26
  251.6 12.2 %collective-permute-start.10 = (f32[8,8320]{1,0:T(8,128)S(1)}, f32[8,8320]{1,0:T(8,128)S(1)}, u32[]{:S(2)}, u32[]{:S(2)}) collective-permute-start(f32[8,8320]{1,0:T(8,128)S(1)} %pad_maximum_fusion.5), channel_id=1, source_target_pairs={{0,64},{8,72},{16,80},{24,88},{32,96},{40,104},{48,112},{56,120},{... | collective-permute-start | bytes 798728 | tf_op jit(solution)/shard_map/ppermute | solution.py:26
  262.3 19.3 %collective-permute-start.24 = (f32[8,8320]{1,0:T(8,128)S(1)}, f32[8,8320]{1,0:T(8,128)S(1)}, u32[]{:S(2)}, u32[]{:S(2)}) collective-permute-start(f32[8,8320]{1,0:T(8,128)S(1)} %pad_maximum_fusion.10), channel_id=1, source_target_pairs={{64,0},{72,8},{80,16},{88,24},{96,32},{104,40},{112,48},{120,56},{... | collective-permute-start | bytes 798728 | tf_op jit(solution)/shard_map/ppermute | solution.py:26
  263.9 59.9 %copy-start.22 = (f32[8]{0:T(128)S(1)}, f32[8]{0:T(128)}, u32[]{:S(2)}) copy-start(f32[8]{0:T(128)} %param.14) | copy-start | bytes 100
  263.9 61.0 %copy-start.5 = (f32[256,128]{1,0:T(8,128)S(1)}, f32[256,128]{1,0:T(8,128)}, u32[]{:S(2)}) copy-start(f32[256,128]{1,0:T(8,128)} %copy-done.4) | copy-start | bytes 393220
  264.0 61.0 %copy-start.15 = (f32[256,8]{0,1:T(8,128)S(1)}, f32[256,8]{0,1:T(8,128)}, u32[]{:S(2)}) copy-start(f32[256,8]{0,1:T(8,128)} %get-tuple-element.199) | copy-start | bytes 24580
  264.0 19.4 %collective-permute-start.11 = (f32[8,8320]{1,0:T(8,128)S(1)}, f32[8,8320]{1,0:T(8,128)S(1)}, u32[]{:S(2)}, u32[]{:S(2)}) collective-permute-start(f32[8,8320]{1,0:T(8,128)S(1)} %pad_maximum_fusion.6), channel_id=1, source_target_pairs={{0,128},{8,136},{16,144},{24,152},{32,160},{40,168},{48,176},{56,1... | collective-permute-start | bytes 798728 | tf_op jit(solution)/shard_map/ppermute | solution.py:26
  281.7 46.0 %copy-start = (f32[256,1,128]{0,2,1:T(8,128)S(1)}, f32[256,1,128]{0,2,1:T(8,128)}, u32[]{:S(2)}) copy-start(f32[256,1,128]{0,2,1:T(8,128)} %get-tuple-element.186) | copy-start | bytes 393220
  281.7 18.7 %collective-permute-start.25 = (f32[8,8320]{1,0:T(8,128)S(1)}, f32[8,8320]{1,0:T(8,128)S(1)}, u32[]{:S(2)}, u32[]{:S(2)}) collective-permute-start(f32[8,8320]{1,0:T(8,128)S(1)} %pad_maximum_fusion.11), channel_id=1, source_target_pairs={{128,0},{136,8},{144,16},{152,24},{160,32},{168,40},{176,48},{184,... | collective-permute-start | bytes 798728 | tf_op jit(solution)/shard_map/ppermute | solution.py:26
  283.5 19.2 %collective-permute-start.12 = (f32[8,8320]{1,0:T(8,128)S(1)}, f32[8,8320]{1,0:T(8,128)S(1)}, u32[]{:S(2)}, u32[]{:S(2)}) collective-permute-start(f32[8,8320]{1,0:T(8,128)S(1)} %pad_maximum_fusion.7), channel_id=1, source_target_pairs={{0,256},{8,264},{16,272},{24,280},{32,288},{40,296},{48,304},{56,3... | collective-permute-start | bytes 798728 | tf_op jit(solution)/shard_map/ppermute | solution.py:26
  300.5 30.4 %copy-start.2 = (f32[256,1,128]{0,2,1:T(8,128)S(1)}, f32[256,1,128]{0,2,1:T(8,128)}, u32[]{:S(2)}) copy-start(f32[256,1,128]{0,2,1:T(8,128)} %get-tuple-element.184) | copy-start | bytes 393220
  300.5 15.4 %collective-permute-start.26 = (f32[8,8320]{1,0:T(8,128)S(1)}, f32[8,8320]{1,0:T(8,128)S(1)}, u32[]{:S(2)}, u32[]{:S(2)}) collective-permute-start(f32[8,8320]{1,0:T(8,128)S(1)} %pad_maximum_fusion.12), channel_id=1, source_target_pairs={{256,0},{264,8},{272,16},{280,24},{288,32},{296,40},{304,48},{312,... | collective-permute-start | bytes 798728 | tf_op jit(solution)/shard_map/ppermute | solution.py:26
  302.8 20.6 %collective-permute-start.13 = (f32[8,8192]{1,0:T(8,128)S(1)}, f32[8,8192]{1,0:T(8,128)S(1)}, u32[]{:S(2)}, u32[]{:S(2)}) collective-permute-start(f32[8,8192]{1,0:T(8,128)S(1)} %fusion.149), channel_id=1, source_target_pairs={{0,8},{8,16},{16,24},{24,32},{32,40},{40,48},{48,56},{56,64},{64,7... | collective-permute-start | bytes 786440 | tf_op jit(solution)/shard_map/ppermute | solution.py:26
  316.1 7.7 %collective-permute-start.27 = (f32[8,8192]{1,0:T(8,128)S(1)}, f32[8,8192]{1,0:T(8,128)S(1)}, u32[]{:S(2)}, u32[]{:S(2)}) collective-permute-start(f32[8,8192]{1,0:T(8,128)S(1)} %fusion.114), channel_id=1, source_target_pairs={{8,0},{16,8},{24,16},{32,24},{40,32},{48,40},{56,48},{64,56},{72,6... | collective-permute-start | bytes 786440 | tf_op jit(solution)/shard_map/ppermute | solution.py:26
  320.1 13.2 %copy-start.17 = (pred[1,256,256]{2,1,0:T(8,128)(4,1)S(1)}, pred[1,256,256]{2,1,0:T(8,128)(4,1)}, u32[]{:S(2)}) copy-start(pred[1,256,256]{2,1,0:T(8,128)(4,1)} %iota_compare_fusion) | copy-start | bytes 196612
  324.9 8.4 %copy-start.25 = (f32[8,256]{1,0:T(8,128)}, f32[8,256]{1,0:T(8,128)S(1)}, u32[]{:S(2)}) copy-start(f32[8,256]{1,0:T(8,128)S(1)} %add_bitcast_fusion.1) | copy-start | bytes 24580
  325.0 8.3 %copy-start.11 = (f32[256,8]{0,1:T(8,128)}, f32[256,8]{0,1:T(8,128)S(1)}, u32[]{:S(2)}) copy-start(f32[256,8]{0,1:T(8,128)S(1)} %get-tuple-element.196) | copy-start | bytes 24580
  327.6 5.6 %copy-start.23 = (f32[8]{0:T(128)}, f32[8]{0:T(128)S(1)}, u32[]{:S(2)}) copy-start(f32[8]{0:T(128)S(1)} %get-tuple-element.207) | copy-start | bytes 100
  327.7 5.6 %copy-start.19 = (f32[256,8]{0,1:T(8,128)}, f32[256,8]{0,1:T(8,128)S(1)}, u32[]{:S(2)}) copy-start(f32[256,8]{0,1:T(8,128)S(1)} %subtract_exponential_fusion) | copy-start | bytes 24580
  333.3 8.3 %copy-start.3 = (f32[256,1,128]{0,2,1:T(8,128)S(1)}, f32[256,1,128]{0,2,1:T(8,128)}, u32[]{:S(2)}) copy-start(f32[256,1,128]{0,2,1:T(8,128)} %get-tuple-element.184) | copy-start | bytes 393220
  333.3 8.3 %copy-start.8 = (f32[256,128]{0,1:T(8,128)S(1)}, f32[256,128]{0,1:T(8,128)}, u32[]{:S(2)}) copy-start(f32[256,128]{0,1:T(8,128)} %convolution_bitcast_fusion.5) | copy-start | bytes 393220
  333.3 9.3 %copy-start.1 = (f32[256,1,128]{0,2,1:T(8,128)S(1)}, f32[256,1,128]{0,2,1:T(8,128)}, u32[]{:S(2)}) copy-start(f32[256,1,128]{0,2,1:T(8,128)} %get-tuple-element.186) | copy-start | bytes 393220
  337.1 6.5 %copy-start.12 = (f32[256,8]{0,1:T(8,128)S(1)}, f32[256,8]{0,1:T(8,128)}, u32[]{:S(2)}) copy-start(f32[256,8]{0,1:T(8,128)} %copy-done.11) | copy-start | bytes 24580
  337.1 6.5 %copy-start.24 = (f32[8]{0:T(128)S(1)}, f32[8]{0:T(128)}, u32[]{:S(2)}) copy-start(f32[8]{0:T(128)} %copy-done.23) | copy-start | bytes 100
  337.1 43.5 %slice-start = ((s8[5767168]{0:T(1024)(128)(4,1)}), s8[1572864]{0:T(1024)(128)(4,1)S(1)}, s32[]{:S(2)}) async-start(s8[5767168]{0:T(1024)(128)(4,1)} %bitcast.170), calls=%async_computation.1 | async-start | bytes 3145728
  348.6 32.0 %slice-start.1 = ((s8[5767168]{0:T(1024)(128)(4,1)}), s8[4194304]{0:T(1024)(128)(4,1)S(1)}, s32[]{:S(2)}) async-start(s8[5767168]{0:T(1024)(128)(4,1)} %bitcast.170), calls=%async_computation.2 | async-start | bytes 8388608
  350.0 31.6 %collective-permute-start.20 = (f32[256,256]{1,0:T(8,128)S(1)}, f32[256,256]{1,0:T(8,128)S(1)}, u32[]{:S(2)}, u32[]{:S(2)}) collective-permute-start(f32[256,256]{1,0:T(8,128)S(1)} %fusion.134), channel_id=1, source_target_pairs={{0,7},{1,0},{2,1},{3,2},{4,3},{5,4},{6,5},{7,6},{8,15},{9,8},{10,9... | collective-permute-start | bytes 786440 | tf_op jit(solution)/shard_map/ppermute | solution.py:140
  355.8 41.9 %collective-permute-start.34 = (f32[256,256]{1,0:T(8,128)S(1)}, f32[256,256]{1,0:T(8,128)S(1)}, u32[]{:S(2)}, u32[]{:S(2)}) collective-permute-start(f32[256,256]{1,0:T(8,128)S(1)} %fusion.85), channel_id=1, source_target_pairs={{0,7},{1,0},{2,1},{3,2},{4,3},{5,4},{6,5},{7,6},{8,15},{9,8},{10,9... | collective-permute-start | bytes 786440 | tf_op jit(solution)/shard_map/ppermute | solution.py:140
  359.0 54.7 %collective-permute-start.19 = (f32[256,256]{1,0:T(8,128)S(1)}, f32[256,256]{1,0:T(8,128)S(1)}, u32[]{:S(2)}, u32[]{:S(2)}) collective-permute-start(f32[256,256]{1,0:T(8,128)S(1)} %fusion.136), channel_id=1, source_target_pairs={{0,6},{1,7},{2,0},{3,1},{4,2},{5,3},{6,4},{7,5},{8,14},{9,15},{10,... | collective-permute-start | bytes 786440 | tf_op jit(solution)/shard_map/ppermute | solution.py:140
  370.5 52.4 %collective-permute-start.33 = (f32[256,256]{1,0:T(8,128)S(1)}, f32[256,256]{1,0:T(8,128)S(1)}, u32[]{:S(2)}, u32[]{:S(2)}) collective-permute-start(f32[256,256]{1,0:T(8,128)S(1)} %fusion.87), channel_id=1, source_target_pairs={{0,6},{1,7},{2,0},{3,1},{4,2},{5,3},{6,4},{7,5},{8,14},{9,15},{10,... | collective-permute-start | bytes 786440 | tf_op jit(solution)/shard_map/ppermute | solution.py:140
  373.9 58.2 %collective-permute-start.18 = (f32[256,256]{1,0:T(8,128)S(1)}, f32[256,256]{1,0:T(8,128)S(1)}, u32[]{:S(2)}, u32[]{:S(2)}) collective-permute-start(f32[256,256]{1,0:T(8,128)S(1)} %fusion.138), channel_id=1, source_target_pairs={{0,5},{1,6},{2,7},{3,0},{4,1},{5,2},{6,3},{7,4},{8,13},{9,14},{10,... | collective-permute-start | bytes 786440 | tf_op jit(solution)/shard_map/ppermute | solution.py:140
  381.6 59.5 %collective-permute-start.17 = (f32[256,256]{1,0:T(8,128)S(1)}, f32[256,256]{1,0:T(8,128)S(1)}, u32[]{:S(2)}, u32[]{:S(2)}) collective-permute-start(f32[256,256]{1,0:T(8,128)S(1)} %fusion.140), channel_id=1, source_target_pairs={{0,4},{1,5},{2,6},{3,7},{4,0},{5,1},{6,2},{7,3},{8,12},{9,13},{10,... | collective-permute-start | bytes 786440 | tf_op jit(solution)/shard_map/ppermute | solution.py:140
  397.7 48.1 %collective-permute-start.16 = (f32[256,256]{1,0:T(8,128)S(1)}, f32[256,256]{1,0:T(8,128)S(1)}, u32[]{:S(2)}, u32[]{:S(2)}) collective-permute-start(f32[256,256]{1,0:T(8,128)S(1)} %fusion.142), channel_id=1, source_target_pairs={{0,3},{1,4},{2,5},{3,6},{4,7},{5,0},{6,1},{7,2},{8,11},{9,12},{10,... | collective-permute-start | bytes 786440 | tf_op jit(solution)/shard_map/ppermute | solution.py:140
  413.7 37.7 %collective-permute-start.15 = (f32[256,256]{1,0:T(8,128)S(1)}, f32[256,256]{1,0:T(8,128)S(1)}, u32[]{:S(2)}, u32[]{:S(2)}) collective-permute-start(f32[256,256]{1,0:T(8,128)S(1)} %fusion.144), channel_id=1, source_target_pairs={{0,2},{1,3},{2,4},{3,5},{4,6},{5,7},{6,0},{7,1},{8,10},{9,11},{10,... | collective-permute-start | bytes 786440 | tf_op jit(solution)/shard_map/ppermute | solution.py:140
  422.9 40.4 %collective-permute-start.14 = (f32[256,256]{1,0:T(8,128)S(1)}, f32[256,256]{1,0:T(8,128)S(1)}, u32[]{:S(2)}, u32[]{:S(2)}) collective-permute-start(f32[256,256]{1,0:T(8,128)S(1)} %fusion.146), channel_id=1, source_target_pairs={{0,1},{1,2},{2,3},{3,4},{4,5},{5,6},{6,7},{7,0},{8,9},{9,10},{10,1... | collective-permute-start | bytes 786440 | tf_op jit(solution)/shard_map/ppermute | solution.py:140
  432.0 34.1 %collective-permute-start.32 = (f32[256,256]{1,0:T(8,128)S(1)}, f32[256,256]{1,0:T(8,128)S(1)}, u32[]{:S(2)}, u32[]{:S(2)}) collective-permute-start(f32[256,256]{1,0:T(8,128)S(1)} %fusion.89), channel_id=1, source_target_pairs={{0,5},{1,6},{2,7},{3,0},{4,1},{5,2},{6,3},{7,4},{8,13},{9,14},{10,... | collective-permute-start | bytes 786440 | tf_op jit(solution)/shard_map/ppermute | solution.py:140
  441.1 25.1 %collective-permute-start.31 = (f32[256,256]{1,0:T(8,128)S(1)}, f32[256,256]{1,0:T(8,128)S(1)}, u32[]{:S(2)}, u32[]{:S(2)}) collective-permute-start(f32[256,256]{1,0:T(8,128)S(1)} %fusion.91), channel_id=1, source_target_pairs={{0,4},{1,5},{2,6},{3,7},{4,0},{5,1},{6,2},{7,3},{8,12},{9,13},{10,... | collective-permute-start | bytes 786440 | tf_op jit(solution)/shard_map/ppermute | solution.py:140
  445.8 20.3 %collective-permute-start.30 = (f32[256,256]{1,0:T(8,128)S(1)}, f32[256,256]{1,0:T(8,128)S(1)}, u32[]{:S(2)}, u32[]{:S(2)}) collective-permute-start(f32[256,256]{1,0:T(8,128)S(1)} %fusion.93), channel_id=1, source_target_pairs={{0,3},{1,4},{2,5},{3,6},{4,7},{5,0},{6,1},{7,2},{8,11},{9,12},{10,... | collective-permute-start | bytes 786440 | tf_op jit(solution)/shard_map/ppermute | solution.py:140
  451.4 22.5 %collective-permute-start.29 = (f32[256,256]{1,0:T(8,128)S(1)}, f32[256,256]{1,0:T(8,128)S(1)}, u32[]{:S(2)}, u32[]{:S(2)}) collective-permute-start(f32[256,256]{1,0:T(8,128)S(1)} %fusion.95), channel_id=1, source_target_pairs={{0,2},{1,3},{2,4},{3,5},{4,6},{5,7},{6,0},{7,1},{8,10},{9,11},{10,... | collective-permute-start | bytes 786440 | tf_op jit(solution)/shard_map/ppermute | solution.py:140
  463.3 19.8 %collective-permute-start.28 = (f32[256,256]{1,0:T(8,128)S(1)}, f32[256,256]{1,0:T(8,128)S(1)}, u32[]{:S(2)}, u32[]{:S(2)}) collective-permute-start(f32[256,256]{1,0:T(8,128)S(1)} %fusion.97), channel_id=1, source_target_pairs={{0,1},{1,2},{2,3},{3,4},{4,5},{5,6},{6,7},{7,0},{8,9},{9,10},{10,1... | collective-permute-start | bytes 786440 | tf_op jit(solution)/shard_map/ppermute | solution.py:140
  (4 other events, 6.5 us)
Sparse Core Ops, SparseCore 0:
  10.7 156.4 all-gather.1

commit v3 on v2

--- a/solution.py
+++ b/solution.py
@@ -11,31 +11,52 @@
 HIGH = lax.Precision.HIGHEST
 
 
-def carried_in(decay, state, axis, reverse):
+def both_carries(decay, forward, backward, axis):
     devices, position = (lax.axis_size(axis), lax.axis_index(axis))
     heads = decay.shape[0]
-    packed = jnp.concatenate(
-        [state.reshape(heads, -1), jnp.broadcast_to(decay[:, None], (heads, 128))], axis=1
-    )
-
-    def shifted(x, shift):
-        if reverse:
-            perm = [(i + shift, i) for i in range(devices - shift)]
-        else:
-            perm = [(i, i + shift) for i in range(devices - shift)]
-        return lax.ppermute(x, axis, perm)
-
-    shift = 1
-    while shift < devices:
-        got = shifted(packed, shift)
-        own = packed[:, -128:]
-        reached = position < devices - shift if reverse else position >= shift
-        mixed_s = own[:, :1] * got[:, :-128] + packed[:, :-128]
-        mixed_a = jnp.where(reached, own * got[:, -128:], own)
-        packed = jnp.concatenate([mixed_s, mixed_a], axis=1)
-        shift *= 2
-    before = shifted(packed[:, :-128], 1)
-    return before.reshape(state.shape)
+    total_a = decay[:, None]
+    total_s = forward.reshape(heads, -1)
+    total_u = backward.reshape(heads, -1)
+    size = total_s.shape[1]
+    before_a = jnp.ones_like(total_a)
+    before_s = jnp.zeros_like(total_s)
+    after_a = jnp.ones_like(total_a)
+    after_u = jnp.zeros_like(total_u)
+    bit = 1
+    while bit < devices:
+        message = jnp.concatenate(
+            [total_s, total_u, jnp.broadcast_to(total_a, (heads, 128))], axis=1
+        )
+        got = lax.ppermute(message, axis, [(i, i ^ bit) for i in range(devices)])
+        got_s = got[:, :size]
+        got_u = got[:, size : 2 * size]
+        got_a = got[:, 2 * size : 2 * size + 1]
+        lower = (position & bit) != 0
+        before_s = jnp.where(lower, before_a * got_s + before_s, before_s)
+        before_a = jnp.where(lower, got_a * before_a, before_a)
+        after_u = jnp.where(lower, after_u, after_u + after_a * got_u)
+        after_a = jnp.where(lower, after_a, after_a * got_a)
+        total_s = jnp.where(lower, total_a * got_s + total_s, got_a * total_s + got_s)
+        total_u = jnp.where(lower, got_u + got_a * total_u, total_u + total_a * got_u)
+        total_a = total_a * got_a
+        bit *= 2
+    return before_s.reshape(forward.shape), after_u.reshape(backward.shape)
+
+
+def scattered_sum(partial, axis, width):
+    devices, position = (lax.axis_size(axis), lax.axis_index(axis))
+    rows = partial.shape[0]
+    blocks = partial.reshape(rows, devices, width)
+    bit = 1
+    while bit < devices:
+        count = blocks.shape[1]
+        paired = blocks.reshape(rows, count // 2, 2, width)
+        mine = (position & bit) != 0
+        keep = jnp.where(mine, paired[:, :, 1], paired[:, :, 0])
+        send = jnp.where(mine, paired[:, :, 0], paired[:, :, 1])
+        blocks = keep + lax.ppermute(send, axis, [(i, i ^ bit) for i in range(devices)])
+        bit *= 2
+    return blocks.reshape(rows, width)
 
 
 def ssd_core(values, b_rows, c_rows, step_size, decay_rate, state):
@@ -130,17 +151,6 @@
     for k in range(1, devices):
         got.append(lax.ppermute(x, axis, [(i, (i + k) % devices) for i in range(devices)]))
     return got
-
-
-def summed_over(part_for, axis):
-    devices, position = (lax.axis_size(axis), lax.axis_index(axis))
-    total = part_for(position)
-    for k in range(1, devices):
-        part = part_for((position + k) % devices)
-        total = total + lax.ppermute(
-            part, axis, [(i, (i + k) % devices) for i in range(devices)]
-        )
-    return total
 
 
 def row_block(w, index, size):
@@ -177,7 +187,9 @@
     c_rows = paired[:, :, 1]
     end_state = local_states(value_f, b_rows, step_size, decay_rate)
     decay_total = jnp.exp(-jnp.sum(step_size * decay_rate[None, :], axis=0))
-    state_in = carried_in(decay_total, end_state, "ctx", False)
+    d_mixed = d_flat.reshape(rows, heads, HEADDIM)
+    own_adjoint = local_adjoint(d_mixed, c_rows, step_size, decay_rate)
+    state_in, adjoint = both_carries(decay_total, end_state, own_adjoint, "ctx")
 
     def with_state(vals, brows, crows, steps):
         return ssd_core(vals, brows, crows, steps, decay_rate, state_in)
@@ -187,16 +199,10 @@
         (core_out + skip_gain[None, :, None] * value_f).reshape(rows, inner).astype(jnp.bfloat16)
     )
 
-    def out_part(dest):
-        block = row_block(w_all, dest, width)[:, :out_cols]
-        return lax.dot_general(
-            mixed, block, (((1,), (1,)), ((), ())), preferred_element_type=jnp.float32
-        )
-
-    output = summed_over(out_part, "tp").astype(jnp.bfloat16)
-    d_mixed = d_flat.reshape(rows, heads, HEADDIM)
-    own_adjoint = local_adjoint(d_mixed, c_rows, step_size, decay_rate)
-    adjoint = carried_in(decay_total, own_adjoint, "ctx", True)
+    partial_out = lax.dot_general(
+        mixed, w_all[:, :out_cols], (((1,), (1,)), ((), ())), preferred_element_type=jnp.float32
+    )
+    output = scattered_sum(partial_out, "tp", width).astype(jnp.bfloat16)
     grads = pullback((d_mixed, adjoint))
     d_values = grads[0] + skip_gain[None, :, None] * d_mixed
     d_pre = grads[3] * jax.nn.sigmoid(pre_step)
@@ -210,13 +216,10 @@
         axis=1,
     )
 
-    def grad_part(dest):
-        block = row_block(w_all, dest, width)[:, out_cols:]
-        return lax.dot_general(
-            d_cat, block, (((1,), (1,)), ((), ())), preferred_element_type=jnp.float32
-        )
-
-    grad = summed_over(grad_part, "tp").astype(jnp.bfloat16)
+    partial_grad = lax.dot_general(
+        d_cat, w_all[:, out_cols:], (((1,), (1,)), ((), ())), preferred_element_type=jnp.float32
+    )
+    grad = scattered_sum(partial_grad, "tp", width).astype(jnp.bfloat16)
     return (output, grad)
 
 

time: 493 us -> 486 us (0.986)
  starting transfers between devices: 166 us -> 85.8 us
  waiting for transfers between devices: 228 us -> 278 us
  other arithmetic: 15.7 us -> 34.4 us
  local copies, waits for them, and re-layouts: 7.83 us -> 20.1 us
  matrix products: 58.8 us -> 48 us
    ppermute x28 -> x12, starting transfers between devices: 132 us -> 53.1 us  [the longest x6 33.5 us: both_carries(): got = lax.ppermute(message, axis, [(i, i ^ bit) for i in range(devices)])]
    ppermute x28 -> x12, waiting for transfers between devices: 86.4 us -> 136 us  [the longest x6 84.1 us: both_carries(): got = lax.ppermute(message, axis, [(i, i ^ bit) for i in range(devices)])]
    dot_general x16 -> x2, matrix products: 14.4 us -> 5.65 us  [the longest x1 3.31 us: per_device(): lax.dot_general(d_cat, w_all[:, out_cols:], (((1,), (1,)), ((), ())), pre...]
    select_n x9 -> x11, other arithmetic: 0.11 us -> 8.66 us  [the longest x5 5.41 us: both_carries(): jnp.where(lower, total_a * got_s + total_s, got_a * total_s + got_s)]
    slice x10 -> x7, local copies, waits for them, and re-layouts: 1.14 us -> 6.63 us  [the longest x1 3.12 us: per_device(): w_all[:, :out_cols]]
  transfers between devices with their start and end apart: 36 -> 20, of which waited for: 21 -> 15; matrix products, arithmetic and copies ran while one was open for 7% -> 8% of each run, Pallas kernels for 0% -> 0%
where the time goes in v3:
time: 486 us; the launch traced here: 482 us
  waiting for transfers between devices  278 us (57%)
  starting transfers between devices  85.8 us (18%)
  matrix products  48 us (10%)
  other arithmetic  34.4 us (7%)
  local copies, waits for them, and re-layouts  20.1 us (4%)
  between operations  15.3 us (3%)
    all_gather x1, waiting for transfers between devices, per_device(): lax.all_gather(jnp.concatenate([w_out.T, w_in, w_bc, w_dt], axis=1), 'ctx...  132 us
    ppermute x6, waiting for transfers between devices, both_carries(): got = lax.ppermute(message, axis, [(i, i ^ bit) for i in range(devices)])  84.1 us
    ppermute x6, waiting for transfers between devices, scattered_sum(): lax.ppermute(send, axis, [(i, i ^ bit) for i in range(devices)])  51.5 us
    ppermute x6, starting transfers between devices, both_carries(): got = lax.ppermute(message, axis, [(i, i ^ bit) for i in range(devices)])  33.5 us
    ppermute x7, starting transfers between devices, from_each(): lax.ppermute(x, axis, [(i, (i + k) % devices) for i in range(devices)])  32.6 us
    ppermute x6, starting transfers between devices, scattered_sum(): lax.ppermute(send, axis, [(i, i ^ bit) for i in range(devices)])  19.6 us
    dot_general x8, matrix products, per_device(): jnp.dot(pieces[k][:, :width], block[:, out_cols:], preferred_element_type...  11 us
    ppermute x7, waiting for transfers between devices, from_each(): lax.ppermute(x, axis, [(i, (i + k) % devices) for i in range(devices)])  10.5 us
  transfers between devices with their start and end apart: 20, of which 15 were waited for; matrix products, arithmetic and copies ran while one was open for 8% of the time, Pallas kernels for 0%

profile of v3, /device:TPU:1, one launch (start us, length us, event | category | flops | bytes accessed | tf_op | source)
XLA Modules:
  0.0 481.7 jit_solution(12803615968081335262)
XLA Ops:
  8.0 1.4 pad_maximum_fusion.7
  11.3 10.5 %collective-permute-start.6 = (bf16[256,512]{1,0:T(8,128)(2,1)S(1)}, bf16[256,512]{1,0:T(8,128)(2,1)S(1)}, u32[]{:S(2)}, u32[]{:S(2)}) collective-permute-start(bf16[256,512]{1,0:T(8,128)(2,1)S(1)} %constant_dynamic-update-slice_fusion), channel_id=1, source_target_pairs={{0,7},{1,0},{2,1},{3,2},{4,3},{5,4},{6,5},{7,6},{8,15},{9,8},{10,9... | collective-permute-start | bytes 786440 | tf_op jit(solution)/shard_map/ppermute | solution.py:152
  21.8 2.4 collective-permute-start.5
  24.2 2.1 collective-permute-start.4
  26.3 7.5 %collective-permute-start.3 = (bf16[256,512]{1,0:T(8,128)(2,1)S(1)}, bf16[256,512]{1,0:T(8,128)(2,1)S(1)}, u32[]{:S(2)}, u32[]{:S(2)}) collective-permute-start(bf16[256,512]{1,0:T(8,128)(2,1)S(1)} %constant_dynamic-update-slice_fusion), channel_id=1, source_target_pairs={{0,4},{1,5},{2,6},{3,7},{4,0},{5,1},{6,2},{7,3},{8,12},{9,13},{10,... | collective-permute-start | bytes 786440 | tf_op jit(solution)/shard_map/ppermute | solution.py:152
  33.7 1.9 collective-permute-start.2
  35.8 131.9 %all-gather.2.cloned.1.call-done = bf16[2048,1288]{1,0:T(8,128)(2,1)} async-done(((bf16[32,1288]{1,0:T(8,128)(2,1)}), bf16[2048,1288]{1,0:T(8,128)(2,1)}) %all-gather.2.cloned.1.call-update) | async-done | bytes 5275664 | tf_op jit(solution)/shard_map/all_gather | solution.py:168
  167.7 1.3 convolution_bitcast_fusion
  169.1 1.9 collective-permute-start.1
  171.0 1.3 fusion.77
  172.4 6.4 %collective-permute-start = (bf16[256,512]{1,0:T(8,128)(2,1)S(1)}, bf16[256,512]{1,0:T(8,128)(2,1)S(1)}, u32[]{:S(2)}, u32[]{:S(2)}) collective-permute-start(bf16[256,512]{1,0:T(8,128)(2,1)S(1)} %constant_dynamic-update-slice_fusion), channel_id=1, source_target_pairs={{0,1},{1,2},{2,3},{3,4},{4,5},{5,6},{6,7},{7,0},{8,9},{9,10},{10,1... | collective-permute-start | bytes 786440 | tf_op jit(solution)/shard_map/ppermute | solution.py:152
  178.7 1.3 fusion.79
  180.1 1.3 fusion.81
  181.5 1.3 fusion.83
  182.8 1.3 fusion.85
  184.2 3.1 collective-permute-done.1
  187.3 1.4 fusion.87
  188.7 7.4 %collective-permute-done = bf16[256,512]{1,0:T(8,128)(2,1)S(1)} collective-permute-done((bf16[256,512]{1,0:T(8,128)(2,1)S(1)}, bf16[256,512]{1,0:T(8,128)(2,1)S(1)}, u32[]{:S(2)}, u32[]{:S(2)}) %collective-permute-start) | collective-permute-done | bytes 262176 | tf_op jit(solution)/shard_map/ppermute | solution.py:152
  196.1 1.6 fusion.178
  202.4 1.3 fusion.108
  203.7 1.3 fusion.106
  211.2 1.3 fusion.32
  214.3 12.6 %collective-permute-start.7 = (f32[8,16512]{1,0:T(8,128)S(1)}, f32[8,16512]{1,0:T(8,128)S(1)}, u32[]{:S(2)}, u32[]{:S(2)}) collective-permute-start(f32[8,16512]{1,0:T(8,128)S(1)} %pad_maximum_fusion), channel_id=1, source_target_pairs={{0,8},{8,0},{16,24},{24,16},{32,40},{40,32},{48,56},{56,48},{64,72... | collective-permute-start | bytes 1585160 | tf_op jit(solution)/shard_map/ppermute | solution.py:30
  226.9 1.5 collective-permute-done.7
  230.4 2.4 collective-permute-start.8
  232.8 12.9 %collective-permute-done.8 = f32[8,16512]{1,0:T(8,128)S(1)} collective-permute-done((f32[8,16512]{1,0:T(8,128)}, f32[8,16512]{1,0:T(8,128)S(1)}, u32[]{:S(2)}, u32[]{:S(2)}) %collective-permute-start.8) | collective-permute-done | bytes 528416 | tf_op jit(solution)/shard_map/ppermute | solution.py:30
  248.3 4.1 collective-permute-start.9
  252.4 24.0 %collective-permute-done.9 = f32[8,16512]{1,0:T(8,128)} collective-permute-done((f32[8,16512]{1,0:T(8,128)}, f32[8,16512]{1,0:T(8,128)}, u32[]{:S(2)}, u32[]{:S(2)}) %collective-permute-start.9) | collective-permute-done | bytes 528416 | tf_op jit(solution)/shard_map/ppermute | solution.py:30
  277.2 1.3 fusion.162
  280.6 6.4 %collective-permute-start.10 = (f32[8,16512]{1,0:T(8,128)}, f32[8,16512]{1,0:T(8,128)}, u32[]{:S(2)}, u32[]{:S(2)}) collective-permute-start(f32[8,16512]{1,0:T(8,128)} %pad_maximum_fusion.3), channel_id=1, source_target_pairs={{0,64},{8,72},{16,80},{24,88},{32,96},{40,104},{48,112},{56,120},{... | collective-permute-start | bytes 1585160 | tf_op jit(solution)/shard_map/ppermute | solution.py:30
  287.0 24.0 %collective-permute-done.10 = f32[8,16512]{1,0:T(8,128)} collective-permute-done((f32[8,16512]{1,0:T(8,128)}, f32[8,16512]{1,0:T(8,128)}, u32[]{:S(2)}, u32[]{:S(2)}) %collective-permute-start.10) | collective-permute-done | bytes 528416 | tf_op jit(solution)/shard_map/ppermute | solution.py:30
  314.5 3.4 collective-permute-start.11
  320.5 1.8 fusion.144
  322.3 6.2 %collective-permute-done.11 = f32[8,16512]{1,0:T(8,128)} collective-permute-done((f32[8,16512]{1,0:T(8,128)}, f32[8,16512]{1,0:T(8,128)}, u32[]{:S(2)}, u32[]{:S(2)}) %collective-permute-start.11) | collective-permute-done | bytes 528416 | tf_op jit(solution)/shard_map/ppermute | solution.py:30
  331.3 4.6 collective-permute-start.12
  336.7 3.1 slice.369
  339.9 3.3 fusion.18
  343.2 15.4 %collective-permute-done.12 = f32[8,16512]{1,0:T(8,128)S(1)} collective-permute-done((f32[8,16512]{1,0:T(8,128)S(1)}, f32[8,16512]{1,0:T(8,128)S(1)}, u32[]{:S(2)}, u32[]{:S(2)}) %collective-permute-start.12) | collective-permute-done | bytes 528416 | tf_op jit(solution)/shard_map/ppermute | solution.py:30
  358.7 1.3 fusion.96
  360.0 1.3 fusion.97
  362.3 2.3 fusion.26
  366.8 1.8 fusion.38
  371.0 3.1 fusion.34
  374.2 3.6 multiply_reduce_fusion.1
  379.5 2.5 reduce-window.44
  382.3 2.3 fusion.114
  385.9 2.1 collective-permute-start.13
  388.9 3.3 fusion
  392.2 1.5 fusion.177
  393.7 1.6 copy.176
  395.2 2.9 copy.177
  399.3 4.6 collective-permute-start.16
  403.9 7.5 %collective-permute-done.13 = f32[256,4,256]{2,0,1:T(8,128)} collective-permute-done((f32[256,4,256]{2,0,1:T(8,128)}, f32[256,4,256]{2,0,1:T(8,128)}, u32[]{:S(2)}, u32[]{:S(2)}) %collective-permute-start.13) | collective-permute-done | bytes 1048608 | tf_op jit(solution)/shard_map/ppermute | solution.py:57
  411.3 1.4 fusion.46
  412.8 1.9 collective-permute-start.14
  414.8 19.0 %collective-permute-done.16 = f32[256,4,256]{2,0,1:T(8,128)} collective-permute-done((f32[256,4,256]{2,0,1:T(8,128)}, f32[256,4,256]{2,0,1:T(8,128)}, u32[]{:S(2)}, u32[]{:S(2)}) %collective-permute-start.16) | collective-permute-done | bytes 1048608 | tf_op jit(solution)/shard_map/ppermute | solution.py:57
  433.8 1.4 bitcast_add_fusion
  436.1 1.9 collective-permute-start.17
  438.0 5.0 %collective-permute-done.14 = f32[256,2,256]{2,0,1:T(8,128)S(1)} collective-permute-done((f32[256,2,256]{2,0,1:T(8,128)S(1)}, f32[256,2,256]{2,0,1:T(8,128)S(1)}, u32[]{:S(2)}, u32[]{:S(2)}) %collective-permute-start.14) | collective-permute-done | bytes 524320 | tf_op jit(solution)/shard_map/ppermute | solution.py:57
  443.2 4.6 collective-permute-start.15
  447.7 6.6 %collective-permute-done.17 = f32[256,2,256]{2,0,1:T(8,128)} collective-permute-done((f32[256,2,256]{2,0,1:T(8,128)}, f32[256,2,256]{2,0,1:T(8,128)}, u32[]{:S(2)}, u32[]{:S(2)}) %collective-permute-start.17) | collective-permute-done | bytes 524320 | tf_op jit(solution)/shard_map/ppermute | solution.py:57
  455.6 4.6 collective-permute-start.18
  460.1 2.3 collective-permute-done.15
  463.1 11.1 %collective-permute-done.18 = f32[256,1,256]{2,0,1:T(8,128)S(1)} collective-permute-done((f32[256,1,256]{2,0,1:T(8,128)S(1)}, f32[256,1,256]{2,0,1:T(8,128)S(1)}, u32[]{:S(2)}, u32[]{:S(2)}) %collective-permute-start.18) | collective-permute-done | bytes 262176 | tf_op jit(solution)/shard_map/ppermute | solution.py:57
  (218 shorter events, 46.4 us)
Async XLA Ops:
  7.2 160.6 %all-gather.2.cloned.1.call-start = ((), (), s32[]{:S(2)}) async-start(), calls=%async_computation | async-start | bytes 5857280 | tf_op jit(solution)/shard_map/all_gather | solution.py:168
  11.3 157.8 %collective-permute-start.6 = (bf16[256,512]{1,0:T(8,128)(2,1)S(1)}, bf16[256,512]{1,0:T(8,128)(2,1)S(1)}, u32[]{:S(2)}, u32[]{:S(2)}) collective-permute-start(bf16[256,512]{1,0:T(8,128)(2,1)S(1)} %constant_dynamic-update-slice_fusion), channel_id=1, source_target_pairs={{0,7},{1,0},{2,1},{3,2},{4,3},{5,4},{6,5},{7,6},{8,15},{9,8},{10,9... | collective-permute-start | bytes 786440 | tf_op jit(solution)/shard_map/ppermute | solution.py:152
  21.8 150.6 %collective-permute-start.5 = (bf16[256,512]{1,0:T(8,128)(2,1)S(1)}, bf16[256,512]{1,0:T(8,128)(2,1)S(1)}, u32[]{:S(2)}, u32[]{:S(2)}) collective-permute-start(bf16[256,512]{1,0:T(8,128)(2,1)S(1)} %constant_dynamic-update-slice_fusion), channel_id=1, source_target_pairs={{0,6},{1,7},{2,0},{3,1},{4,2},{5,3},{6,4},{7,5},{8,14},{9,15},{10,... | collective-permute-start | bytes 786440 | tf_op jit(solution)/shard_map/ppermute | solution.py:152
  24.2 155.9 %collective-permute-start.4 = (bf16[256,512]{1,0:T(8,128)(2,1)S(1)}, bf16[256,512]{1,0:T(8,128)(2,1)S(1)}, u32[]{:S(2)}, u32[]{:S(2)}) collective-permute-start(bf16[256,512]{1,0:T(8,128)(2,1)S(1)} %constant_dynamic-update-slice_fusion), channel_id=1, source_target_pairs={{0,5},{1,6},{2,7},{3,0},{4,1},{5,2},{6,3},{7,4},{8,13},{9,14},{10,... | collective-permute-start | bytes 786440 | tf_op jit(solution)/shard_map/ppermute | solution.py:152
  26.3 155.2 %collective-permute-start.3 = (bf16[256,512]{1,0:T(8,128)(2,1)S(1)}, bf16[256,512]{1,0:T(8,128)(2,1)S(1)}, u32[]{:S(2)}, u32[]{:S(2)}) collective-permute-start(bf16[256,512]{1,0:T(8,128)(2,1)S(1)} %constant_dynamic-update-slice_fusion), channel_id=1, source_target_pairs={{0,4},{1,5},{2,6},{3,7},{4,0},{5,1},{6,2},{7,3},{8,12},{9,13},{10,... | collective-permute-start | bytes 786440 | tf_op jit(solution)/shard_map/ppermute | solution.py:152
  33.7 149.1 %collective-permute-start.2 = (bf16[256,512]{1,0:T(8,128)(2,1)S(1)}, bf16[256,512]{1,0:T(8,128)(2,1)S(1)}, u32[]{:S(2)}, u32[]{:S(2)}) collective-permute-start(bf16[256,512]{1,0:T(8,128)(2,1)S(1)} %constant_dynamic-update-slice_fusion), channel_id=1, source_target_pairs={{0,3},{1,4},{2,5},{3,6},{4,7},{5,0},{6,1},{7,2},{8,11},{9,12},{10,... | collective-permute-start | bytes 786440 | tf_op jit(solution)/shard_map/ppermute | solution.py:152
  169.1 18.2 %collective-permute-start.1 = (bf16[256,512]{1,0:T(8,128)(2,1)S(1)}, bf16[256,512]{1,0:T(8,128)(2,1)S(1)}, u32[]{:S(2)}, u32[]{:S(2)}) collective-permute-start(bf16[256,512]{1,0:T(8,128)(2,1)S(1)} %constant_dynamic-update-slice_fusion), channel_id=1, source_target_pairs={{0,2},{1,3},{2,4},{3,5},{4,6},{5,7},{6,0},{7,1},{8,10},{9,11},{10,... | collective-permute-start | bytes 786440 | tf_op jit(solution)/shard_map/ppermute | solution.py:152
  172.4 23.8 %collective-permute-start = (bf16[256,512]{1,0:T(8,128)(2,1)S(1)}, bf16[256,512]{1,0:T(8,128)(2,1)S(1)}, u32[]{:S(2)}, u32[]{:S(2)}) collective-permute-start(bf16[256,512]{1,0:T(8,128)(2,1)S(1)} %constant_dynamic-update-slice_fusion), channel_id=1, source_target_pairs={{0,1},{1,2},{2,3},{3,4},{4,5},{5,6},{6,7},{7,0},{8,9},{9,10},{10,1... | collective-permute-start | bytes 786440 | tf_op jit(solution)/shard_map/ppermute | solution.py:152
  187.3 10.5 %copy-start.9 = (bf16[256,512]{1,0:T(8,128)(2,1)}, bf16[256,512]{1,0:T(8,128)(2,1)S(1)}, u32[]{:S(2)}) copy-start(bf16[256,512]{1,0:T(8,128)(2,1)S(1)} %collective-permute-done.1) | copy-start | bytes 786436
  188.7 10.0 %copy-start.34 = (f32[8]{0:T(128)S(1)}, f32[8]{0:T(128)}, u32[]{:S(2)}) copy-start(f32[8]{0:T(128)} %param.14) | copy-start | bytes 100
  188.7 10.0 %copy-start.50 = (f32[8]{0:T(128)S(1)}, f32[8]{0:T(128)}, u32[]{:S(2)}) copy-start(f32[8]{0:T(128)} %param.13) | copy-start | bytes 100
  198.9 2.5 copy-start.13
  198.9 2.5 copy-start.45
  199.5 1.8 copy-start.18
  199.8 12.7 %copy-start.19 = (f32[256,8]{0,1:T(8,128)}, f32[256,8]{0,1:T(8,128)S(1)}, u32[]{:S(2)}) copy-start(f32[256,8]{0,1:T(8,128)S(1)} %get-tuple-element.203) | copy-start | bytes 24580
  201.4 12.8 %copy-start.47 = (f32[8]{0:T(128)}, f32[8]{0:T(128)S(1)}, u32[]{:S(2)}) copy-start(f32[8]{0:T(128)S(1)} %negate_exponential_fusion) | copy-start | bytes 100
  202.3 10.2 %copy-start.6 = (f32[256,128]{1,0:T(8,128)}, f32[256,128]{1,0:T(8,128)S(1)}, u32[]{:S(2)}) copy-start(f32[256,128]{1,0:T(8,128)S(1)} %copy.131) | copy-start | bytes 393220
  203.7 6.2 %copy-start.8 = (bf16[256,256]{1,0:T(8,128)(2,1)S(1)}, bf16[256,256]{1,0:T(8,128)(2,1)}, u32[]{:S(2)}) copy-start(bf16[256,256]{1,0:T(8,128)(2,1)} %param.17) | copy-start | bytes 393220
  211.2 2.0 copy-start.23
  212.5 16.0 %copy-start.46 = (f32[8]{0:T(128)S(1)}, f32[8]{0:T(128)}, u32[]{:S(2)}) copy-start(f32[8]{0:T(128)} %copy-done.45) | copy-start | bytes 100
  214.3 14.1 %collective-permute-start.7 = (f32[8,16512]{1,0:T(8,128)S(1)}, f32[8,16512]{1,0:T(8,128)S(1)}, u32[]{:S(2)}, u32[]{:S(2)}) collective-permute-start(f32[8,16512]{1,0:T(8,128)S(1)} %pad_maximum_fusion), channel_id=1, source_target_pairs={{0,8},{8,0},{16,24},{24,16},{32,40},{40,32},{48,56},{56,48},{64,72... | collective-permute-start | bytes 1585160 | tf_op jit(solution)/shard_map/ppermute | solution.py:30
  230.4 15.3 %collective-permute-start.8 = (f32[8,16512]{1,0:T(8,128)}, f32[8,16512]{1,0:T(8,128)S(1)}, u32[]{:S(2)}, u32[]{:S(2)}) collective-permute-start(f32[8,16512]{1,0:T(8,128)} %pad_maximum_fusion.1), channel_id=1, source_target_pairs={{0,16},{8,24},{16,0},{24,8},{32,48},{40,56},{48,32},{56,40},{64,80... | collective-permute-start | bytes 1585160 | tf_op jit(solution)/shard_map/ppermute | solution.py:30
  248.3 28.2 %collective-permute-start.9 = (f32[8,16512]{1,0:T(8,128)}, f32[8,16512]{1,0:T(8,128)}, u32[]{:S(2)}, u32[]{:S(2)}) collective-permute-start(f32[8,16512]{1,0:T(8,128)} %pad_maximum_fusion.2), channel_id=1, source_target_pairs={{0,32},{8,40},{16,48},{24,56},{32,0},{40,8},{48,16},{56,24},{64,96... | collective-permute-start | bytes 1585160 | tf_op jit(solution)/shard_map/ppermute | solution.py:30
  278.4 2.1 copy-start.44
  280.6 30.4 %collective-permute-start.10 = (f32[8,16512]{1,0:T(8,128)}, f32[8,16512]{1,0:T(8,128)}, u32[]{:S(2)}, u32[]{:S(2)}) collective-permute-start(f32[8,16512]{1,0:T(8,128)} %pad_maximum_fusion.3), channel_id=1, source_target_pairs={{0,64},{8,72},{16,80},{24,88},{32,96},{40,104},{48,112},{56,120},{... | collective-permute-start | bytes 1585160 | tf_op jit(solution)/shard_map/ppermute | solution.py:30
  312.4 2.1 copy-start.42
  314.5 14.0 %collective-permute-start.11 = (f32[8,16512]{1,0:T(8,128)}, f32[8,16512]{1,0:T(8,128)}, u32[]{:S(2)}, u32[]{:S(2)}) collective-permute-start(f32[8,16512]{1,0:T(8,128)} %pad_maximum_fusion.4), channel_id=1, source_target_pairs={{0,128},{8,136},{16,144},{24,152},{32,160},{40,168},{48,176},{56,1... | collective-permute-start | bytes 1585160 | tf_op jit(solution)/shard_map/ppermute | solution.py:30
  331.3 27.3 %collective-permute-start.12 = (f32[8,16512]{1,0:T(8,128)S(1)}, f32[8,16512]{1,0:T(8,128)S(1)}, u32[]{:S(2)}, u32[]{:S(2)}) collective-permute-start(f32[8,16512]{1,0:T(8,128)S(1)} %pad_maximum_fusion.5), channel_id=1, source_target_pairs={{0,256},{8,264},{16,272},{24,280},{32,288},{40,296},{48,304},{56,3... | collective-permute-start | bytes 1585160 | tf_op jit(solution)/shard_map/ppermute | solution.py:30
  336.7 3.1 copy-start.10
  336.7 3.1 copy-start.14
  336.7 3.1 copy-start.22
  339.9 3.4 copy-start.31
  339.9 3.3 copy-start.33
  339.9 18.8 %copy-start.53 = (f32[8]{0:T(128)S(1)}, f32[8]{0:T(128)}, u32[]{:S(2)}) copy-start(f32[8]{0:T(128)} %get-tuple-element.234) | copy-start | bytes 100
  339.9 20.1 %copy-start.52 = (f32[8]{0:T(128)S(1)}, f32[8]{0:T(128)}, u32[]{:S(2)}) copy-start(f32[8]{0:T(128)} %get-tuple-element.232) | copy-start | bytes 100
  343.2 18.1 %copy-start.35 = (f32[8]{0:T(128)S(1)}, f32[8]{0:T(128)}, u32[]{:S(2)}) copy-start(f32[8]{0:T(128)} %param.14) | copy-start | bytes 100
  362.0 6.6 %copy-start.3 = (f32[256,1,128]{0,2,1:T(8,128)S(1)}, f32[256,1,128]{0,2,1:T(8,128)}, u32[]{:S(2)}) copy-start(f32[256,1,128]{0,2,1:T(8,128)} %get-tuple-element.186) | copy-start | bytes 393220
  362.0 6.6 %copy-start.4 = (f32[256,1,128]{0,2,1:T(8,128)S(1)}, f32[256,1,128]{0,2,1:T(8,128)}, u32[]{:S(2)}) copy-start(f32[256,1,128]{0,2,1:T(8,128)} %get-tuple-element.184) | copy-start | bytes 393220
  362.3 8.7 %copy-start.39 = (f32[8,256]{1,0:T(8,128)}, f32[8,256]{1,0:T(8,128)S(1)}, u32[]{:S(2)}) copy-start(f32[8,256]{1,0:T(8,128)S(1)} %add_bitcast_fusion.1) | copy-start | bytes 24580
  362.3 2.8 copy-start.16
  364.6 5.7 %copy-start.15 = (f32[256,8]{0,1:T(8,128)S(1)}, f32[256,8]{0,1:T(8,128)}, u32[]{:S(2)}) copy-start(f32[256,8]{0,1:T(8,128)} %copy-done.13) | copy-start | bytes 24580
  365.1 5.9 %copy-start.37 = (f32[8]{0:T(128)}, f32[8]{0:T(128)S(1)}, u32[]{:S(2)}) copy-start(f32[8]{0:T(128)S(1)} %get-tuple-element.225) | copy-start | bytes 100
  365.1 5.8 %copy-start.25 = (f32[256,8]{0,1:T(8,128)}, f32[256,8]{0,1:T(8,128)S(1)}, u32[]{:S(2)}) copy-start(f32[256,8]{0,1:T(8,128)S(1)} %subtract_exponential_fusion) | copy-start | bytes 24580
  366.2 4.9 %copy-start.20 = (pred[1,256,256]{2,1,0:T(8,128)(4,1)S(1)}, pred[1,256,256]{2,1,0:T(8,128)(4,1)}, u32[]{:S(2)}) copy-start(pred[1,256,256]{2,1,0:T(8,128)(4,1)} %iota_compare_fusion) | copy-start | bytes 196612
  369.0 2.0 copy-start.11
  371.0 3.1 copy-start.21
  371.0 3.1 copy-start.26
  374.1 5.0 %copy-start.17 = (f32[256,8]{0,1:T(8,128)S(1)}, f32[256,8]{0,1:T(8,128)}, u32[]{:S(2)}) copy-start(f32[256,8]{0,1:T(8,128)} %copy-done.16) | copy-start | bytes 24580
  374.2 5.0 %copy-start.38 = (f32[8]{0:T(128)S(1)}, f32[8]{0:T(128)}, u32[]{:S(2)}) copy-start(f32[8]{0:T(128)} %copy-done.37) | copy-start | bytes 100
  374.2 5.2 %copy-start.24 = (f32[256,8]{0,1:T(8,128)S(1)}, f32[256,8]{0,1:T(8,128)}, u32[]{:S(2)}) copy-start(f32[256,8]{0,1:T(8,128)} %fusion.38) | copy-start | bytes 24580
  374.2 8.0 %copy-start.41 = (f32[512]{0:T(512)S(1)}, f32[512]{0:T(512)}, u32[]{:S(2)}) copy-start(f32[512]{0:T(512)} %mul.712) | copy-start | bytes 6148
  384.7 3.3 copy-start.12
  384.7 3.3 copy-start.36
  384.7 3.3 copy-start.40
  384.7 3.3 copy-start.51
  385.9 25.5 %collective-permute-start.13 = (f32[256,4,256]{2,0,1:T(8,128)}, f32[256,4,256]{2,0,1:T(8,128)}, u32[]{:S(2)}, u32[]{:S(2)}) collective-permute-start(f32[256,4,256]{2,0,1:T(8,128)} %select_bitcast_fusion.1), channel_id=1, source_target_pairs={{0,1},{1,0},{2,3},{3,2},{4,5},{5,4},{6,7},{7,6},{8,9},{9,8},{10,11... | collective-permute-start | bytes 3145736 | tf_op jit(solution)/shard_map/ppermute | solution.py:57
  395.2 4.0 copy-start
  399.3 34.5 %collective-permute-start.16 = (f32[256,4,256]{2,0,1:T(8,128)}, f32[256,4,256]{2,0,1:T(8,128)}, u32[]{:S(2)}, u32[]{:S(2)}) collective-permute-start(f32[256,4,256]{2,0,1:T(8,128)} %select_bitcast_fusion), channel_id=1, source_target_pairs={{0,1},{1,0},{2,3},{3,2},{4,5},{5,4},{6,7},{7,6},{8,9},{9,8},{10,11... | collective-permute-start | bytes 3145736 | tf_op jit(solution)/shard_map/ppermute | solution.py:57
  403.9 30.0 %copy-start.1 = (f32[256,4,1,256]{3,0,1,2:T(8,128)S(1)}, f32[256,4,1,256]{3,0,1,2:T(8,128)}, u32[]{:S(2)}) copy-start(f32[256,4,1,256]{3,0,1,2:T(8,128)} %copy-done) | copy-start | bytes 3145732
  403.9 29.9 %copy-start.2 = (f32[256,4,1,256]{3,0,1,2:T(8,128)S(1)}, f32[256,4,1,256]{3,0,1,2:T(8,128)}, u32[]{:S(2)}) copy-start(f32[256,4,1,256]{3,0,1,2:T(8,128)} %copy.177) | copy-start | bytes 3145732
  412.8 30.2 %collective-permute-start.14 = (f32[256,2,256]{2,0,1:T(8,128)S(1)}, f32[256,2,256]{2,0,1:T(8,128)S(1)}, u32[]{:S(2)}, u32[]{:S(2)}) collective-permute-start(f32[256,2,256]{2,0,1:T(8,128)S(1)} %select_bitcast_fusion.3), channel_id=1, source_target_pairs={{0,2},{1,3},{2,0},{3,1},{4,6},{5,7},{6,4},{7,5},{8,10},{9,11},{10,... | collective-permute-start | bytes 1572872 | tf_op jit(solution)/shard_map/ppermute | solution.py:57
  436.1 18.3 %collective-permute-start.17 = (f32[256,2,256]{2,0,1:T(8,128)}, f32[256,2,256]{2,0,1:T(8,128)}, u32[]{:S(2)}, u32[]{:S(2)}) collective-permute-start(f32[256,2,256]{2,0,1:T(8,128)} %select_bitcast_fusion.2), channel_id=1, source_target_pairs={{0,2},{1,3},{2,0},{3,1},{4,6},{5,7},{6,4},{7,5},{8,10},{9,11},{10,... | collective-permute-start | bytes 1572872 | tf_op jit(solution)/shard_map/ppermute | solution.py:57
  443.2 19.2 %collective-permute-start.15 = (f32[256,1,256]{2,0,1:T(8,128)S(1)}, f32[256,1,256]{2,0,1:T(8,128)S(1)}, u32[]{:S(2)}, u32[]{:S(2)}) collective-permute-start(f32[256,1,256]{2,0,1:T(8,128)S(1)} %select_bitcast_fusion.5), channel_id=1, source_target_pairs={{0,4},{1,5},{2,6},{3,7},{4,0},{5,1},{6,2},{7,3},{8,12},{9,13},{10,... | collective-permute-start | bytes 786440 | tf_op jit(solution)/shard_map/ppermute | solution.py:57
  455.6 18.6 %collective-permute-start.18 = (f32[256,1,256]{2,0,1:T(8,128)S(1)}, f32[256,1,256]{2,0,1:T(8,128)S(1)}, u32[]{:S(2)}, u32[]{:S(2)}) collective-permute-start(f32[256,1,256]{2,0,1:T(8,128)S(1)} %select_bitcast_fusion.4), channel_id=1, source_target_pairs={{0,4},{1,5},{2,6},{3,7},{4,0},{5,1},{6,2},{7,3},{8,12},{9,13},{10,... | collective-permute-start | bytes 786440 | tf_op jit(solution)/shard_map/ppermute | solution.py:57
  (10 other events, 11.1 us)
Sparse Core Ops, SparseCore 0:
  10.7 156.9 all-gather.1

commit v4 on v3

--- a/solution.py
+++ b/solution.py
@@ -153,6 +153,21 @@
     return got
 
 
+def doubled_rows(x, axis):
+    devices, position = (lax.axis_size(axis), lax.axis_index(axis))
+    order = [b for b in range(1, devices.bit_length() - 1)] + [0]
+    for b in order:
+        bit = 1 << b
+        other = lax.ppermute(x, axis, [(i, i ^ bit) for i in range(devices)])
+        low = (position & bit) == 0
+        x = jnp.where(low, jnp.concatenate([x, other], 0), jnp.concatenate([other, x], 0))
+    rows = x.shape[0] // devices
+    x = x.reshape((2,) * len(order) + (rows,) + x.shape[1:])
+    axes = [len(order) - 1 - order.index(b) for b in reversed(range(len(order)))]
+    x = jnp.transpose(x, axes + list(range(len(order), x.ndim)))
+    return x.reshape((devices * rows,) + x.shape[len(order) + 1 :])
+
+
 def row_block(w, index, size):
     return lax.dynamic_slice_in_dim(w, index * size, size, axis=0)
 
@@ -165,17 +180,20 @@
     pair_cols = w_bc.shape[1]
     groups = pair_cols // (2 * STATE)
     out_cols = w_out.shape[0]
-    w_all = lax.all_gather(
-        jnp.concatenate([w_out.T, w_in, w_bc, w_dt], axis=1), "ctx", axis=0, tiled=True
-    )
+    w_proj = lax.all_gather(
+        jnp.concatenate([w_in, w_bc, w_dt], axis=1), "ctx", axis=0, tiled=True
+    )
+    w_back = doubled_rows(w_out.T, "ctx")
     pieces = from_each(jnp.concatenate([tokens, cotangent], axis=1), "tp")
     projected = None
     d_flat = None
     for k in range(devices):
-        block = row_block(w_all, (position - k) % devices, width)
-        term = jnp.dot(pieces[k][:, :width], block[:, out_cols:], preferred_element_type=jnp.float32)
+        source = (position - k) % devices
+        block = row_block(w_proj, source, width)
+        term = jnp.dot(pieces[k][:, :width], block, preferred_element_type=jnp.float32)
         projected = term if projected is None else projected + term
-        term = jnp.dot(pieces[k][:, width:], block[:, :out_cols], preferred_element_type=jnp.float32)
+        block = row_block(w_back, source, width)
+        term = jnp.dot(pieces[k][:, width:], block, preferred_element_type=jnp.float32)
         d_flat = term if d_flat is None else d_flat + term
     values = projected[:, :inner].astype(jnp.bfloat16)
     pairs = projected[:, inner : inner + pair_cols].astype(jnp.bfloat16)
@@ -200,7 +218,7 @@
     )
 
     partial_out = lax.dot_general(
-        mixed, w_all[:, :out_cols], (((1,), (1,)), ((), ())), preferred_element_type=jnp.float32
+        mixed, w_back, (((1,), (1,)), ((), ())), preferred_element_type=jnp.float32
     )
     output = scattered_sum(partial_out, "tp", width).astype(jnp.bfloat16)
     grads = pullback((d_mixed, adjoint))
@@ -217,7 +235,7 @@
     )
 
     partial_grad = lax.dot_general(
-        d_cat, w_all[:, out_cols:], (((1,), (1,)), ((), ())), preferred_element_type=jnp.float32
+        d_cat, w_proj, (((1,), (1,)), ((), ())), preferred_element_type=jnp.float32
     )
     grad = scattered_sum(partial_grad, "tp", width).astype(jnp.bfloat16)
     return (output, grad)

time: 486 us -> 508 us (1.045)
  the two profiles are of different devices: /device:TPU:1 before, /device:TPU:9 now
where the time goes in v4:
time: 508 us; the launch traced here: 506 us
  waiting for transfers between devices  263 us (52%)
  starting transfers between devices  110 us (22%)
  other arithmetic  49 us (10%)
  matrix products  40.7 us (8%)
  local copies, waits for them, and re-layouts  28.4 us (6%)
  between operations  15.3 us (3%)
    ppermute x6, waiting for transfers between devices, both_carries(): got = lax.ppermute(message, axis, [(i, i ^ bit) for i in range(devices)])  92.7 us
    ppermute x6, waiting for transfers between devices, scattered_sum(): lax.ppermute(send, axis, [(i, i ^ bit) for i in range(devices)])  60.1 us
    all_gather x1, waiting for transfers between devices, per_device(): lax.all_gather(jnp.concatenate([w_in, w_bc, w_dt], axis=1), 'ctx', axis=0...  58.5 us
    ppermute x6, waiting for transfers between devices, doubled_rows(): other = lax.ppermute(x, axis, [(i, i ^ bit) for i in range(devices)])  35.3 us
    ppermute x6, starting transfers between devices, doubled_rows(): other = lax.ppermute(x, axis, [(i, i ^ bit) for i in range(devices)])  31.8 us
    ppermute x7, starting transfers between devices, from_each(): lax.ppermute(x, axis, [(i, (i + k) % devices) for i in range(devices)])  30 us
    ppermute x6, starting transfers between devices, scattered_sum(): lax.ppermute(send, axis, [(i, i ^ bit) for i in range(devices)])  28.2 us
    ppermute x6, starting transfers between devices, both_carries(): got = lax.ppermute(message, axis, [(i, i ^ bit) for i in range(devices)])  19.7 us
  transfers between devices with their start and end apart: 26, of which 21 were waited for; matrix products, arithmetic and copies ran while one was open for 4% of the time, Pallas kernels for 0%

profile of v4, /device:TPU:9, one launch (start us, length us, event | category | flops | bytes accessed | tf_op | source)
XLA Modules:
  0.0 506.0 jit_solution(1864322333778544200)
XLA Ops:
  9.4 4.1 collective-permute-start.7
  13.6 1.5 collective-permute-done.7
  15.9 5.8 %collective-permute-start.8 = (bf16[64,512]{1,0:T(8,128)(2,1)S(1)}, bf16[64,512]{1,0:T(8,128)(2,1)S(1)}, u32[]{:S(2)}, u32[]{:S(2)}) collective-permute-start(bf16[64,512]{1,0:T(8,128)(2,1)S(1)} %maximum_select_fusion.5), channel_id=1, source_target_pairs={{0,32},{8,40},{16,48},{24,56},{32,0},{40,8},{48,16},{56,24},{64,96... | collective-permute-start | bytes 196616 | tf_op jit(solution)/shard_map/ppermute | solution.py:161
  21.7 1.6 collective-permute-done.8
  23.4 8.4 %collective-permute-start.9 = (bf16[128,512]{1,0:T(8,128)(2,1)S(1)}, bf16[128,512]{1,0:T(8,128)(2,1)S(1)}, u32[]{:S(2)}, u32[]{:S(2)}) collective-permute-start(bf16[128,512]{1,0:T(8,128)(2,1)S(1)} %maximum_select_fusion.4), channel_id=1, source_target_pairs={{0,64},{8,72},{16,80},{24,88},{32,96},{40,104},{48,112},{56,120},{... | collective-permute-start | bytes 393224 | tf_op jit(solution)/shard_map/ppermute | solution.py:161
  31.8 2.4 collective-permute-done.9
  34.3 3.2 collective-permute-start.10
  37.6 4.0 collective-permute-done.10
  41.8 6.6 %collective-permute-start.11 = (bf16[512,512]{1,0:T(8,128)(2,1)S(1)}, bf16[512,512]{1,0:T(8,128)(2,1)S(1)}, u32[]{:S(2)}, u32[]{:S(2)}) collective-permute-start(bf16[512,512]{1,0:T(8,128)(2,1)S(1)} %maximum_select_fusion.2), channel_id=1, source_target_pairs={{0,256},{8,264},{16,272},{24,280},{32,288},{40,296},{48,304},{56,3... | collective-permute-start | bytes 1572872 | tf_op jit(solution)/shard_map/ppermute | solution.py:161
  48.3 25.8 %collective-permute-done.11 = bf16[512,512]{1,0:T(8,128)(2,1)S(1)} collective-permute-done((bf16[512,512]{1,0:T(8,128)(2,1)S(1)}, bf16[512,512]{1,0:T(8,128)(2,1)S(1)}, u32[]{:S(2)}, u32[]{:S(2)}) %collective-permute-start.11) | collective-permute-done | bytes 524320 | tf_op jit(solution)/shard_map/ppermute | solution.py:161
  74.6 3.6 collective-permute-start.12
  79.6 6.0 %collective-permute-start.6 = (bf16[256,512]{1,0:T(8,128)(2,1)}, bf16[256,512]{1,0:T(8,128)(2,1)S(1)}, u32[]{:S(2)}, u32[]{:S(2)}) collective-permute-start(bf16[256,512]{1,0:T(8,128)(2,1)} %constant_dynamic-update-slice_fusion), channel_id=1, source_target_pairs={{0,7},{1,0},{2,1},{3,2},{4,3},{5,4},{6,5},{7,6},{8,15},{9,8},{10,9... | collective-permute-start | bytes 786440 | tf_op jit(solution)/shard_map/ppermute | solution.py:152
  85.6 2.4 collective-permute-start.5
  87.9 5.5 %collective-permute-start.4 = (bf16[256,512]{1,0:T(8,128)(2,1)}, bf16[256,512]{1,0:T(8,128)(2,1)S(1)}, u32[]{:S(2)}, u32[]{:S(2)}) collective-permute-start(bf16[256,512]{1,0:T(8,128)(2,1)} %constant_dynamic-update-slice_fusion), channel_id=1, source_target_pairs={{0,5},{1,6},{2,7},{3,0},{4,1},{5,2},{6,3},{7,4},{8,13},{9,14},{10,... | collective-permute-start | bytes 786440 | tf_op jit(solution)/shard_map/ppermute | solution.py:152
  93.4 3.9 collective-permute-start.3
  97.5 2.4 collective-permute-start.2
  100.9 8.0 %collective-permute-start.1 = (bf16[256,512]{1,0:T(8,128)(2,1)}, bf16[256,512]{1,0:T(8,128)(2,1)S(1)}, u32[]{:S(2)}, u32[]{:S(2)}) collective-permute-start(bf16[256,512]{1,0:T(8,128)(2,1)} %constant_dynamic-update-slice_fusion), channel_id=1, source_target_pairs={{0,2},{1,3},{2,4},{3,5},{4,6},{5,7},{6,0},{7,1},{8,10},{9,11},{10,... | collective-permute-start | bytes 786440 | tf_op jit(solution)/shard_map/ppermute | solution.py:152
  109.2 1.9 collective-permute-start
  111.7 9.2 %collective-permute-done.3 = bf16[256,512]{1,0:T(8,128)(2,1)} collective-permute-done((bf16[256,512]{1,0:T(8,128)(2,1)}, bf16[256,512]{1,0:T(8,128)(2,1)}, u32[]{:S(2)}, u32[]{:S(2)}) %collective-permute-start.3) | collective-permute-done | bytes 262176 | tf_op jit(solution)/shard_map/ppermute | solution.py:152
  123.6 2.7 collective-permute-done.1
  127.0 3.1 collective-permute-done
  130.5 58.5 %all-gather.2.cloned.1.call-done = bf16[2048,776]{1,0:T(8,128)(2,1)} async-done(((bf16[32,776]{1,0:T(8,128)(2,1)}), bf16[2048,776]{1,0:T(8,128)(2,1)}) %all-gather.2.cloned.1.call-update) | async-done | bytes 3178512 | tf_op jit(solution)/shard_map/all_gather | solution.py:183
  201.8 1.7 copy.164
  203.4 1.6 copy.173
  205.1 1.5 fusion.37
  206.6 1.6 fusion.38
  209.9 2.2 collective-permute-start.13
  212.1 1.9 collective-permute-done.13
  215.5 1.5 add_select_fusion.19
  218.6 2.6 collective-permute-start.14
  221.2 12.9 %collective-permute-done.14 = f32[8,16512]{1,0:T(8,128)} collective-permute-done((f32[8,16512]{1,0:T(8,128)}, f32[8,16512]{1,0:T(8,128)}, u32[]{:S(2)}, u32[]{:S(2)}) %collective-permute-start.14) | collective-permute-done | bytes 528416 | tf_op jit(solution)/shard_map/ppermute | solution.py:30
  237.7 5.9 %collective-permute-start.15 = (f32[8,16512]{1,0:T(8,128)}, f32[8,16512]{1,0:T(8,128)}, u32[]{:S(2)}, u32[]{:S(2)}) collective-permute-start(f32[8,16512]{1,0:T(8,128)} %pad_maximum_fusion.2), channel_id=1, source_target_pairs={{0,32},{8,40},{16,48},{24,56},{32,0},{40,8},{48,16},{56,24},{64,96... | collective-permute-start | bytes 1585160 | tf_op jit(solution)/shard_map/ppermute | solution.py:30
  243.7 23.2 %collective-permute-done.15 = f32[8,16512]{1,0:T(8,128)} collective-permute-done((f32[8,16512]{1,0:T(8,128)}, f32[8,16512]{1,0:T(8,128)}, u32[]{:S(2)}, u32[]{:S(2)}) %collective-permute-start.15) | collective-permute-done | bytes 528416 | tf_op jit(solution)/shard_map/ppermute | solution.py:30
  271.0 4.7 collective-permute-start.16
  275.8 26.4 %collective-permute-done.16 = f32[8,16512]{1,0:T(8,128)} collective-permute-done((f32[8,16512]{1,0:T(8,128)}, f32[8,16512]{1,0:T(8,128)}, u32[]{:S(2)}, u32[]{:S(2)}) %collective-permute-start.16) | collective-permute-done | bytes 528416 | tf_op jit(solution)/shard_map/ppermute | solution.py:30
  306.4 1.9 collective-permute-start.17
  312.0 9.7 %collective-permute-done.17 = f32[8,16512]{1,0:T(8,128)} collective-permute-done((f32[8,16512]{1,0:T(8,128)}, f32[8,16512]{1,0:T(8,128)}, u32[]{:S(2)}, u32[]{:S(2)}) %collective-permute-start.17) | collective-permute-done | bytes 528416 | tf_op jit(solution)/shard_map/ppermute | solution.py:30
  324.6 2.3 collective-permute-start.18
  327.7 3.4 fusion.16
  331.0 18.6 %collective-permute-done.18 = f32[8,16512]{1,0:T(8,128)S(1)} collective-permute-done((f32[8,16512]{1,0:T(8,128)S(1)}, f32[8,16512]{1,0:T(8,128)S(1)}, u32[]{:S(2)}, u32[]{:S(2)}) %collective-permute-start.18) | collective-permute-done | bytes 528416 | tf_op jit(solution)/shard_map/ppermute | solution.py:30
  349.6 2.2 fusion.96
  351.8 1.5 fusion.95
  354.0 1.8 reduce-window.42
  362.4 1.6 convolution_bitcast_fusion.6
  366.7 3.7 fusion.32
  372.4 1.7 copy.188
  374.1 2.2 convolution_bitcast_fusion.2
  376.3 4.4 multiply_reduce_fusion.1
  382.1 2.1 fusion.36
  385.1 2.7 reduce-window.44
  387.9 2.4 fusion.24
  396.0 1.6 copy.219
  397.5 2.5 copy.220
  401.2 1.9 collective-permute-start.22
  406.4 3.4 collective-permute-start.19
  409.7 17.9 %collective-permute-done.22 = f32[256,4,256]{2,0,1:T(8,128)} collective-permute-done((f32[256,4,256]{2,0,1:T(8,128)}, f32[256,4,256]{2,0,1:T(8,128)}, u32[]{:S(2)}, u32[]{:S(2)}) %collective-permute-start.22) | collective-permute-done | bytes 1048608 | tf_op jit(solution)/shard_map/ppermute | solution.py:57
  429.9 5.6 %collective-permute-start.23 = (f32[256,2,256]{2,0,1:T(8,128)}, f32[256,2,256]{2,0,1:T(8,128)S(1)}, u32[]{:S(2)}, u32[]{:S(2)}) collective-permute-start(f32[256,2,256]{2,0,1:T(8,128)} %select_bitcast_fusion.2), channel_id=1, source_target_pairs={{0,2},{1,3},{2,0},{3,1},{4,6},{5,7},{6,4},{7,5},{8,10},{9,11},{10,... | collective-permute-start | bytes 1572872 | tf_op jit(solution)/shard_map/ppermute | solution.py:57
  435.5 14.6 %collective-permute-done.19 = f32[256,4,256]{2,0,1:T(8,128)} collective-permute-done((f32[256,4,256]{2,0,1:T(8,128)}, f32[256,4,256]{2,0,1:T(8,128)}, u32[]{:S(2)}, u32[]{:S(2)}) %collective-permute-start.19) | collective-permute-done | bytes 1048608 | tf_op jit(solution)/shard_map/ppermute | solution.py:57
  452.4 5.6 %collective-permute-start.20 = (f32[256,2,256]{2,0,1:T(8,128)}, f32[256,2,256]{2,0,1:T(8,128)S(1)}, u32[]{:S(2)}, u32[]{:S(2)}) collective-permute-start(f32[256,2,256]{2,0,1:T(8,128)} %select_bitcast_fusion.3), channel_id=1, source_target_pairs={{0,2},{1,3},{2,0},{3,1},{4,6},{5,7},{6,4},{7,5},{8,10},{9,11},{10,... | collective-permute-start | bytes 1572872 | tf_op jit(solution)/shard_map/ppermute | solution.py:57
  458.0 6.6 %collective-permute-done.23 = f32[256,2,256]{2,0,1:T(8,128)S(1)} collective-permute-done((f32[256,2,256]{2,0,1:T(8,128)}, f32[256,2,256]{2,0,1:T(8,128)S(1)}, u32[]{:S(2)}, u32[]{:S(2)}) %collective-permute-start.23) | collective-permute-done | bytes 524320 | tf_op jit(solution)/shard_map/ppermute | solution.py:57
  464.7 5.9 %collective-permute-start.24 = (f32[256,1,256]{2,0,1:T(8,128)S(1)}, f32[256,1,256]{2,0,1:T(8,128)S(1)}, u32[]{:S(2)}, u32[]{:S(2)}) collective-permute-start(f32[256,1,256]{2,0,1:T(8,128)S(1)} %select_bitcast_fusion.4), channel_id=1, source_target_pairs={{0,4},{1,5},{2,6},{3,7},{4,0},{5,1},{6,2},{7,3},{8,12},{9,13},{10,... | collective-permute-start | bytes 786440 | tf_op jit(solution)/shard_map/ppermute | solution.py:57
  470.6 5.2 %collective-permute-done.20 = f32[256,2,256]{2,0,1:T(8,128)S(1)} collective-permute-done((f32[256,2,256]{2,0,1:T(8,128)}, f32[256,2,256]{2,0,1:T(8,128)S(1)}, u32[]{:S(2)}, u32[]{:S(2)}) %collective-permute-start.20) | collective-permute-done | bytes 524320 | tf_op jit(solution)/shard_map/ppermute | solution.py:57
  475.9 5.9 %collective-permute-start.21 = (f32[256,1,256]{2,0,1:T(8,128)S(1)}, f32[256,1,256]{2,0,1:T(8,128)S(1)}, u32[]{:S(2)}, u32[]{:S(2)}) collective-permute-start(f32[256,1,256]{2,0,1:T(8,128)S(1)} %select_bitcast_fusion.5), channel_id=1, source_target_pairs={{0,4},{1,5},{2,6},{3,7},{4,0},{5,1},{6,2},{7,3},{8,12},{9,13},{10,... | collective-permute-start | bytes 786440 | tf_op jit(solution)/shard_map/ppermute | solution.py:57
  482.5 15.9 %collective-permute-done.21 = f32[256,1,256]{2,0,1:T(8,128)S(1)} collective-permute-done((f32[256,1,256]{2,0,1:T(8,128)S(1)}, f32[256,1,256]{2,0,1:T(8,128)S(1)}, u32[]{:S(2)}, u32[]{:S(2)}) %collective-permute-start.21) | collective-permute-done | bytes 262176 | tf_op jit(solution)/shard_map/ppermute | solution.py:57
  (244 shorter events, 77.7 us)
Async XLA Ops:
  7.2 181.9 %all-gather.2.cloned.1.call-start = ((), (), s32[]{:S(2)}) async-start(), calls=%async_computation | async-start | bytes 3727360 | tf_op jit(solution)/shard_map/all_gather | solution.py:183
  9.4 68.8 %copy-start.21 = (bf16[256,256]{1,0:T(8,128)(2,1)S(1)}, bf16[256,256]{1,0:T(8,128)(2,1)}, u32[]{:S(2)}) copy-start(bf16[256,256]{1,0:T(8,128)(2,1)} %param.9) | copy-start | bytes 393220
  9.4 5.6 %collective-permute-start.7 = (bf16[32,512]{1,0:T(8,128)(2,1)}, bf16[32,512]{1,0:T(8,128)(2,1)S(1)}, u32[]{:S(2)}, u32[]{:S(2)}) collective-permute-start(bf16[32,512]{1,0:T(8,128)(2,1)} %bitcast.314), channel_id=1, source_target_pairs={{0,16},{8,24},{16,0},{24,8},{32,48},{40,56},{48,32},{56,40},{64,80... | collective-permute-start | bytes 98312 | tf_op jit(solution)/shard_map/ppermute | solution.py:161
  15.9 7.5 %collective-permute-start.8 = (bf16[64,512]{1,0:T(8,128)(2,1)S(1)}, bf16[64,512]{1,0:T(8,128)(2,1)S(1)}, u32[]{:S(2)}, u32[]{:S(2)}) collective-permute-start(bf16[64,512]{1,0:T(8,128)(2,1)S(1)} %maximum_select_fusion.5), channel_id=1, source_target_pairs={{0,32},{8,40},{16,48},{24,56},{32,0},{40,8},{48,16},{56,24},{64,96... | collective-permute-start | bytes 196616 | tf_op jit(solution)/shard_map/ppermute | solution.py:161
  21.7 57.2 %copy-start.20 = (bf16[256,256]{1,0:T(8,128)(2,1)S(1)}, bf16[256,256]{1,0:T(8,128)(2,1)}, u32[]{:S(2)}) copy-start(bf16[256,256]{1,0:T(8,128)(2,1)} %param.17) | copy-start | bytes 393220
  23.4 10.9 %collective-permute-start.9 = (bf16[128,512]{1,0:T(8,128)(2,1)S(1)}, bf16[128,512]{1,0:T(8,128)(2,1)S(1)}, u32[]{:S(2)}, u32[]{:S(2)}) collective-permute-start(bf16[128,512]{1,0:T(8,128)(2,1)S(1)} %maximum_select_fusion.4), channel_id=1, source_target_pairs={{0,64},{8,72},{16,80},{24,88},{32,96},{40,104},{48,112},{56,120},{... | collective-permute-start | bytes 393224 | tf_op jit(solution)/shard_map/ppermute | solution.py:161
  34.3 7.2 %collective-permute-start.10 = (bf16[256,512]{1,0:T(8,128)(2,1)S(1)}, bf16[256,512]{1,0:T(8,128)(2,1)S(1)}, u32[]{:S(2)}, u32[]{:S(2)}) collective-permute-start(bf16[256,512]{1,0:T(8,128)(2,1)S(1)} %maximum_select_fusion.3), channel_id=1, source_target_pairs={{0,128},{8,136},{16,144},{24,152},{32,160},{40,168},{48,176},{56,1... | collective-permute-start | bytes 786440 | tf_op jit(solution)/shard_map/ppermute | solution.py:161
  41.8 32.3 %collective-permute-start.11 = (bf16[512,512]{1,0:T(8,128)(2,1)S(1)}, bf16[512,512]{1,0:T(8,128)(2,1)S(1)}, u32[]{:S(2)}, u32[]{:S(2)}) collective-permute-start(bf16[512,512]{1,0:T(8,128)(2,1)S(1)} %maximum_select_fusion.2), channel_id=1, source_target_pairs={{0,256},{8,264},{16,272},{24,280},{32,288},{40,296},{48,304},{56,3... | collective-permute-start | bytes 1572872 | tf_op jit(solution)/shard_map/ppermute | solution.py:161
  74.6 22.9 %collective-permute-start.12 = (bf16[1024,512]{1,0:T(8,128)(2,1)S(1)}, bf16[1024,512]{1,0:T(8,128)(2,1)S(1)}, u32[]{:S(2)}, u32[]{:S(2)}) collective-permute-start(bf16[1024,512]{1,0:T(8,128)(2,1)S(1)} %maximum_select_fusion.1), channel_id=1, source_target_pairs={{0,8},{8,0},{16,24},{24,16},{32,40},{40,32},{48,56},{56,48},{64,72... | collective-permute-start | bytes 3145736 | tf_op jit(solution)/shard_map/ppermute | solution.py:161
  79.6 21.3 %collective-permute-start.6 = (bf16[256,512]{1,0:T(8,128)(2,1)}, bf16[256,512]{1,0:T(8,128)(2,1)S(1)}, u32[]{:S(2)}, u32[]{:S(2)}) collective-permute-start(bf16[256,512]{1,0:T(8,128)(2,1)} %constant_dynamic-update-slice_fusion), channel_id=1, source_target_pairs={{0,7},{1,0},{2,1},{3,2},{4,3},{5,4},{6,5},{7,6},{8,15},{9,8},{10,9... | collective-permute-start | bytes 786440 | tf_op jit(solution)/shard_map/ppermute | solution.py:152
  85.6 23.6 %collective-permute-start.5 = (bf16[256,512]{1,0:T(8,128)(2,1)}, bf16[256,512]{1,0:T(8,128)(2,1)S(1)}, u32[]{:S(2)}, u32[]{:S(2)}) collective-permute-start(bf16[256,512]{1,0:T(8,128)(2,1)} %constant_dynamic-update-slice_fusion), channel_id=1, source_target_pairs={{0,6},{1,7},{2,0},{3,1},{4,2},{5,3},{6,4},{7,5},{8,14},{9,15},{10,... | collective-permute-start | bytes 786440 | tf_op jit(solution)/shard_map/ppermute | solution.py:152
  87.9 23.4 %collective-permute-start.4 = (bf16[256,512]{1,0:T(8,128)(2,1)}, bf16[256,512]{1,0:T(8,128)(2,1)S(1)}, u32[]{:S(2)}, u32[]{:S(2)}) collective-permute-start(bf16[256,512]{1,0:T(8,128)(2,1)} %constant_dynamic-update-slice_fusion), channel_id=1, source_target_pairs={{0,5},{1,6},{2,7},{3,0},{4,1},{5,2},{6,3},{7,4},{8,13},{9,14},{10,... | collective-permute-start | bytes 786440 | tf_op jit(solution)/shard_map/ppermute | solution.py:152
  93.4 27.5 %collective-permute-start.3 = (bf16[256,512]{1,0:T(8,128)(2,1)}, bf16[256,512]{1,0:T(8,128)(2,1)}, u32[]{:S(2)}, u32[]{:S(2)}) collective-permute-start(bf16[256,512]{1,0:T(8,128)(2,1)} %constant_dynamic-update-slice_fusion), channel_id=1, source_target_pairs={{0,4},{1,5},{2,6},{3,7},{4,0},{5,1},{6,2},{7,3},{8,12},{9,13},{10,... | collective-permute-start | bytes 786440 | tf_op jit(solution)/shard_map/ppermute | solution.py:152
  97.5 25.9 %collective-permute-start.2 = (bf16[256,512]{1,0:T(8,128)(2,1)}, bf16[256,512]{1,0:T(8,128)(2,1)S(1)}, u32[]{:S(2)}, u32[]{:S(2)}) collective-permute-start(bf16[256,512]{1,0:T(8,128)(2,1)} %constant_dynamic-update-slice_fusion), channel_id=1, source_target_pairs={{0,3},{1,4},{2,5},{3,6},{4,7},{5,0},{6,1},{7,2},{8,11},{9,12},{10,... | collective-permute-start | bytes 786440 | tf_op jit(solution)/shard_map/ppermute | solution.py:152
  100.9 25.4 %collective-permute-start.1 = (bf16[256,512]{1,0:T(8,128)(2,1)}, bf16[256,512]{1,0:T(8,128)(2,1)S(1)}, u32[]{:S(2)}, u32[]{:S(2)}) collective-permute-start(bf16[256,512]{1,0:T(8,128)(2,1)} %constant_dynamic-update-slice_fusion), channel_id=1, source_target_pairs={{0,2},{1,3},{2,4},{3,5},{4,6},{5,7},{6,0},{7,1},{8,10},{9,11},{10,... | collective-permute-start | bytes 786440 | tf_op jit(solution)/shard_map/ppermute | solution.py:152
  109.2 20.9 %collective-permute-start = (bf16[256,512]{1,0:T(8,128)(2,1)}, bf16[256,512]{1,0:T(8,128)(2,1)S(1)}, u32[]{:S(2)}, u32[]{:S(2)}) collective-permute-start(bf16[256,512]{1,0:T(8,128)(2,1)} %constant_dynamic-update-slice_fusion), channel_id=1, source_target_pairs={{0,1},{1,2},{2,3},{3,4},{4,5},{5,6},{6,7},{7,0},{8,9},{9,10},{10,1... | collective-permute-start | bytes 786440 | tf_op jit(solution)/shard_map/ppermute | solution.py:152
  111.4 15.2 %copy-start.22 = (bf16[256,512]{1,0:T(8,128)(2,1)}, bf16[256,512]{1,0:T(8,128)(2,1)S(1)}, u32[]{:S(2)}) copy-start(bf16[256,512]{1,0:T(8,128)(2,1)S(1)} %collective-permute-done.4) | copy-start | bytes 786436
  123.4 6.8 %copy-start.23 = (bf16[256,512]{1,0:T(8,128)(2,1)}, bf16[256,512]{1,0:T(8,128)(2,1)S(1)}, u32[]{:S(2)}) copy-start(bf16[256,512]{1,0:T(8,128)(2,1)S(1)} %collective-permute-done.2) | copy-start | bytes 786436
  189.0 4.3 copy-start.2
  190.5 4.1 copy-start.24
  191.9 3.0 copy-start.26
  196.2 12.1 %copy-start.5 = (bf16[256,776]{0,1:T(8,128)(2,1)}, bf16[256,776]{0,1:T(8,128)(2,1)S(1)}, u32[]{:S(2)}) copy-start(bf16[256,776]{0,1:T(8,128)(2,1)S(1)} %get-tuple-element.237) | copy-start | bytes 1191940
  197.3 16.7 %copy-start.51 = (f32[8]{0:T(128)}, f32[8]{0:T(128)S(1)}, u32[]{:S(2)}) copy-start(f32[8]{0:T(128)S(1)} %get-tuple-element.205) | copy-start | bytes 100
  205.1 4.8 copy-start.53
  209.9 4.1 collective-permute-start.13
  214.7 20.1 %copy-start.52 = (f32[8]{0:T(128)S(1)}, f32[8]{0:T(128)}, u32[]{:S(2)}) copy-start(f32[8]{0:T(128)} %copy-done.51) | copy-start | bytes 100
  218.6 15.5 %collective-permute-start.14 = (f32[8,16512]{1,0:T(8,128)}, f32[8,16512]{1,0:T(8,128)}, u32[]{:S(2)}, u32[]{:S(2)}) collective-permute-start(f32[8,16512]{1,0:T(8,128)} %pad_maximum_fusion.1), channel_id=1, source_target_pairs={{0,16},{8,24},{16,0},{24,8},{32,48},{40,56},{48,32},{56,40},{64,80... | collective-permute-start | bytes 1585160 | tf_op jit(solution)/shard_map/ppermute | solution.py:30
  234.8 33.4 %copy-start.36 = (f32[8,1]{0,1:T(1,128)}, f32[8,1]{0,1:T(1,128)S(1)}, u32[]{:S(2)}) copy-start(f32[8,1]{0,1:T(1,128)S(1)} %copy.212) | copy-start | bytes 100
  237.7 29.2 %collective-permute-start.15 = (f32[8,16512]{1,0:T(8,128)}, f32[8,16512]{1,0:T(8,128)}, u32[]{:S(2)}, u32[]{:S(2)}) collective-permute-start(f32[8,16512]{1,0:T(8,128)} %pad_maximum_fusion.2), channel_id=1, source_target_pairs={{0,32},{8,40},{16,48},{24,56},{32,0},{40,8},{48,16},{56,24},{64,96... | collective-permute-start | bytes 1585160 | tf_op jit(solution)/shard_map/ppermute | solution.py:30
  269.5 41.5 %copy-start.18 = (bf16[256,256]{0,1:T(8,128)(2,1)S(1)}, bf16[256,256]{0,1:T(8,128)(2,1)}, u32[]{:S(2)}) copy-start(bf16[256,256]{0,1:T(8,128)(2,1)} %copy-done.17) | copy-start | bytes 393220
  271.0 31.1 %collective-permute-start.16 = (f32[8,16512]{1,0:T(8,128)}, f32[8,16512]{1,0:T(8,128)}, u32[]{:S(2)}, u32[]{:S(2)}) collective-permute-start(f32[8,16512]{1,0:T(8,128)} %pad_maximum_fusion.3), channel_id=1, source_target_pairs={{0,64},{8,72},{16,80},{24,88},{32,96},{40,104},{48,112},{56,120},{... | collective-permute-start | bytes 1585160 | tf_op jit(solution)/shard_map/ppermute | solution.py:30
  303.4 3.0 copy-start.49
  306.4 15.3 %collective-permute-start.17 = (f32[8,16512]{1,0:T(8,128)}, f32[8,16512]{1,0:T(8,128)}, u32[]{:S(2)}, u32[]{:S(2)}) collective-permute-start(f32[8,16512]{1,0:T(8,128)} %pad_maximum_fusion.4), channel_id=1, source_target_pairs={{0,128},{8,136},{16,144},{24,152},{32,160},{40,168},{48,176},{56,1... | collective-permute-start | bytes 1585160 | tf_op jit(solution)/shard_map/ppermute | solution.py:30
  311.9 15.7 %copy-start.33 = (pred[256,256]{1,0:T(8,128)(4,1)S(1)}, pred[256,256]{1,0:T(8,128)(4,1)}, u32[]{:S(2)}) copy-start(pred[256,256]{1,0:T(8,128)(4,1)} %iota_compare_fusion.1) | copy-start | bytes 196612
  322.4 5.2 %copy-start.27 = (f32[256,256]{1,0:T(8,128)S(1)}, f32[256,256]{1,0:T(8,128)}, u32[]{:S(2)}) copy-start(f32[256,256]{1,0:T(8,128)} %fusion.143) | copy-start | bytes 786436
  324.6 6.4 %copy-start.40 = (f32[8,1]{0,1:T(1,128)S(1)}, f32[8,1]{0,1:T(1,128)}, u32[]{:S(2)}) copy-start(f32[8,1]{0,1:T(1,128)} %copy-done.39) | copy-start | bytes 100
  324.6 25.0 %copy-start.57 = (f32[8]{0:T(128)S(1)}, f32[8]{0:T(128)}, u32[]{:S(2)}) copy-start(f32[8]{0:T(128)} %get-tuple-element.232) | copy-start | bytes 100
  324.6 25.0 %collective-permute-start.18 = (f32[8,16512]{1,0:T(8,128)S(1)}, f32[8,16512]{1,0:T(8,128)S(1)}, u32[]{:S(2)}, u32[]{:S(2)}) collective-permute-start(f32[8,16512]{1,0:T(8,128)S(1)} %pad_maximum_fusion.5), channel_id=1, source_target_pairs={{0,256},{8,264},{16,272},{24,280},{32,288},{40,296},{48,304},{56,3... | collective-permute-start | bytes 1585160 | tf_op jit(solution)/shard_map/ppermute | solution.py:30
  327.7 24.2 %copy-start.56 = (f32[8]{0:T(128)S(1)}, f32[8]{0:T(128)}, u32[]{:S(2)}) copy-start(f32[8]{0:T(128)} %get-tuple-element.234) | copy-start | bytes 100
  331.0 22.3 %copy-start.42 = (f32[8]{0:T(128)S(1)}, f32[8]{0:T(128)}, u32[]{:S(2)}) copy-start(f32[8]{0:T(128)} %param.14) | copy-start | bytes 100
  351.8 12.1 %copy-start.15 = (f32[256,1,128]{0,2,1:T(8,128)S(1)}, f32[256,1,128]{0,2,1:T(8,128)}, u32[]{:S(2)}) copy-start(f32[256,1,128]{0,2,1:T(8,128)} %get-tuple-element.186) | copy-start | bytes 393220
  360.7 6.0 %copy-start.32 = (pred[1,256,256]{2,1,0:T(8,128)(4,1)S(1)}, pred[1,256,256]{2,1,0:T(8,128)(4,1)}, u32[]{:S(2)}) copy-start(pred[1,256,256]{2,1,0:T(8,128)(4,1)} %iota_compare_fusion) | copy-start | bytes 196612
  360.7 6.0 %copy-start.46 = (f32[8,256]{1,0:T(8,128)S(1)}, f32[8,256]{1,0:T(8,128)}, u32[]{:S(2)}) copy-start(f32[8,256]{1,0:T(8,128)} %add_bitcast_fusion.1) | copy-start | bytes 24580
  361.6 3.7 copy-start.44
  362.4 2.9 copy-start.34
  365.3 5.1 %copy-start.28 = (f32[256,256]{1,0:T(8,128)}, f32[256,256]{1,0:T(8,128)S(1)}, u32[]{:S(2)}) copy-start(f32[256,256]{1,0:T(8,128)S(1)} %fusion.172) | copy-start | bytes 786436
  366.7 4.7 copy-start.16
  376.2 4.5 copy-start.30
  376.2 4.5 copy-start.45
  380.7 9.6 %copy-start.29 = (bf16[256,1,1,128]{0,3,2,1:T(8,128)(2,1)S(1)}, bf16[256,1,1,128]{0,3,2,1:T(8,128)(2,1)}, u32[]{:S(2)}) copy-start(bf16[256,1,1,128]{0,3,2,1:T(8,128)(2,1)} %fusion.42) | copy-start | bytes 196612
  380.7 10.5 %copy-start.43 = (f32[8]{0:T(128)S(1)}, f32[8]{0:T(128)}, u32[]{:S(2)}) copy-start(f32[8]{0:T(128)} %param.14) | copy-start | bytes 100
  380.7 10.5 %copy-start.47 = (f32[256,8]{0,1:T(8,128)S(1)}, f32[256,8]{0,1:T(8,128)}, u32[]{:S(2)}) copy-start(f32[256,8]{0,1:T(8,128)} %get-tuple-element.194) | copy-start | bytes 24580
  380.7 10.5 %copy-start.55 = (f32[8]{0:T(128)S(1)}, f32[8]{0:T(128)}, u32[]{:S(2)}) copy-start(f32[8]{0:T(128)} %param.13) | copy-start | bytes 100
  380.7 11.3 %copy-start.6 = (bf16[256,776]{0,1:T(8,128)(2,1)S(1)}, bf16[256,776]{0,1:T(8,128)(2,1)}, u32[]{:S(2)}) copy-start(bf16[256,776]{0,1:T(8,128)(2,1)} %copy-done.5) | copy-start | bytes 1191940
  380.7 11.3 %copy-start.48 = (f32[512]{0:T(512)S(1)}, f32[512]{0:T(512)}, u32[]{:S(2)}) copy-start(f32[512]{0:T(512)} %mul.720) | copy-start | bytes 6148
  387.9 5.3 %copy-start.3 = (bf16[2048,776]{1,0:T(8,128)(2,1)S(1)}, bf16[2048,776]{1,0:T(8,128)(2,1)}, u32[]{:S(2)}) copy-start(bf16[2048,776]{1,0:T(8,128)(2,1)} %all-gather.2.cloned.1.call-done) | copy-start | bytes 9535492
  401.2 26.4 %collective-permute-start.22 = (f32[256,4,256]{2,0,1:T(8,128)}, f32[256,4,256]{2,0,1:T(8,128)}, u32[]{:S(2)}, u32[]{:S(2)}) collective-permute-start(f32[256,4,256]{2,0,1:T(8,128)} %select_bitcast_fusion), channel_id=1, source_target_pairs={{0,1},{1,0},{2,3},{3,2},{4,5},{5,4},{6,7},{7,6},{8,9},{9,8},{10,11... | collective-permute-start | bytes 3145736 | tf_op jit(solution)/shard_map/ppermute | solution.py:57
  405.2 22.4 %copy-start.4 = (f32[256,4,1,256]{3,0,1,2:T(8,128)S(1)}, f32[256,4,1,256]{3,0,1,2:T(8,128)}, u32[]{:S(2)}) copy-start(f32[256,4,1,256]{3,0,1,2:T(8,128)} %copy.220) | copy-start | bytes 3145732
  406.4 43.7 %collective-permute-start.19 = (f32[256,4,256]{2,0,1:T(8,128)}, f32[256,4,256]{2,0,1:T(8,128)}, u32[]{:S(2)}, u32[]{:S(2)}) collective-permute-start(f32[256,4,256]{2,0,1:T(8,128)} %select_bitcast_fusion.1), channel_id=1, source_target_pairs={{0,1},{1,0},{2,3},{3,2},{4,5},{5,4},{6,7},{7,6},{8,9},{9,8},{10,11... | collective-permute-start | bytes 3145736 | tf_op jit(solution)/shard_map/ppermute | solution.py:57
  409.7 40.3 %copy-start.1 = (f32[256,4,2,256]{3,0,2,1:T(8,128)S(1)}, f32[256,4,2,256]{3,0,2,1:T(8,128)}, u32[]{:S(2)}) copy-start(f32[256,4,2,256]{3,0,2,1:T(8,128)} %copy-done) | copy-start | bytes 6291460
  429.9 34.6 %collective-permute-start.23 = (f32[256,2,256]{2,0,1:T(8,128)}, f32[256,2,256]{2,0,1:T(8,128)S(1)}, u32[]{:S(2)}, u32[]{:S(2)}) collective-permute-start(f32[256,2,256]{2,0,1:T(8,128)} %select_bitcast_fusion.2), channel_id=1, source_target_pairs={{0,2},{1,3},{2,0},{3,1},{4,6},{5,7},{6,4},{7,5},{8,10},{9,11},{10,... | collective-permute-start | bytes 1572872 | tf_op jit(solution)/shard_map/ppermute | solution.py:57
  452.4 23.4 %collective-permute-start.20 = (f32[256,2,256]{2,0,1:T(8,128)}, f32[256,2,256]{2,0,1:T(8,128)S(1)}, u32[]{:S(2)}, u32[]{:S(2)}) collective-permute-start(f32[256,2,256]{2,0,1:T(8,128)} %select_bitcast_fusion.3), channel_id=1, source_target_pairs={{0,2},{1,3},{2,0},{3,1},{4,6},{5,7},{6,4},{7,5},{8,10},{9,11},{10,... | collective-permute-start | bytes 1572872 | tf_op jit(solution)/shard_map/ppermute | solution.py:57
  464.7 17.1 %collective-permute-start.24 = (f32[256,1,256]{2,0,1:T(8,128)S(1)}, f32[256,1,256]{2,0,1:T(8,128)S(1)}, u32[]{:S(2)}, u32[]{:S(2)}) collective-permute-start(f32[256,1,256]{2,0,1:T(8,128)S(1)} %select_bitcast_fusion.4), channel_id=1, source_target_pairs={{0,4},{1,5},{2,6},{3,7},{4,0},{5,1},{6,2},{7,3},{8,12},{9,13},{10,... | collective-permute-start | bytes 786440 | tf_op jit(solution)/shard_map/ppermute | solution.py:57
  475.9 22.5 %collective-permute-start.21 = (f32[256,1,256]{2,0,1:T(8,128)S(1)}, f32[256,1,256]{2,0,1:T(8,128)S(1)}, u32[]{:S(2)}, u32[]{:S(2)}) collective-permute-start(f32[256,1,256]{2,0,1:T(8,128)S(1)} %select_bitcast_fusion.5), channel_id=1, source_target_pairs={{0,4},{1,5},{2,6},{3,7},{4,0},{5,1},{6,2},{7,3},{8,12},{9,13},{10,... | collective-permute-start | bytes 786440 | tf_op jit(solution)/shard_map/ppermute | solution.py:57
  (20 other events, 24.3 us)
Sparse Core Ops, SparseCore 0:
  10.7 178.2 all-gather.1

commit v5 on v3

--- a/solution.py
+++ b/solution.py
@@ -24,6 +24,13 @@
     after_u = jnp.zeros_like(total_u)
     bit = 1
     while bit < devices:
+        if 2 * bit >= devices:
+            lower = (position & bit) != 0
+            send = jnp.where(lower, total_u, total_s)
+            got = lax.ppermute(send, axis, [(i, i ^ bit) for i in range(devices)])
+            before_s = jnp.where(lower, before_a * got + before_s, before_s)
+            after_u = jnp.where(lower, after_u, after_u + after_a * got)
+            break
         message = jnp.concatenate(
             [total_s, total_u, jnp.broadcast_to(total_a, (heads, 128))], axis=1
         )
@@ -145,12 +152,18 @@
     return final
 
 
-def from_each(x, axis):
-    devices = lax.axis_size(axis)
-    got = [x]
-    for k in range(1, devices):
-        got.append(lax.ppermute(x, axis, [(i, (i + k) % devices) for i in range(devices)]))
-    return got
+def doubled_rows(x, axis, order):
+    devices, position = (lax.axis_size(axis), lax.axis_index(axis))
+    for b in order:
+        bit = 1 << b
+        other = lax.ppermute(x, axis, [(i, i ^ bit) for i in range(devices)])
+        low = (position & bit) == 0
+        x = jnp.where(low, jnp.concatenate([x, other], 0), jnp.concatenate([other, x], 0))
+    rows = x.shape[0] // devices
+    x = x.reshape((2,) * len(order) + (rows,) + x.shape[1:])
+    axes = [len(order) - 1 - order.index(b) for b in reversed(range(len(order)))]
+    x = jnp.transpose(x, axes + list(range(len(order), x.ndim)))
+    return x.reshape((devices * rows,) + x.shape[len(order) + 1 :])
 
 
 def row_block(w, index, size):
@@ -158,7 +171,7 @@
 
 
 def per_device(tokens, w_in, w_bc, w_dt, dt_bias, decay_rate, skip_gain, w_out, cotangent):
-    devices, position = (lax.axis_size("tp"), lax.axis_index("tp"))
+    devices = lax.axis_size("tp")
     rows, width = tokens.shape
     heads = decay_rate.shape[0]
     inner = w_in.shape[1]
@@ -168,14 +181,18 @@
     w_all = lax.all_gather(
         jnp.concatenate([w_out.T, w_in, w_bc, w_dt], axis=1), "ctx", axis=0, tiled=True
     )
-    pieces = from_each(jnp.concatenate([tokens, cotangent], axis=1), "tp")
+    bits = devices.bit_length() - 1
+    pieces = doubled_rows(
+        jnp.concatenate([tokens, cotangent], axis=1), "tp", list(reversed(range(bits)))
+    )
     projected = None
     d_flat = None
     for k in range(devices):
-        block = row_block(w_all, (position - k) % devices, width)
-        term = jnp.dot(pieces[k][:, :width], block[:, out_cols:], preferred_element_type=jnp.float32)
+        block = w_all[k * width : (k + 1) * width]
+        piece = pieces[k * rows : (k + 1) * rows]
+        term = jnp.dot(piece[:, :width], block[:, out_cols:], preferred_element_type=jnp.float32)
         projected = term if projected is None else projected + term
-        term = jnp.dot(pieces[k][:, width:], block[:, :out_cols], preferred_element_type=jnp.float32)
+        term = jnp.dot(piece[:, width:], block[:, :out_cols], preferred_element_type=jnp.float32)
         d_flat = term if d_flat is None else d_flat + term
     values = projected[:, :inner].astype(jnp.bfloat16)
     pairs = projected[:, inner : inner + pair_cols].astype(jnp.bfloat16)

time: 486 us -> 412 us (0.85)
  waiting for transfers between devices: 278 us -> 236 us
  starting transfers between devices: 85.8 us -> 70.9 us
  matrix products: 48 us -> 38.9 us
  local copies, waits for them, and re-layouts: 20.1 us -> 14.4 us
    all_gather x1, waiting for transfers between devices: 132 us -> 72.3 us  [per_device(): lax.all_gather(jnp.concatenate([w_out.T, w_in, w_bc, w_dt], axis=1), 'ctx...]
    ppermute x7 -> x4, waiting for transfers between devices: 10.5 us -> 47.7 us  [the longest x3 36 us: doubled_rows(): other = lax.ppermute(x, axis, [(i, i ^ bit) for i in range(devices)])]
    ppermute x6 -> x5, waiting for transfers between devices: 84.1 us -> 65.1 us  [both_carries(): got = lax.ppermute(message, axis, [(i, i ^ bit) for i in range(devices)])]
    ppermute x6 -> x5, starting transfers between devices: 33.5 us -> 20.4 us  [both_carries(): got = lax.ppermute(message, axis, [(i, i ^ bit) for i in range(devices)])]
    ppermute x7 -> x4, starting transfers between devices: 32.6 us -> 22.7 us  [the longest x3 18.1 us: doubled_rows(): other = lax.ppermute(x, axis, [(i, i ^ bit) for i in range(devices)])]
    ppermute x6, starting transfers between devices: 19.6 us -> 27.7 us  [scattered_sum(): lax.ppermute(send, axis, [(i, i ^ bit) for i in range(devices)])]
  transfers between devices with their start and end apart: 20 -> 16, of which waited for: 15 -> 15; matrix products, arithmetic and copies ran while one was open for 8% -> 4% of each run, Pallas kernels for 0% -> 0%
where the time goes in v5:
time: 412 us; the launch traced here: 407 us
  waiting for transfers between devices  236 us (57%)
  starting transfers between devices  70.9 us (17%)
  matrix products  38.9 us (9%)
  other arithmetic  31.9 us (8%)
  between operations  15.2 us (4%)
  local copies, waits for them, and re-layouts  14.4 us (3%)
    all_gather x1, waiting for transfers between devices, per_device(): lax.all_gather(jnp.concatenate([w_out.T, w_in, w_bc, w_dt], axis=1), 'ctx...  72.3 us
    ppermute x5, waiting for transfers between devices, both_carries(): got = lax.ppermute(message, axis, [(i, i ^ bit) for i in range(devices)])  65.1 us
    ppermute x6, waiting for transfers between devices, scattered_sum(): lax.ppermute(send, axis, [(i, i ^ bit) for i in range(devices)])  50.9 us
    ppermute x3, waiting for transfers between devices, doubled_rows(): other = lax.ppermute(x, axis, [(i, i ^ bit) for i in range(devices)])  36 us
    ppermute x6, starting transfers between devices, scattered_sum(): lax.ppermute(send, axis, [(i, i ^ bit) for i in range(devices)])  27.7 us
    ppermute x5, starting transfers between devices, both_carries(): got = lax.ppermute(message, axis, [(i, i ^ bit) for i in range(devices)])  20.4 us
    ppermute x3, starting transfers between devices, doubled_rows(): other = lax.ppermute(x, axis, [(i, i ^ bit) for i in range(devices)])  18.1 us
    ppermute x1, waiting for transfers between devices, both_carries(): got = lax.ppermute(send, axis, [(i, i ^ bit) for i in range(devices)])  11.7 us
  transfers between devices with their start and end apart: 16, of which 15 were waited for; matrix products, arithmetic and copies ran while one was open for 4% of the time, Pallas kernels for 0%

profile of v5, /device:TPU:1, one launch (start us, length us, event | category | flops | bytes accessed | tf_op | source)
XLA Modules:
  0.0 407.3 jit_solution(14958314211909015721)
XLA Ops:
  8.0 1.4 pad_maximum_fusion.6
  11.3 8.3 %collective-permute-start = (bf16[256,512]{1,0:T(8,128)(2,1)S(1)}, bf16[256,512]{1,0:T(8,128)(2,1)S(1)}, u32[]{:S(2)}, u32[]{:S(2)}) collective-permute-start(bf16[256,512]{1,0:T(8,128)(2,1)S(1)} %constant_dynamic-update-slice_fusion), channel_id=1, source_target_pairs={{0,4},{1,5},{2,6},{3,7},{4,0},{5,1},{6,2},{7,3},{8,12},{9,13},{10,... | collective-permute-start | bytes 786440 | tf_op jit(solution)/shard_map/ppermute | solution.py:159
  19.6 8.5 %collective-permute-done = bf16[256,512]{1,0:T(8,128)(2,1)S(1)} collective-permute-done((bf16[256,512]{1,0:T(8,128)(2,1)S(1)}, bf16[256,512]{1,0:T(8,128)(2,1)S(1)}, u32[]{:S(2)}, u32[]{:S(2)}) %collective-permute-start) | collective-permute-done | bytes 262176 | tf_op jit(solution)/shard_map/ppermute | solution.py:159
  28.3 3.7 collective-permute-start.1
  32.0 7.7 %collective-permute-done.1 = bf16[512,512]{1,0:T(8,128)(2,1)S(1)} collective-permute-done((bf16[512,512]{1,0:T(8,128)(2,1)S(1)}, bf16[512,512]{1,0:T(8,128)(2,1)S(1)}, u32[]{:S(2)}, u32[]{:S(2)}) %collective-permute-start.1) | collective-permute-done | bytes 524320 | tf_op jit(solution)/shard_map/ppermute | solution.py:159
  40.2 6.1 %collective-permute-start.2 = (bf16[1024,512]{1,0:T(8,128)(2,1)S(1)}, bf16[1024,512]{1,0:T(8,128)(2,1)S(1)}, u32[]{:S(2)}, u32[]{:S(2)}) collective-permute-start(bf16[1024,512]{1,0:T(8,128)(2,1)S(1)} %maximum_select_fusion.1), channel_id=1, source_target_pairs={{0,1},{1,0},{2,3},{3,2},{4,5},{5,4},{6,7},{7,6},{8,9},{9,8},{10,11... | collective-permute-start | bytes 3145736 | tf_op jit(solution)/shard_map/ppermute | solution.py:159
  46.3 19.8 %collective-permute-done.2 = bf16[1024,512]{1,0:T(8,128)(2,1)S(1)} collective-permute-done((bf16[1024,512]{1,0:T(8,128)(2,1)S(1)}, bf16[1024,512]{1,0:T(8,128)(2,1)S(1)}, u32[]{:S(2)}, u32[]{:S(2)}) %collective-permute-start.2) | collective-permute-done | bytes 1048608 | tf_op jit(solution)/shard_map/ppermute | solution.py:159
  66.9 72.3 %all-gather.2.cloned.1.call-done = bf16[2048,1288]{1,0:T(8,128)(2,1)} async-done(((bf16[32,1288]{1,0:T(8,128)(2,1)}), bf16[2048,1288]{1,0:T(8,128)(2,1)}) %all-gather.2.cloned.1.call-update) | async-done | bytes 5275664 | tf_op jit(solution)/shard_map/all_gather | solution.py:181
  139.2 1.3 fusion.72
  140.5 1.5 convolution_add_fusion.6
  142.0 1.7 convolution_add_fusion.5
  143.7 1.3 convolution_add_fusion.4
  146.0 1.3 fusion.150
  152.3 1.4 fusion.88
  153.7 1.3 convolution_add_fusion.13
  155.0 1.3 convolution_add_fusion.12
  156.3 1.3 convolution_add_fusion.11
  157.6 1.3 convolution_add_fusion.10
  158.9 1.3 convolution_add_fusion.9
  160.3 1.2 convolution_add_fusion.8
  161.5 1.3 convolution_add_fusion.7
  164.7 2.1 collective-permute-start.3
  166.8 1.8 collective-permute-done.3
  168.8 1.0 add_select_fusion.16
  170.7 3.0 collective-permute-start.4
  173.7 12.5 %collective-permute-done.4 = f32[8,16512]{1,0:T(8,128)} collective-permute-done((f32[8,16512]{1,0:T(8,128)}, f32[8,16512]{1,0:T(8,128)}, u32[]{:S(2)}, u32[]{:S(2)}) %collective-permute-start.4) | collective-permute-done | bytes 528416 | tf_op jit(solution)/shard_map/ppermute | solution.py:37
  187.0 1.2 add_select_fusion.14
  189.1 3.9 collective-permute-start.5
  193.1 23.5 %collective-permute-done.5 = f32[8,16512]{1,0:T(8,128)} collective-permute-done((f32[8,16512]{1,0:T(8,128)}, f32[8,16512]{1,0:T(8,128)}, u32[]{:S(2)}, u32[]{:S(2)}) %collective-permute-start.5) | collective-permute-done | bytes 528416 | tf_op jit(solution)/shard_map/ppermute | solution.py:37
  218.0 1.2 add_select_fusion.12
  220.1 6.8 %collective-permute-start.6 = (f32[8,16512]{1,0:T(8,128)}, f32[8,16512]{1,0:T(8,128)}, u32[]{:S(2)}, u32[]{:S(2)}) collective-permute-start(f32[8,16512]{1,0:T(8,128)} %pad_maximum_fusion.3), channel_id=1, source_target_pairs={{0,64},{8,72},{16,80},{24,88},{32,96},{40,104},{48,112},{56,120},{... | collective-permute-start | bytes 1585160 | tf_op jit(solution)/shard_map/ppermute | solution.py:37
  229.0 20.7 %collective-permute-done.6 = f32[8,16512]{1,0:T(8,128)} collective-permute-done((f32[8,16512]{1,0:T(8,128)}, f32[8,16512]{1,0:T(8,128)}, u32[]{:S(2)}, u32[]{:S(2)}) %collective-permute-start.6) | collective-permute-done | bytes 528416 | tf_op jit(solution)/shard_map/ppermute | solution.py:37
  250.5 1.2 add_select_fusion.10
  251.9 4.5 %collective-permute-start.7 = (f32[8,16512]{1,0:T(8,128)S(1)}, f32[8,16512]{1,0:T(8,128)S(1)}, u32[]{:S(2)}, u32[]{:S(2)}) collective-permute-start(f32[8,16512]{1,0:T(8,128)S(1)} %pad_maximum_fusion.4), channel_id=1, source_target_pairs={{0,128},{8,136},{16,144},{24,152},{32,160},{40,168},{48,176},{56,1... | collective-permute-start | bytes 1585160 | tf_op jit(solution)/shard_map/ppermute | solution.py:37
  257.6 2.5 fusion.12
  260.1 6.4 %collective-permute-done.7 = f32[8,16512]{1,0:T(8,128)S(1)} collective-permute-done((f32[8,16512]{1,0:T(8,128)S(1)}, f32[8,16512]{1,0:T(8,128)S(1)}, u32[]{:S(2)}, u32[]{:S(2)}) %collective-permute-start.7) | collective-permute-done | bytes 528416 | tf_op jit(solution)/shard_map/ppermute | solution.py:37
  267.5 1.2 select_select_fusion
  268.7 4.6 %collective-permute-start.8 = (f32[8,8192]{1,0:T(8,128)S(1)}, f32[8,8192]{1,0:T(8,128)S(1)}, u32[]{:S(2)}, u32[]{:S(2)}) collective-permute-start(f32[8,8192]{1,0:T(8,128)S(1)} %select_select_fusion), channel_id=1, source_target_pairs={{0,256},{8,264},{16,272},{24,280},{32,288},{40,296},{48,304},{56,3... | collective-permute-start | bytes 786440 | tf_op jit(solution)/shard_map/ppermute | solution.py:30
  273.4 11.7 %collective-permute-done.8 = f32[8,8192]{1,0:T(8,128)S(1)} collective-permute-done((f32[8,8192]{1,0:T(8,128)S(1)}, f32[8,8192]{1,0:T(8,128)S(1)}, u32[]{:S(2)}, u32[]{:S(2)}) %collective-permute-start.8) | collective-permute-done | bytes 262176 | tf_op jit(solution)/shard_map/ppermute | solution.py:30
  285.1 1.4 fusion.80
  286.5 1.4 fusion.79
  291.2 3.1 fusion.22
  295.1 1.2 convolution_bitcast_fusion.1
  296.3 3.4 multiply_reduce_fusion.1
  300.1 1.2 fusion.26
  301.4 2.7 reduce-window.44
  304.3 1.2 fusion.20
  306.5 3.3 fusion
  311.3 3.1 collective-permute-start.12
  315.1 1.1 select_bitcast_fusion.1
  316.3 2.3 collective-permute-start.9
  318.6 18.3 %collective-permute-done.12 = f32[256,4,256]{2,0,1:T(8,128)} collective-permute-done((f32[256,4,256]{2,0,1:T(8,128)S(1)}, f32[256,4,256]{2,0,1:T(8,128)}, u32[]{:S(2)}, u32[]{:S(2)}) %collective-permute-start.12) | collective-permute-done | bytes 1048608 | tf_op jit(solution)/shard_map/ppermute | solution.py:64
  336.9 1.7 bitcast_add_fusion
  339.6 3.0 collective-permute-start.13
  342.6 16.8 %collective-permute-done.9 = f32[256,4,256]{2,0,1:T(8,128)} collective-permute-done((f32[256,4,256]{2,0,1:T(8,128)}, f32[256,4,256]{2,0,1:T(8,128)}, u32[]{:S(2)}, u32[]{:S(2)}) %collective-permute-start.9) | collective-permute-done | bytes 1048608 | tf_op jit(solution)/shard_map/ppermute | solution.py:64
  359.4 1.4 fusion.34
  360.8 1.0 copy-done.1
  362.7 3.2 collective-permute-start.10
  365.9 5.4 %collective-permute-done.13 = f32[256,2,256]{2,0,1:T(8,128)} collective-permute-done((f32[256,2,256]{2,0,1:T(8,128)}, f32[256,2,256]{2,0,1:T(8,128)}, u32[]{:S(2)}, u32[]{:S(2)}) %collective-permute-start.13) | collective-permute-done | bytes 524320 | tf_op jit(solution)/shard_map/ppermute | solution.py:64
  371.3 1.1 fusion.45
  372.5 8.0 %collective-permute-start.14 = (f32[256,1,256]{2,0,1:T(8,128)S(1)}, f32[256,1,256]{2,0,1:T(8,128)S(1)}, u32[]{:S(2)}, u32[]{:S(2)}) collective-permute-start(f32[256,1,256]{2,0,1:T(8,128)S(1)} %select_bitcast_fusion.4), channel_id=1, source_target_pairs={{0,4},{1,5},{2,6},{3,7},{4,0},{5,1},{6,2},{7,3},{8,12},{9,13},{10,... | collective-permute-start | bytes 786440 | tf_op jit(solution)/shard_map/ppermute | solution.py:64
  380.6 1.9 collective-permute-done.10
  382.6 8.0 %collective-permute-start.11 = (f32[256,1,256]{2,0,1:T(8,128)S(1)}, f32[256,1,256]{2,0,1:T(8,128)S(1)}, u32[]{:S(2)}, u32[]{:S(2)}) collective-permute-start(f32[256,1,256]{2,0,1:T(8,128)S(1)} %select_bitcast_fusion.5), channel_id=1, source_target_pairs={{0,4},{1,5},{2,6},{3,7},{4,0},{5,1},{6,2},{7,3},{8,12},{9,13},{10,... | collective-permute-start | bytes 786440 | tf_op jit(solution)/shard_map/ppermute | solution.py:64
  391.4 8.4 %collective-permute-done.11 = f32[256,1,256]{2,0,1:T(8,128)S(1)} collective-permute-done((f32[256,1,256]{2,0,1:T(8,128)S(1)}, f32[256,1,256]{2,0,1:T(8,128)S(1)}, u32[]{:S(2)}, u32[]{:S(2)}) %collective-permute-start.11) | collective-permute-done | bytes 262176 | tf_op jit(solution)/shard_map/ppermute | solution.py:64
  (204 shorter events, 32.8 us)
Async XLA Ops:
  7.2 132.0 %all-gather.2.cloned.1.call-start = ((), (), s32[]{:S(2)}) async-start(), calls=%async_computation | async-start | bytes 5857280 | tf_op jit(solution)/shard_map/all_gather | solution.py:181
  11.3 16.8 %collective-permute-start = (bf16[256,512]{1,0:T(8,128)(2,1)S(1)}, bf16[256,512]{1,0:T(8,128)(2,1)S(1)}, u32[]{:S(2)}, u32[]{:S(2)}) collective-permute-start(bf16[256,512]{1,0:T(8,128)(2,1)S(1)} %constant_dynamic-update-slice_fusion), channel_id=1, source_target_pairs={{0,4},{1,5},{2,6},{3,7},{4,0},{5,1},{6,2},{7,3},{8,12},{9,13},{10,... | collective-permute-start | bytes 786440 | tf_op jit(solution)/shard_map/ppermute | solution.py:159
  28.3 11.4 %collective-permute-start.1 = (bf16[512,512]{1,0:T(8,128)(2,1)S(1)}, bf16[512,512]{1,0:T(8,128)(2,1)S(1)}, u32[]{:S(2)}, u32[]{:S(2)}) collective-permute-start(bf16[512,512]{1,0:T(8,128)(2,1)S(1)} %maximum_select_fusion.2), channel_id=1, source_target_pairs={{0,2},{1,3},{2,0},{3,1},{4,6},{5,7},{6,4},{7,5},{8,10},{9,11},{10,... | collective-permute-start | bytes 1572872 | tf_op jit(solution)/shard_map/ppermute | solution.py:159
  40.2 26.0 %collective-permute-start.2 = (bf16[1024,512]{1,0:T(8,128)(2,1)S(1)}, bf16[1024,512]{1,0:T(8,128)(2,1)S(1)}, u32[]{:S(2)}, u32[]{:S(2)}) collective-permute-start(bf16[1024,512]{1,0:T(8,128)(2,1)S(1)} %maximum_select_fusion.1), channel_id=1, source_target_pairs={{0,1},{1,0},{2,3},{3,2},{4,5},{5,4},{6,7},{7,6},{8,9},{9,8},{10,11... | collective-permute-start | bytes 3145736 | tf_op jit(solution)/shard_map/ppermute | solution.py:159
  66.9 78.8 %copy-start.5 = (bf16[2,2,2,256,512]{4,3,2,1,0:T(8,128)(2,1)}, bf16[2,2,2,256,512]{4,3,2,1,0:T(8,128)(2,1)S(1)}, u32[]{:S(2)}) copy-start(bf16[2,2,2,256,512]{4,3,2,1,0:T(8,128)(2,1)S(1)} %copy.126) | copy-start | bytes 6291460
  140.5 4.5 %copy-start = (bf16[2048,1288]{1,0:T(8,128)(2,1)S(1)}, bf16[2048,1288]{1,0:T(8,128)(2,1)}, u32[]{:S(2)}) copy-start(bf16[2048,1288]{1,0:T(8,128)(2,1)} %all-gather.2.cloned.1.call-done) | copy-start | bytes 15826948
  145.7 2.6 copy-start.32
  145.7 2.6 copy-start.44
  146.0 14.2 %slice-start = ((s8[5767168]{0:T(1024)(128)(4,1)}), s8[1572864]{0:T(1024)(128)(4,1)S(1)}, s32[]{:S(2)}) async-start(s8[5767168]{0:T(1024)(128)(4,1)} %bitcast.279), calls=%async_computation.1 | async-start | bytes 3145728
  147.4 0.9 copy-start.13
  148.5 5.2 %copy-start.37 = (f32[8]{0:T(128)}, f32[8]{0:T(128)S(1)}, u32[]{:S(2)}) copy-start(f32[8]{0:T(128)S(1)} %get-tuple-element.205) | copy-start | bytes 100
  149.4 13.3 %copy-start.17 = (f32[256,8]{0,1:T(8,128)}, f32[256,8]{0,1:T(8,128)S(1)}, u32[]{:S(2)}) copy-start(f32[256,8]{0,1:T(8,128)S(1)} %get-tuple-element.203) | copy-start | bytes 24580
  150.0 0.7 copy-start.9
  151.6 11.2 %copy-start.11 = (f32[256,128]{1,0:T(8,128)}, f32[256,128]{1,0:T(8,128)S(1)}, u32[]{:S(2)}) copy-start(f32[256,128]{1,0:T(8,128)S(1)} %copy.137) | copy-start | bytes 393220
  151.6 12.2 %copy-start.40 = (f32[8]{0:T(128)}, f32[8]{0:T(128)S(1)}, u32[]{:S(2)}) copy-start(f32[8]{0:T(128)S(1)} %negate_exponential_fusion) | copy-start | bytes 100
  152.2 8.0 %slice-start.1 = ((s8[5767168]{0:T(1024)(128)(4,1)}), s8[4194304]{0:T(1024)(128)(4,1)S(1)}, s32[]{:S(2)}) async-start(s8[5767168]{0:T(1024)(128)(4,1)} %bitcast.279), calls=%async_computation.2 | async-start | bytes 8388608
  161.4 7.3 %copy-start.38 = (f32[8]{0:T(128)S(1)}, f32[8]{0:T(128)}, u32[]{:S(2)}) copy-start(f32[8]{0:T(128)} %copy-done.37) | copy-start | bytes 100
  164.7 4.0 collective-permute-start.3
  168.8 18.3 %copy-start.21 = (f32[8,1]{0,1:T(1,128)}, f32[8,1]{0,1:T(1,128)S(1)}, u32[]{:S(2)}) copy-start(f32[8,1]{0,1:T(1,128)S(1)} %copy.175) | copy-start | bytes 100
  168.8 18.3 %copy-start.43 = (f32[8]{0:T(128)}, f32[8]{0:T(128)S(1)}, u32[]{:S(2)}) copy-start(f32[8]{0:T(128)S(1)} %fusion.132) | copy-start | bytes 100
  169.7 47.6 %copy-start.39 = (f32[8]{0:T(128)S(1)}, f32[8]{0:T(128)}, u32[]{:S(2)}) copy-start(f32[8]{0:T(128)} %copy-done.37) | copy-start | bytes 100
  170.7 15.6 %collective-permute-start.4 = (f32[8,16512]{1,0:T(8,128)}, f32[8,16512]{1,0:T(8,128)}, u32[]{:S(2)}, u32[]{:S(2)}) collective-permute-start(f32[8,16512]{1,0:T(8,128)} %pad_maximum_fusion.1), channel_id=1, source_target_pairs={{0,16},{8,24},{16,0},{24,8},{32,48},{40,56},{48,32},{56,40},{64,80... | collective-permute-start | bytes 1585160 | tf_op jit(solution)/shard_map/ppermute | solution.py:37
  187.0 31.0 %copy-start.24 = (f32[8,1]{0,1:T(1,128)}, f32[8,1]{0,1:T(1,128)S(1)}, u32[]{:S(2)}) copy-start(f32[8,1]{0,1:T(1,128)S(1)} %copy.176) | copy-start | bytes 100
  187.0 30.3 %copy-start.22 = (f32[8,1]{0,1:T(1,128)S(1)}, f32[8,1]{0,1:T(1,128)}, u32[]{:S(2)}) copy-start(f32[8,1]{0,1:T(1,128)} %copy-done.21) | copy-start | bytes 100
  188.2 38.8 %copy-start.46 = (f32[8]{0:T(128)S(1)}, f32[8]{0:T(128)}, u32[]{:S(2)}) copy-start(f32[8]{0:T(128)} %param.15) | copy-start | bytes 100
  189.1 27.5 %collective-permute-start.5 = (f32[8,16512]{1,0:T(8,128)}, f32[8,16512]{1,0:T(8,128)}, u32[]{:S(2)}, u32[]{:S(2)}) collective-permute-start(f32[8,16512]{1,0:T(8,128)} %pad_maximum_fusion.2), channel_id=1, source_target_pairs={{0,32},{8,40},{16,48},{24,56},{32,0},{40,8},{48,16},{56,24},{64,96... | collective-permute-start | bytes 1585160 | tf_op jit(solution)/shard_map/ppermute | solution.py:37
  217.4 0.6 copy-start.28
  219.2 37.2 %copy-start.16 = (f32[8,2,128]{2,0,1:T(8,128)S(1)}, f32[8,2,128]{2,0,1:T(8,128)}, u32[]{:S(2)}) copy-start(f32[8,2,128]{2,0,1:T(8,128)} %copy-done.15) | copy-start | bytes 24580
  219.2 37.2 %copy-start.27 = (f32[8,2]{0,1:T(2,128)S(1)}, f32[8,2]{0,1:T(2,128)}, u32[]{:S(2)}) copy-start(f32[8,2]{0,1:T(2,128)} %copy-done.26) | copy-start | bytes 196
  220.1 29.6 %collective-permute-start.6 = (f32[8,16512]{1,0:T(8,128)}, f32[8,16512]{1,0:T(8,128)}, u32[]{:S(2)}, u32[]{:S(2)}) collective-permute-start(f32[8,16512]{1,0:T(8,128)} %pad_maximum_fusion.3), channel_id=1, source_target_pairs={{0,64},{8,72},{16,80},{24,88},{32,96},{40,104},{48,112},{56,120},{... | collective-permute-start | bytes 1585160 | tf_op jit(solution)/shard_map/ppermute | solution.py:37
  250.5 5.9 %copy-start.30 = (f32[8,1]{0,1:T(1,128)}, f32[8,1]{0,1:T(1,128)S(1)}, u32[]{:S(2)}) copy-start(f32[8,1]{0,1:T(1,128)S(1)} %copy.178) | copy-start | bytes 100
  250.5 5.9 %copy-start.41 = (f32[8]{0:T(128)}, f32[8]{0:T(128)S(1)}, u32[]{:S(2)}) copy-start(f32[8]{0:T(128)S(1)} %multiply_bitcast_fusion.2) | copy-start | bytes 100
  251.9 14.7 %collective-permute-start.7 = (f32[8,16512]{1,0:T(8,128)S(1)}, f32[8,16512]{1,0:T(8,128)S(1)}, u32[]{:S(2)}, u32[]{:S(2)}) collective-permute-start(f32[8,16512]{1,0:T(8,128)S(1)} %pad_maximum_fusion.4), channel_id=1, source_target_pairs={{0,128},{8,136},{16,144},{24,152},{32,160},{40,168},{48,176},{56,1... | collective-permute-start | bytes 1585160 | tf_op jit(solution)/shard_map/ppermute | solution.py:37
  256.4 0.9 copy-start.10
  256.5 1.1 copy-start.20
  257.6 9.9 %copy-start.42 = (f32[8]{0:T(128)S(1)}, f32[8]{0:T(128)}, u32[]{:S(2)}) copy-start(f32[8]{0:T(128)} %copy-done.41) | copy-start | bytes 100
  257.6 15.7 %copy-start.23 = (f32[8,1]{0,1:T(1,128)S(1)}, f32[8,1]{0,1:T(1,128)}, u32[]{:S(2)}) copy-start(f32[8,1]{0,1:T(1,128)} %copy-done.21) | copy-start | bytes 100
  257.6 15.7 %copy-start.25 = (f32[8,1]{0,1:T(1,128)S(1)}, f32[8,1]{0,1:T(1,128)}, u32[]{:S(2)}) copy-start(f32[8,1]{0,1:T(1,128)} %copy-done.24) | copy-start | bytes 100
  257.6 15.7 %copy-start.29 = (f32[8,1]{0,1:T(1,128)S(1)}, f32[8,1]{0,1:T(1,128)}, u32[]{:S(2)}) copy-start(f32[8,1]{0,1:T(1,128)} %copy-done.28) | copy-start | bytes 100
  257.6 15.7 %copy-start.31 = (f32[8,1]{0,1:T(1,128)S(1)}, f32[8,1]{0,1:T(1,128)}, u32[]{:S(2)}) copy-start(f32[8,1]{0,1:T(1,128)} %copy-done.30) | copy-start | bytes 100
  266.6 0.8 copy-start.6
  268.7 19.3 %copy-start.33 = (f32[8]{0:T(128)S(1)}, f32[8]{0:T(128)}, u32[]{:S(2)}) copy-start(f32[8]{0:T(128)} %param.14) | copy-start | bytes 100
  268.7 16.4 %collective-permute-start.8 = (f32[8,8192]{1,0:T(8,128)S(1)}, f32[8,8192]{1,0:T(8,128)S(1)}, u32[]{:S(2)}, u32[]{:S(2)}) collective-permute-start(f32[8,8192]{1,0:T(8,128)S(1)} %select_select_fusion), channel_id=1, source_target_pairs={{0,256},{8,264},{16,272},{24,280},{32,288},{40,296},{48,304},{56,3... | collective-permute-start | bytes 786440 | tf_op jit(solution)/shard_map/ppermute | solution.py:30
  286.5 3.7 copy-start.7
  286.5 3.7 copy-start.8
  288.0 3.3 copy-start.19
  296.3 7.9 %copy-start.12 = (f32[256,128]{1,0:T(8,128)S(1)}, f32[256,128]{1,0:T(8,128)}, u32[]{:S(2)}) copy-start(f32[256,128]{1,0:T(8,128)} %copy-done.11) | copy-start | bytes 393220
  296.3 7.9 %copy-start.18 = (f32[256,8]{0,1:T(8,128)S(1)}, f32[256,8]{0,1:T(8,128)}, u32[]{:S(2)}) copy-start(f32[256,8]{0,1:T(8,128)} %copy-done.17) | copy-start | bytes 24580
  299.7 5.8 %copy-start.34 = (f32[8]{0:T(128)S(1)}, f32[8]{0:T(128)}, u32[]{:S(2)}) copy-start(f32[8]{0:T(128)} %param.14) | copy-start | bytes 100
  299.7 5.8 %copy-start.35 = (f32[256,8]{0,1:T(8,128)S(1)}, f32[256,8]{0,1:T(8,128)}, u32[]{:S(2)}) copy-start(f32[256,8]{0,1:T(8,128)} %get-tuple-element.194) | copy-start | bytes 24580
  299.7 5.8 %copy-start.45 = (f32[8]{0:T(128)S(1)}, f32[8]{0:T(128)}, u32[]{:S(2)}) copy-start(f32[8]{0:T(128)} %param.13) | copy-start | bytes 100
  299.7 6.6 %copy-start.14 = (f32[256,8,64]{0,2,1:T(8,128)S(1)}, f32[256,8,64]{0,2,1:T(8,128)}, u32[]{:S(2)}) copy-start(f32[256,8,64]{0,2,1:T(8,128)} %get-tuple-element.209) | copy-start | bytes 1572868
  299.7 6.6 %copy-start.36 = (f32[512]{0:T(512)S(1)}, f32[512]{0:T(512)}, u32[]{:S(2)}) copy-start(f32[512]{0:T(512)} %mul.676) | copy-start | bytes 6148
  310.3 1.0 copy-start.3
  310.6 3.7 copy-start.4
  310.6 3.7 slice-start.2
  311.3 25.7 %collective-permute-start.12 = (f32[256,4,256]{2,0,1:T(8,128)S(1)}, f32[256,4,256]{2,0,1:T(8,128)}, u32[]{:S(2)}, u32[]{:S(2)}) collective-permute-start(f32[256,4,256]{2,0,1:T(8,128)S(1)} %select_bitcast_fusion), channel_id=1, source_target_pairs={{0,1},{1,0},{2,3},{3,2},{4,5},{5,4},{6,7},{7,6},{8,9},{9,8},{10,11... | collective-permute-start | bytes 3145736 | tf_op jit(solution)/shard_map/ppermute | solution.py:64
  316.3 43.1 %collective-permute-start.9 = (f32[256,4,256]{2,0,1:T(8,128)}, f32[256,4,256]{2,0,1:T(8,128)}, u32[]{:S(2)}, u32[]{:S(2)}) collective-permute-start(f32[256,4,256]{2,0,1:T(8,128)} %select_bitcast_fusion.1), channel_id=1, source_target_pairs={{0,1},{1,0},{2,3},{3,2},{4,5},{5,4},{6,7},{7,6},{8,9},{9,8},{10,11... | collective-permute-start | bytes 3145736 | tf_op jit(solution)/shard_map/ppermute | solution.py:64
  339.6 31.8 %collective-permute-start.13 = (f32[256,2,256]{2,0,1:T(8,128)}, f32[256,2,256]{2,0,1:T(8,128)}, u32[]{:S(2)}, u32[]{:S(2)}) collective-permute-start(f32[256,2,256]{2,0,1:T(8,128)} %select_bitcast_fusion.2), channel_id=1, source_target_pairs={{0,2},{1,3},{2,0},{3,1},{4,6},{5,7},{6,4},{7,5},{8,10},{9,11},{10,... | collective-permute-start | bytes 1572872 | tf_op jit(solution)/shard_map/ppermute | solution.py:64
  360.8 1.0 copy-start.1
  362.7 19.7 %copy-start.2 = (f32[256,4,256]{2,0,1:T(8,128)S(1)}, f32[256,4,256]{2,0,1:T(8,128)}, u32[]{:S(2)}) copy-start(f32[256,4,256]{2,0,1:T(8,128)} %copy-done.1) | copy-start | bytes 3145732
  362.7 19.7 %collective-permute-start.10 = (f32[256,2,256]{2,0,1:T(8,128)}, f32[256,2,256]{2,0,1:T(8,128)S(1)}, u32[]{:S(2)}, u32[]{:S(2)}) collective-permute-start(f32[256,2,256]{2,0,1:T(8,128)} %select_bitcast_fusion.3), channel_id=1, source_target_pairs={{0,2},{1,3},{2,0},{3,1},{4,6},{5,7},{6,4},{7,5},{8,10},{9,11},{10,... | collective-permute-start | bytes 1572872 | tf_op jit(solution)/shard_map/ppermute | solution.py:64
  372.5 18.1 %collective-permute-start.14 = (f32[256,1,256]{2,0,1:T(8,128)S(1)}, f32[256,1,256]{2,0,1:T(8,128)S(1)}, u32[]{:S(2)}, u32[]{:S(2)}) collective-permute-start(f32[256,1,256]{2,0,1:T(8,128)S(1)} %select_bitcast_fusion.4), channel_id=1, source_target_pairs={{0,4},{1,5},{2,6},{3,7},{4,0},{5,1},{6,2},{7,3},{8,12},{9,13},{10,... | collective-permute-start | bytes 786440 | tf_op jit(solution)/shard_map/ppermute | solution.py:64
  382.6 17.2 %collective-permute-start.11 = (f32[256,1,256]{2,0,1:T(8,128)S(1)}, f32[256,1,256]{2,0,1:T(8,128)S(1)}, u32[]{:S(2)}, u32[]{:S(2)}) collective-permute-start(f32[256,1,256]{2,0,1:T(8,128)S(1)} %select_bitcast_fusion.5), channel_id=1, source_target_pairs={{0,4},{1,5},{2,6},{3,7},{4,0},{5,1},{6,2},{7,3},{8,12},{9,13},{10,... | collective-permute-start | bytes 786440 | tf_op jit(solution)/shard_map/ppermute | solution.py:64
  (2 other events, 1.2 us)
Sparse Core Ops, SparseCore 0:
  10.7 128.4 all-gather.1

commit v6 on v5

--- a/solution.py
+++ b/solution.py
@@ -1,7 +1,7 @@
 import jax
 import jax.numpy as jnp
 from jax import lax
-from jax.sharding import PartitionSpec as P
+from jax.sharding import Mesh, PartitionSpec as P
 
 HEADDIM = 64
 STATE = 128
@@ -9,6 +9,7 @@
 
 
 HIGH = lax.Precision.HIGHEST
+CTX = ("rest", "core")
 
 
 def both_carries(decay, forward, backward, axis):
@@ -178,9 +179,15 @@
     pair_cols = w_bc.shape[1]
     groups = pair_cols // (2 * STATE)
     out_cols = w_out.shape[0]
-    w_all = lax.all_gather(
-        jnp.concatenate([w_out.T, w_in, w_bc, w_dt], axis=1), "ctx", axis=0, tiled=True
-    )
+    w_own = jnp.concatenate([w_out.T, w_in, w_bc, w_dt], axis=1)
+    w_same = lax.all_gather(w_own, "rest", axis=0, tiled=True)
+    w_other = lax.ppermute(w_same, "core", [(0, 1), (1, 0)])
+    core = lax.axis_index("core")
+    pair = (w_same.shape[0] // w_own.shape[0], 1, w_own.shape[0], w_own.shape[1])
+    low, high = (w_same.reshape(pair), w_other.reshape(pair))
+    w_all = jnp.where(
+        core == 0, jnp.concatenate([low, high], axis=1), jnp.concatenate([high, low], axis=1)
+    ).reshape(-1, w_own.shape[1])
     bits = devices.bit_length() - 1
     pieces = doubled_rows(
         jnp.concatenate([tokens, cotangent], axis=1), "tp", list(reversed(range(bits)))
@@ -206,7 +213,7 @@
     decay_total = jnp.exp(-jnp.sum(step_size * decay_rate[None, :], axis=0))
     d_mixed = d_flat.reshape(rows, heads, HEADDIM)
     own_adjoint = local_adjoint(d_mixed, c_rows, step_size, decay_rate)
-    state_in, adjoint = both_carries(decay_total, end_state, own_adjoint, "ctx")
+    state_in, adjoint = both_carries(decay_total, end_state, own_adjoint, CTX)
 
     def with_state(vals, brows, crows, steps):
         return ssd_core(vals, brows, crows, steps, decay_rate, state_in)
@@ -241,21 +248,14 @@
 
 
 def solution(mesh):
-    placed = (
-        P("ctx", "tp"),
-        P("ctx", "tp"),
-        P("ctx", "tp"),
-        P("ctx", "tp"),
-        P("tp"),
-        P("tp"),
-        P("tp"),
-        P("tp", "ctx"),
-        P("ctx", "tp"),
-    )
+    ctx, tp = (mesh.shape["ctx"], mesh.shape["tp"])
+    split = Mesh(mesh.devices.reshape(ctx // 2, 2, tp), ("rest", "core", "tp"))
+    rows = P(CTX, "tp")
+    placed = (rows, rows, rows, rows, P("tp"), P("tp"), P("tp"), P("tp", CTX), rows)
     return jax.shard_map(
         per_device,
-        mesh=mesh,
+        mesh=split,
         in_specs=placed,
-        out_specs=(P("ctx", "tp"), P("ctx", "tp")),
+        out_specs=(rows, rows),
         check_vma=False,
     )

time: 412 us -> 534 us (1.30)
  waiting for transfers between devices: 236 us -> 318 us
  local copies, waits for them, and re-layouts: 14.4 us -> 37.2 us
  starting transfers between devices: 70.9 us -> 78.4 us
  other arithmetic: 31.9 us -> 37.5 us
    all_gather x1, waiting for transfers between devices: 72.3 us -> 143 us  [per_device(): w_same = lax.all_gather(w_own, 'rest', axis=0, tiled=True)]
    ppermute x0 -> x1, starting transfers between devices: none -> 25.3 us  [per_device(): w_other = lax.ppermute(w_same, 'core', [(0, 1), (1, 0)])]
    ppermute x5, starting transfers between devices: 20.4 us -> 12.3 us  [both_carries(): got = lax.ppermute(message, axis, [(i, i ^ bit) for i in range(devices)])]
    ppermute x3, waiting for transfers between devices: 36 us -> 42.7 us  [doubled_rows(): other = lax.ppermute(x, axis, [(i, i ^ bit) for i in range(devices)])]
    ppermute x3, starting transfers between devices: 18.1 us -> 11.9 us  [doubled_rows(): other = lax.ppermute(x, axis, [(i, i ^ bit) for i in range(devices)])]
    unnamed x107 -> x113, local copies, waits for them, and re-layouts: 7.86 us -> 13.9 us
    dot_general x8, matrix products: 8.03 us -> 2.47 us  [per_device(): jnp.dot(piece[:, :width], block[:, out_cols:], preferred_element_type=jnp...]
  transfers between devices with their start and end apart: 16 -> 17, of which waited for: 15 -> 16; matrix products, arithmetic and copies ran while one was open for 4% -> 4% of each run, Pallas kernels for 0% -> 0%
where the time goes in v6:
time: 534 us; the launch traced here: 525 us
  waiting for transfers between devices  318 us (60%)
  starting transfers between devices  78.4 us (15%)
  matrix products  38.6 us (7%)
  other arithmetic  37.5 us (7%)
  local copies, waits for them, and re-layouts  37.2 us (7%)
  between operations  15.3 us (3%)
    all_gather x1, waiting for transfers between devices, per_device(): w_same = lax.all_gather(w_own, 'rest', axis=0, tiled=True)  143 us
    ppermute x5, waiting for transfers between devices, both_carries(): got = lax.ppermute(message, axis, [(i, i ^ bit) for i in range(devices)])  66.4 us
    ppermute x6, waiting for transfers between devices, scattered_sum(): lax.ppermute(send, axis, [(i, i ^ bit) for i in range(devices)])  53.5 us
    ppermute x3, waiting for transfers between devices, doubled_rows(): other = lax.ppermute(x, axis, [(i, i ^ bit) for i in range(devices)])  42.7 us
    ppermute x1, starting transfers between devices, per_device(): w_other = lax.ppermute(w_same, 'core', [(0, 1), (1, 0)])  25.3 us
    ppermute x6, starting transfers between devices, scattered_sum(): lax.ppermute(send, axis, [(i, i ^ bit) for i in range(devices)])  24 us
    unnamed x113, local copies, waits for them, and re-layouts  13.9 us
    ppermute x5, starting transfers between devices, both_carries(): got = lax.ppermute(message, axis, [(i, i ^ bit) for i in range(devices)])  12.3 us
  transfers between devices with their start and end apart: 17, of which 16 were waited for; matrix products, arithmetic and copies ran while one was open for 4% of the time, Pallas kernels for 0%

profile of v6, /device:TPU:1, one launch (start us, length us, event | category | flops | bytes accessed | tf_op | source)
XLA Modules:
  0.0 525.2 jit_solution(5630819596224769940)
XLA Ops:
  8.0 1.4 pad_maximum_fusion.6
  9.5 143.3 %all-gather.2.cloned.1.call-done = bf16[1024,1288]{1,0:T(8,128)(2,1)} async-done(((bf16[32,1288]{1,0:T(8,128)(2,1)}), bf16[1024,1288]{1,0:T(8,128)(2,1)}) %all-gather.2.cloned.1.call-update) | async-done | bytes 2637840 | tf_op jit(solution)/shard_map/all_gather | solution.py:183
  152.8 4.6 copy.229
  157.4 25.3 %collective-permute-start.3 = (bf16[1024,1288]{0,1:T(8,128)(2,1)}, bf16[1024,1288]{0,1:T(8,128)(2,1)}, u32[]{:S(2)}, u32[]{:S(2)}) collective-permute-start(bf16[1024,1288]{0,1:T(8,128)(2,1)} %copy.229), channel_id=1, source_target_pairs={{0,8},{8,0},{1,9},{9,1},{2,10},{10,2},{3,11},{11,3},{4,12},{12,4},... | collective-permute-start | bytes 7913480 | tf_op jit(solution)/shard_map/ppermute | solution.py:184
  182.8 4.7 collective-permute-start
  187.4 9.1 %collective-permute-done = bf16[256,512]{1,0:T(8,128)(2,1)S(1)} collective-permute-done((bf16[256,512]{1,0:T(8,128)(2,1)S(1)}, bf16[256,512]{1,0:T(8,128)(2,1)S(1)}, u32[]{:S(2)}, u32[]{:S(2)}) %collective-permute-start) | collective-permute-done | bytes 262176 | tf_op jit(solution)/shard_map/ppermute | solution.py:160
  196.7 4.4 collective-permute-start.1
  201.1 11.7 %collective-permute-done.1 = bf16[512,512]{1,0:T(8,128)(2,1)S(1)} collective-permute-done((bf16[512,512]{1,0:T(8,128)(2,1)S(1)}, bf16[512,512]{1,0:T(8,128)(2,1)S(1)}, u32[]{:S(2)}, u32[]{:S(2)}) %collective-permute-start.1) | collective-permute-done | bytes 524320 | tf_op jit(solution)/shard_map/ppermute | solution.py:160
  213.2 2.9 collective-permute-start.2
  216.1 22.0 %collective-permute-done.2 = bf16[1024,512]{1,0:T(8,128)(2,1)S(1)} collective-permute-done((bf16[1024,512]{1,0:T(8,128)(2,1)S(1)}, bf16[1024,512]{1,0:T(8,128)(2,1)S(1)}, u32[]{:S(2)}, u32[]{:S(2)}) %collective-permute-start.2) | collective-permute-done | bytes 1048608 | tf_op jit(solution)/shard_map/ppermute | solution.py:160
  238.7 1.4 copy.227
  240.1 4.7 copy.230
  244.8 4.6 maximum_select_fusion
  250.1 1.8 copy-done
  252.9 2.6 copy-done.7
  262.8 1.2 fusion.88
  264.9 1.6 copy.239
  266.6 1.2 convolution_add_fusion.13
  267.8 1.2 convolution_add_fusion.12
  269.0 1.2 convolution_add_fusion.11
  270.2 1.2 convolution_add_fusion.10
  271.5 1.2 convolution_add_fusion.9
  272.7 1.2 convolution_add_fusion.8
  273.9 1.2 convolution_add_fusion.7
  276.8 1.5 fusion.27
  278.3 1.3 fusion.28
  280.1 4.5 collective-permute-start.4
  284.6 1.5 collective-permute-done.4
  287.0 1.4 add_select_fusion.16
  289.3 1.9 collective-permute-start.5
  291.2 13.4 %collective-permute-done.5 = f32[8,16512]{1,0:T(8,128)S(1)} collective-permute-done((f32[8,16512]{1,0:T(8,128)}, f32[8,16512]{1,0:T(8,128)S(1)}, u32[]{:S(2)}, u32[]{:S(2)}) %collective-permute-start.5) | collective-permute-done | bytes 528416 | tf_op jit(solution)/shard_map/ppermute | solution.py:38
  307.5 1.9 collective-permute-start.6
  309.4 26.3 %collective-permute-done.6 = f32[8,16512]{1,0:T(8,128)S(1)} collective-permute-done((f32[8,16512]{1,0:T(8,128)}, f32[8,16512]{1,0:T(8,128)S(1)}, u32[]{:S(2)}, u32[]{:S(2)}) %collective-permute-start.6) | collective-permute-done | bytes 528416 | tf_op jit(solution)/shard_map/ppermute | solution.py:38
  336.9 2.1 collective-permute-start.7
  340.4 24.3 %collective-permute-done.7 = f32[8,16512]{1,0:T(8,128)} collective-permute-done((f32[8,16512]{1,0:T(8,128)}, f32[8,16512]{1,0:T(8,128)}, u32[]{:S(2)}, u32[]{:S(2)}) %collective-permute-start.7) | collective-permute-done | bytes 528416 | tf_op jit(solution)/shard_map/ppermute | solution.py:38
  366.8 1.9 collective-permute-start.8
  368.8 3.4 copy.255
  372.2 2.4 copy-done.2
  374.6 1.5 slice.482
  376.3 3.3 fusion.12
  382.7 4.8 collective-permute-start.9
  387.6 12.2 %collective-permute-done.9 = f32[8,8192]{1,0:T(8,128)S(1)} collective-permute-done((f32[8,8192]{1,0:T(8,128)S(1)}, f32[8,8192]{1,0:T(8,128)S(1)}, u32[]{:S(2)}, u32[]{:S(2)}) %collective-permute-start.9) | collective-permute-done | bytes 262176 | tf_op jit(solution)/shard_map/ppermute | solution.py:31
  399.7 1.4 fusion.80
  401.2 1.4 fusion.79
  405.9 3.6 fusion.22
  412.8 4.4 multiply_reduce_fusion.1
  417.6 1.2 fusion.26
  418.9 2.7 reduce-window.44
  421.8 1.9 fusion.20
  425.4 3.3 fusion
  430.2 3.0 collective-permute-start.13
  435.1 2.4 collective-permute-start.10
  437.5 18.8 %collective-permute-done.13 = f32[256,4,256]{2,0,1:T(8,128)} collective-permute-done((f32[256,4,256]{2,0,1:T(8,128)S(1)}, f32[256,4,256]{2,0,1:T(8,128)}, u32[]{:S(2)}, u32[]{:S(2)}) %collective-permute-start.13) | collective-permute-done | bytes 1048608 | tf_op jit(solution)/shard_map/ppermute | solution.py:65
  456.3 1.7 bitcast_add_fusion
  458.9 4.4 collective-permute-start.14
  463.3 15.5 %collective-permute-done.10 = f32[256,4,256]{2,0,1:T(8,128)} collective-permute-done((f32[256,4,256]{2,0,1:T(8,128)}, f32[256,4,256]{2,0,1:T(8,128)}, u32[]{:S(2)}, u32[]{:S(2)}) %collective-permute-start.10) | collective-permute-done | bytes 1048608 | tf_op jit(solution)/shard_map/ppermute | solution.py:65
  478.8 1.4 fusion.34
  482.1 4.5 collective-permute-start.11
  486.6 5.3 %collective-permute-done.14 = f32[256,2,256]{2,0,1:T(8,128)} collective-permute-done((f32[256,2,256]{2,0,1:T(8,128)}, f32[256,2,256]{2,0,1:T(8,128)}, u32[]{:S(2)}, u32[]{:S(2)}) %collective-permute-start.14) | collective-permute-done | bytes 524320 | tf_op jit(solution)/shard_map/ppermute | solution.py:65
  493.1 4.9 collective-permute-start.15
  498.0 5.0 collective-permute-done.11
  503.2 4.9 collective-permute-start.12
  508.1 4.4 collective-permute-done.15
  513.2 4.4 collective-permute-done.12
  (223 shorter events, 43.8 us)
Async XLA Ops:
  7.2 145.6 %all-gather.2.cloned.1.call-start = ((), (), s32[]{:S(2)}) async-start(), calls=%async_computation | async-start | bytes 2973696 | tf_op jit(solution)/shard_map/all_gather | solution.py:183
  9.4 173.3 %copy-start.37 = (bf16[256,256]{1,0:T(8,128)(2,1)S(1)}, bf16[256,256]{1,0:T(8,128)(2,1)}, u32[]{:S(2)}) copy-start(bf16[256,256]{1,0:T(8,128)(2,1)} %param.9) | copy-start | bytes 393220
  9.4 173.3 %copy-start.38 = (bf16[256,256]{1,0:T(8,128)(2,1)S(1)}, bf16[256,256]{1,0:T(8,128)(2,1)}, u32[]{:S(2)}) copy-start(bf16[256,256]{1,0:T(8,128)(2,1)} %param.17) | copy-start | bytes 393220
  157.4 82.7 %collective-permute-start.3 = (bf16[1024,1288]{0,1:T(8,128)(2,1)}, bf16[1024,1288]{0,1:T(8,128)(2,1)}, u32[]{:S(2)}, u32[]{:S(2)}) collective-permute-start(bf16[1024,1288]{0,1:T(8,128)(2,1)} %copy.229), channel_id=1, source_target_pairs={{0,8},{8,0},{1,9},{9,1},{2,10},{10,2},{3,11},{11,3},{4,12},{12,4},... | collective-permute-start | bytes 7913480 | tf_op jit(solution)/shard_map/ppermute | solution.py:184
  182.8 13.7 %collective-permute-start = (bf16[256,512]{1,0:T(8,128)(2,1)S(1)}, bf16[256,512]{1,0:T(8,128)(2,1)S(1)}, u32[]{:S(2)}, u32[]{:S(2)}) collective-permute-start(bf16[256,512]{1,0:T(8,128)(2,1)S(1)} %constant_dynamic-update-slice_fusion), channel_id=1, source_target_pairs={{0,4},{1,5},{2,6},{3,7},{4,0},{5,1},{6,2},{7,3},{8,12},{9,13},{10,... | collective-permute-start | bytes 786440 | tf_op jit(solution)/shard_map/ppermute | solution.py:160
  196.7 16.1 %collective-permute-start.1 = (bf16[512,512]{1,0:T(8,128)(2,1)S(1)}, bf16[512,512]{1,0:T(8,128)(2,1)S(1)}, u32[]{:S(2)}, u32[]{:S(2)}) collective-permute-start(bf16[512,512]{1,0:T(8,128)(2,1)S(1)} %maximum_select_fusion.3), channel_id=1, source_target_pairs={{0,2},{1,3},{2,0},{3,1},{4,6},{5,7},{6,4},{7,5},{8,10},{9,11},{10,... | collective-permute-start | bytes 1572872 | tf_op jit(solution)/shard_map/ppermute | solution.py:160
  213.2 24.9 %collective-permute-start.2 = (bf16[1024,512]{1,0:T(8,128)(2,1)S(1)}, bf16[1024,512]{1,0:T(8,128)(2,1)S(1)}, u32[]{:S(2)}, u32[]{:S(2)}) collective-permute-start(bf16[1024,512]{1,0:T(8,128)(2,1)S(1)} %maximum_select_fusion.2), channel_id=1, source_target_pairs={{0,1},{1,0},{2,3},{3,2},{4,5},{5,4},{6,7},{7,6},{8,9},{9,8},{10,11... | collective-permute-start | bytes 3145736 | tf_op jit(solution)/shard_map/ppermute | solution.py:160
  240.1 4.7 copy-start.1
  249.5 2.5 copy-start
  252.1 3.7 copy-start.15
  252.2 4.0 copy-start.14
  252.3 4.2 copy-start.13
  252.4 4.5 copy-start.12
  252.4 3.2 copy-start.7
  252.4 4.7 copy-start.11
  252.5 4.9 copy-start.10
  252.6 5.2 copy-start.9
  257.5 1.6 copy-start.40
  257.5 1.6 copy-start.49
  260.4 2.3 copy-start.35
  262.8 1.3 copy-start.24
  275.2 11.1 %copy-start.48 = (f32[8]{0:T(128)S(1)}, f32[8]{0:T(128)}, u32[]{:S(2)}) copy-start(f32[8]{0:T(128)} %get-tuple-element.205) | copy-start | bytes 100
  280.1 6.0 %collective-permute-start.4 = (f32[8,16512]{1,0:T(8,128)S(1)}, f32[8,16512]{1,0:T(8,128)S(1)}, u32[]{:S(2)}, u32[]{:S(2)}) collective-permute-start(f32[8,16512]{1,0:T(8,128)S(1)} %pad_maximum_fusion), channel_id=1, source_target_pairs={{0,8},{8,0},{16,24},{24,16},{32,40},{40,32},{48,56},{56,48},{64,72... | collective-permute-start | bytes 1585160 | tf_op jit(solution)/shard_map/ppermute | solution.py:38
  289.3 15.3 %collective-permute-start.5 = (f32[8,16512]{1,0:T(8,128)}, f32[8,16512]{1,0:T(8,128)S(1)}, u32[]{:S(2)}, u32[]{:S(2)}) collective-permute-start(f32[8,16512]{1,0:T(8,128)} %pad_maximum_fusion.1), channel_id=1, source_target_pairs={{0,16},{8,24},{16,0},{24,8},{32,48},{40,56},{48,32},{56,40},{64,80... | collective-permute-start | bytes 1585160 | tf_op jit(solution)/shard_map/ppermute | solution.py:38
  306.6 32.4 %copy-start.51 = (f32[8]{0:T(128)S(1)}, f32[8]{0:T(128)}, u32[]{:S(2)}) copy-start(f32[8]{0:T(128)} %param.15) | copy-start | bytes 100
  307.5 28.2 %collective-permute-start.6 = (f32[8,16512]{1,0:T(8,128)}, f32[8,16512]{1,0:T(8,128)S(1)}, u32[]{:S(2)}, u32[]{:S(2)}) collective-permute-start(f32[8,16512]{1,0:T(8,128)} %pad_maximum_fusion.2), channel_id=1, source_target_pairs={{0,32},{8,40},{16,48},{24,56},{32,0},{40,8},{48,16},{56,24},{64,96... | collective-permute-start | bytes 1585160 | tf_op jit(solution)/shard_map/ppermute | solution.py:38
  335.7 30.9 %copy-start.20 = (f32[8,16512]{1,0:T(8,128)}, f32[8,16512]{1,0:T(8,128)S(1)}, u32[]{:S(2)}) copy-start(f32[8,16512]{1,0:T(8,128)S(1)} %collective-permute-done.6) | copy-start | bytes 1585156
  336.0 32.7 %copy-start.36 = (f32[8,2,128]{2,0,1:T(8,128)S(1)}, f32[8,2,128]{2,0,1:T(8,128)}, u32[]{:S(2)}) copy-start(f32[8,2,128]{2,0,1:T(8,128)} %copy-done.35) | copy-start | bytes 24580
  336.9 27.8 %collective-permute-start.7 = (f32[8,16512]{1,0:T(8,128)}, f32[8,16512]{1,0:T(8,128)}, u32[]{:S(2)}, u32[]{:S(2)}) collective-permute-start(f32[8,16512]{1,0:T(8,128)} %pad_maximum_fusion.3), channel_id=1, source_target_pairs={{0,64},{8,72},{16,80},{24,88},{32,96},{40,104},{48,112},{56,120},{... | collective-permute-start | bytes 1585160 | tf_op jit(solution)/shard_map/ppermute | solution.py:38
  366.8 13.9 %collective-permute-start.8 = (f32[8,16512]{1,0:T(8,128)S(1)}, f32[8,16512]{1,0:T(8,128)S(1)}, u32[]{:S(2)}, u32[]{:S(2)}) collective-permute-start(f32[8,16512]{1,0:T(8,128)S(1)} %pad_maximum_fusion.4), channel_id=1, source_target_pairs={{0,128},{8,136},{16,144},{24,152},{32,160},{40,168},{48,176},{56,1... | collective-permute-start | bytes 1585160 | tf_op jit(solution)/shard_map/ppermute | solution.py:38
  372.2 2.5 copy-start.2
  374.6 1.5 copy-start.25
  374.6 1.7 copy-start.39
  376.3 23.4 %copy-start.18 = (f32[8,16512]{1,0:T(8,128)S(1)}, f32[8,16512]{1,0:T(8,128)}, u32[]{:S(2)}) copy-start(f32[8,16512]{1,0:T(8,128)} %copy-done.17) | copy-start | bytes 1585156
  382.7 19.9 %copy-start.41 = (f32[8]{0:T(128)S(1)}, f32[8]{0:T(128)}, u32[]{:S(2)}) copy-start(f32[8]{0:T(128)} %param.14) | copy-start | bytes 100
  382.7 17.0 %collective-permute-start.9 = (f32[8,8192]{1,0:T(8,128)S(1)}, f32[8,8192]{1,0:T(8,128)S(1)}, u32[]{:S(2)}, u32[]{:S(2)}) collective-permute-start(f32[8,8192]{1,0:T(8,128)S(1)} %select_select_fusion), channel_id=1, source_target_pairs={{0,256},{8,264},{16,272},{24,280},{32,288},{40,296},{48,304},{56,3... | collective-permute-start | bytes 786440 | tf_op jit(solution)/shard_map/ppermute | solution.py:31
  401.1 3.7 copy-start.22
  401.1 3.7 copy-start.23
  403.5 6.0 %copy-start.33 = (f32[256,8]{0,1:T(8,128)}, f32[256,8]{0,1:T(8,128)S(1)}, u32[]{:S(2)}) copy-start(f32[256,8]{0,1:T(8,128)S(1)} %get-tuple-element.196) | copy-start | bytes 24580
  404.1 5.4 %copy-start.42 = (f32[8]{0:T(128)}, f32[8]{0:T(128)S(1)}, u32[]{:S(2)}) copy-start(f32[8]{0:T(128)S(1)} %get-tuple-element.231) | copy-start | bytes 100
  405.2 4.3 copy-start.30
  412.8 4.5 copy-start.34
  412.8 4.5 copy-start.43
  412.8 6.0 %copy-start.44 = (f32[8,256]{1,0:T(8,128)S(1)}, f32[8,256]{1,0:T(8,128)}, u32[]{:S(2)}) copy-start(f32[8,256]{1,0:T(8,128)} %get-tuple-element.190) | copy-start | bytes 24580
  412.8 6.0 %copy-start.45 = (f32[8,256]{1,0:T(8,128)S(1)}, f32[8,256]{1,0:T(8,128)}, u32[]{:S(2)}) copy-start(f32[8,256]{1,0:T(8,128)} %get-tuple-element.191) | copy-start | bytes 24580
  412.8 9.0 %copy-start.28 = (f32[256,8,64]{0,2,1:T(8,128)S(1)}, f32[256,8,64]{0,2,1:T(8,128)}, u32[]{:S(2)}) copy-start(f32[256,8,64]{0,2,1:T(8,128)} %fusion.12) | copy-start | bytes 1572868
  417.2 6.5 %copy-start.31 = (bf16[256,1,1,128]{0,3,2,1:T(8,128)(2,1)S(1)}, bf16[256,1,1,128]{0,3,2,1:T(8,128)(2,1)}, u32[]{:S(2)}) copy-start(bf16[256,1,1,128]{0,3,2,1:T(8,128)(2,1)} %fusion.32) | copy-start | bytes 196612
  417.2 6.5 %copy-start.32 = (bf16[256,1,1,128]{0,3,2,1:T(8,128)(2,1)S(1)}, bf16[256,1,1,128]{0,3,2,1:T(8,128)(2,1)}, u32[]{:S(2)}) copy-start(bf16[256,1,1,128]{0,3,2,1:T(8,128)(2,1)} %fusion.31) | copy-start | bytes 196612
  417.2 6.5 %copy-start.46 = (f32[256,8]{0,1:T(8,128)S(1)}, f32[256,8]{0,1:T(8,128)}, u32[]{:S(2)}) copy-start(f32[256,8]{0,1:T(8,128)} %get-tuple-element.194) | copy-start | bytes 24580
  417.2 6.5 %copy-start.50 = (f32[8]{0:T(128)S(1)}, f32[8]{0:T(128)}, u32[]{:S(2)}) copy-start(f32[8]{0:T(128)} %param.13) | copy-start | bytes 100
  417.2 7.3 %copy-start.29 = (f32[256,8,64]{0,2,1:T(8,128)S(1)}, f32[256,8,64]{0,2,1:T(8,128)}, u32[]{:S(2)}) copy-start(f32[256,8,64]{0,2,1:T(8,128)} %get-tuple-element.217) | copy-start | bytes 1572868
  417.2 7.3 %copy-start.47 = (f32[512]{0:T(512)S(1)}, f32[512]{0:T(512)}, u32[]{:S(2)}) copy-start(f32[512]{0:T(512)} %mul.680) | copy-start | bytes 6148
  429.2 1.0 copy-start.5
  429.5 3.6 copy-start.6
  429.5 3.6 copy-start.8
  429.6 3.6 copy-start.26
  430.2 26.1 %collective-permute-start.13 = (f32[256,4,256]{2,0,1:T(8,128)S(1)}, f32[256,4,256]{2,0,1:T(8,128)}, u32[]{:S(2)}, u32[]{:S(2)}) collective-permute-start(f32[256,4,256]{2,0,1:T(8,128)S(1)} %select_bitcast_fusion), channel_id=1, source_target_pairs={{0,1},{1,0},{2,3},{3,2},{4,5},{5,4},{6,7},{7,6},{8,9},{9,8},{10,11... | collective-permute-start | bytes 3145736 | tf_op jit(solution)/shard_map/ppermute | solution.py:65
  435.1 43.7 %collective-permute-start.10 = (f32[256,4,256]{2,0,1:T(8,128)}, f32[256,4,256]{2,0,1:T(8,128)}, u32[]{:S(2)}, u32[]{:S(2)}) collective-permute-start(f32[256,4,256]{2,0,1:T(8,128)} %select_bitcast_fusion.1), channel_id=1, source_target_pairs={{0,1},{1,0},{2,3},{3,2},{4,5},{5,4},{6,7},{7,6},{8,9},{9,8},{10,11... | collective-permute-start | bytes 3145736 | tf_op jit(solution)/shard_map/ppermute | solution.py:65
  458.9 33.0 %collective-permute-start.14 = (f32[256,2,256]{2,0,1:T(8,128)}, f32[256,2,256]{2,0,1:T(8,128)}, u32[]{:S(2)}, u32[]{:S(2)}) collective-permute-start(f32[256,2,256]{2,0,1:T(8,128)} %select_bitcast_fusion.2), channel_id=1, source_target_pairs={{0,2},{1,3},{2,0},{3,1},{4,6},{5,7},{6,4},{7,5},{8,10},{9,11},{10,... | collective-permute-start | bytes 1572872 | tf_op jit(solution)/shard_map/ppermute | solution.py:65
  480.2 1.0 copy-start.3
  482.1 21.0 %copy-start.4 = (f32[256,4,256]{2,0,1:T(8,128)S(1)}, f32[256,4,256]{2,0,1:T(8,128)}, u32[]{:S(2)}) copy-start(f32[256,4,256]{2,0,1:T(8,128)} %copy-done.3) | copy-start | bytes 3145732
  482.1 21.0 %collective-permute-start.11 = (f32[256,2,256]{2,0,1:T(8,128)}, f32[256,2,256]{2,0,1:T(8,128)S(1)}, u32[]{:S(2)}, u32[]{:S(2)}) collective-permute-start(f32[256,2,256]{2,0,1:T(8,128)} %select_bitcast_fusion.3), channel_id=1, source_target_pairs={{0,2},{1,3},{2,0},{3,1},{4,6},{5,7},{6,4},{7,5},{8,10},{9,11},{10,... | collective-permute-start | bytes 1572872 | tf_op jit(solution)/shard_map/ppermute | solution.py:65
  493.1 19.4 %collective-permute-start.15 = (f32[256,1,256]{2,0,1:T(8,128)S(1)}, f32[256,1,256]{2,0,1:T(8,128)S(1)}, u32[]{:S(2)}, u32[]{:S(2)}) collective-permute-start(f32[256,1,256]{2,0,1:T(8,128)S(1)} %select_bitcast_fusion.4), channel_id=1, source_target_pairs={{0,4},{1,5},{2,6},{3,7},{4,0},{5,1},{6,2},{7,3},{8,12},{9,13},{10,... | collective-permute-start | bytes 786440 | tf_op jit(solution)/shard_map/ppermute | solution.py:65
  503.2 14.4 %collective-permute-start.12 = (f32[256,1,256]{2,0,1:T(8,128)S(1)}, f32[256,1,256]{2,0,1:T(8,128)S(1)}, u32[]{:S(2)}, u32[]{:S(2)}) collective-permute-start(f32[256,1,256]{2,0,1:T(8,128)S(1)} %select_bitcast_fusion.5), channel_id=1, source_target_pairs={{0,4},{1,5},{2,6},{3,7},{4,0},{5,1},{6,2},{7,3},{8,12},{9,13},{10,... | collective-permute-start | bytes 786440 | tf_op jit(solution)/shard_map/ppermute | solution.py:65
  (5 other events, 4.2 us)
Sparse Core Ops, SparseCore 0:
  10.7 142.1 all-gather.1

commit v7 on v5

--- a/solution.py
+++ b/solution.py
@@ -9,6 +9,7 @@
 
 
 HIGH = lax.Precision.HIGHEST
+RING = 4
 
 
 def both_carries(decay, forward, backward, axis):
@@ -50,18 +51,36 @@
     return before_s.reshape(forward.shape), after_u.reshape(backward.shape)
 
 
-def scattered_sum(partial, axis, width):
-    devices, position = (lax.axis_size(axis), lax.axis_index(axis))
+def scattered_sum(partial, rows_axis, axis, width):
+    chains, devices = (lax.axis_size(rows_axis), lax.axis_size(axis))
+    chain, position = (lax.axis_index(rows_axis), lax.axis_index(axis))
+    ring = RING if devices % RING == 0 else 1
+
+    def label(t, turn):
+        return t - t % ring + (t + turn) % ring
+
+    def place(lab, turn):
+        return lab - lab % ring + (lab - turn) % ring
+
+    turn = chain % 2
+    mine_label = label(position, turn)
+    order = [place(lab, 1) for lab in range(devices)]
     rows = partial.shape[0]
     blocks = partial.reshape(rows, devices, width)
+    blocks = jnp.where(turn == 1, blocks[:, order], blocks)
     bit = 1
     while bit < devices:
         count = blocks.shape[1]
         paired = blocks.reshape(rows, count // 2, 2, width)
-        mine = (position & bit) != 0
+        mine = (mine_label & bit) != 0
         keep = jnp.where(mine, paired[:, :, 1], paired[:, :, 0])
         send = jnp.where(mine, paired[:, :, 0], paired[:, :, 1])
-        blocks = keep + lax.ppermute(send, axis, [(i, i ^ bit) for i in range(devices)])
+        pairs = []
+        for c in range(chains):
+            for t in range(devices):
+                partner = place(label(t, c % 2) ^ bit, c % 2)
+                pairs.append((c * devices + t, c * devices + partner))
+        blocks = keep + lax.ppermute(send, (rows_axis, axis), pairs)
         bit *= 2
     return blocks.reshape(rows, width)
 
@@ -219,7 +238,7 @@
     partial_out = lax.dot_general(
         mixed, w_all[:, :out_cols], (((1,), (1,)), ((), ())), preferred_element_type=jnp.float32
     )
-    output = scattered_sum(partial_out, "tp", width).astype(jnp.bfloat16)
+    output = scattered_sum(partial_out, "ctx", "tp", width).astype(jnp.bfloat16)
     grads = pullback((d_mixed, adjoint))
     d_values = grads[0] + skip_gain[None, :, None] * d_mixed
     d_pre = grads[3] * jax.nn.sigmoid(pre_step)
@@ -236,7 +255,7 @@
     partial_grad = lax.dot_general(
         d_cat, w_all[:, out_cols:], (((1,), (1,)), ((), ())), preferred_element_type=jnp.float32
     )
-    grad = scattered_sum(partial_grad, "tp", width).astype(jnp.bfloat16)
+    grad = scattered_sum(partial_grad, "ctx", "tp", width).astype(jnp.bfloat16)
     return (output, grad)
 
 

time: 412 us -> 402 us (0.976)
  waiting for transfers between devices: 236 us -> 212 us
  local copies, waits for them, and re-layouts: 14.4 us -> 24.4 us
  matrix products: 38.9 us -> 43.3 us
    ppermute x6, waiting for transfers between devices: 50.9 us -> 28.2 us  [scattered_sum(): blocks = keep + lax.ppermute(send, (rows_axis, axis), pairs)]
    gather x0 -> x2, local copies, waits for them, and re-layouts: none -> 7.46 us  [scattered_sum(): blocks = jnp.where(turn == 1, blocks[:, order], blocks)]
    select_n x0 -> x2, other arithmetic: none -> 4.83 us  [scattered_sum(): blocks = jnp.where(turn == 1, blocks[:, order], blocks)]
    reshape x0 -> x2, local copies, waits for them, and re-layouts: none -> 4.5 us  [scattered_sum(): blocks = partial.reshape(rows, devices, width)]
  transfers between devices with their start and end apart: 16 -> 16, of which waited for: 15 -> 14; matrix products, arithmetic and copies ran while one was open for 4% -> 6% of each run, Pallas kernels for 0% -> 0%
where the time goes in v7:
time: 402 us; the launch traced here: 399 us
  waiting for transfers between devices  212 us (53%)
  starting transfers between devices  71.5 us (18%)
  matrix products  43.3 us (11%)
  other arithmetic  32.8 us (8%)
  local copies, waits for them, and re-layouts  24.4 us (6%)
  between operations  15.2 us (4%)
    all_gather x1, waiting for transfers between devices, per_device(): lax.all_gather(jnp.concatenate([w_out.T, w_in, w_bc, w_dt], axis=1), 'ctx...  72.3 us
    ppermute x5, waiting for transfers between devices, both_carries(): got = lax.ppermute(message, axis, [(i, i ^ bit) for i in range(devices)])  63.7 us
    ppermute x3, waiting for transfers between devices, doubled_rows(): other = lax.ppermute(x, axis, [(i, i ^ bit) for i in range(devices)])  36 us
    ppermute x6, starting transfers between devices, scattered_sum(): blocks = keep + lax.ppermute(send, (rows_axis, axis), pairs)  28.3 us
    ppermute x6, waiting for transfers between devices, scattered_sum(): blocks = keep + lax.ppermute(send, (rows_axis, axis), pairs)  28.2 us
    ppermute x5, starting transfers between devices, both_carries(): got = lax.ppermute(message, axis, [(i, i ^ bit) for i in range(devices)])  20.4 us
    ppermute x3, starting transfers between devices, doubled_rows(): other = lax.ppermute(x, axis, [(i, i ^ bit) for i in range(devices)])  18.1 us
    ppermute x1, waiting for transfers between devices, both_carries(): got = lax.ppermute(send, axis, [(i, i ^ bit) for i in range(devices)])  11.7 us
  transfers between devices with their start and end apart: 16, of which 14 were waited for; matrix products, arithmetic and copies ran while one was open for 6% of the time, Pallas kernels for 0%

profile of v7, /device:TPU:1, one launch (start us, length us, event | category | flops | bytes accessed | tf_op | source)
XLA Modules:
  0.0 399.2 jit_solution(110275574049709453)
XLA Ops:
  8.0 1.4 pad_maximum_fusion.6
  11.3 8.3 %collective-permute-start = (bf16[256,512]{1,0:T(8,128)(2,1)S(1)}, bf16[256,512]{1,0:T(8,128)(2,1)S(1)}, u32[]{:S(2)}, u32[]{:S(2)}) collective-permute-start(bf16[256,512]{1,0:T(8,128)(2,1)S(1)} %constant_dynamic-update-slice_fusion), channel_id=1, source_target_pairs={{0,4},{1,5},{2,6},{3,7},{4,0},{5,1},{6,2},{7,3},{8,12},{9,13},{10,... | collective-permute-start | bytes 786440 | tf_op jit(solution)/shard_map/ppermute | solution.py:178
  19.6 8.5 %collective-permute-done = bf16[256,512]{1,0:T(8,128)(2,1)S(1)} collective-permute-done((bf16[256,512]{1,0:T(8,128)(2,1)S(1)}, bf16[256,512]{1,0:T(8,128)(2,1)S(1)}, u32[]{:S(2)}, u32[]{:S(2)}) %collective-permute-start) | collective-permute-done | bytes 262176 | tf_op jit(solution)/shard_map/ppermute | solution.py:178
  28.3 3.7 collective-permute-start.1
  32.0 7.7 %collective-permute-done.1 = bf16[512,512]{1,0:T(8,128)(2,1)S(1)} collective-permute-done((bf16[512,512]{1,0:T(8,128)(2,1)S(1)}, bf16[512,512]{1,0:T(8,128)(2,1)S(1)}, u32[]{:S(2)}, u32[]{:S(2)}) %collective-permute-start.1) | collective-permute-done | bytes 524320 | tf_op jit(solution)/shard_map/ppermute | solution.py:178
  40.2 6.1 %collective-permute-start.2 = (bf16[1024,512]{1,0:T(8,128)(2,1)S(1)}, bf16[1024,512]{1,0:T(8,128)(2,1)S(1)}, u32[]{:S(2)}, u32[]{:S(2)}) collective-permute-start(bf16[1024,512]{1,0:T(8,128)(2,1)S(1)} %maximum_select_fusion.1), channel_id=1, source_target_pairs={{0,1},{1,0},{2,3},{3,2},{4,5},{5,4},{6,7},{7,6},{8,9},{9,8},{10,11... | collective-permute-start | bytes 3145736 | tf_op jit(solution)/shard_map/ppermute | solution.py:178
  46.3 19.8 %collective-permute-done.2 = bf16[1024,512]{1,0:T(8,128)(2,1)S(1)} collective-permute-done((bf16[1024,512]{1,0:T(8,128)(2,1)S(1)}, bf16[1024,512]{1,0:T(8,128)(2,1)S(1)}, u32[]{:S(2)}, u32[]{:S(2)}) %collective-permute-start.2) | collective-permute-done | bytes 1048608 | tf_op jit(solution)/shard_map/ppermute | solution.py:178
  66.9 72.3 %all-gather.2.cloned.1.call-done = bf16[2048,1288]{1,0:T(8,128)(2,1)} async-done(((bf16[32,1288]{1,0:T(8,128)(2,1)}), bf16[2048,1288]{1,0:T(8,128)(2,1)}) %all-gather.2.cloned.1.call-update) | async-done | bytes 5275664 | tf_op jit(solution)/shard_map/all_gather | solution.py:200
  139.2 1.3 fusion.72
  140.5 1.5 convolution_add_fusion.6
  142.0 1.7 convolution_add_fusion.5
  143.7 1.3 convolution_add_fusion.4
  146.0 1.3 fusion.149
  152.0 1.4 fusion.88
  153.4 1.3 convolution_add_fusion.13
  154.7 1.3 convolution_add_fusion.12
  156.0 1.3 convolution_add_fusion.11
  157.3 1.3 convolution_add_fusion.10
  158.6 1.3 convolution_add_fusion.9
  161.1 1.2 convolution_add_fusion.7
  163.4 2.2 collective-permute-start.3
  165.6 1.6 collective-permute-done.3
  168.1 1.4 add_select_fusion.16
  170.3 3.0 collective-permute-start.4
  173.4 12.4 %collective-permute-done.4 = f32[8,16512]{1,0:T(8,128)S(1)} collective-permute-done((f32[8,16512]{1,0:T(8,128)}, f32[8,16512]{1,0:T(8,128)S(1)}, u32[]{:S(2)}, u32[]{:S(2)}) %collective-permute-start.4) | collective-permute-done | bytes 528416 | tf_op jit(solution)/shard_map/ppermute | solution.py:38
  187.0 3.9 collective-permute-start.5
  191.0 23.5 %collective-permute-done.5 = f32[8,16512]{1,0:T(8,128)} collective-permute-done((f32[8,16512]{1,0:T(8,128)}, f32[8,16512]{1,0:T(8,128)}, u32[]{:S(2)}, u32[]{:S(2)}) %collective-permute-start.5) | collective-permute-done | bytes 528416 | tf_op jit(solution)/shard_map/ppermute | solution.py:38
  215.3 1.2 add_select_fusion.12
  216.6 6.9 %collective-permute-start.6 = (f32[8,16512]{1,0:T(8,128)S(1)}, f32[8,16512]{1,0:T(8,128)S(1)}, u32[]{:S(2)}, u32[]{:S(2)}) collective-permute-start(f32[8,16512]{1,0:T(8,128)S(1)} %pad_maximum_fusion.3), channel_id=1, source_target_pairs={{0,64},{8,72},{16,80},{24,88},{32,96},{40,104},{48,112},{56,120},{... | collective-permute-start | bytes 1585160 | tf_op jit(solution)/shard_map/ppermute | solution.py:38
  225.5 20.4 %collective-permute-done.6 = f32[8,16512]{1,0:T(8,128)S(1)} collective-permute-done((f32[8,16512]{1,0:T(8,128)S(1)}, f32[8,16512]{1,0:T(8,128)S(1)}, u32[]{:S(2)}, u32[]{:S(2)}) %collective-permute-start.6) | collective-permute-done | bytes 528416 | tf_op jit(solution)/shard_map/ppermute | solution.py:38
  246.3 4.5 %collective-permute-start.7 = (f32[8,16512]{1,0:T(8,128)S(1)}, f32[8,16512]{1,0:T(8,128)S(1)}, u32[]{:S(2)}, u32[]{:S(2)}) collective-permute-start(f32[8,16512]{1,0:T(8,128)S(1)} %pad_maximum_fusion.4), channel_id=1, source_target_pairs={{0,128},{8,136},{16,144},{24,152},{32,160},{40,168},{48,176},{56,1... | collective-permute-start | bytes 1585160 | tf_op jit(solution)/shard_map/ppermute | solution.py:38
  252.0 3.3 fusion.12
  255.4 5.7 %collective-permute-done.7 = f32[8,16512]{1,0:T(8,128)S(1)} collective-permute-done((f32[8,16512]{1,0:T(8,128)S(1)}, f32[8,16512]{1,0:T(8,128)S(1)}, u32[]{:S(2)}, u32[]{:S(2)}) %collective-permute-start.7) | collective-permute-done | bytes 528416 | tf_op jit(solution)/shard_map/ppermute | solution.py:38
  261.9 1.2 select_select_fusion
  263.1 4.6 %collective-permute-start.8 = (f32[8,8192]{1,0:T(8,128)S(1)}, f32[8,8192]{1,0:T(8,128)S(1)}, u32[]{:S(2)}, u32[]{:S(2)}) collective-permute-start(f32[8,8192]{1,0:T(8,128)S(1)} %select_select_fusion), channel_id=1, source_target_pairs={{0,256},{8,264},{16,272},{24,280},{32,288},{40,296},{48,304},{56,3... | collective-permute-start | bytes 786440 | tf_op jit(solution)/shard_map/ppermute | solution.py:31
  267.8 11.7 %collective-permute-done.8 = f32[8,8192]{1,0:T(8,128)S(1)} collective-permute-done((f32[8,8192]{1,0:T(8,128)S(1)}, f32[8,8192]{1,0:T(8,128)S(1)}, u32[]{:S(2)}, u32[]{:S(2)}) %collective-permute-start.8) | collective-permute-done | bytes 262176 | tf_op jit(solution)/shard_map/ppermute | solution.py:31
  279.5 1.4 fusion.80
  281.0 1.4 fusion.79
  285.7 3.6 fusion.22
  290.2 1.2 convolution_bitcast_fusion.1
  291.4 4.5 %multiply_reduce_fusion.1 = (f32[256,8]{0,1:T(8,128)S(1)}, f32[256,8]{0,1:T(8,128)}, f32[256,8,64]{0,2,1:T(8,128)}) fusion(f32[256,8,64]{0,2,1:T(8,128)S(1)} %convolution_bitcast_fusion.1, f32[256,8,64]{0,2,1:T(8,128)S(1)} %bitcast.323, f32[256,8]{0,1:T(8,128)S(1)} %get-tuple-element.181, f32[8,256]{1,0:T(8,128)} %copy-done.37, f32[256,256]{1,0:T(8,128)} %copy-done.20, ...), kind=kOutput, calls=%fused_computation.99 | convolution fusion | flops 405794816 | bytes 2465792 | tf_op jit(solution)/shard_map/transpose(jvp())/while/body/eval_jaxpr/checkpoint/hts,shp->thp/dot_general | solution.py:106
  296.3 1.2 fusion.26
  297.6 2.5 reduce-window.44
  300.2 1.9 fusion.20
  303.2 3.3 fusion
  306.5 3.0 reshape.520
  309.5 1.5 copy.205
  311.0 3.8 gather_fusion.1
  314.8 2.9 copy_select_fusion
  318.8 3.2 collective-permute-start.12
  322.1 2.1 fusion.92
  324.1 3.7 gather_fusion
  327.8 1.9 bitcast_select_fusion
  329.8 1.3 copy-done
  332.2 3.3 collective-permute-start.9
  335.9 1.6 bitcast_add_fusion
  337.6 2.3 collective-permute-start.13
  339.9 15.0 %collective-permute-done.9 = f32[256,4,256]{2,0,1:T(8,128)} collective-permute-done((f32[256,4,256]{2,0,1:T(8,128)}, f32[256,4,256]{2,0,1:T(8,128)}, u32[]{:S(2)}, u32[]{:S(2)}) %collective-permute-start.9) | collective-permute-done | bytes 1048608 | tf_op jit(solution)/shard_map/ppermute | solution.py:83
  354.9 1.4 bitcast_add_fusion.1
  357.3 2.5 collective-permute-start.10
  359.9 7.6 %collective-permute-start.14 = (f32[256,1,256]{2,0,1:T(8,128)S(1)}, f32[256,1,256]{2,0,1:T(8,128)S(1)}, u32[]{:S(2)}, u32[]{:S(2)}) collective-permute-start(f32[256,1,256]{2,0,1:T(8,128)S(1)} %select_bitcast_fusion.4), channel_id=1, source_target_pairs={{0,4},{1,5},{2,6},{3,7},{4,0},{5,1},{6,2},{7,3},{8,12},{9,13},{10,... | collective-permute-start | bytes 786440 | tf_op jit(solution)/shard_map/ppermute | solution.py:83
  367.6 5.2 %collective-permute-done.10 = f32[256,2,256]{2,0,1:T(8,128)} collective-permute-done((f32[256,2,256]{2,0,1:T(8,128)}, f32[256,2,256]{2,0,1:T(8,128)}, u32[]{:S(2)}, u32[]{:S(2)}) %collective-permute-start.10) | collective-permute-done | bytes 524320 | tf_op jit(solution)/shard_map/ppermute | solution.py:83
  374.0 9.4 %collective-permute-start.11 = (f32[256,1,256]{2,0,1:T(8,128)S(1)}, f32[256,1,256]{2,0,1:T(8,128)S(1)}, u32[]{:S(2)}, u32[]{:S(2)}) collective-permute-start(f32[256,1,256]{2,0,1:T(8,128)S(1)} %select_bitcast_fusion.5), channel_id=1, source_target_pairs={{0,4},{1,5},{2,6},{3,7},{4,0},{5,1},{6,2},{7,3},{8,12},{9,13},{10,... | collective-permute-start | bytes 786440 | tf_op jit(solution)/shard_map/ppermute | solution.py:83
  384.2 7.5 %collective-permute-done.11 = f32[256,1,256]{2,0,1:T(8,128)S(1)} collective-permute-done((f32[256,1,256]{2,0,1:T(8,128)S(1)}, f32[256,1,256]{2,0,1:T(8,128)S(1)}, u32[]{:S(2)}, u32[]{:S(2)}) %collective-permute-start.11) | collective-permute-done | bytes 262176 | tf_op jit(solution)/shard_map/ppermute | solution.py:83
  (206 shorter events, 31.9 us)
Async XLA Ops:
  7.2 132.0 %all-gather.2.cloned.1.call-start = ((), (), s32[]{:S(2)}) async-start(), calls=%async_computation | async-start | bytes 5857280 | tf_op jit(solution)/shard_map/all_gather | solution.py:200
  11.3 16.8 %collective-permute-start = (bf16[256,512]{1,0:T(8,128)(2,1)S(1)}, bf16[256,512]{1,0:T(8,128)(2,1)S(1)}, u32[]{:S(2)}, u32[]{:S(2)}) collective-permute-start(bf16[256,512]{1,0:T(8,128)(2,1)S(1)} %constant_dynamic-update-slice_fusion), channel_id=1, source_target_pairs={{0,4},{1,5},{2,6},{3,7},{4,0},{5,1},{6,2},{7,3},{8,12},{9,13},{10,... | collective-permute-start | bytes 786440 | tf_op jit(solution)/shard_map/ppermute | solution.py:178
  28.3 11.4 %collective-permute-start.1 = (bf16[512,512]{1,0:T(8,128)(2,1)S(1)}, bf16[512,512]{1,0:T(8,128)(2,1)S(1)}, u32[]{:S(2)}, u32[]{:S(2)}) collective-permute-start(bf16[512,512]{1,0:T(8,128)(2,1)S(1)} %maximum_select_fusion.2), channel_id=1, source_target_pairs={{0,2},{1,3},{2,0},{3,1},{4,6},{5,7},{6,4},{7,5},{8,10},{9,11},{10,... | collective-permute-start | bytes 1572872 | tf_op jit(solution)/shard_map/ppermute | solution.py:178
  40.2 26.0 %collective-permute-start.2 = (bf16[1024,512]{1,0:T(8,128)(2,1)S(1)}, bf16[1024,512]{1,0:T(8,128)(2,1)S(1)}, u32[]{:S(2)}, u32[]{:S(2)}) collective-permute-start(bf16[1024,512]{1,0:T(8,128)(2,1)S(1)} %maximum_select_fusion.1), channel_id=1, source_target_pairs={{0,1},{1,0},{2,3},{3,2},{4,5},{5,4},{6,7},{7,6},{8,9},{9,8},{10,11... | collective-permute-start | bytes 3145736 | tf_op jit(solution)/shard_map/ppermute | solution.py:178
  66.9 78.8 %copy-start.5 = (bf16[2,2,2,256,512]{4,3,2,1,0:T(8,128)(2,1)}, bf16[2,2,2,256,512]{4,3,2,1,0:T(8,128)(2,1)S(1)}, u32[]{:S(2)}) copy-start(bf16[2,2,2,256,512]{4,3,2,1,0:T(8,128)(2,1)S(1)} %copy.125) | copy-start | bytes 6291460
  140.5 4.5 %copy-start.2 = (bf16[2048,1288]{1,0:T(8,128)(2,1)S(1)}, bf16[2048,1288]{1,0:T(8,128)(2,1)}, u32[]{:S(2)}) copy-start(bf16[2048,1288]{1,0:T(8,128)(2,1)} %all-gather.2.cloned.1.call-done) | copy-start | bytes 15826948
  145.7 2.6 copy-start.30
  145.7 2.6 copy-start.42
  146.0 13.9 %slice-start = ((s8[5767168]{0:T(1024)(128)(4,1)}), s8[1572864]{0:T(1024)(128)(4,1)S(1)}, s32[]{:S(2)}) async-start(s8[5767168]{0:T(1024)(128)(4,1)} %bitcast.292), calls=%async_computation.1 | async-start | bytes 3145728
  147.4 0.9 copy-start.17
  148.5 18.8 %copy-start.40 = (f32[8]{0:T(128)}, f32[8]{0:T(128)S(1)}, u32[]{:S(2)}) copy-start(f32[8]{0:T(128)S(1)} %get-tuple-element.205) | copy-start | bytes 100
  149.2 1.0 copy-start.23
  149.4 12.9 %copy-start.25 = (f32[256,8]{0,1:T(8,128)}, f32[256,8]{0,1:T(8,128)S(1)}, u32[]{:S(2)}) copy-start(f32[256,8]{0,1:T(8,128)S(1)} %get-tuple-element.203) | copy-start | bytes 24580
  150.2 1.1 copy-start.13
  151.3 11.1 %copy-start.15 = (f32[256,128]{1,0:T(8,128)}, f32[256,128]{1,0:T(8,128)S(1)}, u32[]{:S(2)}) copy-start(f32[256,128]{1,0:T(8,128)S(1)} %copy.136) | copy-start | bytes 393220
  152.0 8.0 %slice-start.1 = ((s8[5767168]{0:T(1024)(128)(4,1)}), s8[4194304]{0:T(1024)(128)(4,1)S(1)}, s32[]{:S(2)}) async-start(s8[5767168]{0:T(1024)(128)(4,1)} %bitcast.292), calls=%async_computation.2 | async-start | bytes 8388608
  163.4 3.8 collective-permute-start.3
  167.2 0.8 copy-start.6
  168.1 17.8 %copy-start.41 = (f32[8]{0:T(128)S(1)}, f32[8]{0:T(128)}, u32[]{:S(2)}) copy-start(f32[8]{0:T(128)} %copy-done.40) | copy-start | bytes 100
  170.3 15.5 %collective-permute-start.4 = (f32[8,16512]{1,0:T(8,128)}, f32[8,16512]{1,0:T(8,128)S(1)}, u32[]{:S(2)}, u32[]{:S(2)}) collective-permute-start(f32[8,16512]{1,0:T(8,128)} %pad_maximum_fusion.1), channel_id=1, source_target_pairs={{0,16},{8,24},{16,0},{24,8},{32,48},{40,56},{48,32},{56,40},{64,80... | collective-permute-start | bytes 1585160 | tf_op jit(solution)/shard_map/ppermute | solution.py:38
  185.8 30.7 %copy-start.8 = (f32[8,16512]{1,0:T(8,128)}, f32[8,16512]{1,0:T(8,128)S(1)}, u32[]{:S(2)}) copy-start(f32[8,16512]{1,0:T(8,128)S(1)} %collective-permute-done.4) | copy-start | bytes 1585156
  186.1 37.4 %copy-start.44 = (f32[8]{0:T(128)S(1)}, f32[8]{0:T(128)}, u32[]{:S(2)}) copy-start(f32[8]{0:T(128)} %param.17) | copy-start | bytes 100
  186.1 38.2 %copy-start.45 = (s32[8]{0:T(128)S(1)}, s32[8]{0:T(128)}, u32[]{:S(2)}) copy-start(s32[8]{0:T(128)} %constant.154) | copy-start | bytes 100
  187.0 27.5 %collective-permute-start.5 = (f32[8,16512]{1,0:T(8,128)}, f32[8,16512]{1,0:T(8,128)}, u32[]{:S(2)}, u32[]{:S(2)}) collective-permute-start(f32[8,16512]{1,0:T(8,128)} %pad_maximum_fusion.2), channel_id=1, source_target_pairs={{0,32},{8,40},{16,48},{24,56},{32,0},{40,8},{48,16},{56,24},{64,96... | collective-permute-start | bytes 1585160 | tf_op jit(solution)/shard_map/ppermute | solution.py:38
  216.5 34.4 %copy-start.24 = (f32[8,2,128]{2,0,1:T(8,128)S(1)}, f32[8,2,128]{2,0,1:T(8,128)}, u32[]{:S(2)}) copy-start(f32[8,2,128]{2,0,1:T(8,128)} %copy-done.23) | copy-start | bytes 24580
  216.5 34.4 %copy-start.29 = (f32[8,2]{0,1:T(2,128)S(1)}, f32[8,2]{0,1:T(2,128)}, u32[]{:S(2)}) copy-start(f32[8,2]{0,1:T(2,128)} %copy-done.28) | copy-start | bytes 196
  216.6 29.3 %collective-permute-start.6 = (f32[8,16512]{1,0:T(8,128)S(1)}, f32[8,16512]{1,0:T(8,128)S(1)}, u32[]{:S(2)}, u32[]{:S(2)}) collective-permute-start(f32[8,16512]{1,0:T(8,128)S(1)} %pad_maximum_fusion.3), channel_id=1, source_target_pairs={{0,64},{8,72},{16,80},{24,88},{32,96},{40,104},{48,112},{56,120},{... | collective-permute-start | bytes 1585160 | tf_op jit(solution)/shard_map/ppermute | solution.py:38
  245.9 5.0 %copy-start.9 = (f32[8,16512]{1,0:T(8,128)}, f32[8,16512]{1,0:T(8,128)S(1)}, u32[]{:S(2)}) copy-start(f32[8,16512]{1,0:T(8,128)S(1)} %collective-permute-done.6) | copy-start | bytes 1585156
  246.3 14.7 %collective-permute-start.7 = (f32[8,16512]{1,0:T(8,128)S(1)}, f32[8,16512]{1,0:T(8,128)S(1)}, u32[]{:S(2)}, u32[]{:S(2)}) collective-permute-start(f32[8,16512]{1,0:T(8,128)S(1)} %pad_maximum_fusion.4), channel_id=1, source_target_pairs={{0,128},{8,136},{16,144},{24,152},{32,160},{40,168},{48,176},{56,1... | collective-permute-start | bytes 1585160 | tf_op jit(solution)/shard_map/ppermute | solution.py:38
  250.9 0.9 copy-start.14
  252.0 27.5 %copy-start.7 = (f32[8,16512]{1,0:T(8,128)S(1)}, f32[8,16512]{1,0:T(8,128)}, u32[]{:S(2)}) copy-start(f32[8,16512]{1,0:T(8,128)} %copy-done.6) | copy-start | bytes 1585156
  261.0 0.8 copy-start.10
  263.1 19.3 %copy-start.31 = (f32[8]{0:T(128)S(1)}, f32[8]{0:T(128)}, u32[]{:S(2)}) copy-start(f32[8]{0:T(128)} %param.16) | copy-start | bytes 100
  263.1 16.4 %collective-permute-start.8 = (f32[8,8192]{1,0:T(8,128)S(1)}, f32[8,8192]{1,0:T(8,128)S(1)}, u32[]{:S(2)}, u32[]{:S(2)}) collective-permute-start(f32[8,8192]{1,0:T(8,128)S(1)} %select_select_fusion), channel_id=1, source_target_pairs={{0,256},{8,264},{16,272},{24,280},{32,288},{40,296},{48,304},{56,3... | collective-permute-start | bytes 786440 | tf_op jit(solution)/shard_map/ppermute | solution.py:31
  280.9 3.7 copy-start.11
  280.9 3.7 copy-start.12
  282.4 3.3 copy-start.26
  283.3 6.0 %copy-start.21 = (f32[256,8]{0,1:T(8,128)}, f32[256,8]{0,1:T(8,128)S(1)}, u32[]{:S(2)}) copy-start(f32[256,8]{0,1:T(8,128)S(1)} %get-tuple-element.196) | copy-start | bytes 24580
  283.4 5.9 %copy-start.37 = (f32[8,256]{1,0:T(8,128)}, f32[8,256]{1,0:T(8,128)S(1)}, u32[]{:S(2)}) copy-start(f32[8,256]{1,0:T(8,128)S(1)} %add_bitcast_fusion.1) | copy-start | bytes 24580
  283.9 5.4 %copy-start.33 = (f32[8]{0:T(128)}, f32[8]{0:T(128)S(1)}, u32[]{:S(2)}) copy-start(f32[8]{0:T(128)S(1)} %get-tuple-element.221) | copy-start | bytes 100
  284.0 5.4 %copy-start.27 = (f32[256,8]{0,1:T(8,128)}, f32[256,8]{0,1:T(8,128)S(1)}, u32[]{:S(2)}) copy-start(f32[256,8]{0,1:T(8,128)S(1)} %subtract_exponential_fusion) | copy-start | bytes 24580
  285.0 4.3 %copy-start.20 = (f32[256,256]{1,0:T(8,128)}, f32[256,256]{1,0:T(8,128)S(1)}, u32[]{:S(2)}) copy-start(f32[256,256]{1,0:T(8,128)S(1)} %fusion.137) | copy-start | bytes 786436
  291.4 4.5 %copy-start.22 = (f32[256,8]{0,1:T(8,128)S(1)}, f32[256,8]{0,1:T(8,128)}, u32[]{:S(2)}) copy-start(f32[256,8]{0,1:T(8,128)} %copy-done.21) | copy-start | bytes 24580
  291.4 4.6 %copy-start.34 = (f32[8]{0:T(128)S(1)}, f32[8]{0:T(128)}, u32[]{:S(2)}) copy-start(f32[8]{0:T(128)} %copy-done.33) | copy-start | bytes 100
  291.4 6.1 %copy-start.35 = (f32[8,256]{1,0:T(8,128)S(1)}, f32[8,256]{1,0:T(8,128)}, u32[]{:S(2)}) copy-start(f32[8,256]{1,0:T(8,128)} %get-tuple-element.190) | copy-start | bytes 24580
  291.4 6.1 %copy-start.36 = (f32[8,256]{1,0:T(8,128)S(1)}, f32[8,256]{1,0:T(8,128)}, u32[]{:S(2)}) copy-start(f32[8,256]{1,0:T(8,128)} %get-tuple-element.191) | copy-start | bytes 24580
  291.4 8.8 %copy-start.16 = (f32[256,128]{1,0:T(8,128)S(1)}, f32[256,128]{1,0:T(8,128)}, u32[]{:S(2)}) copy-start(f32[256,128]{1,0:T(8,128)} %copy-done.15) | copy-start | bytes 393220
  291.4 8.8 %copy-start.18 = (f32[256,8,64]{0,2,1:T(8,128)S(1)}, f32[256,8,64]{0,2,1:T(8,128)}, u32[]{:S(2)}) copy-start(f32[256,8,64]{0,2,1:T(8,128)} %fusion.12) | copy-start | bytes 1572868
  295.9 6.3 %copy-start.32 = (f32[8]{0:T(128)S(1)}, f32[8]{0:T(128)}, u32[]{:S(2)}) copy-start(f32[8]{0:T(128)} %param.16) | copy-start | bytes 100
  295.9 6.3 %copy-start.38 = (f32[256,8]{0,1:T(8,128)S(1)}, f32[256,8]{0,1:T(8,128)}, u32[]{:S(2)}) copy-start(f32[256,8]{0,1:T(8,128)} %get-tuple-element.194) | copy-start | bytes 24580
  295.9 6.3 %copy-start.43 = (f32[8]{0:T(128)S(1)}, f32[8]{0:T(128)}, u32[]{:S(2)}) copy-start(f32[8]{0:T(128)} %param.15) | copy-start | bytes 100
  295.9 7.1 %copy-start.19 = (f32[256,8,64]{0,2,1:T(8,128)S(1)}, f32[256,8,64]{0,2,1:T(8,128)}, u32[]{:S(2)}) copy-start(f32[256,8,64]{0,2,1:T(8,128)} %get-tuple-element.207) | copy-start | bytes 1572868
  295.9 7.1 %copy-start.39 = (f32[512]{0:T(512)S(1)}, f32[512]{0:T(512)}, u32[]{:S(2)}) copy-start(f32[512]{0:T(512)} %mul.676) | copy-start | bytes 6148
  317.7 4.4 %slice-start.2 = ((bf16[2048,1288]{1,0:T(8,128)(2,1)}), bf16[2048,512]{1,0:T(8,128)(2,1)S(1)}, s32[]{:S(2)}) async-start(bf16[2048,1288]{1,0:T(8,128)(2,1)} %all-gather.2.cloned.1.call-done), calls=%async_computation.3 | async-start | bytes 4194304 | tf_op jit(solution)/shard_map/slice | solution.py:239
  318.8 17.1 %collective-permute-start.12 = (f32[256,4,256]{2,0,1:T(8,128)}, f32[256,4,256]{2,0,1:T(8,128)}, u32[]{:S(2)}, u32[]{:S(2)}) collective-permute-start(f32[256,4,256]{2,0,1:T(8,128)} %select_bitcast_fusion), channel_id=1, source_target_pairs={{0,1},{1,0},{2,3},{3,2},{4,5},{5,4},{6,7},{7,6},{8,11},{9,10},{10,... | collective-permute-start | bytes 3145736 | tf_op jit(solution)/shard_map/ppermute | solution.py:83
  329.8 1.3 copy-start
  332.2 22.7 %collective-permute-start.9 = (f32[256,4,256]{2,0,1:T(8,128)}, f32[256,4,256]{2,0,1:T(8,128)}, u32[]{:S(2)}, u32[]{:S(2)}) collective-permute-start(f32[256,4,256]{2,0,1:T(8,128)} %select_bitcast_fusion.1), channel_id=1, source_target_pairs={{0,1},{1,0},{2,3},{3,2},{4,5},{5,4},{6,7},{7,6},{8,11},{9,10},{10,... | collective-permute-start | bytes 3145736 | tf_op jit(solution)/shard_map/ppermute | solution.py:83
  335.5 19.4 %copy-start.1 = (f32[256,8,256]{2,0,1:T(8,128)S(1)}, f32[256,8,256]{2,0,1:T(8,128)}, u32[]{:S(2)}) copy-start(f32[256,8,256]{2,0,1:T(8,128)} %copy-done) | copy-start | bytes 6291460
  337.5 18.9 %copy-start.3 = (f32[256,4,256]{2,0,1:T(8,128)}, f32[256,4,256]{2,0,1:T(8,128)S(1)}, u32[]{:S(2)}) copy-start(f32[256,4,256]{2,0,1:T(8,128)S(1)} %bitcast_add_fusion) | copy-start | bytes 3145732
  337.6 22.2 %collective-permute-start.13 = (f32[256,2,256]{2,0,1:T(8,128)S(1)}, f32[256,2,256]{2,0,1:T(8,128)S(1)}, u32[]{:S(2)}, u32[]{:S(2)}) collective-permute-start(f32[256,2,256]{2,0,1:T(8,128)S(1)} %select_bitcast_fusion.2), channel_id=1, source_target_pairs={{0,2},{1,3},{2,0},{3,1},{4,6},{5,7},{6,4},{7,5},{8,10},{9,11},{10,... | collective-permute-start | bytes 1572872 | tf_op jit(solution)/shard_map/ppermute | solution.py:83
  356.4 3.4 copy-start.4
  357.3 15.6 %collective-permute-start.10 = (f32[256,2,256]{2,0,1:T(8,128)}, f32[256,2,256]{2,0,1:T(8,128)}, u32[]{:S(2)}, u32[]{:S(2)}) collective-permute-start(f32[256,2,256]{2,0,1:T(8,128)} %select_bitcast_fusion.3), channel_id=1, source_target_pairs={{0,2},{1,3},{2,0},{3,1},{4,6},{5,7},{6,4},{7,5},{8,10},{9,11},{10,... | collective-permute-start | bytes 1572872 | tf_op jit(solution)/shard_map/ppermute | solution.py:83
  359.9 23.5 %collective-permute-start.14 = (f32[256,1,256]{2,0,1:T(8,128)S(1)}, f32[256,1,256]{2,0,1:T(8,128)S(1)}, u32[]{:S(2)}, u32[]{:S(2)}) collective-permute-start(f32[256,1,256]{2,0,1:T(8,128)S(1)} %select_bitcast_fusion.4), channel_id=1, source_target_pairs={{0,4},{1,5},{2,6},{3,7},{4,0},{5,1},{6,2},{7,3},{8,12},{9,13},{10,... | collective-permute-start | bytes 786440 | tf_op jit(solution)/shard_map/ppermute | solution.py:83
  374.0 17.7 %collective-permute-start.11 = (f32[256,1,256]{2,0,1:T(8,128)S(1)}, f32[256,1,256]{2,0,1:T(8,128)S(1)}, u32[]{:S(2)}, u32[]{:S(2)}) collective-permute-start(f32[256,1,256]{2,0,1:T(8,128)S(1)} %select_bitcast_fusion.5), channel_id=1, source_target_pairs={{0,4},{1,5},{2,6},{3,7},{4,0},{5,1},{6,2},{7,3},{8,12},{9,13},{10,... | collective-permute-start | bytes 786440 | tf_op jit(solution)/shard_map/ppermute | solution.py:83
  (1 other events, 0.6 us)
Sparse Core Ops, SparseCore 0:
  10.7 128.4 all-gather.1

commit v8 on v7

--- a/solution.py
+++ b/solution.py
@@ -51,7 +51,7 @@
     return before_s.reshape(forward.shape), after_u.reshape(backward.shape)
 
 
-def scattered_sum(partial, rows_axis, axis, width):
+def scattered_sum(part_of, rows_axis, axis, width):
     chains, devices = (lax.axis_size(rows_axis), lax.axis_size(axis))
     chain, position = (lax.axis_index(rows_axis), lax.axis_index(axis))
     ring = RING if devices % RING == 0 else 1
@@ -64,10 +64,8 @@
 
     turn = chain % 2
     mine_label = label(position, turn)
-    order = [place(lab, 1) for lab in range(devices)]
-    rows = partial.shape[0]
-    blocks = partial.reshape(rows, devices, width)
-    blocks = jnp.where(turn == 1, blocks[:, order], blocks)
+    blocks = jnp.stack([part_of(place(lab, turn)) for lab in range(devices)], axis=1)
+    rows = blocks.shape[0]
     bit = 1
     while bit < devices:
         count = blocks.shape[1]
@@ -235,10 +233,13 @@
         (core_out + skip_gain[None, :, None] * value_f).reshape(rows, inner).astype(jnp.bfloat16)
     )
 
-    partial_out = lax.dot_general(
-        mixed, w_all[:, :out_cols], (((1,), (1,)), ((), ())), preferred_element_type=jnp.float32
-    )
-    output = scattered_sum(partial_out, "ctx", "tp", width).astype(jnp.bfloat16)
+    def out_part(dest):
+        block = row_block(w_all, dest, width)[:, :out_cols]
+        return lax.dot_general(
+            mixed, block, (((1,), (1,)), ((), ())), preferred_element_type=jnp.float32
+        )
+
+    output = scattered_sum(out_part, "ctx", "tp", width).astype(jnp.bfloat16)
     grads = pullback((d_mixed, adjoint))
     d_values = grads[0] + skip_gain[None, :, None] * d_mixed
     d_pre = grads[3] * jax.nn.sigmoid(pre_step)
@@ -252,10 +253,13 @@
         axis=1,
     )
 
-    partial_grad = lax.dot_general(
-        d_cat, w_all[:, out_cols:], (((1,), (1,)), ((), ())), preferred_element_type=jnp.float32
-    )
-    grad = scattered_sum(partial_grad, "ctx", "tp", width).astype(jnp.bfloat16)
+    def grad_part(dest):
+        block = row_block(w_all, dest, width)[:, out_cols:]
+        return lax.dot_general(
+            d_cat, block, (((1,), (1,)), ((), ())), preferred_element_type=jnp.float32
+        )
+
+    grad = scattered_sum(grad_part, "ctx", "tp", width).astype(jnp.bfloat16)
     return (output, grad)
 
 

time: 402 us -> 407 us (1.012)
  local copies, waits for them, and re-layouts: 24.4 us -> 13.6 us
  matrix products: 43.3 us -> 51 us
  waiting for transfers between devices: 212 us -> 218 us
    gather x2 -> x0, local copies, waits for them, and re-layouts: 7.46 us -> none  [scattered_sum(): blocks = jnp.where(turn == 1, blocks[:, order], blocks)]
    select_n x2 -> x0, other arithmetic: 4.83 us -> none  [scattered_sum(): blocks = jnp.where(turn == 1, blocks[:, order], blocks)]
    reshape x2 -> x0, local copies, waits for them, and re-layouts: 4.5 us -> none  [scattered_sum(): blocks = partial.reshape(rows, devices, width)]
    dot_general x2 -> x16, matrix products: 5.44 us -> 8.18 us  [the longest x8 5.96 us: grad_part(): lax.dot_general(d_cat, block, (((1,), (1,)), ((), ())), preferred_element...]
  transfers between devices with their start and end apart: 16 -> 16, of which waited for: 14 -> 15; matrix products, arithmetic and copies ran while one was open for 6% -> 4% of each run, Pallas kernels for 0% -> 0%
where the time goes in v8:
time: 407 us; the launch traced here: 400 us
  waiting for transfers between devices  218 us (54%)
  starting transfers between devices  69.5 us (17%)
  matrix products  51 us (13%)
  other arithmetic  32.8 us (8%)
  between operations  15.2 us (4%)
  local copies, waits for them, and re-layouts  13.6 us (3%)
    all_gather x1, waiting for transfers between devices, per_device(): lax.all_gather(jnp.concatenate([w_out.T, w_in, w_bc, w_dt], axis=1), 'ctx...  72.3 us
    ppermute x5, waiting for transfers between devices, both_carries(): got = lax.ppermute(message, axis, [(i, i ^ bit) for i in range(devices)])  66.3 us
    ppermute x3, waiting for transfers between devices, doubled_rows(): other = lax.ppermute(x, axis, [(i, i ^ bit) for i in range(devices)])  36 us
    ppermute x6, waiting for transfers between devices, scattered_sum(): blocks = keep + lax.ppermute(send, (rows_axis, axis), pairs)  32.2 us
    ppermute x6, starting transfers between devices, scattered_sum(): blocks = keep + lax.ppermute(send, (rows_axis, axis), pairs)  26.4 us
    ppermute x5, starting transfers between devices, both_carries(): got = lax.ppermute(message, axis, [(i, i ^ bit) for i in range(devices)])  20.3 us
    ppermute x3, starting transfers between devices, doubled_rows(): other = lax.ppermute(x, axis, [(i, i ^ bit) for i in range(devices)])  18.1 us
    dot_general x3, matrix products, ssd_advance(): inside = jnp.einsum('hts,shp->thp', scores * weight, inputs, precision=HIGH)  11.6 us
  transfers between devices with their start and end apart: 16, of which 15 were waited for; matrix products, arithmetic and copies ran while one was open for 4% of the time, Pallas kernels for 0%

profile of v8, /device:TPU:1, one launch (start us, length us, event | category | flops | bytes accessed | tf_op | source)
XLA Modules:
  0.0 400.3 jit_solution(2756454586193707068)
XLA Ops:
  8.0 1.4 pad_maximum_fusion.7
  11.3 8.3 %collective-permute-start = (bf16[256,512]{1,0:T(8,128)(2,1)S(1)}, bf16[256,512]{1,0:T(8,128)(2,1)S(1)}, u32[]{:S(2)}, u32[]{:S(2)}) collective-permute-start(bf16[256,512]{1,0:T(8,128)(2,1)S(1)} %constant_dynamic-update-slice_fusion), channel_id=1, source_target_pairs={{0,4},{1,5},{2,6},{3,7},{4,0},{5,1},{6,2},{7,3},{8,12},{9,13},{10,... | collective-permute-start | bytes 786440 | tf_op jit(solution)/shard_map/ppermute | solution.py:176
  19.6 8.5 %collective-permute-done = bf16[256,512]{1,0:T(8,128)(2,1)S(1)} collective-permute-done((bf16[256,512]{1,0:T(8,128)(2,1)S(1)}, bf16[256,512]{1,0:T(8,128)(2,1)S(1)}, u32[]{:S(2)}, u32[]{:S(2)}) %collective-permute-start) | collective-permute-done | bytes 262176 | tf_op jit(solution)/shard_map/ppermute | solution.py:176
  28.3 3.7 collective-permute-start.1
  32.0 7.7 %collective-permute-done.1 = bf16[512,512]{1,0:T(8,128)(2,1)S(1)} collective-permute-done((bf16[512,512]{1,0:T(8,128)(2,1)S(1)}, bf16[512,512]{1,0:T(8,128)(2,1)S(1)}, u32[]{:S(2)}, u32[]{:S(2)}) %collective-permute-start.1) | collective-permute-done | bytes 524320 | tf_op jit(solution)/shard_map/ppermute | solution.py:176
  40.2 6.1 %collective-permute-start.2 = (bf16[1024,512]{1,0:T(8,128)(2,1)S(1)}, bf16[1024,512]{1,0:T(8,128)(2,1)S(1)}, u32[]{:S(2)}, u32[]{:S(2)}) collective-permute-start(bf16[1024,512]{1,0:T(8,128)(2,1)S(1)} %maximum_select_fusion.1), channel_id=1, source_target_pairs={{0,1},{1,0},{2,3},{3,2},{4,5},{5,4},{6,7},{7,6},{8,9},{9,8},{10,11... | collective-permute-start | bytes 3145736 | tf_op jit(solution)/shard_map/ppermute | solution.py:176
  46.3 19.8 %collective-permute-done.2 = bf16[1024,512]{1,0:T(8,128)(2,1)S(1)} collective-permute-done((bf16[1024,512]{1,0:T(8,128)(2,1)S(1)}, bf16[1024,512]{1,0:T(8,128)(2,1)S(1)}, u32[]{:S(2)}, u32[]{:S(2)}) %collective-permute-start.2) | collective-permute-done | bytes 1048608 | tf_op jit(solution)/shard_map/ppermute | solution.py:176
  66.9 72.3 %all-gather.2.cloned.1.call-done = bf16[2048,1288]{1,0:T(8,128)(2,1)} async-done(((bf16[32,1288]{1,0:T(8,128)(2,1)}), bf16[2048,1288]{1,0:T(8,128)(2,1)}) %all-gather.2.cloned.1.call-update) | async-done | bytes 5275664 | tf_op jit(solution)/shard_map/all_gather | solution.py:198
  139.2 1.3 fusion.94
  140.5 1.3 convolution_add_fusion.6
  141.9 1.3 convolution_add_fusion.5
  143.2 1.3 convolution_add_fusion.4
  144.6 1.3 convolution_add_fusion.3
  145.9 1.3 convolution_add_fusion.2
  147.3 1.3 convolution_add_fusion.1
  148.6 1.3 fusion.179
  157.9 1.3 fusion.41
  159.2 1.3 fusion.113
  160.6 1.2 convolution_add_fusion.13
  161.8 1.2 convolution_add_fusion.12
  163.0 1.2 convolution_add_fusion.11
  164.3 1.2 convolution_add_fusion.10
  165.5 1.3 convolution_add_fusion.9
  166.8 1.2 convolution_add_fusion.8
  168.0 1.2 convolution_add_fusion.7
  170.4 2.2 collective-permute-start.3
  172.6 1.6 collective-permute-done.3
  174.3 1.3 add_select_fusion.16
  176.5 3.0 collective-permute-start.4
  179.5 12.5 %collective-permute-done.4 = f32[8,16512]{1,0:T(8,128)} collective-permute-done((f32[8,16512]{1,0:T(8,128)}, f32[8,16512]{1,0:T(8,128)}, u32[]{:S(2)}, u32[]{:S(2)}) %collective-permute-start.4) | collective-permute-done | bytes 528416 | tf_op jit(solution)/shard_map/ppermute | solution.py:38
  192.9 1.2 add_select_fusion.14
  195.0 4.0 collective-permute-start.5
  199.0 23.5 %collective-permute-done.5 = f32[8,16512]{1,0:T(8,128)} collective-permute-done((f32[8,16512]{1,0:T(8,128)}, f32[8,16512]{1,0:T(8,128)}, u32[]{:S(2)}, u32[]{:S(2)}) %collective-permute-start.5) | collective-permute-done | bytes 528416 | tf_op jit(solution)/shard_map/ppermute | solution.py:38
  225.4 6.9 %collective-permute-start.6 = (f32[8,16512]{1,0:T(8,128)}, f32[8,16512]{1,0:T(8,128)}, u32[]{:S(2)}, u32[]{:S(2)}) collective-permute-start(f32[8,16512]{1,0:T(8,128)} %pad_maximum_fusion.3), channel_id=1, source_target_pairs={{0,64},{8,72},{16,80},{24,88},{32,96},{40,104},{48,112},{56,120},{... | collective-permute-start | bytes 1585160 | tf_op jit(solution)/shard_map/ppermute | solution.py:38
  233.3 21.8 %collective-permute-done.6 = f32[8,16512]{1,0:T(8,128)} collective-permute-done((f32[8,16512]{1,0:T(8,128)}, f32[8,16512]{1,0:T(8,128)}, u32[]{:S(2)}, u32[]{:S(2)}) %collective-permute-start.6) | collective-permute-done | bytes 528416 | tf_op jit(solution)/shard_map/ppermute | solution.py:38
  257.2 4.3 %collective-permute-start.7 = (f32[8,16512]{1,0:T(8,128)S(1)}, f32[8,16512]{1,0:T(8,128)S(1)}, u32[]{:S(2)}, u32[]{:S(2)}) collective-permute-start(f32[8,16512]{1,0:T(8,128)S(1)} %pad_maximum_fusion.4), channel_id=1, source_target_pairs={{0,128},{8,136},{16,144},{24,152},{32,160},{40,168},{48,176},{56,1... | collective-permute-start | bytes 1585160 | tf_op jit(solution)/shard_map/ppermute | solution.py:38
  261.8 3.4 fusion.10
  265.2 6.8 %collective-permute-done.7 = f32[8,16512]{1,0:T(8,128)S(1)} collective-permute-done((f32[8,16512]{1,0:T(8,128)S(1)}, f32[8,16512]{1,0:T(8,128)S(1)}, u32[]{:S(2)}, u32[]{:S(2)}) %collective-permute-start.7) | collective-permute-done | bytes 528416 | tf_op jit(solution)/shard_map/ppermute | solution.py:38
  272.9 1.2 select_select_fusion
  274.1 4.6 %collective-permute-start.8 = (f32[8,8192]{1,0:T(8,128)S(1)}, f32[8,8192]{1,0:T(8,128)S(1)}, u32[]{:S(2)}, u32[]{:S(2)}) collective-permute-start(f32[8,8192]{1,0:T(8,128)S(1)} %select_select_fusion), channel_id=1, source_target_pairs={{0,256},{8,264},{16,272},{24,280},{32,288},{40,296},{48,304},{56,3... | collective-permute-start | bytes 786440 | tf_op jit(solution)/shard_map/ppermute | solution.py:31
  278.8 11.4 %collective-permute-done.8 = f32[8,8192]{1,0:T(8,128)S(1)} collective-permute-done((f32[8,8192]{1,0:T(8,128)S(1)}, f32[8,8192]{1,0:T(8,128)S(1)}, u32[]{:S(2)}, u32[]{:S(2)}) %collective-permute-start.8) | collective-permute-done | bytes 262176 | tf_op jit(solution)/shard_map/ppermute | solution.py:31
  290.2 1.4 fusion.97
  291.6 1.5 fusion.96
  296.9 3.8 fusion.20
  304.0 4.5 %multiply_reduce_fusion.1 = (f32[256,8]{0,1:T(8,128)S(1)}, f32[256,8]{0,1:T(8,128)}, f32[256,8,64]{0,2,1:T(8,128)}) fusion(f32[256,8,64]{0,2,1:T(8,128)S(1)} %convolution_bitcast_fusion.1, f32[256,8,64]{0,2,1:T(8,128)S(1)} %bitcast.392, f32[256,8]{0,1:T(8,128)S(1)} %get-tuple-element.181, f32[8,256]{1,0:T(8,128)} %copy-done.28, f32[256,256]{1,0:T(8,128)} %copy-done.13, ...), kind=kOutput, calls=%fused_computation.126 | convolution fusion | flops 405794816 | bytes 2465792 | tf_op jit(solution)/shard_map/transpose(jvp())/while/body/eval_jaxpr/checkpoint/hts,shp->thp/dot_general | solution.py:104
  311.4 2.7 reduce-window.44
  314.2 2.3 fusion.18
  317.7 1.4 fusion.32
  319.2 1.4 fusion.31
  320.5 1.4 fusion.30
  323.8 1.3 select_bitcast_fusion
  325.1 4.0 collective-permute-start.12
  331.4 1.3 copy-done
  332.8 2.5 collective-permute-start.9
  335.4 6.8 %collective-permute-done.12 = f32[256,4,256]{2,0,1:T(8,128)} collective-permute-done((f32[256,4,256]{2,0,1:T(8,128)}, f32[256,4,256]{2,0,1:T(8,128)}, u32[]{:S(2)}, u32[]{:S(2)}) %collective-permute-start.12) | collective-permute-done | bytes 1048608 | tf_op jit(solution)/shard_map/ppermute | solution.py:81
  342.1 2.1 bitcast_add_fusion
  345.1 3.0 collective-permute-start.13
  348.1 7.2 %collective-permute-done.9 = f32[256,4,256]{2,0,1:T(8,128)S(1)} collective-permute-done((f32[256,4,256]{2,0,1:T(8,128)S(1)}, f32[256,4,256]{2,0,1:T(8,128)S(1)}, u32[]{:S(2)}, u32[]{:S(2)}) %collective-permute-start.9) | collective-permute-done | bytes 1048608 | tf_op jit(solution)/shard_map/ppermute | solution.py:81
  355.7 2.8 collective-permute-start.10
  358.4 4.4 %collective-permute-done.13 = f32[256,2,256]{2,0,1:T(8,128)} collective-permute-done((f32[256,2,256]{2,0,1:T(8,128)}, f32[256,2,256]{2,0,1:T(8,128)}, u32[]{:S(2)}, u32[]{:S(2)}) %collective-permute-start.13) | collective-permute-done | bytes 524320 | tf_op jit(solution)/shard_map/ppermute | solution.py:81
  364.0 7.1 %collective-permute-start.14 = (f32[256,1,256]{2,0,1:T(8,128)S(1)}, f32[256,1,256]{2,0,1:T(8,128)S(1)}, u32[]{:S(2)}, u32[]{:S(2)}) collective-permute-start(f32[256,1,256]{2,0,1:T(8,128)S(1)} %select_bitcast_fusion.4), channel_id=1, source_target_pairs={{0,4},{1,5},{2,6},{3,7},{4,0},{5,1},{6,2},{7,3},{8,12},{9,13},{10,... | collective-permute-start | bytes 786440 | tf_op jit(solution)/shard_map/ppermute | solution.py:81
  371.0 2.9 collective-permute-done.10
  374.1 7.1 %collective-permute-start.11 = (f32[256,1,256]{2,0,1:T(8,128)S(1)}, f32[256,1,256]{2,0,1:T(8,128)S(1)}, u32[]{:S(2)}, u32[]{:S(2)}) collective-permute-start(f32[256,1,256]{2,0,1:T(8,128)S(1)} %select_bitcast_fusion.5), channel_id=1, source_target_pairs={{0,4},{1,5},{2,6},{3,7},{4,0},{5,1},{6,2},{7,3},{8,12},{9,13},{10,... | collective-permute-start | bytes 786440 | tf_op jit(solution)/shard_map/ppermute | solution.py:81
  381.9 10.9 %collective-permute-done.11 = f32[256,1,256]{2,0,1:T(8,128)S(1)} collective-permute-done((f32[256,1,256]{2,0,1:T(8,128)S(1)}, f32[256,1,256]{2,0,1:T(8,128)S(1)}, u32[]{:S(2)}, u32[]{:S(2)}) %collective-permute-start.11) | collective-permute-done | bytes 262176 | tf_op jit(solution)/shard_map/ppermute | solution.py:81
  (193 shorter events, 41.9 us)
Async XLA Ops:
  7.2 132.0 %all-gather.2.cloned.1.call-start = ((), (), s32[]{:S(2)}) async-start(), calls=%async_computation | async-start | bytes 5857280 | tf_op jit(solution)/shard_map/all_gather | solution.py:198
  11.3 16.8 %collective-permute-start = (bf16[256,512]{1,0:T(8,128)(2,1)S(1)}, bf16[256,512]{1,0:T(8,128)(2,1)S(1)}, u32[]{:S(2)}, u32[]{:S(2)}) collective-permute-start(bf16[256,512]{1,0:T(8,128)(2,1)S(1)} %constant_dynamic-update-slice_fusion), channel_id=1, source_target_pairs={{0,4},{1,5},{2,6},{3,7},{4,0},{5,1},{6,2},{7,3},{8,12},{9,13},{10,... | collective-permute-start | bytes 786440 | tf_op jit(solution)/shard_map/ppermute | solution.py:176
  28.3 11.4 %collective-permute-start.1 = (bf16[512,512]{1,0:T(8,128)(2,1)S(1)}, bf16[512,512]{1,0:T(8,128)(2,1)S(1)}, u32[]{:S(2)}, u32[]{:S(2)}) collective-permute-start(bf16[512,512]{1,0:T(8,128)(2,1)S(1)} %maximum_select_fusion.2), channel_id=1, source_target_pairs={{0,2},{1,3},{2,0},{3,1},{4,6},{5,7},{6,4},{7,5},{8,10},{9,11},{10,... | collective-permute-start | bytes 1572872 | tf_op jit(solution)/shard_map/ppermute | solution.py:176
  40.2 26.0 %collective-permute-start.2 = (bf16[1024,512]{1,0:T(8,128)(2,1)S(1)}, bf16[1024,512]{1,0:T(8,128)(2,1)S(1)}, u32[]{:S(2)}, u32[]{:S(2)}) collective-permute-start(bf16[1024,512]{1,0:T(8,128)(2,1)S(1)} %maximum_select_fusion.1), channel_id=1, source_target_pairs={{0,1},{1,0},{2,3},{3,2},{4,5},{5,4},{6,7},{7,6},{8,9},{9,8},{10,11... | collective-permute-start | bytes 3145736 | tf_op jit(solution)/shard_map/ppermute | solution.py:176
  147.2 3.6 copy-start.24
  147.3 3.6 copy-start.34
  150.0 0.9 copy-start.11
  152.2 2.3 copy-start.18
  154.6 3.3 copy-start.7
  157.9 12.4 %copy-start.32 = (f32[8]{0:T(128)}, f32[8]{0:T(128)S(1)}, u32[]{:S(2)}) copy-start(f32[8]{0:T(128)S(1)} %negate_exponential_fusion) | copy-start | bytes 100
  159.2 10.8 %copy-start.3 = (f32[1,8,64,128]{3,2,1,0:T(8,128)}, f32[1,8,64,128]{3,2,1,0:T(8,128)S(1)}, u32[]{:S(2)}) copy-start(f32[1,8,64,128]{3,2,1,0:T(8,128)S(1)} %fusion.41) | copy-start | bytes 786436
  165.5 3.8 copy-start.9
  165.5 3.8 copy-start.20
  165.5 3.8 copy-start.33
  169.3 5.1 %copy-start.31 = (f32[8]{0:T(128)S(1)}, f32[8]{0:T(128)}, u32[]{:S(2)}) copy-start(f32[8]{0:T(128)} %get-tuple-element.205) | copy-start | bytes 100
  170.4 3.8 collective-permute-start.3
  176.5 15.6 %collective-permute-start.4 = (f32[8,16512]{1,0:T(8,128)}, f32[8,16512]{1,0:T(8,128)}, u32[]{:S(2)}, u32[]{:S(2)}) collective-permute-start(f32[8,16512]{1,0:T(8,128)} %pad_maximum_fusion.1), channel_id=1, source_target_pairs={{0,16},{8,24},{16,0},{24,8},{32,48},{40,56},{48,32},{56,40},{64,80... | collective-permute-start | bytes 1585160 | tf_op jit(solution)/shard_map/ppermute | solution.py:38
  194.1 38.4 %copy-start.36 = (f32[8]{0:T(128)S(1)}, f32[8]{0:T(128)}, u32[]{:S(2)}) copy-start(f32[8]{0:T(128)} %param.15) | copy-start | bytes 100
  195.0 27.5 %collective-permute-start.5 = (f32[8,16512]{1,0:T(8,128)}, f32[8,16512]{1,0:T(8,128)}, u32[]{:S(2)}, u32[]{:S(2)}) collective-permute-start(f32[8,16512]{1,0:T(8,128)} %pad_maximum_fusion.2), channel_id=1, source_target_pairs={{0,32},{8,40},{16,48},{24,56},{32,0},{40,8},{48,16},{56,24},{64,96... | collective-permute-start | bytes 1585160 | tf_op jit(solution)/shard_map/ppermute | solution.py:38
  224.5 37.0 %copy-start.19 = (f32[8,2,128]{2,0,1:T(8,128)S(1)}, f32[8,2,128]{2,0,1:T(8,128)}, u32[]{:S(2)}) copy-start(f32[8,2,128]{2,0,1:T(8,128)} %copy-done.18) | copy-start | bytes 24580
  224.5 37.0 %copy-start.8 = (bf16[256,256]{0,1:T(8,128)(2,1)S(1)}, bf16[256,256]{0,1:T(8,128)(2,1)}, u32[]{:S(2)}) copy-start(bf16[256,256]{0,1:T(8,128)(2,1)} %copy-done.7) | copy-start | bytes 393220
  225.4 29.6 %collective-permute-start.6 = (f32[8,16512]{1,0:T(8,128)}, f32[8,16512]{1,0:T(8,128)}, u32[]{:S(2)}, u32[]{:S(2)}) collective-permute-start(f32[8,16512]{1,0:T(8,128)} %pad_maximum_fusion.3), channel_id=1, source_target_pairs={{0,64},{8,72},{16,80},{24,88},{32,96},{40,104},{48,112},{56,120},{... | collective-permute-start | bytes 1585160 | tf_op jit(solution)/shard_map/ppermute | solution.py:38
  233.2 63.7 %copy-start.21 = (pred[1,256,256]{2,1,0:T(8,128)(4,1)}, pred[1,256,256]{2,1,0:T(8,128)(4,1)S(1)}, u32[]{:S(2)}) copy-start(pred[1,256,256]{2,1,0:T(8,128)(4,1)S(1)} %iota_compare_fusion) | copy-start | bytes 196612
  257.2 14.8 %collective-permute-start.7 = (f32[8,16512]{1,0:T(8,128)S(1)}, f32[8,16512]{1,0:T(8,128)S(1)}, u32[]{:S(2)}, u32[]{:S(2)}) collective-permute-start(f32[8,16512]{1,0:T(8,128)S(1)} %pad_maximum_fusion.4), channel_id=1, source_target_pairs={{0,128},{8,136},{16,144},{24,152},{32,160},{40,168},{48,176},{56,1... | collective-permute-start | bytes 1585160 | tf_op jit(solution)/shard_map/ppermute | solution.py:38
  271.9 0.8 copy-start.4
  274.1 18.9 %copy-start.25 = (f32[8]{0:T(128)S(1)}, f32[8]{0:T(128)}, u32[]{:S(2)}) copy-start(f32[8]{0:T(128)} %param.14) | copy-start | bytes 100
  274.1 16.0 %collective-permute-start.8 = (f32[8,8192]{1,0:T(8,128)S(1)}, f32[8,8192]{1,0:T(8,128)S(1)}, u32[]{:S(2)}, u32[]{:S(2)}) collective-permute-start(f32[8,8192]{1,0:T(8,128)S(1)} %select_select_fusion), channel_id=1, source_target_pairs={{0,256},{8,264},{16,272},{24,280},{32,288},{40,296},{48,304},{56,3... | collective-permute-start | bytes 786440 | tf_op jit(solution)/shard_map/ppermute | solution.py:31
  291.6 4.3 %copy-start.5 = (f32[256,1,128]{0,2,1:T(8,128)S(1)}, f32[256,1,128]{0,2,1:T(8,128)}, u32[]{:S(2)}) copy-start(f32[256,1,128]{0,2,1:T(8,128)} %get-tuple-element.186) | copy-start | bytes 393220
  291.6 4.3 %copy-start.6 = (f32[256,1,128]{0,2,1:T(8,128)S(1)}, f32[256,1,128]{0,2,1:T(8,128)}, u32[]{:S(2)}) copy-start(f32[256,1,128]{0,2,1:T(8,128)} %get-tuple-element.184) | copy-start | bytes 393220
  294.0 6.7 %copy-start.16 = (f32[256,8]{0,1:T(8,128)}, f32[256,8]{0,1:T(8,128)S(1)}, u32[]{:S(2)}) copy-start(f32[256,8]{0,1:T(8,128)S(1)} %get-tuple-element.196) | copy-start | bytes 24580
  294.1 6.7 %copy-start.28 = (f32[8,256]{1,0:T(8,128)}, f32[8,256]{1,0:T(8,128)S(1)}, u32[]{:S(2)}) copy-start(f32[8,256]{1,0:T(8,128)S(1)} %add_bitcast_fusion.1) | copy-start | bytes 24580
  295.1 13.5 %copy-start.27 = (f32[8]{0:T(128)}, f32[8]{0:T(128)S(1)}, u32[]{:S(2)}) copy-start(f32[8]{0:T(128)S(1)} %get-tuple-element.221) | copy-start | bytes 100
  295.2 5.5 %copy-start.22 = (f32[256,8]{0,1:T(8,128)}, f32[256,8]{0,1:T(8,128)S(1)}, u32[]{:S(2)}) copy-start(f32[256,8]{0,1:T(8,128)S(1)} %subtract_exponential_fusion) | copy-start | bytes 24580
  296.3 4.4 %copy-start.13 = (f32[256,256]{1,0:T(8,128)}, f32[256,256]{1,0:T(8,128)S(1)}, u32[]{:S(2)}) copy-start(f32[256,256]{1,0:T(8,128)S(1)} %fusion.167) | copy-start | bytes 786436
  304.0 4.6 %copy-start.17 = (f32[256,8]{0,1:T(8,128)S(1)}, f32[256,8]{0,1:T(8,128)}, u32[]{:S(2)}) copy-start(f32[256,8]{0,1:T(8,128)} %copy-done.16) | copy-start | bytes 24580
  304.0 10.2 %copy-start.10 = (f32[256,128]{1,0:T(8,128)S(1)}, f32[256,128]{1,0:T(8,128)}, u32[]{:S(2)}) copy-start(f32[256,128]{1,0:T(8,128)} %copy.130) | copy-start | bytes 393220
  304.0 17.9 %slice-start = ((s8[5767168]{0:T(1024)(128)(4,1)}), s8[1572864]{0:T(1024)(128)(4,1)S(1)}, s32[]{:S(2)}) async-start(s8[5767168]{0:T(1024)(128)(4,1)} %bitcast.361), calls=%async_computation.1 | async-start | bytes 3145728
  308.5 0.6 copy-start.23
  308.6 8.0 %copy-start.14 = (bf16[256,1,1,128]{0,3,2,1:T(8,128)(2,1)S(1)}, bf16[256,1,1,128]{0,3,2,1:T(8,128)(2,1)}, u32[]{:S(2)}) copy-start(bf16[256,1,1,128]{0,3,2,1:T(8,128)(2,1)} %fusion.46) | copy-start | bytes 196612
  308.6 8.0 %copy-start.15 = (bf16[256,1,1,128]{0,3,2,1:T(8,128)(2,1)S(1)}, bf16[256,1,1,128]{0,3,2,1:T(8,128)(2,1)}, u32[]{:S(2)}) copy-start(bf16[256,1,1,128]{0,3,2,1:T(8,128)(2,1)} %fusion.45) | copy-start | bytes 196612
  308.6 8.0 %copy-start.26 = (f32[8]{0:T(128)S(1)}, f32[8]{0:T(128)}, u32[]{:S(2)}) copy-start(f32[8]{0:T(128)} %param.14) | copy-start | bytes 100
  308.6 8.0 %copy-start.29 = (f32[256,8]{0,1:T(8,128)S(1)}, f32[256,8]{0,1:T(8,128)}, u32[]{:S(2)}) copy-start(f32[256,8]{0,1:T(8,128)} %get-tuple-element.194) | copy-start | bytes 24580
  308.6 8.0 %copy-start.35 = (f32[8]{0:T(128)S(1)}, f32[8]{0:T(128)}, u32[]{:S(2)}) copy-start(f32[8]{0:T(128)} %param.13) | copy-start | bytes 100
  308.6 8.9 %copy-start.30 = (f32[512]{0:T(512)S(1)}, f32[512]{0:T(512)}, u32[]{:S(2)}) copy-start(f32[512]{0:T(512)} %mul.708) | copy-start | bytes 6148
  314.2 3.3 copy-start.12
  316.5 5.4 %slice-start.1 = ((s8[5767168]{0:T(1024)(128)(4,1)}), s8[4194304]{0:T(1024)(128)(4,1)S(1)}, s32[]{:S(2)}) async-start(s8[5767168]{0:T(1024)(128)(4,1)} %bitcast.361), calls=%async_computation.2 | async-start | bytes 8388608
  323.8 5.3 %copy-start.2 = (f32[256,8,256]{2,0,1:T(8,128)}, f32[256,8,256]{2,0,1:T(8,128)S(1)}, u32[]{:S(2)}) copy-start(f32[256,8,256]{2,0,1:T(8,128)S(1)} %fusion.25) | copy-start | bytes 6291460
  325.1 17.1 %collective-permute-start.12 = (f32[256,4,256]{2,0,1:T(8,128)}, f32[256,4,256]{2,0,1:T(8,128)}, u32[]{:S(2)}, u32[]{:S(2)}) collective-permute-start(f32[256,4,256]{2,0,1:T(8,128)} %select_bitcast_fusion), channel_id=1, source_target_pairs={{0,1},{1,0},{2,3},{3,2},{4,5},{5,4},{6,7},{7,6},{8,11},{9,10},{10,... | collective-permute-start | bytes 3145736 | tf_op jit(solution)/shard_map/ppermute | solution.py:81
  331.4 1.3 copy-start
  332.8 22.5 %collective-permute-start.9 = (f32[256,4,256]{2,0,1:T(8,128)S(1)}, f32[256,4,256]{2,0,1:T(8,128)S(1)}, u32[]{:S(2)}, u32[]{:S(2)}) collective-permute-start(f32[256,4,256]{2,0,1:T(8,128)S(1)} %select_bitcast_fusion.1), channel_id=1, source_target_pairs={{0,1},{1,0},{2,3},{3,2},{4,5},{5,4},{6,7},{7,6},{8,11},{9,10},{10,... | collective-permute-start | bytes 3145736 | tf_op jit(solution)/shard_map/ppermute | solution.py:81
  335.3 20.0 %copy-start.1 = (f32[256,8,256]{2,0,1:T(8,128)S(1)}, f32[256,8,256]{2,0,1:T(8,128)}, u32[]{:S(2)}) copy-start(f32[256,8,256]{2,0,1:T(8,128)} %copy-done) | copy-start | bytes 6291460
  345.1 17.7 %collective-permute-start.13 = (f32[256,2,256]{2,0,1:T(8,128)}, f32[256,2,256]{2,0,1:T(8,128)}, u32[]{:S(2)}, u32[]{:S(2)}) collective-permute-start(f32[256,2,256]{2,0,1:T(8,128)} %select_bitcast_fusion.2), channel_id=1, source_target_pairs={{0,2},{1,3},{2,0},{3,1},{4,6},{5,7},{6,4},{7,5},{8,10},{9,11},{10,... | collective-permute-start | bytes 1572872 | tf_op jit(solution)/shard_map/ppermute | solution.py:81
  355.7 18.3 %collective-permute-start.10 = (f32[256,2,256]{2,0,1:T(8,128)S(1)}, f32[256,2,256]{2,0,1:T(8,128)S(1)}, u32[]{:S(2)}, u32[]{:S(2)}) collective-permute-start(f32[256,2,256]{2,0,1:T(8,128)S(1)} %select_bitcast_fusion.3), channel_id=1, source_target_pairs={{0,2},{1,3},{2,0},{3,1},{4,6},{5,7},{6,4},{7,5},{8,10},{9,11},{10,... | collective-permute-start | bytes 1572872 | tf_op jit(solution)/shard_map/ppermute | solution.py:81
  364.0 17.2 %collective-permute-start.14 = (f32[256,1,256]{2,0,1:T(8,128)S(1)}, f32[256,1,256]{2,0,1:T(8,128)S(1)}, u32[]{:S(2)}, u32[]{:S(2)}) collective-permute-start(f32[256,1,256]{2,0,1:T(8,128)S(1)} %select_bitcast_fusion.4), channel_id=1, source_target_pairs={{0,4},{1,5},{2,6},{3,7},{4,0},{5,1},{6,2},{7,3},{8,12},{9,13},{10,... | collective-permute-start | bytes 786440 | tf_op jit(solution)/shard_map/ppermute | solution.py:81
  374.1 18.7 %collective-permute-start.11 = (f32[256,1,256]{2,0,1:T(8,128)S(1)}, f32[256,1,256]{2,0,1:T(8,128)S(1)}, u32[]{:S(2)}, u32[]{:S(2)}) collective-permute-start(f32[256,1,256]{2,0,1:T(8,128)S(1)} %select_bitcast_fusion.5), channel_id=1, source_target_pairs={{0,4},{1,5},{2,6},{3,7},{4,0},{5,1},{6,2},{7,3},{8,12},{9,13},{10,... | collective-permute-start | bytes 786440 | tf_op jit(solution)/shard_map/ppermute | solution.py:81
Sparse Core Ops, SparseCore 0:
  10.7 128.4 all-gather.1

commit v9 on v7

--- a/solution.py
+++ b/solution.py
@@ -15,40 +15,42 @@
 def both_carries(decay, forward, backward, axis):
     devices, position = (lax.axis_size(axis), lax.axis_index(axis))
     heads = decay.shape[0]
-    total_a = decay[:, None]
-    total_s = forward.reshape(heads, -1)
-    total_u = backward.reshape(heads, -1)
-    size = total_s.shape[1]
+    own_a = decay[:, None]
+    own_s = forward.reshape(heads, -1)
+    own_u = backward.reshape(heads, -1)
+    size = own_s.shape[1]
+    message = jnp.concatenate([own_s, own_u, jnp.broadcast_to(own_a, (heads, 128))], axis=1)
+    got = lax.ppermute(message, axis, [(i, i ^ 1) for i in range(devices)])
+    sib_s = got[:, :size]
+    sib_u = got[:, size : 2 * size]
+    sib_a = got[:, 2 * size : 2 * size + 1]
+    second = (position & 1) != 0
+    first_a = jnp.where(second, sib_a, own_a)
+    first_s = jnp.where(second, sib_s, own_s)
+    last_a = jnp.where(second, own_a, sib_a)
+    last_s = jnp.where(second, own_s, sib_s)
+    first_u = jnp.where(second, sib_u, own_u)
+    last_u = jnp.where(second, own_u, sib_u)
+    total_a = first_a * last_a
+    total_m = jnp.where(second, first_u + first_a * last_u, last_a * first_s + last_s)
     before_a = jnp.ones_like(total_a)
-    before_s = jnp.zeros_like(total_s)
-    after_a = jnp.ones_like(total_a)
-    after_u = jnp.zeros_like(total_u)
-    bit = 1
+    before_m = jnp.zeros_like(total_m)
+    bit = 2
     while bit < devices:
-        if 2 * bit >= devices:
-            lower = (position & bit) != 0
-            send = jnp.where(lower, total_u, total_s)
-            got = lax.ppermute(send, axis, [(i, i ^ bit) for i in range(devices)])
-            before_s = jnp.where(lower, before_a * got + before_s, before_s)
-            after_u = jnp.where(lower, after_u, after_u + after_a * got)
-            break
-        message = jnp.concatenate(
-            [total_s, total_u, jnp.broadcast_to(total_a, (heads, 128))], axis=1
-        )
+        message = jnp.concatenate([total_m, jnp.broadcast_to(total_a, (heads, 128))], axis=1)
         got = lax.ppermute(message, axis, [(i, i ^ bit) for i in range(devices)])
-        got_s = got[:, :size]
-        got_u = got[:, size : 2 * size]
-        got_a = got[:, 2 * size : 2 * size + 1]
-        lower = (position & bit) != 0
-        before_s = jnp.where(lower, before_a * got_s + before_s, before_s)
-        before_a = jnp.where(lower, got_a * before_a, before_a)
-        after_u = jnp.where(lower, after_u, after_u + after_a * got_u)
-        after_a = jnp.where(lower, after_a, after_a * got_a)
-        total_s = jnp.where(lower, total_a * got_s + total_s, got_a * total_s + got_s)
-        total_u = jnp.where(lower, got_u + got_a * total_u, total_u + total_a * got_u)
+        got_m = got[:, :size]
+        got_a = got[:, size : size + 1]
+        flag = ((position & bit) != 0) != second
+        before_m = jnp.where(flag, before_a * got_m + before_m, before_m)
+        before_a = jnp.where(flag, before_a * got_a, before_a)
+        total_m = jnp.where(flag, total_a * got_m + total_m, got_a * total_m + got_m)
         total_a = total_a * got_a
         bit *= 2
-    return before_s.reshape(forward.shape), after_u.reshape(backward.shape)
+    got = lax.ppermute(before_m, axis, [(i, i ^ 1) for i in range(devices)])
+    state_in = jnp.where(second, first_a * got + first_s, before_m)
+    adjoint = jnp.where(second, before_m, last_u + last_a * got)
+    return state_in.reshape(forward.shape), adjoint.reshape(backward.shape)
 
 
 def scattered_sum(partial, rows_axis, axis, width):

time: 402 us -> 377 us (0.938)
  waiting for transfers between devices: 212 us -> 179 us
  starting transfers between devices: 71.5 us -> 85 us
    ppermute x5, waiting for transfers between devices: 63.7 us -> 42.9 us  [both_carries(): got = lax.ppermute(message, axis, [(i, i ^ bit) for i in range(devices)])]
    ppermute x1 -> x2, waiting for transfers between devices: 11.7 us -> 1.85 us  [the longest x1 1.85 us: both_carries(): got = lax.ppermute(message, axis, [(i, i ^ 1) for i in range(devices)])]
    ppermute x6, starting transfers between devices: 28.3 us -> 36.4 us  [scattered_sum(): blocks = keep + lax.ppermute(send, (rows_axis, axis), pairs)]
    ppermute x5, starting transfers between devices: 20.4 us -> 25.4 us  [both_carries(): got = lax.ppermute(message, axis, [(i, i ^ bit) for i in range(devices)])]
  transfers between devices with their start and end apart: 16 -> 17, of which waited for: 14 -> 13; matrix products, arithmetic and copies ran while one was open for 6% -> 5% of each run, Pallas kernels for 0% -> 0%
where the time goes in v9:
time: 377 us; the launch traced here: 375 us
  waiting for transfers between devices  179 us (47%)
  starting transfers between devices  85 us (23%)
  matrix products  40.7 us (11%)
  other arithmetic  32.3 us (9%)
  local copies, waits for them, and re-layouts  22.4 us (6%)
  between operations  15.1 us (4%)
    all_gather x1, waiting for transfers between devices, per_device(): lax.all_gather(jnp.concatenate([w_out.T, w_in, w_bc, w_dt], axis=1), 'ctx...  72.3 us
    ppermute x5, waiting for transfers between devices, both_carries(): got = lax.ppermute(message, axis, [(i, i ^ bit) for i in range(devices)])  42.9 us
    ppermute x6, starting transfers between devices, scattered_sum(): blocks = keep + lax.ppermute(send, (rows_axis, axis), pairs)  36.4 us
    ppermute x3, waiting for transfers between devices, doubled_rows(): other = lax.ppermute(x, axis, [(i, i ^ bit) for i in range(devices)])  36 us
    ppermute x6, waiting for transfers between devices, scattered_sum(): blocks = keep + lax.ppermute(send, (rows_axis, axis), pairs)  26.3 us
    ppermute x5, starting transfers between devices, both_carries(): got = lax.ppermute(message, axis, [(i, i ^ bit) for i in range(devices)])  25.4 us
    ppermute x3, starting transfers between devices, doubled_rows(): other = lax.ppermute(x, axis, [(i, i ^ bit) for i in range(devices)])  18.1 us
    dot_general x8, matrix products, per_device(): jnp.dot(piece[:, width:], block[:, :out_cols], preferred_element_type=jnp...  10.3 us
  transfers between devices with their start and end apart: 17, of which 13 were waited for; matrix products, arithmetic and copies ran while one was open for 5% of the time, Pallas kernels for 0%

profile of v9, /device:TPU:1, one launch (start us, length us, event | category | flops | bytes accessed | tf_op | source)
XLA Modules:
  0.0 374.9 jit_solution(11623606803291648422)
XLA Ops:
  8.0 1.4 pad_maximum_fusion.7
  11.3 8.3 %collective-permute-start = (bf16[256,512]{1,0:T(8,128)(2,1)S(1)}, bf16[256,512]{1,0:T(8,128)(2,1)S(1)}, u32[]{:S(2)}, u32[]{:S(2)}) collective-permute-start(bf16[256,512]{1,0:T(8,128)(2,1)S(1)} %constant_dynamic-update-slice_fusion), channel_id=1, source_target_pairs={{0,4},{1,5},{2,6},{3,7},{4,0},{5,1},{6,2},{7,3},{8,12},{9,13},{10,... | collective-permute-start | bytes 786440 | tf_op jit(solution)/shard_map/ppermute | solution.py:180
  19.6 8.5 %collective-permute-done = bf16[256,512]{1,0:T(8,128)(2,1)S(1)} collective-permute-done((bf16[256,512]{1,0:T(8,128)(2,1)S(1)}, bf16[256,512]{1,0:T(8,128)(2,1)S(1)}, u32[]{:S(2)}, u32[]{:S(2)}) %collective-permute-start) | collective-permute-done | bytes 262176 | tf_op jit(solution)/shard_map/ppermute | solution.py:180
  28.3 3.7 collective-permute-start.1
  32.0 7.7 %collective-permute-done.1 = bf16[512,512]{1,0:T(8,128)(2,1)S(1)} collective-permute-done((bf16[512,512]{1,0:T(8,128)(2,1)S(1)}, bf16[512,512]{1,0:T(8,128)(2,1)S(1)}, u32[]{:S(2)}, u32[]{:S(2)}) %collective-permute-start.1) | collective-permute-done | bytes 524320 | tf_op jit(solution)/shard_map/ppermute | solution.py:180
  40.2 6.1 %collective-permute-start.2 = (bf16[1024,512]{1,0:T(8,128)(2,1)S(1)}, bf16[1024,512]{1,0:T(8,128)(2,1)S(1)}, u32[]{:S(2)}, u32[]{:S(2)}) collective-permute-start(bf16[1024,512]{1,0:T(8,128)(2,1)S(1)} %maximum_select_fusion.1), channel_id=1, source_target_pairs={{0,1},{1,0},{2,3},{3,2},{4,5},{5,4},{6,7},{7,6},{8,9},{9,8},{10,11... | collective-permute-start | bytes 3145736 | tf_op jit(solution)/shard_map/ppermute | solution.py:180
  46.3 19.8 %collective-permute-done.2 = bf16[1024,512]{1,0:T(8,128)(2,1)S(1)} collective-permute-done((bf16[1024,512]{1,0:T(8,128)(2,1)S(1)}, bf16[1024,512]{1,0:T(8,128)(2,1)S(1)}, u32[]{:S(2)}, u32[]{:S(2)}) %collective-permute-start.2) | collective-permute-done | bytes 1048608 | tf_op jit(solution)/shard_map/ppermute | solution.py:180
  66.9 72.3 %all-gather.2.cloned.1.call-done = bf16[2048,1288]{1,0:T(8,128)(2,1)} async-done(((bf16[32,1288]{1,0:T(8,128)(2,1)}), bf16[2048,1288]{1,0:T(8,128)(2,1)}) %all-gather.2.cloned.1.call-update) | async-done | bytes 5275664 | tf_op jit(solution)/shard_map/all_gather | solution.py:202
  139.2 1.3 fusion.72
  140.5 1.5 convolution_add_fusion.6
  142.0 1.7 convolution_add_fusion.5
  143.7 1.3 convolution_add_fusion.4
  145.7 1.3 convolution_add_fusion.1
  147.1 1.2 fusion.145
  152.3 1.4 fusion.86
  153.7 1.3 convolution_add_fusion.13
  155.0 1.3 convolution_add_fusion.12
  156.3 1.3 convolution_add_fusion.11
  157.6 1.3 convolution_add_fusion.10
  158.9 1.3 convolution_add_fusion.9
  160.3 1.2 convolution_add_fusion.8
  161.4 1.2 convolution_add_fusion.7
  165.2 2.1 collective-permute-start.3
  167.3 1.8 collective-permute-done.3
  170.4 3.1 collective-permute-start.4
  173.6 6.8 %collective-permute-done.4 = f32[8,8320]{1,0:T(8,128)S(1)} collective-permute-done((f32[8,8320]{1,0:T(8,128)}, f32[8,8320]{1,0:T(8,128)S(1)}, u32[]{:S(2)}, u32[]{:S(2)}) %collective-permute-start.4) | collective-permute-done | bytes 266272 | tf_op jit(solution)/shard_map/ppermute | solution.py:41
  181.4 3.9 %collective-permute-start.5 = (f32[8,8320]{1,0:T(8,128)}, f32[8,8320]{1,0:T(8,128)}, u32[]{:S(2)}, u32[]{:S(2)}) collective-permute-start(f32[8,8320]{1,0:T(8,128)} %pad_maximum_fusion.2), channel_id=1, source_target_pairs={{0,32},{8,40},{16,48},{24,56},{32,0},{40,8},{48,16},{56,24},{64,96... | collective-permute-start | bytes 798728 | tf_op jit(solution)/shard_map/ppermute | solution.py:41
  185.3 12.3 %collective-permute-done.5 = f32[8,8320]{1,0:T(8,128)} collective-permute-done((f32[8,8320]{1,0:T(8,128)}, f32[8,8320]{1,0:T(8,128)}, u32[]{:S(2)}, u32[]{:S(2)}) %collective-permute-start.5) | collective-permute-done | bytes 266272 | tf_op jit(solution)/shard_map/ppermute | solution.py:41
  198.4 1.1 add_select_fusion.6
  200.3 6.8 %collective-permute-start.6 = (f32[8,8320]{1,0:T(8,128)}, f32[8,8320]{1,0:T(8,128)}, u32[]{:S(2)}, u32[]{:S(2)}) collective-permute-start(f32[8,8320]{1,0:T(8,128)} %pad_maximum_fusion.3), channel_id=1, source_target_pairs={{0,64},{8,72},{16,80},{24,88},{32,96},{40,104},{48,112},{56,120},{... | collective-permute-start | bytes 798728 | tf_op jit(solution)/shard_map/ppermute | solution.py:41
  207.1 9.0 %collective-permute-done.6 = f32[8,8320]{1,0:T(8,128)} collective-permute-done((f32[8,8320]{1,0:T(8,128)}, f32[8,8320]{1,0:T(8,128)}, u32[]{:S(2)}, u32[]{:S(2)}) %collective-permute-start.6) | collective-permute-done | bytes 266272 | tf_op jit(solution)/shard_map/ppermute | solution.py:41
  218.7 6.8 %collective-permute-start.7 = (f32[8,8320]{1,0:T(8,128)}, f32[8,8320]{1,0:T(8,128)}, u32[]{:S(2)}, u32[]{:S(2)}) collective-permute-start(f32[8,8320]{1,0:T(8,128)} %pad_maximum_fusion.4), channel_id=1, source_target_pairs={{0,128},{8,136},{16,144},{24,152},{32,160},{40,168},{48,176},{56,1... | collective-permute-start | bytes 798728 | tf_op jit(solution)/shard_map/ppermute | solution.py:41
  227.6 3.1 collective-permute-done.7
  232.6 4.7 %collective-permute-start.8 = (f32[8,8320]{1,0:T(8,128)S(1)}, f32[8,8320]{1,0:T(8,128)S(1)}, u32[]{:S(2)}, u32[]{:S(2)}) collective-permute-start(f32[8,8320]{1,0:T(8,128)S(1)} %pad_maximum_fusion.5), channel_id=1, source_target_pairs={{0,256},{8,264},{16,272},{24,280},{32,288},{40,296},{48,304},{56,3... | collective-permute-start | bytes 798728 | tf_op jit(solution)/shard_map/ppermute | solution.py:41
  237.5 11.8 %collective-permute-done.8 = f32[8,8320]{1,0:T(8,128)S(1)} collective-permute-done((f32[8,8320]{1,0:T(8,128)S(1)}, f32[8,8320]{1,0:T(8,128)S(1)}, u32[]{:S(2)}, u32[]{:S(2)}) %collective-permute-start.8) | collective-permute-done | bytes 266272 | tf_op jit(solution)/shard_map/ppermute | solution.py:41
  249.3 1.3 add_select_fusion
  250.6 2.9 collective-permute-start.9
  253.6 3.3 fusion.12
  258.5 2.2 fusion.20
  262.0 1.2 fusion.26
  263.7 1.2 convolution_bitcast_fusion.1
  265.5 3.1 fusion.22
  268.6 2.6 multiply_reduce_fusion.1
  272.3 2.5 reduce-window.44
  276.6 3.4 fusion
  280.0 3.0 reshape.520
  283.0 1.6 copy.209
  286.1 3.7 gather_fusion.1
  289.8 2.1 gather_fusion
  292.0 2.0 bitcast_select_fusion
  294.0 1.2 select_bitcast_fusion.1
  295.2 3.7 collective-permute-start.10
  299.6 1.1 select_bitcast_fusion
  300.7 2.9 collective-permute-start.13
  303.7 8.7 %collective-permute-done.10 = f32[256,4,256]{2,0,1:T(8,128)} collective-permute-done((f32[256,4,256]{2,0,1:T(8,128)}, f32[256,4,256]{2,0,1:T(8,128)}, u32[]{:S(2)}, u32[]{:S(2)}) %collective-permute-start.10) | collective-permute-done | bytes 1048608 | tf_op jit(solution)/shard_map/ppermute | solution.py:85
  312.4 2.1 bitcast_add_fusion.1
  314.6 2.7 collective-permute-start.11
  317.3 9.4 %collective-permute-done.13 = f32[256,4,256]{2,0,1:T(8,128)} collective-permute-done((f32[256,4,256]{2,0,1:T(8,128)}, f32[256,4,256]{2,0,1:T(8,128)}, u32[]{:S(2)}, u32[]{:S(2)}) %collective-permute-start.13) | collective-permute-done | bytes 1048608 | tf_op jit(solution)/shard_map/ppermute | solution.py:85
  326.7 1.4 bitcast_add_fusion
  330.1 2.6 collective-permute-start.14
  332.8 17.1 %collective-permute-start.12 = (f32[256,1,256]{2,0,1:T(8,128)S(1)}, f32[256,1,256]{2,0,1:T(8,128)S(1)}, u32[]{:S(2)}, u32[]{:S(2)}) collective-permute-start(f32[256,1,256]{2,0,1:T(8,128)S(1)} %select_bitcast_fusion.6), channel_id=1, source_target_pairs={{0,4},{1,5},{2,6},{3,7},{4,0},{5,1},{6,2},{7,3},{8,12},{9,13},{10,... | collective-permute-start | bytes 786440 | tf_op jit(solution)/shard_map/ppermute | solution.py:85
  350.0 1.1 fusion.46
  351.2 7.4 %collective-permute-start.15 = (f32[256,1,256]{2,0,1:T(8,128)S(1)}, f32[256,1,256]{2,0,1:T(8,128)S(1)}, u32[]{:S(2)}, u32[]{:S(2)}) collective-permute-start(f32[256,1,256]{2,0,1:T(8,128)S(1)} %select_bitcast_fusion.4), channel_id=1, source_target_pairs={{0,4},{1,5},{2,6},{3,7},{4,0},{5,1},{6,2},{7,3},{8,12},{9,13},{10,... | collective-permute-start | bytes 786440 | tf_op jit(solution)/shard_map/ppermute | solution.py:85
  359.2 8.1 %collective-permute-done.15 = f32[256,1,256]{2,0,1:T(8,128)S(1)} collective-permute-done((f32[256,1,256]{2,0,1:T(8,128)S(1)}, f32[256,1,256]{2,0,1:T(8,128)S(1)}, u32[]{:S(2)}, u32[]{:S(2)}) %collective-permute-start.15) | collective-permute-done | bytes 262176 | tf_op jit(solution)/shard_map/ppermute | solution.py:85
  (180 shorter events, 34.2 us)
Async XLA Ops:
  7.2 132.0 %all-gather.2.cloned.1.call-start = ((), (), s32[]{:S(2)}) async-start(), calls=%async_computation | async-start | bytes 5857280 | tf_op jit(solution)/shard_map/all_gather | solution.py:202
  11.3 16.8 %collective-permute-start = (bf16[256,512]{1,0:T(8,128)(2,1)S(1)}, bf16[256,512]{1,0:T(8,128)(2,1)S(1)}, u32[]{:S(2)}, u32[]{:S(2)}) collective-permute-start(bf16[256,512]{1,0:T(8,128)(2,1)S(1)} %constant_dynamic-update-slice_fusion), channel_id=1, source_target_pairs={{0,4},{1,5},{2,6},{3,7},{4,0},{5,1},{6,2},{7,3},{8,12},{9,13},{10,... | collective-permute-start | bytes 786440 | tf_op jit(solution)/shard_map/ppermute | solution.py:180
  28.3 11.4 %collective-permute-start.1 = (bf16[512,512]{1,0:T(8,128)(2,1)S(1)}, bf16[512,512]{1,0:T(8,128)(2,1)S(1)}, u32[]{:S(2)}, u32[]{:S(2)}) collective-permute-start(bf16[512,512]{1,0:T(8,128)(2,1)S(1)} %maximum_select_fusion.2), channel_id=1, source_target_pairs={{0,2},{1,3},{2,0},{3,1},{4,6},{5,7},{6,4},{7,5},{8,10},{9,11},{10,... | collective-permute-start | bytes 1572872 | tf_op jit(solution)/shard_map/ppermute | solution.py:180
  40.2 26.0 %collective-permute-start.2 = (bf16[1024,512]{1,0:T(8,128)(2,1)S(1)}, bf16[1024,512]{1,0:T(8,128)(2,1)S(1)}, u32[]{:S(2)}, u32[]{:S(2)}) collective-permute-start(bf16[1024,512]{1,0:T(8,128)(2,1)S(1)} %maximum_select_fusion.1), channel_id=1, source_target_pairs={{0,1},{1,0},{2,3},{3,2},{4,5},{5,4},{6,7},{7,6},{8,9},{9,8},{10,11... | collective-permute-start | bytes 3145736 | tf_op jit(solution)/shard_map/ppermute | solution.py:180
  66.9 78.5 %copy-start.6 = (bf16[2,2,2,256,512]{4,3,2,1,0:T(8,128)(2,1)}, bf16[2,2,2,256,512]{4,3,2,1,0:T(8,128)(2,1)S(1)}, u32[]{:S(2)}) copy-start(bf16[2,2,2,256,512]{4,3,2,1,0:T(8,128)(2,1)S(1)} %copy.125) | copy-start | bytes 6291460
  140.5 4.5 %copy-start.1 = (bf16[2048,1288]{1,0:T(8,128)(2,1)S(1)}, bf16[2048,1288]{1,0:T(8,128)(2,1)}, u32[]{:S(2)}) copy-start(bf16[2048,1288]{1,0:T(8,128)(2,1)} %all-gather.2.cloned.1.call-done) | copy-start | bytes 15826948
  145.7 3.6 copy-start.23
  145.7 3.6 copy-start.28
  145.7 14.5 %slice-start = ((s8[5767168]{0:T(1024)(128)(4,1)}), s8[1572864]{0:T(1024)(128)(4,1)S(1)}, s32[]{:S(2)}) async-start(s8[5767168]{0:T(1024)(128)(4,1)} %bitcast.295), calls=%async_computation.1 | async-start | bytes 3145728
  148.3 1.0 copy-start.15
  149.5 5.6 %copy-start.26 = (f32[8]{0:T(128)}, f32[8]{0:T(128)S(1)}, u32[]{:S(2)}) copy-start(f32[8]{0:T(128)S(1)} %get-tuple-element.201) | copy-start | bytes 100
  150.1 1.0 copy-start.16
  150.3 0.6 copy-start.21
  150.4 12.3 %copy-start.18 = (f32[256,8]{0,1:T(8,128)}, f32[256,8]{0,1:T(8,128)S(1)}, u32[]{:S(2)}) copy-start(f32[256,8]{0,1:T(8,128)S(1)} %get-tuple-element.199) | copy-start | bytes 24580
  151.2 1.0 copy-start.11
  152.1 10.5 %copy-start.13 = (f32[256,128]{1,0:T(8,128)}, f32[256,128]{1,0:T(8,128)S(1)}, u32[]{:S(2)}) copy-start(f32[256,128]{1,0:T(8,128)S(1)} %copy.136) | copy-start | bytes 393220
  152.2 8.0 %slice-start.1 = ((s8[5767168]{0:T(1024)(128)(4,1)}), s8[4194304]{0:T(1024)(128)(4,1)S(1)}, s32[]{:S(2)}) async-start(s8[5767168]{0:T(1024)(128)(4,1)} %bitcast.295), calls=%async_computation.2 | async-start | bytes 8388608
  162.6 6.6 %copy-start.27 = (f32[8]{0:T(128)S(1)}, f32[8]{0:T(128)}, u32[]{:S(2)}) copy-start(f32[8]{0:T(128)} %copy-done.26) | copy-start | bytes 100
  165.2 4.0 %collective-permute-start.3 = (f32[8,16512]{1,0:T(8,128)}, f32[8,16512]{1,0:T(8,128)S(1)}, u32[]{:S(2)}, u32[]{:S(2)}) collective-permute-start(f32[8,16512]{1,0:T(8,128)} %pad_maximum_fusion), channel_id=1, source_target_pairs={{0,8},{8,0},{16,24},{24,16},{32,40},{40,32},{48,56},{56,48},{64,72... | collective-permute-start | bytes 1585160 | tf_op jit(solution)/shard_map/ppermute | solution.py:23
  170.4 55.1 %copy-start.30 = (s32[8]{0:T(128)S(1)}, s32[8]{0:T(128)}, u32[]{:S(2)}) copy-start(s32[8]{0:T(128)} %constant.154) | copy-start | bytes 100
  170.4 55.7 %copy-start.29 = (f32[8]{0:T(128)S(1)}, f32[8]{0:T(128)}, u32[]{:S(2)}) copy-start(f32[8]{0:T(128)} %param.17) | copy-start | bytes 100
  170.4 10.0 %collective-permute-start.4 = (f32[8,8320]{1,0:T(8,128)}, f32[8,8320]{1,0:T(8,128)S(1)}, u32[]{:S(2)}, u32[]{:S(2)}) collective-permute-start(f32[8,8320]{1,0:T(8,128)} %pad_maximum_fusion.1), channel_id=1, source_target_pairs={{0,16},{8,24},{16,0},{24,8},{32,48},{40,56},{48,32},{56,40},{64,80... | collective-permute-start | bytes 798728 | tf_op jit(solution)/shard_map/ppermute | solution.py:41
  181.4 16.2 %collective-permute-start.5 = (f32[8,8320]{1,0:T(8,128)}, f32[8,8320]{1,0:T(8,128)}, u32[]{:S(2)}, u32[]{:S(2)}) collective-permute-start(f32[8,8320]{1,0:T(8,128)} %pad_maximum_fusion.2), channel_id=1, source_target_pairs={{0,32},{8,40},{16,48},{24,56},{32,0},{40,8},{48,16},{56,24},{64,96... | collective-permute-start | bytes 798728 | tf_op jit(solution)/shard_map/ppermute | solution.py:41
  198.4 38.9 %copy-start.12 = (bf16[256,256]{0,1:T(8,128)(2,1)S(1)}, bf16[256,256]{0,1:T(8,128)(2,1)}, u32[]{:S(2)}) copy-start(bf16[256,256]{0,1:T(8,128)(2,1)} %copy-done.11) | copy-start | bytes 393220
  200.3 15.8 %collective-permute-start.6 = (f32[8,8320]{1,0:T(8,128)}, f32[8,8320]{1,0:T(8,128)}, u32[]{:S(2)}, u32[]{:S(2)}) collective-permute-start(f32[8,8320]{1,0:T(8,128)} %pad_maximum_fusion.3), channel_id=1, source_target_pairs={{0,64},{8,72},{16,80},{24,88},{32,96},{40,104},{48,112},{56,120},{... | collective-permute-start | bytes 798728 | tf_op jit(solution)/shard_map/ppermute | solution.py:41
  217.9 35.6 %copy-start.17 = (f32[8,2,128]{2,0,1:T(8,128)S(1)}, f32[8,2,128]{2,0,1:T(8,128)}, u32[]{:S(2)}) copy-start(f32[8,2,128]{2,0,1:T(8,128)} %copy-done.16) | copy-start | bytes 24580
  217.9 35.6 %copy-start.22 = (f32[8,2]{0,1:T(2,128)S(1)}, f32[8,2]{0,1:T(2,128)}, u32[]{:S(2)}) copy-start(f32[8,2]{0,1:T(2,128)} %copy-done.21) | copy-start | bytes 196
  218.7 11.9 %collective-permute-start.7 = (f32[8,8320]{1,0:T(8,128)}, f32[8,8320]{1,0:T(8,128)}, u32[]{:S(2)}, u32[]{:S(2)}) collective-permute-start(f32[8,8320]{1,0:T(8,128)} %pad_maximum_fusion.4), channel_id=1, source_target_pairs={{0,128},{8,136},{16,144},{24,152},{32,160},{40,168},{48,176},{56,1... | collective-permute-start | bytes 798728 | tf_op jit(solution)/shard_map/ppermute | solution.py:41
  232.6 16.8 %collective-permute-start.8 = (f32[8,8320]{1,0:T(8,128)S(1)}, f32[8,8320]{1,0:T(8,128)S(1)}, u32[]{:S(2)}, u32[]{:S(2)}) collective-permute-start(f32[8,8320]{1,0:T(8,128)S(1)} %pad_maximum_fusion.5), channel_id=1, source_target_pairs={{0,256},{8,264},{16,272},{24,280},{32,288},{40,296},{48,304},{56,3... | collective-permute-start | bytes 798728 | tf_op jit(solution)/shard_map/ppermute | solution.py:41
  250.6 6.3 %collective-permute-start.9 = (f32[8,8192]{1,0:T(8,128)S(1)}, f32[8,8192]{1,0:T(8,128)S(1)}, u32[]{:S(2)}, u32[]{:S(2)}) collective-permute-start(f32[8,8192]{1,0:T(8,128)S(1)} %add_select_fusion), channel_id=1, source_target_pairs={{0,8},{8,0},{16,24},{24,16},{32,40},{40,32},{48,56},{56,48},{64,72... | collective-permute-start | bytes 786440 | tf_op jit(solution)/shard_map/ppermute | solution.py:50
  253.6 3.7 copy-start.24
  253.6 4.8 %copy-start.14 = (f32[256,128]{1,0:T(8,128)S(1)}, f32[256,128]{1,0:T(8,128)}, u32[]{:S(2)}) copy-start(f32[256,128]{1,0:T(8,128)} %copy-done.13) | copy-start | bytes 393220
  253.6 4.8 %copy-start.19 = (f32[256,8]{0,1:T(8,128)S(1)}, f32[256,8]{0,1:T(8,128)}, u32[]{:S(2)}) copy-start(f32[256,8]{0,1:T(8,128)} %copy-done.18) | copy-start | bytes 24580
  256.9 4.3 %copy-start.9 = (f32[256,1,128]{0,2,1:T(8,128)S(1)}, f32[256,1,128]{0,2,1:T(8,128)}, u32[]{:S(2)}) copy-start(f32[256,1,128]{0,2,1:T(8,128)} %get-tuple-element.186) | copy-start | bytes 393220
  258.1 5.1 %copy-start.10 = (f32[256,1,128]{0,2,1:T(8,128)S(1)}, f32[256,1,128]{0,2,1:T(8,128)}, u32[]{:S(2)}) copy-start(f32[256,1,128]{0,2,1:T(8,128)} %get-tuple-element.184) | copy-start | bytes 393220
  261.3 4.2 %copy-start.20 = (pred[1,256,256]{2,1,0:T(8,128)(4,1)S(1)}, pred[1,256,256]{2,1,0:T(8,128)(4,1)}, u32[]{:S(2)}) copy-start(pred[1,256,256]{2,1,0:T(8,128)(4,1)} %iota_compare_fusion) | copy-start | bytes 196612
  268.6 6.3 %copy-start.25 = (f32[8]{0:T(128)S(1)}, f32[8]{0:T(128)}, u32[]{:S(2)}) copy-start(f32[8]{0:T(128)} %param.16) | copy-start | bytes 100
  283.0 2.3 slice-start.2
  292.0 7.0 %copy-start.8 = (f32[8,256,256]{2,1,0:T(8,128)S(1)}, f32[8,256,256]{2,1,0:T(8,128)}, u32[]{:S(2)}) copy-start(f32[8,256,256]{2,1,0:T(8,128)} %gather_fusion.1) | copy-start | bytes 6291460
  294.0 5.6 %copy-start = (f32[256,8,256]{2,0,1:T(8,128)}, f32[256,8,256]{2,0,1:T(8,128)S(1)}, u32[]{:S(2)}) copy-start(f32[256,8,256]{2,0,1:T(8,128)S(1)} %bitcast_select_fusion) | copy-start | bytes 6291460
  294.0 4.9 %copy-start.7 = (f32[256,4,2,256]{3,2,1,0:T(2,128)S(1)}, f32[256,4,2,256]{3,2,1,0:T(2,128)}, u32[]{:S(2)}) copy-start(f32[256,4,2,256]{3,2,1,0:T(2,128)} %reshape.520) | copy-start | bytes 6291460
  295.2 17.2 %collective-permute-start.10 = (f32[256,4,256]{2,0,1:T(8,128)}, f32[256,4,256]{2,0,1:T(8,128)}, u32[]{:S(2)}, u32[]{:S(2)}) collective-permute-start(f32[256,4,256]{2,0,1:T(8,128)} %select_bitcast_fusion.1), channel_id=1, source_target_pairs={{0,1},{1,0},{2,3},{3,2},{4,5},{5,4},{6,7},{7,6},{8,11},{9,10},{10,... | collective-permute-start | bytes 3145736 | tf_op jit(solution)/shard_map/ppermute | solution.py:85
  300.7 26.0 %collective-permute-start.13 = (f32[256,4,256]{2,0,1:T(8,128)}, f32[256,4,256]{2,0,1:T(8,128)}, u32[]{:S(2)}, u32[]{:S(2)}) collective-permute-start(f32[256,4,256]{2,0,1:T(8,128)} %select_bitcast_fusion), channel_id=1, source_target_pairs={{0,1},{1,0},{2,3},{3,2},{4,5},{5,4},{6,7},{7,6},{8,11},{9,10},{10,... | collective-permute-start | bytes 3145736 | tf_op jit(solution)/shard_map/ppermute | solution.py:85
  314.5 2.8 copy-start.4
  314.6 18.1 %collective-permute-start.11 = (f32[256,2,256]{2,0,1:T(8,128)S(1)}, f32[256,2,256]{2,0,1:T(8,128)S(1)}, u32[]{:S(2)}, u32[]{:S(2)}) collective-permute-start(f32[256,2,256]{2,0,1:T(8,128)S(1)} %select_bitcast_fusion.3), channel_id=1, source_target_pairs={{0,2},{1,3},{2,0},{3,1},{4,6},{5,7},{6,4},{7,5},{8,10},{9,11},{10,... | collective-permute-start | bytes 1572872 | tf_op jit(solution)/shard_map/ppermute | solution.py:85
  328.2 1.0 copy-start.2
  328.2 4.5 %copy-start.5 = (f32[256,4,256]{2,0,1:T(8,128)S(1)}, f32[256,4,256]{2,0,1:T(8,128)}, u32[]{:S(2)}) copy-start(f32[256,4,256]{2,0,1:T(8,128)} %copy-done.4) | copy-start | bytes 3145732
  330.1 19.9 %copy-start.3 = (f32[256,4,256]{2,0,1:T(8,128)S(1)}, f32[256,4,256]{2,0,1:T(8,128)}, u32[]{:S(2)}) copy-start(f32[256,4,256]{2,0,1:T(8,128)} %copy-done.2) | copy-start | bytes 3145732
  330.1 19.9 %collective-permute-start.14 = (f32[256,2,256]{2,0,1:T(8,128)}, f32[256,2,256]{2,0,1:T(8,128)}, u32[]{:S(2)}, u32[]{:S(2)}) collective-permute-start(f32[256,2,256]{2,0,1:T(8,128)} %select_bitcast_fusion.2), channel_id=1, source_target_pairs={{0,2},{1,3},{2,0},{3,1},{4,6},{5,7},{6,4},{7,5},{8,10},{9,11},{10,... | collective-permute-start | bytes 1572872 | tf_op jit(solution)/shard_map/ppermute | solution.py:85
  332.8 25.7 %collective-permute-start.12 = (f32[256,1,256]{2,0,1:T(8,128)S(1)}, f32[256,1,256]{2,0,1:T(8,128)S(1)}, u32[]{:S(2)}, u32[]{:S(2)}) collective-permute-start(f32[256,1,256]{2,0,1:T(8,128)S(1)} %select_bitcast_fusion.6), channel_id=1, source_target_pairs={{0,4},{1,5},{2,6},{3,7},{4,0},{5,1},{6,2},{7,3},{8,12},{9,13},{10,... | collective-permute-start | bytes 786440 | tf_op jit(solution)/shard_map/ppermute | solution.py:85
  351.2 16.2 %collective-permute-start.15 = (f32[256,1,256]{2,0,1:T(8,128)S(1)}, f32[256,1,256]{2,0,1:T(8,128)S(1)}, u32[]{:S(2)}, u32[]{:S(2)}) collective-permute-start(f32[256,1,256]{2,0,1:T(8,128)S(1)} %select_bitcast_fusion.4), channel_id=1, source_target_pairs={{0,4},{1,5},{2,6},{3,7},{4,0},{5,1},{6,2},{7,3},{8,12},{9,13},{10,... | collective-permute-start | bytes 786440 | tf_op jit(solution)/shard_map/ppermute | solution.py:85
Sparse Core Ops, SparseCore 0:
  10.7 128.4 all-gather.1

commit v10 on v9

--- a/solution.py
+++ b/solution.py
@@ -66,10 +66,10 @@
 
     turn = chain % 2
     mine_label = label(position, turn)
-    order = [place(lab, 1) for lab in range(devices)]
     rows = partial.shape[0]
-    blocks = partial.reshape(rows, devices, width)
-    blocks = jnp.where(turn == 1, blocks[:, order], blocks)
+    grouped = partial.reshape(rows, devices // ring, ring, width)
+    rolled = jnp.concatenate([grouped[:, :, ring - 1 :], grouped[:, :, : ring - 1]], axis=2)
+    blocks = jnp.where(turn == 1, rolled, grouped).reshape(rows, devices, width)
     bit = 1
     while bit < devices:
         count = blocks.shape[1]

time: 377 us -> 379 us (level)
  starting transfers between devices: 85 us -> 78 us
    ppermute x6, starting transfers between devices: 36.4 us -> 29.4 us  [scattered_sum(): blocks = keep + lax.ppermute(send, (rows_axis, axis), pairs)]
    gather x2 -> x0, local copies, waits for them, and re-layouts: 5.85 us -> none  [scattered_sum(): blocks = jnp.where(turn == 1, blocks[:, order], blocks)]
    unnamed x73 -> x103, local copies, waits for them, and re-layouts: 4.7 us -> 8.2 us
  transfers between devices with their start and end apart: 17 -> 17, of which waited for: 13 -> 14; matrix products, arithmetic and copies ran while one was open for 5% -> 5% of each run, Pallas kernels for 0% -> 0%
where the time goes in v10:
time: 379 us; the launch traced here: 374 us
  waiting for transfers between devices  181 us (48%)
  starting transfers between devices  78 us (21%)
  matrix products  43.7 us (12%)
  other arithmetic  33.7 us (9%)
  local copies, waits for them, and re-layouts  22.4 us (6%)
  between operations  15.3 us (4%)
    all_gather x1, waiting for transfers between devices, per_device(): lax.all_gather(jnp.concatenate([w_out.T, w_in, w_bc, w_dt], axis=1), 'ctx...  72.3 us
    ppermute x5, waiting for transfers between devices, both_carries(): got = lax.ppermute(message, axis, [(i, i ^ bit) for i in range(devices)])  43.7 us
    ppermute x3, waiting for transfers between devices, doubled_rows(): other = lax.ppermute(x, axis, [(i, i ^ bit) for i in range(devices)])  36 us
    ppermute x6, starting transfers between devices, scattered_sum(): blocks = keep + lax.ppermute(send, (rows_axis, axis), pairs)  29.4 us
    ppermute x6, waiting for transfers between devices, scattered_sum(): blocks = keep + lax.ppermute(send, (rows_axis, axis), pairs)  26.9 us
    ppermute x5, starting transfers between devices, both_carries(): got = lax.ppermute(message, axis, [(i, i ^ bit) for i in range(devices)])  25.5 us
    ppermute x3, starting transfers between devices, doubled_rows(): other = lax.ppermute(x, axis, [(i, i ^ bit) for i in range(devices)])  18.1 us
    dot_general x3, matrix products, ssd_advance(): inside = jnp.einsum('hts,shp->thp', scores * weight, inputs, precision=HIGH)  10.5 us
  transfers between devices with their start and end apart: 17, of which 14 were waited for; matrix products, arithmetic and copies ran while one was open for 5% of the time, Pallas kernels for 0%

profile of v10, /device:TPU:1, one launch (start us, length us, event | category | flops | bytes accessed | tf_op | source)
XLA Modules:
  0.0 373.9 jit_solution(13103040953425204161)
XLA Ops:
  8.0 1.4 pad_maximum_fusion.8
  11.3 8.3 %collective-permute-start = (bf16[256,512]{1,0:T(8,128)(2,1)S(1)}, bf16[256,512]{1,0:T(8,128)(2,1)S(1)}, u32[]{:S(2)}, u32[]{:S(2)}) collective-permute-start(bf16[256,512]{1,0:T(8,128)(2,1)S(1)} %constant_dynamic-update-slice_fusion), channel_id=1, source_target_pairs={{0,4},{1,5},{2,6},{3,7},{4,0},{5,1},{6,2},{7,3},{8,12},{9,13},{10,... | collective-permute-start | bytes 786440 | tf_op jit(solution)/shard_map/ppermute | solution.py:180
  19.6 8.5 %collective-permute-done = bf16[256,512]{1,0:T(8,128)(2,1)S(1)} collective-permute-done((bf16[256,512]{1,0:T(8,128)(2,1)S(1)}, bf16[256,512]{1,0:T(8,128)(2,1)S(1)}, u32[]{:S(2)}, u32[]{:S(2)}) %collective-permute-start) | collective-permute-done | bytes 262176 | tf_op jit(solution)/shard_map/ppermute | solution.py:180
  28.3 3.7 collective-permute-start.1
  32.0 7.7 %collective-permute-done.1 = bf16[512,512]{1,0:T(8,128)(2,1)S(1)} collective-permute-done((bf16[512,512]{1,0:T(8,128)(2,1)S(1)}, bf16[512,512]{1,0:T(8,128)(2,1)S(1)}, u32[]{:S(2)}, u32[]{:S(2)}) %collective-permute-start.1) | collective-permute-done | bytes 524320 | tf_op jit(solution)/shard_map/ppermute | solution.py:180
  40.2 6.1 %collective-permute-start.2 = (bf16[1024,512]{1,0:T(8,128)(2,1)S(1)}, bf16[1024,512]{1,0:T(8,128)(2,1)S(1)}, u32[]{:S(2)}, u32[]{:S(2)}) collective-permute-start(bf16[1024,512]{1,0:T(8,128)(2,1)S(1)} %maximum_select_fusion.2), channel_id=1, source_target_pairs={{0,1},{1,0},{2,3},{3,2},{4,5},{5,4},{6,7},{7,6},{8,9},{9,8},{10,11... | collective-permute-start | bytes 3145736 | tf_op jit(solution)/shard_map/ppermute | solution.py:180
  46.3 19.8 %collective-permute-done.2 = bf16[1024,512]{1,0:T(8,128)(2,1)S(1)} collective-permute-done((bf16[1024,512]{1,0:T(8,128)(2,1)S(1)}, bf16[1024,512]{1,0:T(8,128)(2,1)S(1)}, u32[]{:S(2)}, u32[]{:S(2)}) %collective-permute-start.2) | collective-permute-done | bytes 1048608 | tf_op jit(solution)/shard_map/ppermute | solution.py:180
  66.9 72.3 %all-gather.2.cloned.1.call-done = bf16[2048,1288]{1,0:T(8,128)(2,1)} async-done(((bf16[32,1288]{1,0:T(8,128)(2,1)}), bf16[2048,1288]{1,0:T(8,128)(2,1)}) %all-gather.2.cloned.1.call-update) | async-done | bytes 5275664 | tf_op jit(solution)/shard_map/all_gather | solution.py:202
  139.2 1.3 fusion.72
  140.5 1.5 convolution_add_fusion.6
  142.0 1.7 convolution_add_fusion.5
  143.7 1.3 convolution_add_fusion.4
  145.7 1.3 convolution_add_fusion.1
  147.1 1.2 fusion.145
  152.3 1.4 fusion.86
  153.8 1.3 convolution_add_fusion.13
  155.1 1.3 convolution_add_fusion.12
  156.4 1.3 convolution_add_fusion.11
  157.7 1.3 convolution_add_fusion.10
  159.0 1.3 convolution_add_fusion.9
  160.4 1.2 convolution_add_fusion.8
  161.5 1.2 convolution_add_fusion.7
  165.3 2.1 collective-permute-start.3
  167.5 1.8 collective-permute-done.3
  170.5 3.1 collective-permute-start.4
  173.7 6.9 %collective-permute-done.4 = f32[8,8320]{1,0:T(8,128)} collective-permute-done((f32[8,8320]{1,0:T(8,128)}, f32[8,8320]{1,0:T(8,128)}, u32[]{:S(2)}, u32[]{:S(2)}) %collective-permute-start.4) | collective-permute-done | bytes 266272 | tf_op jit(solution)/shard_map/ppermute | solution.py:41
  183.3 3.9 %collective-permute-start.5 = (f32[8,8320]{1,0:T(8,128)}, f32[8,8320]{1,0:T(8,128)}, u32[]{:S(2)}, u32[]{:S(2)}) collective-permute-start(f32[8,8320]{1,0:T(8,128)} %pad_maximum_fusion.3), channel_id=1, source_target_pairs={{0,32},{8,40},{16,48},{24,56},{32,0},{40,8},{48,16},{56,24},{64,96... | collective-permute-start | bytes 798728 | tf_op jit(solution)/shard_map/ppermute | solution.py:41
  187.2 12.3 %collective-permute-done.5 = f32[8,8320]{1,0:T(8,128)} collective-permute-done((f32[8,8320]{1,0:T(8,128)}, f32[8,8320]{1,0:T(8,128)}, u32[]{:S(2)}, u32[]{:S(2)}) %collective-permute-start.5) | collective-permute-done | bytes 266272 | tf_op jit(solution)/shard_map/ppermute | solution.py:41
  202.2 6.8 %collective-permute-start.6 = (f32[8,8320]{1,0:T(8,128)}, f32[8,8320]{1,0:T(8,128)}, u32[]{:S(2)}, u32[]{:S(2)}) collective-permute-start(f32[8,8320]{1,0:T(8,128)} %pad_maximum_fusion.4), channel_id=1, source_target_pairs={{0,64},{8,72},{16,80},{24,88},{32,96},{40,104},{48,112},{56,120},{... | collective-permute-start | bytes 798728 | tf_op jit(solution)/shard_map/ppermute | solution.py:41
  209.0 9.0 %collective-permute-done.6 = f32[8,8320]{1,0:T(8,128)} collective-permute-done((f32[8,8320]{1,0:T(8,128)}, f32[8,8320]{1,0:T(8,128)}, u32[]{:S(2)}, u32[]{:S(2)}) %collective-permute-start.6) | collective-permute-done | bytes 266272 | tf_op jit(solution)/shard_map/ppermute | solution.py:41
  220.6 6.8 %collective-permute-start.7 = (f32[8,8320]{1,0:T(8,128)}, f32[8,8320]{1,0:T(8,128)}, u32[]{:S(2)}, u32[]{:S(2)}) collective-permute-start(f32[8,8320]{1,0:T(8,128)} %pad_maximum_fusion.5), channel_id=1, source_target_pairs={{0,128},{8,136},{16,144},{24,152},{32,160},{40,168},{48,176},{56,1... | collective-permute-start | bytes 798728 | tf_op jit(solution)/shard_map/ppermute | solution.py:41
  228.8 3.7 collective-permute-done.7
  234.5 4.8 %collective-permute-start.8 = (f32[8,8320]{1,0:T(8,128)S(1)}, f32[8,8320]{1,0:T(8,128)S(1)}, u32[]{:S(2)}, u32[]{:S(2)}) collective-permute-start(f32[8,8320]{1,0:T(8,128)S(1)} %pad_maximum_fusion.6), channel_id=1, source_target_pairs={{0,256},{8,264},{16,272},{24,280},{32,288},{40,296},{48,304},{56,3... | collective-permute-start | bytes 798728 | tf_op jit(solution)/shard_map/ppermute | solution.py:41
  239.5 11.9 %collective-permute-done.8 = f32[8,8320]{1,0:T(8,128)S(1)} collective-permute-done((f32[8,8320]{1,0:T(8,128)S(1)}, f32[8,8320]{1,0:T(8,128)S(1)}, u32[]{:S(2)}, u32[]{:S(2)}) %collective-permute-start.8) | collective-permute-done | bytes 266272 | tf_op jit(solution)/shard_map/ppermute | solution.py:41
  251.4 1.4 add_select_fusion
  252.7 2.8 collective-permute-start.9
  255.7 3.3 fusion.12
  261.7 2.2 fusion.20
  265.2 1.2 convolution_bitcast_fusion.1
  266.8 2.0 convolution_bitcast_fusion.4
  268.8 4.6 %fusion.22 = (f32[8,256]{1,0:T(8,128)}, f32[8,256]{1,0:T(8,128)}, f32[256,256]{1,0:T(8,128)}) fusion(f32[8,256]{1,0:T(8,128)} %add_bitcast_fusion.1, f32[256,256]{1,0:T(8,128)S(1)} %fusion.131, pred[256,256]{1,0:T(8,128)(4,1)} %bitcast.324, f32[256,8,64]{0,2,1:T(8,128)S(1)} %bitcast.317, f32[256,8]{0,1:T(8,128)S(1)} %get-tuple-element.181, ...), kind=kOutput, calls=%fused_computation.41 | convolution fusion | flops 408481792 | bytes 1671168 | tf_op jit(solution)/shard_map/transpose(jvp())/while/body/eval_jaxpr/checkpoint/hts,shp->thp/dot_general | solution.py:108
  273.4 2.6 multiply_reduce_fusion.1
  278.5 1.3 copy-done
  280.6 1.2 fusion.26
  282.9 2.7 reduce-window.44
  286.6 3.4 fusion
  290.1 1.3 copy-done.9
  291.4 2.4 reshape.514
  293.8 4.1 %reshape.515 = f32[256,4,2,256]{3,2,1,0:T(2,128)} reshape(f32[256,2048]{1,0:T(8,128)} %copy-done.9) | data formatting | bytes 4194304 | tf_op jit(solution)/shard_map/reshape | solution.py:70
  298.3 3.8 %collective-permute-start.10 = (f32[256,4,256]{2,0,1:T(8,128)S(1)}, f32[256,4,256]{2,0,1:T(8,128)}, u32[]{:S(2)}, u32[]{:S(2)}) collective-permute-start(f32[256,4,256]{2,0,1:T(8,128)S(1)} %select_bitcast_fusion.1), channel_id=1, source_target_pairs={{0,1},{1,0},{2,3},{3,2},{4,5},{5,4},{6,7},{7,6},{8,11},{9,10},{10,... | collective-permute-start | bytes 3145736 | tf_op jit(solution)/shard_map/ppermute | solution.py:85
  303.5 1.4 copy-done.8
  305.6 1.3 copy-done.3
  308.0 2.9 collective-permute-start.13
  310.9 4.5 %collective-permute-done.10 = f32[256,4,256]{2,0,1:T(8,128)} collective-permute-done((f32[256,4,256]{2,0,1:T(8,128)S(1)}, f32[256,4,256]{2,0,1:T(8,128)}, u32[]{:S(2)}, u32[]{:S(2)}) %collective-permute-start.10) | collective-permute-done | bytes 1048608 | tf_op jit(solution)/shard_map/ppermute | solution.py:85
  315.5 1.4 bitcast_add_fusion.1
  317.0 2.6 collective-permute-start.11
  319.6 10.8 %collective-permute-done.13 = f32[256,4,256]{2,0,1:T(8,128)} collective-permute-done((f32[256,4,256]{2,0,1:T(8,128)}, f32[256,4,256]{2,0,1:T(8,128)}, u32[]{:S(2)}, u32[]{:S(2)}) %collective-permute-start.13) | collective-permute-done | bytes 1048608 | tf_op jit(solution)/shard_map/ppermute | solution.py:85
  330.4 1.4 bitcast_add_fusion
  332.8 2.3 collective-permute-start.14
  335.3 9.0 %collective-permute-start.12 = (f32[256,1,256]{2,0,1:T(8,128)S(1)}, f32[256,1,256]{2,0,1:T(8,128)S(1)}, u32[]{:S(2)}, u32[]{:S(2)}) collective-permute-start(f32[256,1,256]{2,0,1:T(8,128)S(1)} %select_bitcast_fusion.6), channel_id=1, source_target_pairs={{0,4},{1,5},{2,6},{3,7},{4,0},{5,1},{6,2},{7,3},{8,12},{9,13},{10,... | collective-permute-start | bytes 786440 | tf_op jit(solution)/shard_map/ppermute | solution.py:85
  344.3 5.0 %collective-permute-done.14 = f32[256,2,256]{2,0,1:T(8,128)} collective-permute-done((f32[256,2,256]{2,0,1:T(8,128)}, f32[256,2,256]{2,0,1:T(8,128)}, u32[]{:S(2)}, u32[]{:S(2)}) %collective-permute-start.14) | collective-permute-done | bytes 524320 | tf_op jit(solution)/shard_map/ppermute | solution.py:85
  349.3 1.1 fusion.46
  350.5 8.7 %collective-permute-start.15 = (f32[256,1,256]{2,0,1:T(8,128)S(1)}, f32[256,1,256]{2,0,1:T(8,128)S(1)}, u32[]{:S(2)}, u32[]{:S(2)}) collective-permute-start(f32[256,1,256]{2,0,1:T(8,128)S(1)} %select_bitcast_fusion.4), channel_id=1, source_target_pairs={{0,4},{1,5},{2,6},{3,7},{4,0},{5,1},{6,2},{7,3},{8,12},{9,13},{10,... | collective-permute-start | bytes 786440 | tf_op jit(solution)/shard_map/ppermute | solution.py:85
  359.8 6.6 %collective-permute-done.15 = f32[256,1,256]{2,0,1:T(8,128)S(1)} collective-permute-done((f32[256,1,256]{2,0,1:T(8,128)S(1)}, f32[256,1,256]{2,0,1:T(8,128)S(1)}, u32[]{:S(2)}, u32[]{:S(2)}) %collective-permute-start.15) | collective-permute-done | bytes 262176 | tf_op jit(solution)/shard_map/ppermute | solution.py:85
  (213 shorter events, 39.4 us)
Async XLA Ops:
  7.2 132.0 %all-gather.2.cloned.1.call-start = ((), (), s32[]{:S(2)}) async-start(), calls=%async_computation | async-start | bytes 5857280 | tf_op jit(solution)/shard_map/all_gather | solution.py:202
  11.3 16.8 %collective-permute-start = (bf16[256,512]{1,0:T(8,128)(2,1)S(1)}, bf16[256,512]{1,0:T(8,128)(2,1)S(1)}, u32[]{:S(2)}, u32[]{:S(2)}) collective-permute-start(bf16[256,512]{1,0:T(8,128)(2,1)S(1)} %constant_dynamic-update-slice_fusion), channel_id=1, source_target_pairs={{0,4},{1,5},{2,6},{3,7},{4,0},{5,1},{6,2},{7,3},{8,12},{9,13},{10,... | collective-permute-start | bytes 786440 | tf_op jit(solution)/shard_map/ppermute | solution.py:180
  28.3 11.4 %collective-permute-start.1 = (bf16[512,512]{1,0:T(8,128)(2,1)S(1)}, bf16[512,512]{1,0:T(8,128)(2,1)S(1)}, u32[]{:S(2)}, u32[]{:S(2)}) collective-permute-start(bf16[512,512]{1,0:T(8,128)(2,1)S(1)} %maximum_select_fusion.3), channel_id=1, source_target_pairs={{0,2},{1,3},{2,0},{3,1},{4,6},{5,7},{6,4},{7,5},{8,10},{9,11},{10,... | collective-permute-start | bytes 1572872 | tf_op jit(solution)/shard_map/ppermute | solution.py:180
  40.2 26.0 %collective-permute-start.2 = (bf16[1024,512]{1,0:T(8,128)(2,1)S(1)}, bf16[1024,512]{1,0:T(8,128)(2,1)S(1)}, u32[]{:S(2)}, u32[]{:S(2)}) collective-permute-start(bf16[1024,512]{1,0:T(8,128)(2,1)S(1)} %maximum_select_fusion.2), channel_id=1, source_target_pairs={{0,1},{1,0},{2,3},{3,2},{4,5},{5,4},{6,7},{7,6},{8,9},{9,8},{10,11... | collective-permute-start | bytes 3145736 | tf_op jit(solution)/shard_map/ppermute | solution.py:180
  66.9 78.5 %copy-start.7 = (bf16[2,2,2,256,512]{4,3,2,1,0:T(8,128)(2,1)}, bf16[2,2,2,256,512]{4,3,2,1,0:T(8,128)(2,1)S(1)}, u32[]{:S(2)}) copy-start(bf16[2,2,2,256,512]{4,3,2,1,0:T(8,128)(2,1)S(1)} %copy.125) | copy-start | bytes 6291460
  140.5 4.5 %copy-start.5 = (bf16[2048,1288]{1,0:T(8,128)(2,1)S(1)}, bf16[2048,1288]{1,0:T(8,128)(2,1)}, u32[]{:S(2)}) copy-start(bf16[2048,1288]{1,0:T(8,128)(2,1)} %all-gather.2.cloned.1.call-done) | copy-start | bytes 15826948
  145.7 2.6 copy-start.28
  145.7 2.6 copy-start.41
  145.7 14.6 %slice-start.2 = ((s8[5767168]{0:T(1024)(128)(4,1)}), s8[1572864]{0:T(1024)(128)(4,1)S(1)}, s32[]{:S(2)}) async-start(s8[5767168]{0:T(1024)(128)(4,1)} %bitcast.288), calls=%async_computation.3 | async-start | bytes 3145728
  148.3 3.1 copy-start.15
  148.5 3.5 copy-start.38
  149.2 2.9 copy-start.19
  152.2 10.6 %copy-start.12 = (f32[256,128]{1,0:T(8,128)}, f32[256,128]{1,0:T(8,128)S(1)}, u32[]{:S(2)}) copy-start(f32[256,128]{1,0:T(8,128)S(1)} %copy.136) | copy-start | bytes 393220
  152.3 8.0 %slice-start.3 = ((s8[5767168]{0:T(1024)(128)(4,1)}), s8[4194304]{0:T(1024)(128)(4,1)S(1)}, s32[]{:S(2)}) async-start(s8[5767168]{0:T(1024)(128)(4,1)} %bitcast.288), calls=%async_computation.4 | async-start | bytes 8388608
  159.0 3.8 %copy-start.21 = (f32[256,8]{0,1:T(8,128)S(1)}, f32[256,8]{0,1:T(8,128)}, u32[]{:S(2)}) copy-start(f32[256,8]{0,1:T(8,128)} %get-tuple-element.199) | copy-start | bytes 24580
  159.0 3.8 %copy-start.40 = (f32[8]{0:T(128)S(1)}, f32[8]{0:T(128)}, u32[]{:S(2)}) copy-start(f32[8]{0:T(128)} %exponential_multiply_fusion.2) | copy-start | bytes 100
  160.3 3.1 copy-start.25
  161.5 2.8 copy-start.44
  162.7 6.7 %copy-start.39 = (f32[8]{0:T(128)S(1)}, f32[8]{0:T(128)}, u32[]{:S(2)}) copy-start(f32[8]{0:T(128)} %copy-done.38) | copy-start | bytes 100
  165.3 4.0 %collective-permute-start.3 = (f32[8,16512]{1,0:T(8,128)}, f32[8,16512]{1,0:T(8,128)S(1)}, u32[]{:S(2)}, u32[]{:S(2)}) collective-permute-start(f32[8,16512]{1,0:T(8,128)} %pad_maximum_fusion.1), channel_id=1, source_target_pairs={{0,8},{8,0},{16,24},{24,16},{32,40},{40,32},{48,56},{56,48},{64,72... | collective-permute-start | bytes 1585160 | tf_op jit(solution)/shard_map/ppermute | solution.py:23
  170.5 56.9 %copy-start.43 = (f32[8]{0:T(128)S(1)}, f32[8]{0:T(128)}, u32[]{:S(2)}) copy-start(f32[8]{0:T(128)} %param.15) | copy-start | bytes 100
  170.5 10.1 %collective-permute-start.4 = (f32[8,8320]{1,0:T(8,128)}, f32[8,8320]{1,0:T(8,128)}, u32[]{:S(2)}, u32[]{:S(2)}) collective-permute-start(f32[8,8320]{1,0:T(8,128)} %pad_maximum_fusion.2), channel_id=1, source_target_pairs={{0,16},{8,24},{16,0},{24,8},{32,48},{40,56},{48,32},{56,40},{64,80... | collective-permute-start | bytes 798728 | tf_op jit(solution)/shard_map/ppermute | solution.py:41
  183.3 16.2 %collective-permute-start.5 = (f32[8,8320]{1,0:T(8,128)}, f32[8,8320]{1,0:T(8,128)}, u32[]{:S(2)}, u32[]{:S(2)}) collective-permute-start(f32[8,8320]{1,0:T(8,128)} %pad_maximum_fusion.3), channel_id=1, source_target_pairs={{0,32},{8,40},{16,48},{24,56},{32,0},{40,8},{48,16},{56,24},{64,96... | collective-permute-start | bytes 798728 | tf_op jit(solution)/shard_map/ppermute | solution.py:41
  200.3 39.0 %copy-start.11 = (bf16[256,256]{0,1:T(8,128)(2,1)S(1)}, bf16[256,256]{0,1:T(8,128)(2,1)}, u32[]{:S(2)}) copy-start(bf16[256,256]{0,1:T(8,128)(2,1)} %copy-done.10) | copy-start | bytes 393220
  202.2 15.8 %collective-permute-start.6 = (f32[8,8320]{1,0:T(8,128)}, f32[8,8320]{1,0:T(8,128)}, u32[]{:S(2)}, u32[]{:S(2)}) collective-permute-start(f32[8,8320]{1,0:T(8,128)} %pad_maximum_fusion.4), channel_id=1, source_target_pairs={{0,64},{8,72},{16,80},{24,88},{32,96},{40,104},{48,112},{56,120},{... | collective-permute-start | bytes 798728 | tf_op jit(solution)/shard_map/ppermute | solution.py:41
  219.8 35.8 %copy-start.20 = (f32[8,2,128]{2,0,1:T(8,128)S(1)}, f32[8,2,128]{2,0,1:T(8,128)}, u32[]{:S(2)}) copy-start(f32[8,2,128]{2,0,1:T(8,128)} %copy-done.19) | copy-start | bytes 24580
  220.6 11.9 %collective-permute-start.7 = (f32[8,8320]{1,0:T(8,128)}, f32[8,8320]{1,0:T(8,128)}, u32[]{:S(2)}, u32[]{:S(2)}) collective-permute-start(f32[8,8320]{1,0:T(8,128)} %pad_maximum_fusion.5), channel_id=1, source_target_pairs={{0,128},{8,136},{16,144},{24,152},{32,160},{40,168},{48,176},{56,1... | collective-permute-start | bytes 798728 | tf_op jit(solution)/shard_map/ppermute | solution.py:41
  234.5 16.9 %collective-permute-start.8 = (f32[8,8320]{1,0:T(8,128)S(1)}, f32[8,8320]{1,0:T(8,128)S(1)}, u32[]{:S(2)}, u32[]{:S(2)}) collective-permute-start(f32[8,8320]{1,0:T(8,128)S(1)} %pad_maximum_fusion.6), channel_id=1, source_target_pairs={{0,256},{8,264},{16,272},{24,280},{32,288},{40,296},{48,304},{56,3... | collective-permute-start | bytes 798728 | tf_op jit(solution)/shard_map/ppermute | solution.py:41
  252.7 6.2 %collective-permute-start.9 = (f32[8,8192]{1,0:T(8,128)S(1)}, f32[8,8192]{1,0:T(8,128)S(1)}, u32[]{:S(2)}, u32[]{:S(2)}) collective-permute-start(f32[8,8192]{1,0:T(8,128)S(1)} %add_select_fusion), channel_id=1, source_target_pairs={{0,8},{8,0},{16,24},{24,16},{32,40},{40,32},{48,56},{56,48},{64,72... | collective-permute-start | bytes 786440 | tf_op jit(solution)/shard_map/ppermute | solution.py:50
  255.7 3.7 copy-start.29
  255.7 6.0 %copy-start.13 = (f32[256,128]{1,0:T(8,128)S(1)}, f32[256,128]{1,0:T(8,128)}, u32[]{:S(2)}) copy-start(f32[256,128]{1,0:T(8,128)} %copy-done.12) | copy-start | bytes 393220
  255.7 6.0 %copy-start.22 = (f32[256,8]{0,1:T(8,128)S(1)}, f32[256,8]{0,1:T(8,128)}, u32[]{:S(2)}) copy-start(f32[256,8]{0,1:T(8,128)} %get-tuple-element.199) | copy-start | bytes 24580
  261.7 3.5 copy-start.17
  268.8 4.6 %copy-start.23 = (pred[1,256,256]{2,1,0:T(8,128)(4,1)S(1)}, pred[1,256,256]{2,1,0:T(8,128)(4,1)}, u32[]{:S(2)}) copy-start(pred[1,256,256]{2,1,0:T(8,128)(4,1)} %iota_compare_fusion) | copy-start | bytes 196612
  268.8 4.6 %copy-start.26 = (f32[256,8]{0,1:T(8,128)S(1)}, f32[256,8]{0,1:T(8,128)}, u32[]{:S(2)}) copy-start(f32[256,8]{0,1:T(8,128)} %subtract_exponential_fusion) | copy-start | bytes 24580
  268.8 4.6 %copy-start.35 = (f32[8,256]{1,0:T(8,128)S(1)}, f32[8,256]{1,0:T(8,128)}, u32[]{:S(2)}) copy-start(f32[8,256]{1,0:T(8,128)} %add_bitcast_fusion.1) | copy-start | bytes 24580
  273.4 2.6 copy-start.37
  276.0 1.7 slice-start.4
  278.4 1.3 copy-start
  278.4 1.3 copy-start.24
  278.5 3.3 copy-start.14
  279.8 2.7 copy-start.18
  279.8 6.0 %copy-start.30 = (f32[8]{0:T(128)S(1)}, f32[8]{0:T(128)}, u32[]{:S(2)}) copy-start(f32[8]{0:T(128)} %param.14) | copy-start | bytes 100
  279.8 2.4 copy-start.16
  279.8 2.7 copy-start.27
  279.8 2.7 copy-start.32
  279.8 3.0 copy-start.33
  279.8 3.0 copy-start.34
  279.8 6.0 %copy-start.36 = (f32[256,8]{0,1:T(8,128)S(1)}, f32[256,8]{0,1:T(8,128)}, u32[]{:S(2)}) copy-start(f32[256,8]{0,1:T(8,128)} %get-tuple-element.194) | copy-start | bytes 24580
  279.9 6.0 %copy-start.42 = (f32[8]{0:T(128)S(1)}, f32[8]{0:T(128)}, u32[]{:S(2)}) copy-start(f32[8]{0:T(128)} %param.13) | copy-start | bytes 100
  290.0 1.3 copy-start.9
  293.8 4.1 %slice-start = ((f32[256,2,4,256]{3,0,2,1:T(8,128)}), f32[256,2,1,256]{3,0,2,1:T(8,128)S(1)}, s32[]{:S(2)}) async-start(f32[256,2,4,256]{3,0,2,1:T(8,128)} %copy-done), calls=%async_computation.1 | async-start | bytes 1048576 | tf_op jit(solution)/shard_map/slice | solution.py:71
  293.8 4.1 %slice-start.1 = ((f32[256,2,4,256]{3,0,2,1:T(8,128)}), f32[256,2,3,256]{3,0,2,1:T(8,128)S(1)}, s32[]{:S(2)}) async-start(f32[256,2,4,256]{3,0,2,1:T(8,128)} %copy-done), calls=%async_computation.2 | async-start | bytes 3145728 | tf_op jit(solution)/shard_map/slice | solution.py:71
  298.2 4.6 %copy-start.1 = (f32[256,2,4,256]{3,0,2,1:T(8,128)}, f32[256,2,4,256]{3,0,2,1:T(8,128)S(1)}, u32[]{:S(2)}) copy-start(f32[256,2,4,256]{3,0,2,1:T(8,128)S(1)} %maximum_select_fusion.1) | copy-start | bytes 6291460
  298.2 4.0 %copy-start.6 = (f32[256,2,4,256]{3,2,1,0:T(4,128)S(1)}, f32[256,2,4,256]{3,2,1,0:T(4,128)}, u32[]{:S(2)}) copy-start(f32[256,2,4,256]{3,2,1,0:T(4,128)} %reshape.514) | copy-start | bytes 6291460
  298.3 17.1 %collective-permute-start.10 = (f32[256,4,256]{2,0,1:T(8,128)S(1)}, f32[256,4,256]{2,0,1:T(8,128)}, u32[]{:S(2)}, u32[]{:S(2)}) collective-permute-start(f32[256,4,256]{2,0,1:T(8,128)S(1)} %select_bitcast_fusion.1), channel_id=1, source_target_pairs={{0,1},{1,0},{2,3},{3,2},{4,5},{5,4},{6,7},{7,6},{8,11},{9,10},{10,... | collective-permute-start | bytes 3145736 | tf_op jit(solution)/shard_map/ppermute | solution.py:85
  303.3 1.6 copy-start.8
  306.9 8.6 %copy-start.2 = (f32[256,2,4,256]{3,0,2,1:T(8,128)S(1)}, f32[256,2,4,256]{3,0,2,1:T(8,128)}, u32[]{:S(2)}) copy-start(f32[256,2,4,256]{3,0,2,1:T(8,128)} %copy-done.1) | copy-start | bytes 6291460
  308.0 22.5 %collective-permute-start.13 = (f32[256,4,256]{2,0,1:T(8,128)}, f32[256,4,256]{2,0,1:T(8,128)}, u32[]{:S(2)}, u32[]{:S(2)}) collective-permute-start(f32[256,4,256]{2,0,1:T(8,128)} %select_bitcast_fusion), channel_id=1, source_target_pairs={{0,1},{1,0},{2,3},{3,2},{4,5},{5,4},{6,7},{7,6},{8,11},{9,10},{10,... | collective-permute-start | bytes 3145736 | tf_op jit(solution)/shard_map/ppermute | solution.py:85
  310.9 19.5 %copy-start.4 = (f32[256,4,2,256]{3,0,1,2:T(8,128)S(1)}, f32[256,4,2,256]{3,0,1,2:T(8,128)}, u32[]{:S(2)}) copy-start(f32[256,4,2,256]{3,0,1,2:T(8,128)} %copy-done.3) | copy-start | bytes 6291460
  317.0 18.1 %collective-permute-start.11 = (f32[256,2,256]{2,0,1:T(8,128)S(1)}, f32[256,2,256]{2,0,1:T(8,128)S(1)}, u32[]{:S(2)}, u32[]{:S(2)}) collective-permute-start(f32[256,2,256]{2,0,1:T(8,128)S(1)} %select_bitcast_fusion.3), channel_id=1, source_target_pairs={{0,2},{1,3},{2,0},{3,1},{4,6},{5,7},{6,4},{7,5},{8,10},{9,11},{10,... | collective-permute-start | bytes 1572872 | tf_op jit(solution)/shard_map/ppermute | solution.py:85
  332.8 16.5 %collective-permute-start.14 = (f32[256,2,256]{2,0,1:T(8,128)}, f32[256,2,256]{2,0,1:T(8,128)}, u32[]{:S(2)}, u32[]{:S(2)}) collective-permute-start(f32[256,2,256]{2,0,1:T(8,128)} %select_bitcast_fusion.2), channel_id=1, source_target_pairs={{0,2},{1,3},{2,0},{3,1},{4,6},{5,7},{6,4},{7,5},{8,10},{9,11},{10,... | collective-permute-start | bytes 1572872 | tf_op jit(solution)/shard_map/ppermute | solution.py:85
  335.3 23.9 %collective-permute-start.12 = (f32[256,1,256]{2,0,1:T(8,128)S(1)}, f32[256,1,256]{2,0,1:T(8,128)S(1)}, u32[]{:S(2)}, u32[]{:S(2)}) collective-permute-start(f32[256,1,256]{2,0,1:T(8,128)S(1)} %select_bitcast_fusion.6), channel_id=1, source_target_pairs={{0,4},{1,5},{2,6},{3,7},{4,0},{5,1},{6,2},{7,3},{8,12},{9,13},{10,... | collective-permute-start | bytes 786440 | tf_op jit(solution)/shard_map/ppermute | solution.py:85
  350.5 15.9 %collective-permute-start.15 = (f32[256,1,256]{2,0,1:T(8,128)S(1)}, f32[256,1,256]{2,0,1:T(8,128)S(1)}, u32[]{:S(2)}, u32[]{:S(2)}) collective-permute-start(f32[256,1,256]{2,0,1:T(8,128)S(1)} %select_bitcast_fusion.4), channel_id=1, source_target_pairs={{0,4},{1,5},{2,6},{3,7},{4,0},{5,1},{6,2},{7,3},{8,12},{9,13},{10,... | collective-permute-start | bytes 786440 | tf_op jit(solution)/shard_map/ppermute | solution.py:85
  (3 other events, 2.9 us)
Sparse Core Ops, SparseCore 0:
  10.7 128.4 all-gather.1

commit v11 on v9

--- a/solution.py
+++ b/solution.py
@@ -8,7 +8,7 @@
 SPAN = 256
 
 
-HIGH = lax.Precision.HIGHEST
+HIGH = lax.Precision.HIGH
 RING = 4
 
 

time: 377 us -> 371 us (0.984)
  matrix products: 40.7 us -> 35.3 us
  transfers between devices with their start and end apart: 17 -> 17, of which waited for: 13 -> 13; matrix products, arithmetic and copies ran while one was open for 5% -> 4% of each run, Pallas kernels for 0% -> 0%
where the time goes in v11:
time: 371 us; the launch traced here: 369 us
  waiting for transfers between devices  179 us (48%)
  starting transfers between devices  85.2 us (23%)
  matrix products  35.3 us (10%)
  other arithmetic  32.3 us (9%)
  local copies, waits for them, and re-layouts  22.2 us (6%)
  between operations  15 us (4%)
    all_gather x1, waiting for transfers between devices, per_device(): lax.all_gather(jnp.concatenate([w_out.T, w_in, w_bc, w_dt], axis=1), 'ctx...  72.3 us
    ppermute x5, waiting for transfers between devices, both_carries(): got = lax.ppermute(message, axis, [(i, i ^ bit) for i in range(devices)])  42.9 us
    ppermute x6, starting transfers between devices, scattered_sum(): blocks = keep + lax.ppermute(send, (rows_axis, axis), pairs)  36.6 us
    ppermute x3, waiting for transfers between devices, doubled_rows(): other = lax.ppermute(x, axis, [(i, i ^ bit) for i in range(devices)])  36 us
    ppermute x6, waiting for transfers between devices, scattered_sum(): blocks = keep + lax.ppermute(send, (rows_axis, axis), pairs)  26 us
    ppermute x5, starting transfers between devices, both_carries(): got = lax.ppermute(message, axis, [(i, i ^ bit) for i in range(devices)])  25.4 us
    ppermute x3, starting transfers between devices, doubled_rows(): other = lax.ppermute(x, axis, [(i, i ^ bit) for i in range(devices)])  18.1 us
    dot_general x8, matrix products, per_device(): jnp.dot(piece[:, width:], block[:, :out_cols], preferred_element_type=jnp...  10.3 us
  transfers between devices with their start and end apart: 17, of which 13 were waited for; matrix products, arithmetic and copies ran while one was open for 4% of the time, Pallas kernels for 0%

profile of v11, /device:TPU:1, one launch (start us, length us, event | category | flops | bytes accessed | tf_op | source)
XLA Modules:
  0.0 369.1 jit_solution(510133752366914189)
XLA Ops:
  8.0 1.4 pad_maximum_fusion.7
  11.3 8.3 %collective-permute-start = (bf16[256,512]{1,0:T(8,128)(2,1)S(1)}, bf16[256,512]{1,0:T(8,128)(2,1)S(1)}, u32[]{:S(2)}, u32[]{:S(2)}) collective-permute-start(bf16[256,512]{1,0:T(8,128)(2,1)S(1)} %constant_dynamic-update-slice_fusion), channel_id=1, source_target_pairs={{0,4},{1,5},{2,6},{3,7},{4,0},{5,1},{6,2},{7,3},{8,12},{9,13},{10,... | collective-permute-start | bytes 786440 | tf_op jit(solution)/shard_map/ppermute | solution.py:180
  19.6 8.5 %collective-permute-done = bf16[256,512]{1,0:T(8,128)(2,1)S(1)} collective-permute-done((bf16[256,512]{1,0:T(8,128)(2,1)S(1)}, bf16[256,512]{1,0:T(8,128)(2,1)S(1)}, u32[]{:S(2)}, u32[]{:S(2)}) %collective-permute-start) | collective-permute-done | bytes 262176 | tf_op jit(solution)/shard_map/ppermute | solution.py:180
  28.3 3.7 %collective-permute-start.1 = (bf16[512,512]{1,0:T(8,128)(2,1)S(1)}, bf16[512,512]{1,0:T(8,128)(2,1)S(1)}, u32[]{:S(2)}, u32[]{:S(2)}) collective-permute-start(bf16[512,512]{1,0:T(8,128)(2,1)S(1)} %maximum_select_fusion.2), channel_id=1, source_target_pairs={{0,2},{1,3},{2,0},{3,1},{4,6},{5,7},{6,4},{7,5},{8,10},{9,11},{10,... | collective-permute-start | bytes 1572872 | tf_op jit(solution)/shard_map/ppermute | solution.py:180
  32.0 7.7 %collective-permute-done.1 = bf16[512,512]{1,0:T(8,128)(2,1)S(1)} collective-permute-done((bf16[512,512]{1,0:T(8,128)(2,1)S(1)}, bf16[512,512]{1,0:T(8,128)(2,1)S(1)}, u32[]{:S(2)}, u32[]{:S(2)}) %collective-permute-start.1) | collective-permute-done | bytes 524320 | tf_op jit(solution)/shard_map/ppermute | solution.py:180
  40.2 6.1 %collective-permute-start.2 = (bf16[1024,512]{1,0:T(8,128)(2,1)S(1)}, bf16[1024,512]{1,0:T(8,128)(2,1)S(1)}, u32[]{:S(2)}, u32[]{:S(2)}) collective-permute-start(bf16[1024,512]{1,0:T(8,128)(2,1)S(1)} %maximum_select_fusion.1), channel_id=1, source_target_pairs={{0,1},{1,0},{2,3},{3,2},{4,5},{5,4},{6,7},{7,6},{8,9},{9,8},{10,11... | collective-permute-start | bytes 3145736 | tf_op jit(solution)/shard_map/ppermute | solution.py:180
  46.3 19.8 %collective-permute-done.2 = bf16[1024,512]{1,0:T(8,128)(2,1)S(1)} collective-permute-done((bf16[1024,512]{1,0:T(8,128)(2,1)S(1)}, bf16[1024,512]{1,0:T(8,128)(2,1)S(1)}, u32[]{:S(2)}, u32[]{:S(2)}) %collective-permute-start.2) | collective-permute-done | bytes 1048608 | tf_op jit(solution)/shard_map/ppermute | solution.py:180
  66.9 72.3 %all-gather.2.cloned.1.call-done = bf16[2048,1288]{1,0:T(8,128)(2,1)} async-done(((bf16[32,1288]{1,0:T(8,128)(2,1)}), bf16[2048,1288]{1,0:T(8,128)(2,1)}) %all-gather.2.cloned.1.call-update) | async-done | bytes 5275664 | tf_op jit(solution)/shard_map/all_gather | solution.py:202
  139.2 1.3 fusion.72
  140.5 1.5 convolution_add_fusion.6
  142.0 1.7 convolution_add_fusion.5
  143.7 1.3 convolution_add_fusion.4
  145.7 1.3 convolution_add_fusion.1
  147.1 1.2 fusion.145
  152.3 1.4 fusion.86
  153.7 1.3 convolution_add_fusion.13
  155.0 1.3 convolution_add_fusion.12
  156.3 1.3 convolution_add_fusion.11
  157.6 1.3 convolution_add_fusion.10
  158.9 1.3 convolution_add_fusion.9
  160.3 1.2 convolution_add_fusion.8
  161.4 1.2 convolution_add_fusion.7
  164.6 2.1 collective-permute-start.3
  166.8 1.8 collective-permute-done.3
  169.9 3.1 collective-permute-start.4
  173.0 6.8 %collective-permute-done.4 = f32[8,8320]{1,0:T(8,128)S(1)} collective-permute-done((f32[8,8320]{1,0:T(8,128)}, f32[8,8320]{1,0:T(8,128)S(1)}, u32[]{:S(2)}, u32[]{:S(2)}) %collective-permute-start.4) | collective-permute-done | bytes 266272 | tf_op jit(solution)/shard_map/ppermute | solution.py:41
  180.9 3.9 %collective-permute-start.5 = (f32[8,8320]{1,0:T(8,128)}, f32[8,8320]{1,0:T(8,128)}, u32[]{:S(2)}, u32[]{:S(2)}) collective-permute-start(f32[8,8320]{1,0:T(8,128)} %pad_maximum_fusion.2), channel_id=1, source_target_pairs={{0,32},{8,40},{16,48},{24,56},{32,0},{40,8},{48,16},{56,24},{64,96... | collective-permute-start | bytes 798728 | tf_op jit(solution)/shard_map/ppermute | solution.py:41
  184.8 12.3 %collective-permute-done.5 = f32[8,8320]{1,0:T(8,128)} collective-permute-done((f32[8,8320]{1,0:T(8,128)}, f32[8,8320]{1,0:T(8,128)}, u32[]{:S(2)}, u32[]{:S(2)}) %collective-permute-start.5) | collective-permute-done | bytes 266272 | tf_op jit(solution)/shard_map/ppermute | solution.py:41
  197.9 1.1 add_select_fusion.6
  199.8 6.8 %collective-permute-start.6 = (f32[8,8320]{1,0:T(8,128)}, f32[8,8320]{1,0:T(8,128)}, u32[]{:S(2)}, u32[]{:S(2)}) collective-permute-start(f32[8,8320]{1,0:T(8,128)} %pad_maximum_fusion.3), channel_id=1, source_target_pairs={{0,64},{8,72},{16,80},{24,88},{32,96},{40,104},{48,112},{56,120},{... | collective-permute-start | bytes 798728 | tf_op jit(solution)/shard_map/ppermute | solution.py:41
  206.6 9.0 %collective-permute-done.6 = f32[8,8320]{1,0:T(8,128)} collective-permute-done((f32[8,8320]{1,0:T(8,128)}, f32[8,8320]{1,0:T(8,128)}, u32[]{:S(2)}, u32[]{:S(2)}) %collective-permute-start.6) | collective-permute-done | bytes 266272 | tf_op jit(solution)/shard_map/ppermute | solution.py:41
  216.3 1.1 add_select_fusion.5
  218.2 6.8 %collective-permute-start.7 = (f32[8,8320]{1,0:T(8,128)}, f32[8,8320]{1,0:T(8,128)}, u32[]{:S(2)}, u32[]{:S(2)}) collective-permute-start(f32[8,8320]{1,0:T(8,128)} %pad_maximum_fusion.4), channel_id=1, source_target_pairs={{0,128},{8,136},{16,144},{24,152},{32,160},{40,168},{48,176},{56,1... | collective-permute-start | bytes 798728 | tf_op jit(solution)/shard_map/ppermute | solution.py:41
  227.0 3.1 collective-permute-done.7
  230.9 1.1 add_select_fusion.4
  232.0 4.7 %collective-permute-start.8 = (f32[8,8320]{1,0:T(8,128)S(1)}, f32[8,8320]{1,0:T(8,128)S(1)}, u32[]{:S(2)}, u32[]{:S(2)}) collective-permute-start(f32[8,8320]{1,0:T(8,128)S(1)} %pad_maximum_fusion.5), channel_id=1, source_target_pairs={{0,256},{8,264},{16,272},{24,280},{32,288},{40,296},{48,304},{56,3... | collective-permute-start | bytes 798728 | tf_op jit(solution)/shard_map/ppermute | solution.py:41
  237.0 11.8 %collective-permute-done.8 = f32[8,8320]{1,0:T(8,128)S(1)} collective-permute-done((f32[8,8320]{1,0:T(8,128)S(1)}, f32[8,8320]{1,0:T(8,128)S(1)}, u32[]{:S(2)}, u32[]{:S(2)}) %collective-permute-start.8) | collective-permute-done | bytes 266272 | tf_op jit(solution)/shard_map/ppermute | solution.py:41
  248.8 1.3 add_select_fusion
  250.1 2.9 collective-permute-start.9
  253.1 2.2 fusion.12
  256.9 1.7 fusion.20
  261.9 2.2 fusion.22
  264.1 1.9 multiply_reduce_fusion.1
  266.9 2.5 reduce-window.44
  271.2 3.3 fusion
  274.6 2.8 reshape.520
  277.3 1.6 copy.209
  280.4 3.7 %gather_fusion.1 = f32[8,256,256]{2,1,0:T(8,128)} fusion(f32[256,8,256]{2,0,1:T(8,128)} %bitcast.320, s32[1024]{0:T(1024)} %pad_clamp_fusion), kind=kCustom, calls=%fused_computation.1 | custom fusion | bytes 4194336 | tf_op jit(solution)/shard_map/gather | solution.py:72
  284.1 2.1 gather_fusion
  286.3 2.0 bitcast_select_fusion
  288.3 1.2 select_bitcast_fusion.1
  289.6 3.9 %collective-permute-start.10 = (f32[256,4,256]{2,0,1:T(8,128)}, f32[256,4,256]{2,0,1:T(8,128)}, u32[]{:S(2)}, u32[]{:S(2)}) collective-permute-start(f32[256,4,256]{2,0,1:T(8,128)} %select_bitcast_fusion.1), channel_id=1, source_target_pairs={{0,1},{1,0},{2,3},{3,2},{4,5},{5,4},{6,7},{7,6},{8,11},{9,10},{10,... | collective-permute-start | bytes 3145736 | tf_op jit(solution)/shard_map/ppermute | solution.py:85
  294.2 1.1 select_bitcast_fusion
  295.3 2.9 collective-permute-start.13
  298.2 8.5 %collective-permute-done.10 = f32[256,4,256]{2,0,1:T(8,128)} collective-permute-done((f32[256,4,256]{2,0,1:T(8,128)}, f32[256,4,256]{2,0,1:T(8,128)}, u32[]{:S(2)}, u32[]{:S(2)}) %collective-permute-start.10) | collective-permute-done | bytes 1048608 | tf_op jit(solution)/shard_map/ppermute | solution.py:85
  306.7 2.1 bitcast_add_fusion.1
  308.9 2.7 collective-permute-start.11
  311.6 9.4 %collective-permute-done.13 = f32[256,4,256]{2,0,1:T(8,128)} collective-permute-done((f32[256,4,256]{2,0,1:T(8,128)}, f32[256,4,256]{2,0,1:T(8,128)}, u32[]{:S(2)}, u32[]{:S(2)}) %collective-permute-start.13) | collective-permute-done | bytes 1048608 | tf_op jit(solution)/shard_map/ppermute | solution.py:85
  321.1 1.4 bitcast_add_fusion
  324.4 2.6 collective-permute-start.14
  327.1 17.1 %collective-permute-start.12 = (f32[256,1,256]{2,0,1:T(8,128)S(1)}, f32[256,1,256]{2,0,1:T(8,128)S(1)}, u32[]{:S(2)}, u32[]{:S(2)}) collective-permute-start(f32[256,1,256]{2,0,1:T(8,128)S(1)} %select_bitcast_fusion.6), channel_id=1, source_target_pairs={{0,4},{1,5},{2,6},{3,7},{4,0},{5,1},{6,2},{7,3},{8,12},{9,13},{10,... | collective-permute-start | bytes 786440 | tf_op jit(solution)/shard_map/ppermute | solution.py:85
  344.3 1.1 fusion.46
  345.5 7.4 %collective-permute-start.15 = (f32[256,1,256]{2,0,1:T(8,128)S(1)}, f32[256,1,256]{2,0,1:T(8,128)S(1)}, u32[]{:S(2)}, u32[]{:S(2)}) collective-permute-start(f32[256,1,256]{2,0,1:T(8,128)S(1)} %select_bitcast_fusion.4), channel_id=1, source_target_pairs={{0,4},{1,5},{2,6},{3,7},{4,0},{5,1},{6,2},{7,3},{8,12},{9,13},{10,... | collective-permute-start | bytes 786440 | tf_op jit(solution)/shard_map/ppermute | solution.py:85
  353.6 8.0 %collective-permute-done.15 = f32[256,1,256]{2,0,1:T(8,128)S(1)} collective-permute-done((f32[256,1,256]{2,0,1:T(8,128)S(1)}, f32[256,1,256]{2,0,1:T(8,128)S(1)}, u32[]{:S(2)}, u32[]{:S(2)}) %collective-permute-start.15) | collective-permute-done | bytes 262176 | tf_op jit(solution)/shard_map/ppermute | solution.py:85
  (180 shorter events, 32.1 us)
Async XLA Ops:
  7.2 132.0 %all-gather.2.cloned.1.call-start = ((), (), s32[]{:S(2)}) async-start(), calls=%async_computation | async-start | bytes 5857280 | tf_op jit(solution)/shard_map/all_gather | solution.py:202
  11.3 16.8 %collective-permute-start = (bf16[256,512]{1,0:T(8,128)(2,1)S(1)}, bf16[256,512]{1,0:T(8,128)(2,1)S(1)}, u32[]{:S(2)}, u32[]{:S(2)}) collective-permute-start(bf16[256,512]{1,0:T(8,128)(2,1)S(1)} %constant_dynamic-update-slice_fusion), channel_id=1, source_target_pairs={{0,4},{1,5},{2,6},{3,7},{4,0},{5,1},{6,2},{7,3},{8,12},{9,13},{10,... | collective-permute-start | bytes 786440 | tf_op jit(solution)/shard_map/ppermute | solution.py:180
  28.3 11.4 %collective-permute-start.1 = (bf16[512,512]{1,0:T(8,128)(2,1)S(1)}, bf16[512,512]{1,0:T(8,128)(2,1)S(1)}, u32[]{:S(2)}, u32[]{:S(2)}) collective-permute-start(bf16[512,512]{1,0:T(8,128)(2,1)S(1)} %maximum_select_fusion.2), channel_id=1, source_target_pairs={{0,2},{1,3},{2,0},{3,1},{4,6},{5,7},{6,4},{7,5},{8,10},{9,11},{10,... | collective-permute-start | bytes 1572872 | tf_op jit(solution)/shard_map/ppermute | solution.py:180
  40.2 26.0 %collective-permute-start.2 = (bf16[1024,512]{1,0:T(8,128)(2,1)S(1)}, bf16[1024,512]{1,0:T(8,128)(2,1)S(1)}, u32[]{:S(2)}, u32[]{:S(2)}) collective-permute-start(bf16[1024,512]{1,0:T(8,128)(2,1)S(1)} %maximum_select_fusion.1), channel_id=1, source_target_pairs={{0,1},{1,0},{2,3},{3,2},{4,5},{5,4},{6,7},{7,6},{8,9},{9,8},{10,11... | collective-permute-start | bytes 3145736 | tf_op jit(solution)/shard_map/ppermute | solution.py:180
  66.9 78.5 %copy-start.6 = (bf16[2,2,2,256,512]{4,3,2,1,0:T(8,128)(2,1)}, bf16[2,2,2,256,512]{4,3,2,1,0:T(8,128)(2,1)S(1)}, u32[]{:S(2)}) copy-start(bf16[2,2,2,256,512]{4,3,2,1,0:T(8,128)(2,1)S(1)} %copy.125) | copy-start | bytes 6291460
  140.5 4.5 %copy-start.1 = (bf16[2048,1288]{1,0:T(8,128)(2,1)S(1)}, bf16[2048,1288]{1,0:T(8,128)(2,1)}, u32[]{:S(2)}) copy-start(bf16[2048,1288]{1,0:T(8,128)(2,1)} %all-gather.2.cloned.1.call-done) | copy-start | bytes 15826948
  145.7 3.6 copy-start.23
  145.7 3.6 copy-start.28
  145.7 14.5 %slice-start = ((s8[5767168]{0:T(1024)(128)(4,1)}), s8[1572864]{0:T(1024)(128)(4,1)S(1)}, s32[]{:S(2)}) async-start(s8[5767168]{0:T(1024)(128)(4,1)} %bitcast.295), calls=%async_computation.1 | async-start | bytes 3145728
  148.3 1.0 copy-start.15
  149.5 5.6 %copy-start.26 = (f32[8]{0:T(128)}, f32[8]{0:T(128)S(1)}, u32[]{:S(2)}) copy-start(f32[8]{0:T(128)S(1)} %get-tuple-element.201) | copy-start | bytes 100
  150.1 1.0 copy-start.16
  150.3 0.6 copy-start.21
  150.4 12.3 %copy-start.18 = (f32[256,8]{0,1:T(8,128)}, f32[256,8]{0,1:T(8,128)S(1)}, u32[]{:S(2)}) copy-start(f32[256,8]{0,1:T(8,128)S(1)} %get-tuple-element.199) | copy-start | bytes 24580
  151.2 1.0 copy-start.11
  152.1 10.5 %copy-start.13 = (f32[256,128]{1,0:T(8,128)}, f32[256,128]{1,0:T(8,128)S(1)}, u32[]{:S(2)}) copy-start(f32[256,128]{1,0:T(8,128)S(1)} %copy.136) | copy-start | bytes 393220
  152.2 8.0 %slice-start.1 = ((s8[5767168]{0:T(1024)(128)(4,1)}), s8[4194304]{0:T(1024)(128)(4,1)S(1)}, s32[]{:S(2)}) async-start(s8[5767168]{0:T(1024)(128)(4,1)} %bitcast.295), calls=%async_computation.2 | async-start | bytes 8388608
  162.6 6.1 %copy-start.27 = (f32[8]{0:T(128)S(1)}, f32[8]{0:T(128)}, u32[]{:S(2)}) copy-start(f32[8]{0:T(128)} %copy-done.26) | copy-start | bytes 100
  164.6 4.0 %collective-permute-start.3 = (f32[8,16512]{1,0:T(8,128)}, f32[8,16512]{1,0:T(8,128)S(1)}, u32[]{:S(2)}, u32[]{:S(2)}) collective-permute-start(f32[8,16512]{1,0:T(8,128)} %pad_maximum_fusion), channel_id=1, source_target_pairs={{0,8},{8,0},{16,24},{24,16},{32,40},{40,32},{48,56},{56,48},{64,72... | collective-permute-start | bytes 1585160 | tf_op jit(solution)/shard_map/ppermute | solution.py:23
  169.9 55.1 %copy-start.30 = (s32[8]{0:T(128)S(1)}, s32[8]{0:T(128)}, u32[]{:S(2)}) copy-start(s32[8]{0:T(128)} %constant.154) | copy-start | bytes 100
  169.9 55.7 %copy-start.29 = (f32[8]{0:T(128)S(1)}, f32[8]{0:T(128)}, u32[]{:S(2)}) copy-start(f32[8]{0:T(128)} %param.17) | copy-start | bytes 100
  169.9 10.0 %collective-permute-start.4 = (f32[8,8320]{1,0:T(8,128)}, f32[8,8320]{1,0:T(8,128)S(1)}, u32[]{:S(2)}, u32[]{:S(2)}) collective-permute-start(f32[8,8320]{1,0:T(8,128)} %pad_maximum_fusion.1), channel_id=1, source_target_pairs={{0,16},{8,24},{16,0},{24,8},{32,48},{40,56},{48,32},{56,40},{64,80... | collective-permute-start | bytes 798728 | tf_op jit(solution)/shard_map/ppermute | solution.py:41
  180.9 16.2 %collective-permute-start.5 = (f32[8,8320]{1,0:T(8,128)}, f32[8,8320]{1,0:T(8,128)}, u32[]{:S(2)}, u32[]{:S(2)}) collective-permute-start(f32[8,8320]{1,0:T(8,128)} %pad_maximum_fusion.2), channel_id=1, source_target_pairs={{0,32},{8,40},{16,48},{24,56},{32,0},{40,8},{48,16},{56,24},{64,96... | collective-permute-start | bytes 798728 | tf_op jit(solution)/shard_map/ppermute | solution.py:41
  197.9 38.9 %copy-start.12 = (bf16[256,256]{0,1:T(8,128)(2,1)S(1)}, bf16[256,256]{0,1:T(8,128)(2,1)}, u32[]{:S(2)}) copy-start(bf16[256,256]{0,1:T(8,128)(2,1)} %copy-done.11) | copy-start | bytes 393220
  199.8 15.8 %collective-permute-start.6 = (f32[8,8320]{1,0:T(8,128)}, f32[8,8320]{1,0:T(8,128)}, u32[]{:S(2)}, u32[]{:S(2)}) collective-permute-start(f32[8,8320]{1,0:T(8,128)} %pad_maximum_fusion.3), channel_id=1, source_target_pairs={{0,64},{8,72},{16,80},{24,88},{32,96},{40,104},{48,112},{56,120},{... | collective-permute-start | bytes 798728 | tf_op jit(solution)/shard_map/ppermute | solution.py:41
  217.4 35.6 %copy-start.17 = (f32[8,2,128]{2,0,1:T(8,128)S(1)}, f32[8,2,128]{2,0,1:T(8,128)}, u32[]{:S(2)}) copy-start(f32[8,2,128]{2,0,1:T(8,128)} %copy-done.16) | copy-start | bytes 24580
  217.4 35.6 %copy-start.22 = (f32[8,2]{0,1:T(2,128)S(1)}, f32[8,2]{0,1:T(2,128)}, u32[]{:S(2)}) copy-start(f32[8,2]{0,1:T(2,128)} %copy-done.21) | copy-start | bytes 196
  218.2 11.9 %collective-permute-start.7 = (f32[8,8320]{1,0:T(8,128)}, f32[8,8320]{1,0:T(8,128)}, u32[]{:S(2)}, u32[]{:S(2)}) collective-permute-start(f32[8,8320]{1,0:T(8,128)} %pad_maximum_fusion.4), channel_id=1, source_target_pairs={{0,128},{8,136},{16,144},{24,152},{32,160},{40,168},{48,176},{56,1... | collective-permute-start | bytes 798728 | tf_op jit(solution)/shard_map/ppermute | solution.py:41
  232.0 16.8 %collective-permute-start.8 = (f32[8,8320]{1,0:T(8,128)S(1)}, f32[8,8320]{1,0:T(8,128)S(1)}, u32[]{:S(2)}, u32[]{:S(2)}) collective-permute-start(f32[8,8320]{1,0:T(8,128)S(1)} %pad_maximum_fusion.5), channel_id=1, source_target_pairs={{0,256},{8,264},{16,272},{24,280},{32,288},{40,296},{48,304},{56,3... | collective-permute-start | bytes 798728 | tf_op jit(solution)/shard_map/ppermute | solution.py:41
  250.1 5.3 %collective-permute-start.9 = (f32[8,8192]{1,0:T(8,128)S(1)}, f32[8,8192]{1,0:T(8,128)S(1)}, u32[]{:S(2)}, u32[]{:S(2)}) collective-permute-start(f32[8,8192]{1,0:T(8,128)S(1)} %add_select_fusion), channel_id=1, source_target_pairs={{0,8},{8,0},{16,24},{24,16},{32,40},{40,32},{48,56},{56,48},{64,72... | collective-permute-start | bytes 786440 | tf_op jit(solution)/shard_map/ppermute | solution.py:50
  253.1 2.6 copy-start.24
  253.1 3.8 %copy-start.14 = (f32[256,128]{1,0:T(8,128)S(1)}, f32[256,128]{1,0:T(8,128)}, u32[]{:S(2)}) copy-start(f32[256,128]{1,0:T(8,128)} %copy-done.13) | copy-start | bytes 393220
  253.1 3.8 %copy-start.19 = (f32[256,8]{0,1:T(8,128)S(1)}, f32[256,8]{0,1:T(8,128)}, u32[]{:S(2)}) copy-start(f32[256,8]{0,1:T(8,128)} %copy-done.18) | copy-start | bytes 24580
  255.4 3.8 %copy-start.9 = (f32[256,1,128]{0,2,1:T(8,128)S(1)}, f32[256,1,128]{0,2,1:T(8,128)}, u32[]{:S(2)}) copy-start(f32[256,1,128]{0,2,1:T(8,128)} %get-tuple-element.186) | copy-start | bytes 393220
  256.5 3.8 %copy-start.10 = (f32[256,1,128]{0,2,1:T(8,128)S(1)}, f32[256,1,128]{0,2,1:T(8,128)}, u32[]{:S(2)}) copy-start(f32[256,1,128]{0,2,1:T(8,128)} %get-tuple-element.184) | copy-start | bytes 393220
  259.3 2.6 copy-start.20
  264.1 5.4 %copy-start.25 = (f32[8]{0:T(128)S(1)}, f32[8]{0:T(128)}, u32[]{:S(2)}) copy-start(f32[8]{0:T(128)} %param.16) | copy-start | bytes 100
  277.3 2.3 slice-start.2
  286.3 7.2 %copy-start.8 = (f32[8,256,256]{2,1,0:T(8,128)S(1)}, f32[8,256,256]{2,1,0:T(8,128)}, u32[]{:S(2)}) copy-start(f32[8,256,256]{2,1,0:T(8,128)} %gather_fusion.1) | copy-start | bytes 6291460
  288.3 5.9 %copy-start = (f32[256,8,256]{2,0,1:T(8,128)}, f32[256,8,256]{2,0,1:T(8,128)S(1)}, u32[]{:S(2)}) copy-start(f32[256,8,256]{2,0,1:T(8,128)S(1)} %bitcast_select_fusion) | copy-start | bytes 6291460
  288.3 5.1 %copy-start.7 = (f32[256,4,2,256]{3,2,1,0:T(2,128)S(1)}, f32[256,4,2,256]{3,2,1,0:T(2,128)}, u32[]{:S(2)}) copy-start(f32[256,4,2,256]{3,2,1,0:T(2,128)} %reshape.520) | copy-start | bytes 6291460
  289.6 17.2 %collective-permute-start.10 = (f32[256,4,256]{2,0,1:T(8,128)}, f32[256,4,256]{2,0,1:T(8,128)}, u32[]{:S(2)}, u32[]{:S(2)}) collective-permute-start(f32[256,4,256]{2,0,1:T(8,128)} %select_bitcast_fusion.1), channel_id=1, source_target_pairs={{0,1},{1,0},{2,3},{3,2},{4,5},{5,4},{6,7},{7,6},{8,11},{9,10},{10,... | collective-permute-start | bytes 3145736 | tf_op jit(solution)/shard_map/ppermute | solution.py:85
  295.3 25.8 %collective-permute-start.13 = (f32[256,4,256]{2,0,1:T(8,128)}, f32[256,4,256]{2,0,1:T(8,128)}, u32[]{:S(2)}, u32[]{:S(2)}) collective-permute-start(f32[256,4,256]{2,0,1:T(8,128)} %select_bitcast_fusion), channel_id=1, source_target_pairs={{0,1},{1,0},{2,3},{3,2},{4,5},{5,4},{6,7},{7,6},{8,11},{9,10},{10,... | collective-permute-start | bytes 3145736 | tf_op jit(solution)/shard_map/ppermute | solution.py:85
  308.8 2.8 copy-start.4
  308.9 18.1 %collective-permute-start.11 = (f32[256,2,256]{2,0,1:T(8,128)S(1)}, f32[256,2,256]{2,0,1:T(8,128)S(1)}, u32[]{:S(2)}, u32[]{:S(2)}) collective-permute-start(f32[256,2,256]{2,0,1:T(8,128)S(1)} %select_bitcast_fusion.3), channel_id=1, source_target_pairs={{0,2},{1,3},{2,0},{3,1},{4,6},{5,7},{6,4},{7,5},{8,10},{9,11},{10,... | collective-permute-start | bytes 1572872 | tf_op jit(solution)/shard_map/ppermute | solution.py:85
  322.5 1.0 copy-start.2
  322.5 4.5 %copy-start.5 = (f32[256,4,256]{2,0,1:T(8,128)S(1)}, f32[256,4,256]{2,0,1:T(8,128)}, u32[]{:S(2)}) copy-start(f32[256,4,256]{2,0,1:T(8,128)} %copy-done.4) | copy-start | bytes 3145732
  324.4 19.9 %copy-start.3 = (f32[256,4,256]{2,0,1:T(8,128)S(1)}, f32[256,4,256]{2,0,1:T(8,128)}, u32[]{:S(2)}) copy-start(f32[256,4,256]{2,0,1:T(8,128)} %copy-done.2) | copy-start | bytes 3145732
  324.4 19.9 %collective-permute-start.14 = (f32[256,2,256]{2,0,1:T(8,128)}, f32[256,2,256]{2,0,1:T(8,128)}, u32[]{:S(2)}, u32[]{:S(2)}) collective-permute-start(f32[256,2,256]{2,0,1:T(8,128)} %select_bitcast_fusion.2), channel_id=1, source_target_pairs={{0,2},{1,3},{2,0},{3,1},{4,6},{5,7},{6,4},{7,5},{8,10},{9,11},{10,... | collective-permute-start | bytes 1572872 | tf_op jit(solution)/shard_map/ppermute | solution.py:85
  327.1 25.7 %collective-permute-start.12 = (f32[256,1,256]{2,0,1:T(8,128)S(1)}, f32[256,1,256]{2,0,1:T(8,128)S(1)}, u32[]{:S(2)}, u32[]{:S(2)}) collective-permute-start(f32[256,1,256]{2,0,1:T(8,128)S(1)} %select_bitcast_fusion.6), channel_id=1, source_target_pairs={{0,4},{1,5},{2,6},{3,7},{4,0},{5,1},{6,2},{7,3},{8,12},{9,13},{10,... | collective-permute-start | bytes 786440 | tf_op jit(solution)/shard_map/ppermute | solution.py:85
  345.5 16.1 %collective-permute-start.15 = (f32[256,1,256]{2,0,1:T(8,128)S(1)}, f32[256,1,256]{2,0,1:T(8,128)S(1)}, u32[]{:S(2)}, u32[]{:S(2)}) collective-permute-start(f32[256,1,256]{2,0,1:T(8,128)S(1)} %select_bitcast_fusion.4), channel_id=1, source_target_pairs={{0,4},{1,5},{2,6},{3,7},{4,0},{5,1},{6,2},{7,3},{8,12},{9,13},{10,... | collective-permute-start | bytes 786440 | tf_op jit(solution)/shard_map/ppermute | solution.py:85
Sparse Core Ops, SparseCore 0:
  10.7 128.4 all-gather.1

commit v12 on v11

--- a/solution.py
+++ b/solution.py
@@ -199,9 +199,11 @@
     pair_cols = w_bc.shape[1]
     groups = pair_cols // (2 * STATE)
     out_cols = w_out.shape[0]
+    w_own = jnp.concatenate([w_out.T, w_in, w_bc, w_dt], axis=1)
+    lanes = 128 if w_own.size % 128 == 0 else w_own.shape[1]
     w_all = lax.all_gather(
-        jnp.concatenate([w_out.T, w_in, w_bc, w_dt], axis=1), "ctx", axis=0, tiled=True
-    )
+        w_own.reshape(-1, lanes), "ctx", axis=0, tiled=True
+    ).reshape(-1, w_own.shape[1])
     bits = devices.bit_length() - 1
     pieces = doubled_rows(
         jnp.concatenate([tokens, cotangent], axis=1), "tp", list(reversed(range(bits)))

time: 371 us -> 429 us (1.16); the launches traced: 369 us -> 422 us
  local copies, waits for them, and re-layouts: 22.2 us -> 66.1 us
  other arithmetic: 32.3 us -> 47.7 us
  starting transfers between devices: 85.2 us -> 76.2 us
    slice x0 -> x9, local copies, waits for them, and re-layouts: none -> 27.2 us  [per_device(): block = w_all[k * width:(k + 1) * width]]
    reshape x0 -> x1, local copies, waits for them, and re-layouts: none -> 12.4 us  [per_device(): w_all = lax.all_gather(w_own.reshape(-1, lanes), 'ctx', axis=0, tiled=Tru...]
    another operation x10, other arithmetic: 4.19 us -> 15.6 us
    ppermute x6, starting transfers between devices: 36.6 us -> 27.6 us  [scattered_sum(): blocks = keep + lax.ppermute(send, (rows_axis, axis), pairs)]
    ppermute x6, waiting for transfers between devices: 26 us -> 30.3 us  [scattered_sum(): blocks = keep + lax.ppermute(send, (rows_axis, axis), pairs)]
  transfers between devices with their start and end apart: 17 -> 17, of which waited for: 13 -> 14; matrix products, arithmetic and copies ran while one was open for 4% -> 8% of each run, Pallas kernels for 0% -> 0%
where the time goes in v12:
time: 429 us; the launch traced here: 422 us
  waiting for transfers between devices  182 us (42%)
  starting transfers between devices  76.2 us (18%)
  local copies, waits for them, and re-layouts  66.1 us (15%)
  other arithmetic  47.7 us (11%)
  matrix products  34.7 us (8%)
  between operations  15.2 us (4%)
    all_gather x1, waiting for transfers between devices, per_device(): lax.all_gather(w_own.reshape(-1, lanes), 'ctx', axis=0, tiled=True)  71.7 us
    ppermute x5, waiting for transfers between devices, both_carries(): got = lax.ppermute(message, axis, [(i, i ^ bit) for i in range(devices)])  42.5 us
    ppermute x3, waiting for transfers between devices, doubled_rows(): other = lax.ppermute(x, axis, [(i, i ^ bit) for i in range(devices)])  36 us
    ppermute x6, waiting for transfers between devices, scattered_sum(): blocks = keep + lax.ppermute(send, (rows_axis, axis), pairs)  30.3 us
    ppermute x6, starting transfers between devices, scattered_sum(): blocks = keep + lax.ppermute(send, (rows_axis, axis), pairs)  27.6 us
    slice x9, local copies, waits for them, and re-layouts, per_device(): block = w_all[k * width:(k + 1) * width]  27.2 us
    ppermute x5, starting transfers between devices, both_carries(): got = lax.ppermute(message, axis, [(i, i ^ bit) for i in range(devices)])  24.9 us
    ppermute x3, starting transfers between devices, doubled_rows(): other = lax.ppermute(x, axis, [(i, i ^ bit) for i in range(devices)])  18.1 us
  transfers between devices with their start and end apart: 17, of which 14 were waited for; matrix products, arithmetic and copies ran while one was open for 8% of the time, Pallas kernels for 0%

profile of v12, /device:TPU:1, one launch (start us, length us, event | category | flops | bytes accessed | tf_op | source)
XLA Modules:
  0.0 422.4 jit_solution(16293838161768040293)
XLA Ops:
  11.5 8.3 %collective-permute-start = (bf16[256,512]{1,0:T(8,128)(2,1)S(1)}, bf16[256,512]{1,0:T(8,128)(2,1)S(1)}, u32[]{:S(2)}, u32[]{:S(2)}) collective-permute-start(bf16[256,512]{1,0:T(8,128)(2,1)S(1)} %constant_dynamic-update-slice_fusion), channel_id=1, source_target_pairs={{0,4},{1,5},{2,6},{3,7},{4,0},{5,1},{6,2},{7,3},{8,12},{9,13},{10,... | collective-permute-start | bytes 786440 | tf_op jit(solution)/shard_map/ppermute | solution.py:180
  19.8 8.5 %collective-permute-done = bf16[256,512]{1,0:T(8,128)(2,1)S(1)} collective-permute-done((bf16[256,512]{1,0:T(8,128)(2,1)S(1)}, bf16[256,512]{1,0:T(8,128)(2,1)S(1)}, u32[]{:S(2)}, u32[]{:S(2)}) %collective-permute-start) | collective-permute-done | bytes 262176 | tf_op jit(solution)/shard_map/ppermute | solution.py:180
  28.5 3.7 collective-permute-start.1
  32.2 7.7 %collective-permute-done.1 = bf16[512,512]{1,0:T(8,128)(2,1)S(1)} collective-permute-done((bf16[512,512]{1,0:T(8,128)(2,1)S(1)}, bf16[512,512]{1,0:T(8,128)(2,1)S(1)}, u32[]{:S(2)}, u32[]{:S(2)}) %collective-permute-start.1) | collective-permute-done | bytes 524320 | tf_op jit(solution)/shard_map/ppermute | solution.py:180
  40.4 6.1 %collective-permute-start.2 = (bf16[1024,512]{1,0:T(8,128)(2,1)S(1)}, bf16[1024,512]{1,0:T(8,128)(2,1)S(1)}, u32[]{:S(2)}, u32[]{:S(2)}) collective-permute-start(bf16[1024,512]{1,0:T(8,128)(2,1)S(1)} %maximum_select_fusion.1), channel_id=1, source_target_pairs={{0,1},{1,0},{2,3},{3,2},{4,5},{5,4},{6,7},{7,6},{8,9},{9,8},{10,11... | collective-permute-start | bytes 3145736 | tf_op jit(solution)/shard_map/ppermute | solution.py:180
  46.5 19.8 %collective-permute-done.2 = bf16[1024,512]{1,0:T(8,128)(2,1)S(1)} collective-permute-done((bf16[1024,512]{1,0:T(8,128)(2,1)S(1)}, bf16[1024,512]{1,0:T(8,128)(2,1)S(1)}, u32[]{:S(2)}, u32[]{:S(2)}) %collective-permute-start.2) | collective-permute-done | bytes 1048608 | tf_op jit(solution)/shard_map/ppermute | solution.py:180
  67.0 71.7 %all-gather.3.cloned.1.call-done = bf16[64,322,128]{2,1,0:T(8,128)(2,1)} async-done(((bf16[1,322,128]{2,1,0:T(8,128)(2,1)}), bf16[64,322,128]{2,1,0:T(8,128)(2,1)}) %all-gather.3.cloned.1.call-update) | async-done | bytes 5275664 | tf_op jit(solution)/shard_map/all_gather | solution.py:204
  138.8 4.7 %fusion.145 = (bf16[8,322,128]{2,1,0:T(8,128)(2,1)}, bf16[8,322,128]{2,1,0:T(8,128)(2,1)S(1)}, bf16[8,322,128]{2,1,0:T(8,128)(2,1)}, bf16[8,322,128]{2,1,0:T(8,1...) fusion(bf16[64,322,128]{2,1,0:T(8,128)(2,1)} %all-gather.3.clon, ...), kind=kLoop, calls=%fused_computation.261 | loop fusion | bytes 10551296 | tf_op jit(solution)/shard_map/slice | solution.py:214
  143.4 3.3 slice.323
  146.8 3.0 slice.327
  149.8 3.0 slice.331
  152.7 3.0 slice.335
  155.7 3.0 slice.339
  158.7 3.0 slice.343
  161.7 2.0 slice.347
  163.7 2.3 slice.351
  166.0 1.6 fusion.72
  167.6 1.4 convolution_add_fusion.6
  173.6 12.1 %reduce-window.40 = f32[8,2,128]{2,0,1:T(8,128)S(1)} reduce-window(f32[8,2,128]{2,0,1:T(8,128)S(1)} %multiply_bitcast_fusion.1, f32[]{:T(128)} %constant.136.clone.1), window={size=1x1x128 pad=0_0x0_0x127_0}, to_apply=%region_0.1 | reduce-window | flops 260096 | bytes 16388 | tf_op jit(solution)/shard_map/reduce-window.14
  188.1 2.0 fusion.86
  190.9 1.7 copy.127
  192.5 1.4 convolution_add_fusion.13
  195.2 1.2 convolution_add_fusion.11
  202.9 1.3 fusion.27
  206.5 2.1 collective-permute-start.3
  208.7 1.8 collective-permute-done.3
  211.7 3.4 collective-permute-start.4
  215.2 6.5 %collective-permute-done.4 = f32[8,8320]{1,0:T(8,128)S(1)} collective-permute-done((f32[8,8320]{1,0:T(8,128)}, f32[8,8320]{1,0:T(8,128)S(1)}, u32[]{:S(2)}, u32[]{:S(2)}) %collective-permute-start.4) | collective-permute-done | bytes 266272 | tf_op jit(solution)/shard_map/ppermute | solution.py:41
  222.7 4.0 collective-permute-start.5
  226.8 11.9 %collective-permute-done.5 = f32[8,8320]{1,0:T(8,128)} collective-permute-done((f32[8,8320]{1,0:T(8,128)}, f32[8,8320]{1,0:T(8,128)}, u32[]{:S(2)}, u32[]{:S(2)}) %collective-permute-start.5) | collective-permute-done | bytes 266272 | tf_op jit(solution)/shard_map/ppermute | solution.py:41
  241.3 7.1 %collective-permute-start.6 = (f32[8,8320]{1,0:T(8,128)}, f32[8,8320]{1,0:T(8,128)}, u32[]{:S(2)}, u32[]{:S(2)}) collective-permute-start(f32[8,8320]{1,0:T(8,128)} %pad_maximum_fusion.3), channel_id=1, source_target_pairs={{0,64},{8,72},{16,80},{24,88},{32,96},{40,104},{48,112},{56,120},{... | collective-permute-start | bytes 798728 | tf_op jit(solution)/shard_map/ppermute | solution.py:41
  248.4 8.2 %collective-permute-done.6 = f32[8,8320]{1,0:T(8,128)} collective-permute-done((f32[8,8320]{1,0:T(8,128)}, f32[8,8320]{1,0:T(8,128)}, u32[]{:S(2)}, u32[]{:S(2)}) %collective-permute-start.6) | collective-permute-done | bytes 266272 | tf_op jit(solution)/shard_map/ppermute | solution.py:41
  259.2 7.2 %collective-permute-start.7 = (f32[8,8320]{1,0:T(8,128)}, f32[8,8320]{1,0:T(8,128)}, u32[]{:S(2)}, u32[]{:S(2)}) collective-permute-start(f32[8,8320]{1,0:T(8,128)} %pad_maximum_fusion.4), channel_id=1, source_target_pairs={{0,128},{8,136},{16,144},{24,152},{32,160},{40,168},{48,176},{56,1... | collective-permute-start | bytes 798728 | tf_op jit(solution)/shard_map/ppermute | solution.py:41
  267.9 3.5 collective-permute-done.7
  273.3 3.2 collective-permute-start.8
  276.7 12.4 %collective-permute-done.8 = f32[8,8320]{1,0:T(8,128)S(1)} collective-permute-done((f32[8,8320]{1,0:T(8,128)S(1)}, f32[8,8320]{1,0:T(8,128)S(1)}, u32[]{:S(2)}, u32[]{:S(2)}) %collective-permute-start.8) | collective-permute-done | bytes 266272 | tf_op jit(solution)/shard_map/ppermute | solution.py:41
  289.2 1.3 add_select_fusion
  290.5 3.4 collective-permute-start.9
  293.9 12.4 %reshape.518 = bf16[2048,1288]{1,0:T(8,128)(2,1)} reshape(bf16[64,322,128]{2,1,0:T(8,128)(2,1)} %all-gather.3.cloned.1.call-done) | data formatting | bytes 10551296 | tf_op jit(solution)/shard_map/reshape | solution.py:206
  306.4 2.3 fusion.12
  308.6 1.3 select_bitcast_fusion.5
  312.7 2.2 fusion.22
  316.2 3.1 multiply_reduce_fusion.1
  320.4 2.5 reduce-window.44
  324.7 3.4 fusion
  328.1 2.9 reshape.536
  331.0 1.5 copy.209
  332.5 3.8 gather_fusion.1
  336.3 2.9 copy_select_fusion
  340.4 4.6 %collective-permute-start.13 = (f32[256,4,256]{2,0,1:T(8,128)}, f32[256,4,256]{2,0,1:T(8,128)}, u32[]{:S(2)}, u32[]{:S(2)}) collective-permute-start(f32[256,4,256]{2,0,1:T(8,128)} %select_bitcast_fusion), channel_id=1, source_target_pairs={{0,1},{1,0},{2,3},{3,2},{4,5},{5,4},{6,7},{7,6},{8,11},{9,10},{10,... | collective-permute-start | bytes 3145736 | tf_op jit(solution)/shard_map/ppermute | solution.py:85
  345.0 2.1 fusion.90
  347.1 3.7 gather_fusion
  350.8 1.9 bitcast_select_fusion
  352.7 1.3 copy-done
  355.2 1.9 collective-permute-start.10
  357.5 1.6 bitcast_add_fusion
  359.2 3.9 collective-permute-start.14
  363.1 14.8 %collective-permute-done.10 = f32[256,4,256]{2,0,1:T(8,128)} collective-permute-done((f32[256,4,256]{2,0,1:T(8,128)}, f32[256,4,256]{2,0,1:T(8,128)}, u32[]{:S(2)}, u32[]{:S(2)}) %collective-permute-start.10) | collective-permute-done | bytes 1048608 | tf_op jit(solution)/shard_map/ppermute | solution.py:85
  377.8 1.4 bitcast_add_fusion.1
  380.2 1.9 collective-permute-start.11
  382.3 8.0 %collective-permute-start.15 = (f32[256,1,256]{2,0,1:T(8,128)S(1)}, f32[256,1,256]{2,0,1:T(8,128)S(1)}, u32[]{:S(2)}, u32[]{:S(2)}) collective-permute-start(f32[256,1,256]{2,0,1:T(8,128)S(1)} %select_bitcast_fusion.4), channel_id=1, source_target_pairs={{0,4},{1,5},{2,6},{3,7},{4,0},{5,1},{6,2},{7,3},{8,12},{9,13},{10,... | collective-permute-start | bytes 786440 | tf_op jit(solution)/shard_map/ppermute | solution.py:85
  390.3 7.5 %collective-permute-done.11 = f32[256,2,256]{2,0,1:T(8,128)} collective-permute-done((f32[256,2,256]{2,0,1:T(8,128)}, f32[256,2,256]{2,0,1:T(8,128)}, u32[]{:S(2)}, u32[]{:S(2)}) %collective-permute-start.11) | collective-permute-done | bytes 524320 | tf_op jit(solution)/shard_map/ppermute | solution.py:85
  399.0 7.2 %collective-permute-start.12 = (f32[256,1,256]{2,0,1:T(8,128)S(1)}, f32[256,1,256]{2,0,1:T(8,128)S(1)}, u32[]{:S(2)}, u32[]{:S(2)}) collective-permute-start(f32[256,1,256]{2,0,1:T(8,128)S(1)} %select_bitcast_fusion.6), channel_id=1, source_target_pairs={{0,4},{1,5},{2,6},{3,7},{4,0},{5,1},{6,2},{7,3},{8,12},{9,13},{10,... | collective-permute-start | bytes 786440 | tf_op jit(solution)/shard_map/ppermute | solution.py:85
  406.9 7.7 %collective-permute-done.12 = f32[256,1,256]{2,0,1:T(8,128)S(1)} collective-permute-done((f32[256,1,256]{2,0,1:T(8,128)S(1)}, f32[256,1,256]{2,0,1:T(8,128)S(1)}, u32[]{:S(2)}, u32[]{:S(2)}) %collective-permute-start.12) | collective-permute-done | bytes 262176 | tf_op jit(solution)/shard_map/ppermute | solution.py:85
  (182 shorter events, 47.5 us)
Async XLA Ops:
  7.2 131.6 %all-gather.3.cloned.1.call-start = ((), (), s32[]{:S(2)}) async-start(), calls=%async_computation | async-start | bytes 5457920 | tf_op jit(solution)/shard_map/all_gather | solution.py:204
  11.5 16.8 %collective-permute-start = (bf16[256,512]{1,0:T(8,128)(2,1)S(1)}, bf16[256,512]{1,0:T(8,128)(2,1)S(1)}, u32[]{:S(2)}, u32[]{:S(2)}) collective-permute-start(bf16[256,512]{1,0:T(8,128)(2,1)S(1)} %constant_dynamic-update-slice_fusion), channel_id=1, source_target_pairs={{0,4},{1,5},{2,6},{3,7},{4,0},{5,1},{6,2},{7,3},{8,12},{9,13},{10,... | collective-permute-start | bytes 786440 | tf_op jit(solution)/shard_map/ppermute | solution.py:180
  28.5 11.4 %collective-permute-start.1 = (bf16[512,512]{1,0:T(8,128)(2,1)S(1)}, bf16[512,512]{1,0:T(8,128)(2,1)S(1)}, u32[]{:S(2)}, u32[]{:S(2)}) collective-permute-start(bf16[512,512]{1,0:T(8,128)(2,1)S(1)} %maximum_select_fusion.2), channel_id=1, source_target_pairs={{0,2},{1,3},{2,0},{3,1},{4,6},{5,7},{6,4},{7,5},{8,10},{9,11},{10,... | collective-permute-start | bytes 1572872 | tf_op jit(solution)/shard_map/ppermute | solution.py:180
  40.4 26.0 %collective-permute-start.2 = (bf16[1024,512]{1,0:T(8,128)(2,1)S(1)}, bf16[1024,512]{1,0:T(8,128)(2,1)S(1)}, u32[]{:S(2)}, u32[]{:S(2)}) collective-permute-start(bf16[1024,512]{1,0:T(8,128)(2,1)S(1)} %maximum_select_fusion.1), channel_id=1, source_target_pairs={{0,1},{1,0},{2,3},{3,2},{4,5},{5,4},{6,7},{7,6},{8,9},{9,8},{10,11... | collective-permute-start | bytes 3145736 | tf_op jit(solution)/shard_map/ppermute | solution.py:180
  166.0 5.6 %copy-start.4 = (bf16[256,1288]{1,0:T(8,128)(2,1)}, bf16[256,1288]{1,0:T(8,128)(2,1)S(1)}, u32[]{:S(2)}) copy-start(bf16[256,1288]{1,0:T(8,128)(2,1)S(1)} %slice.351) | copy-start | bytes 1978372
  166.0 3.0 copy-start.9
  167.6 1.7 copy-start.8
  169.1 1.1 copy-start.7
  169.4 1.2 copy-start.6
  170.2 1.2 copy-start.5
  171.3 1.5 copy-start.22
  171.3 1.5 copy-start.25
  172.0 0.9 copy-start.14
  172.0 21.9 %copy-start.10 = (bf16[256,776]{0,1:T(8,128)(2,1)}, bf16[256,776]{0,1:T(8,128)(2,1)S(1)}, u32[]{:S(2)}) copy-start(bf16[256,776]{0,1:T(8,128)(2,1)S(1)} %get-tuple-element.227) | copy-start | bytes 1191940
  185.9 8.0 %copy-start.20 = (f32[8,2]{0,1:T(2,128)}, f32[8,2]{0,1:T(2,128)S(1)}, u32[]{:S(2)}) copy-start(f32[8,2]{0,1:T(2,128)S(1)} %slice.359) | copy-start | bytes 196
  201.3 9.3 %copy-start.24 = (f32[8]{0:T(128)S(1)}, f32[8]{0:T(128)}, u32[]{:S(2)}) copy-start(f32[8]{0:T(128)} %get-tuple-element.201) | copy-start | bytes 100
  206.5 4.0 collective-permute-start.3
  211.7 54.7 %copy-start.28 = (s32[8]{0:T(128)S(1)}, s32[8]{0:T(128)}, u32[]{:S(2)}) copy-start(s32[8]{0:T(128)} %constant.154) | copy-start | bytes 100
  211.7 55.3 %copy-start.27 = (f32[8]{0:T(128)S(1)}, f32[8]{0:T(128)}, u32[]{:S(2)}) copy-start(f32[8]{0:T(128)} %param.17) | copy-start | bytes 100
  211.7 10.0 %collective-permute-start.4 = (f32[8,8320]{1,0:T(8,128)}, f32[8,8320]{1,0:T(8,128)S(1)}, u32[]{:S(2)}, u32[]{:S(2)}) collective-permute-start(f32[8,8320]{1,0:T(8,128)} %pad_maximum_fusion.1), channel_id=1, source_target_pairs={{0,16},{8,24},{16,0},{24,8},{32,48},{40,56},{48,32},{56,40},{64,80... | collective-permute-start | bytes 798728 | tf_op jit(solution)/shard_map/ppermute | solution.py:41
  222.7 16.0 %collective-permute-start.5 = (f32[8,8320]{1,0:T(8,128)}, f32[8,8320]{1,0:T(8,128)}, u32[]{:S(2)}, u32[]{:S(2)}) collective-permute-start(f32[8,8320]{1,0:T(8,128)} %pad_maximum_fusion.2), channel_id=1, source_target_pairs={{0,32},{8,40},{16,48},{24,56},{32,0},{40,8},{48,16},{56,24},{64,96... | collective-permute-start | bytes 798728 | tf_op jit(solution)/shard_map/ppermute | solution.py:41
  241.3 15.3 %collective-permute-start.6 = (f32[8,8320]{1,0:T(8,128)}, f32[8,8320]{1,0:T(8,128)}, u32[]{:S(2)}, u32[]{:S(2)}) collective-permute-start(f32[8,8320]{1,0:T(8,128)} %pad_maximum_fusion.3), channel_id=1, source_target_pairs={{0,64},{8,72},{16,80},{24,88},{32,96},{40,104},{48,112},{56,120},{... | collective-permute-start | bytes 798728 | tf_op jit(solution)/shard_map/ppermute | solution.py:41
  258.4 35.4 %copy-start.21 = (f32[8,2]{0,1:T(2,128)S(1)}, f32[8,2]{0,1:T(2,128)}, u32[]{:S(2)}) copy-start(f32[8,2]{0,1:T(2,128)} %copy-done.20) | copy-start | bytes 196
  259.2 12.1 %collective-permute-start.7 = (f32[8,8320]{1,0:T(8,128)}, f32[8,8320]{1,0:T(8,128)}, u32[]{:S(2)}, u32[]{:S(2)}) collective-permute-start(f32[8,8320]{1,0:T(8,128)} %pad_maximum_fusion.4), channel_id=1, source_target_pairs={{0,128},{8,136},{16,144},{24,152},{32,160},{40,168},{48,176},{56,1... | collective-permute-start | bytes 798728 | tf_op jit(solution)/shard_map/ppermute | solution.py:41
  273.3 15.9 %collective-permute-start.8 = (f32[8,8320]{1,0:T(8,128)S(1)}, f32[8,8320]{1,0:T(8,128)S(1)}, u32[]{:S(2)}, u32[]{:S(2)}) collective-permute-start(f32[8,8320]{1,0:T(8,128)S(1)} %pad_maximum_fusion.5), channel_id=1, source_target_pairs={{0,256},{8,264},{16,272},{24,280},{32,288},{40,296},{48,304},{56,3... | collective-permute-start | bytes 798728 | tf_op jit(solution)/shard_map/ppermute | solution.py:41
  290.4 15.9 %copy-start.12 = (f32[8,8192]{1,0:T(8,128)}, f32[8,8192]{1,0:T(8,128)S(1)}, u32[]{:S(2)}) copy-start(f32[8,8192]{1,0:T(8,128)S(1)} %add_select_fusion) | copy-start | bytes 786436
  290.5 18.2 %collective-permute-start.9 = (f32[8,8192]{1,0:T(8,128)S(1)}, f32[8,8192]{1,0:T(8,128)}, u32[]{:S(2)}, u32[]{:S(2)}) collective-permute-start(f32[8,8192]{1,0:T(8,128)S(1)} %add_select_fusion), channel_id=1, source_target_pairs={{0,8},{8,0},{16,24},{24,16},{32,40},{40,32},{48,56},{56,48},{64,72... | collective-permute-start | bytes 786440 | tf_op jit(solution)/shard_map/ppermute | solution.py:50
  306.4 2.3 copy-start.13
  306.4 3.6 copy-start.23
  308.6 4.0 copy-start.19
  312.2 2.6 copy-start.17
  316.1 6.9 %copy-start.15 = (f32[256,8,64]{0,2,1:T(8,128)S(1)}, f32[256,8,64]{0,2,1:T(8,128)}, u32[]{:S(2)}) copy-start(f32[256,8,64]{0,2,1:T(8,128)} %fusion.12) | copy-start | bytes 1572868
  316.2 6.9 %copy-start.18 = (f32[256,8]{0,1:T(8,128)S(1)}, f32[256,8]{0,1:T(8,128)}, u32[]{:S(2)}) copy-start(f32[256,8]{0,1:T(8,128)} %get-tuple-element.199) | copy-start | bytes 24580
  319.2 4.5 %copy-start.26 = (f32[8]{0:T(128)S(1)}, f32[8]{0:T(128)}, u32[]{:S(2)}) copy-start(f32[8]{0:T(128)} %param.15) | copy-start | bytes 100
  319.2 5.3 %copy-start.11 = (bf16[256,776]{0,1:T(8,128)(2,1)S(1)}, bf16[256,776]{0,1:T(8,128)(2,1)}, u32[]{:S(2)}) copy-start(bf16[256,776]{0,1:T(8,128)(2,1)} %copy-done.10) | copy-start | bytes 1191940
  319.6 4.9 %copy-start.16 = (f32[256,8,64]{0,2,1:T(8,128)S(1)}, f32[256,8,64]{0,2,1:T(8,128)}, u32[]{:S(2)}) copy-start(f32[256,8,64]{0,2,1:T(8,128)} %get-tuple-element.213) | copy-start | bytes 1572868
  339.2 5.8 %slice-start = ((bf16[2048,1288]{1,0:T(8,128)(2,1)}), bf16[2048,512]{1,0:T(8,128)(2,1)S(1)}, s32[]{:S(2)}) async-start(bf16[2048,1288]{1,0:T(8,128)(2,1)} %reshape.518), calls=%async_computation.1 | async-start | bytes 4194304 | tf_op jit(solution)/shard_map/slice | solution.py:243
  340.4 17.1 %collective-permute-start.13 = (f32[256,4,256]{2,0,1:T(8,128)}, f32[256,4,256]{2,0,1:T(8,128)}, u32[]{:S(2)}, u32[]{:S(2)}) collective-permute-start(f32[256,4,256]{2,0,1:T(8,128)} %select_bitcast_fusion), channel_id=1, source_target_pairs={{0,1},{1,0},{2,3},{3,2},{4,5},{5,4},{6,7},{7,6},{8,11},{9,10},{10,... | collective-permute-start | bytes 3145736 | tf_op jit(solution)/shard_map/ppermute | solution.py:85
  352.7 1.3 copy-start
  355.2 22.7 %collective-permute-start.10 = (f32[256,4,256]{2,0,1:T(8,128)}, f32[256,4,256]{2,0,1:T(8,128)}, u32[]{:S(2)}, u32[]{:S(2)}) collective-permute-start(f32[256,4,256]{2,0,1:T(8,128)} %select_bitcast_fusion.1), channel_id=1, source_target_pairs={{0,1},{1,0},{2,3},{3,2},{4,5},{5,4},{6,7},{7,6},{8,11},{9,10},{10,... | collective-permute-start | bytes 3145736 | tf_op jit(solution)/shard_map/ppermute | solution.py:85
  357.1 20.8 %copy-start.1 = (f32[256,8,256]{2,0,1:T(8,128)S(1)}, f32[256,8,256]{2,0,1:T(8,128)}, u32[]{:S(2)}) copy-start(f32[256,8,256]{2,0,1:T(8,128)} %copy-done) | copy-start | bytes 6291460
  359.1 20.2 %copy-start.2 = (f32[256,4,256]{2,0,1:T(8,128)}, f32[256,4,256]{2,0,1:T(8,128)S(1)}, u32[]{:S(2)}) copy-start(f32[256,4,256]{2,0,1:T(8,128)S(1)} %bitcast_add_fusion) | copy-start | bytes 3145732
  359.2 22.9 %collective-permute-start.14 = (f32[256,2,256]{2,0,1:T(8,128)S(1)}, f32[256,2,256]{2,0,1:T(8,128)S(1)}, u32[]{:S(2)}, u32[]{:S(2)}) collective-permute-start(f32[256,2,256]{2,0,1:T(8,128)S(1)} %select_bitcast_fusion.2), channel_id=1, source_target_pairs={{0,2},{1,3},{2,0},{3,1},{4,6},{5,7},{6,4},{7,5},{8,10},{9,11},{10,... | collective-permute-start | bytes 1572872 | tf_op jit(solution)/shard_map/ppermute | solution.py:85
  379.3 2.8 copy-start.3
  380.2 17.6 %collective-permute-start.11 = (f32[256,2,256]{2,0,1:T(8,128)}, f32[256,2,256]{2,0,1:T(8,128)}, u32[]{:S(2)}, u32[]{:S(2)}) collective-permute-start(f32[256,2,256]{2,0,1:T(8,128)} %select_bitcast_fusion.3), channel_id=1, source_target_pairs={{0,2},{1,3},{2,0},{3,1},{4,6},{5,7},{6,4},{7,5},{8,10},{9,11},{10,... | collective-permute-start | bytes 1572872 | tf_op jit(solution)/shard_map/ppermute | solution.py:85
  382.3 23.9 %collective-permute-start.15 = (f32[256,1,256]{2,0,1:T(8,128)S(1)}, f32[256,1,256]{2,0,1:T(8,128)S(1)}, u32[]{:S(2)}, u32[]{:S(2)}) collective-permute-start(f32[256,1,256]{2,0,1:T(8,128)S(1)} %select_bitcast_fusion.4), channel_id=1, source_target_pairs={{0,4},{1,5},{2,6},{3,7},{4,0},{5,1},{6,2},{7,3},{8,12},{9,13},{10,... | collective-permute-start | bytes 786440 | tf_op jit(solution)/shard_map/ppermute | solution.py:85
  399.0 15.7 %collective-permute-start.12 = (f32[256,1,256]{2,0,1:T(8,128)S(1)}, f32[256,1,256]{2,0,1:T(8,128)S(1)}, u32[]{:S(2)}, u32[]{:S(2)}) collective-permute-start(f32[256,1,256]{2,0,1:T(8,128)S(1)} %select_bitcast_fusion.6), channel_id=1, source_target_pairs={{0,4},{1,5},{2,6},{3,7},{4,0},{5,1},{6,2},{7,3},{8,12},{9,13},{10,... | collective-permute-start | bytes 786440 | tf_op jit(solution)/shard_map/ppermute | solution.py:85
Sparse Core Ops, SparseCore 0:
  10.7 127.9 all-gather.2

commit v13 on v11

--- a/solution.py
+++ b/solution.py
@@ -206,15 +206,17 @@
     pieces = doubled_rows(
         jnp.concatenate([tokens, cotangent], axis=1), "tp", list(reversed(range(bits)))
     )
-    projected = None
-    d_flat = None
-    for k in range(devices):
-        block = w_all[k * width : (k + 1) * width]
-        piece = pieces[k * rows : (k + 1) * rows]
-        term = jnp.dot(piece[:, :width], block[:, out_cols:], preferred_element_type=jnp.float32)
-        projected = term if projected is None else projected + term
-        term = jnp.dot(piece[:, width:], block[:, :out_cols], preferred_element_type=jnp.float32)
-        d_flat = term if d_flat is None else d_flat + term
+    stacked = pieces.reshape(devices, rows, 2 * width)
+    w_blocks = w_all.reshape(devices, width, w_all.shape[1])
+    both_dims = (((0, 2), (0, 1)), ((), ()))
+    projected = lax.dot_general(
+        stacked[:, :, :width], w_blocks[:, :, out_cols:], both_dims,
+        preferred_element_type=jnp.float32,
+    )
+    d_flat = lax.dot_general(
+        stacked[:, :, width:], w_blocks[:, :, :out_cols], both_dims,
+        preferred_element_type=jnp.float32,
+    )
     values = projected[:, :inner].astype(jnp.bfloat16)
     pairs = projected[:, inner : inner + pair_cols].astype(jnp.bfloat16)
     pre_step = projected[:, inner + pair_cols :] + dt_bias[None, :]

time: 371 us -> 375 us (1.011)
  other arithmetic: 32.3 us -> 42.4 us
  matrix products: 35.3 us -> 26.6 us
  waiting for transfers between devices: 179 us -> 183 us
    dot_general x16 -> x2, matrix products: 19.2 us -> 6.04 us  [the longest x1 3.52 us: per_device(): lax.dot_general(stacked[:, :, :width], w_blocks[:, :, out_cols:], both_di...]
    ppermute x6, waiting for transfers between devices: 26 us -> 32.1 us  [scattered_sum(): blocks = keep + lax.ppermute(send, (rows_axis, axis), pairs)]
  transfers between devices with their start and end apart: 17 -> 17, of which waited for: 13 -> 15; matrix products, arithmetic and copies ran while one was open for 4% -> 6% of each run, Pallas kernels for 0% -> 0%
where the time goes in v13:
time: 375 us; the launch traced here: 373 us
  waiting for transfers between devices  183 us (49%)
  starting transfers between devices  82.5 us (22%)
  other arithmetic  42.4 us (11%)
  matrix products  26.6 us (7%)
  local copies, waits for them, and re-layouts  24.6 us (7%)
  between operations  14.8 us (4%)
    all_gather x1, waiting for transfers between devices, per_device(): lax.all_gather(jnp.concatenate([w_out.T, w_in, w_bc, w_dt], axis=1), 'ctx...  72.3 us
    ppermute x5, waiting for transfers between devices, both_carries(): got = lax.ppermute(message, axis, [(i, i ^ bit) for i in range(devices)])  40.3 us
    ppermute x3, waiting for transfers between devices, doubled_rows(): other = lax.ppermute(x, axis, [(i, i ^ bit) for i in range(devices)])  36 us
    ppermute x6, starting transfers between devices, scattered_sum(): blocks = keep + lax.ppermute(send, (rows_axis, axis), pairs)  34 us
    ppermute x6, waiting for transfers between devices, scattered_sum(): blocks = keep + lax.ppermute(send, (rows_axis, axis), pairs)  32.1 us
    ppermute x5, starting transfers between devices, both_carries(): got = lax.ppermute(message, axis, [(i, i ^ bit) for i in range(devices)])  25.1 us
    ppermute x3, starting transfers between devices, doubled_rows(): other = lax.ppermute(x, axis, [(i, i ^ bit) for i in range(devices)])  18.1 us
    dot_general x3, matrix products, ssd_advance(): inside = jnp.einsum('hts,shp->thp', scores * weight, inputs, precision=HIGH)  8.82 us
  transfers between devices with their start and end apart: 17, of which 15 were waited for; matrix products, arithmetic and copies ran while one was open for 6% of the time, Pallas kernels for 0%

profile of v13, /device:TPU:1, one launch (start us, length us, event | category | flops | bytes accessed | tf_op | source)
XLA Modules:
  0.0 373.5 jit_solution(17041903011691746726)
XLA Ops:
  8.0 1.4 pad_maximum_fusion.7
  9.4 0.9 constant_dynamic-update-slice_fusion.1
  11.3 8.3 %collective-permute-start = (bf16[256,512]{1,0:T(8,128)(2,1)S(1)}, bf16[256,512]{1,0:T(8,128)(2,1)S(1)}, u32[]{:S(2)}, u32[]{:S(2)}) collective-permute-start(bf16[256,512]{1,0:T(8,128)(2,1)S(1)} %constant_dynamic-update-slice_fusion), channel_id=1, source_target_pairs={{0,4},{1,5},{2,6},{3,7},{4,0},{5,1},{6,2},{7,3},{8,12},{9,13},{10,... | collective-permute-start | bytes 786440 | tf_op jit(solution)/shard_map/ppermute | solution.py:180
  19.6 8.5 %collective-permute-done = bf16[256,512]{1,0:T(8,128)(2,1)S(1)} collective-permute-done((bf16[256,512]{1,0:T(8,128)(2,1)S(1)}, bf16[256,512]{1,0:T(8,128)(2,1)S(1)}, u32[]{:S(2)}, u32[]{:S(2)}) %collective-permute-start) | collective-permute-done | bytes 262176 | tf_op jit(solution)/shard_map/ppermute | solution.py:180
  28.3 3.7 collective-permute-start.1
  32.0 7.7 %collective-permute-done.1 = bf16[512,512]{1,0:T(8,128)(2,1)S(1)} collective-permute-done((bf16[512,512]{1,0:T(8,128)(2,1)S(1)}, bf16[512,512]{1,0:T(8,128)(2,1)S(1)}, u32[]{:S(2)}, u32[]{:S(2)}) %collective-permute-start.1) | collective-permute-done | bytes 524320 | tf_op jit(solution)/shard_map/ppermute | solution.py:180
  40.2 6.1 %collective-permute-start.2 = (bf16[1024,512]{1,0:T(8,128)(2,1)S(1)}, bf16[1024,512]{1,0:T(8,128)(2,1)S(1)}, u32[]{:S(2)}, u32[]{:S(2)}) collective-permute-start(bf16[1024,512]{1,0:T(8,128)(2,1)S(1)} %maximum_select_fusion.1), channel_id=1, source_target_pairs={{0,1},{1,0},{2,3},{3,2},{4,5},{5,4},{6,7},{7,6},{8,9},{9,8},{10,11... | collective-permute-start | bytes 3145736 | tf_op jit(solution)/shard_map/ppermute | solution.py:180
  46.3 19.8 %collective-permute-done.2 = bf16[1024,512]{1,0:T(8,128)(2,1)S(1)} collective-permute-done((bf16[1024,512]{1,0:T(8,128)(2,1)S(1)}, bf16[1024,512]{1,0:T(8,128)(2,1)S(1)}, u32[]{:S(2)}, u32[]{:S(2)}) %collective-permute-start.2) | collective-permute-done | bytes 1048608 | tf_op jit(solution)/shard_map/ppermute | solution.py:180
  66.9 72.3 %all-gather.2.cloned.1.call-done = bf16[2048,1288]{1,0:T(8,128)(2,1)} async-done(((bf16[32,1288]{1,0:T(8,128)(2,1)}), bf16[2048,1288]{1,0:T(8,128)(2,1)}) %all-gather.2.cloned.1.call-update) | async-done | bytes 5275664 | tf_op jit(solution)/shard_map/all_gather | solution.py:202
  139.2 2.5 fusion.4
  141.8 3.5 fusion.121
  150.0 2.1 collective-permute-start.3
  152.1 1.8 collective-permute-done.3
  156.1 3.0 collective-permute-start.4
  159.1 6.9 %collective-permute-done.4 = f32[8,8320]{1,0:T(8,128)} collective-permute-done((f32[8,8320]{1,0:T(8,128)}, f32[8,8320]{1,0:T(8,128)}, u32[]{:S(2)}, u32[]{:S(2)}) %collective-permute-start.4) | collective-permute-done | bytes 266272 | tf_op jit(solution)/shard_map/ppermute | solution.py:41
  167.5 1.1 add_select_fusion.7
  169.4 4.0 %collective-permute-start.5 = (f32[8,8320]{1,0:T(8,128)}, f32[8,8320]{1,0:T(8,128)}, u32[]{:S(2)}, u32[]{:S(2)}) collective-permute-start(f32[8,8320]{1,0:T(8,128)} %pad_maximum_fusion.2), channel_id=1, source_target_pairs={{0,32},{8,40},{16,48},{24,56},{32,0},{40,8},{48,16},{56,24},{64,96... | collective-permute-start | bytes 798728 | tf_op jit(solution)/shard_map/ppermute | solution.py:41
  173.3 12.3 %collective-permute-done.5 = f32[8,8320]{1,0:T(8,128)} collective-permute-done((f32[8,8320]{1,0:T(8,128)}, f32[8,8320]{1,0:T(8,128)}, u32[]{:S(2)}, u32[]{:S(2)}) %collective-permute-start.5) | collective-permute-done | bytes 266272 | tf_op jit(solution)/shard_map/ppermute | solution.py:41
  187.0 1.1 add_select_fusion.6
  188.9 6.8 %collective-permute-start.6 = (f32[8,8320]{1,0:T(8,128)}, f32[8,8320]{1,0:T(8,128)}, u32[]{:S(2)}, u32[]{:S(2)}) collective-permute-start(f32[8,8320]{1,0:T(8,128)} %pad_maximum_fusion.3), channel_id=1, source_target_pairs={{0,64},{8,72},{16,80},{24,88},{32,96},{40,104},{48,112},{56,120},{... | collective-permute-start | bytes 798728 | tf_op jit(solution)/shard_map/ppermute | solution.py:41
  195.7 9.0 %collective-permute-done.6 = f32[8,8320]{1,0:T(8,128)} collective-permute-done((f32[8,8320]{1,0:T(8,128)}, f32[8,8320]{1,0:T(8,128)}, u32[]{:S(2)}, u32[]{:S(2)}) %collective-permute-start.6) | collective-permute-done | bytes 266272 | tf_op jit(solution)/shard_map/ppermute | solution.py:41
  206.1 1.1 add_select_fusion.5
  208.0 6.8 %collective-permute-start.7 = (f32[8,8320]{1,0:T(8,128)}, f32[8,8320]{1,0:T(8,128)}, u32[]{:S(2)}, u32[]{:S(2)}) collective-permute-start(f32[8,8320]{1,0:T(8,128)} %pad_maximum_fusion.4), channel_id=1, source_target_pairs={{0,128},{8,136},{16,144},{24,152},{32,160},{40,168},{48,176},{56,1... | collective-permute-start | bytes 798728 | tf_op jit(solution)/shard_map/ppermute | solution.py:41
  214.8 1.3 pad_clamp_fusion
  218.8 1.2 collective-permute-done.7
  221.4 1.1 add_select_fusion.4
  222.6 4.5 %collective-permute-start.8 = (f32[8,8320]{1,0:T(8,128)S(1)}, f32[8,8320]{1,0:T(8,128)S(1)}, u32[]{:S(2)}, u32[]{:S(2)}) collective-permute-start(f32[8,8320]{1,0:T(8,128)S(1)} %pad_maximum_fusion.5), channel_id=1, source_target_pairs={{0,256},{8,264},{16,272},{24,280},{32,288},{40,296},{48,304},{56,3... | collective-permute-start | bytes 798728 | tf_op jit(solution)/shard_map/ppermute | solution.py:41
  228.0 10.9 %collective-permute-done.8 = f32[8,8320]{1,0:T(8,128)S(1)} collective-permute-done((f32[8,8320]{1,0:T(8,128)S(1)}, f32[8,8320]{1,0:T(8,128)S(1)}, u32[]{:S(2)}, u32[]{:S(2)}) %collective-permute-start.8) | collective-permute-done | bytes 266272 | tf_op jit(solution)/shard_map/ppermute | solution.py:41
  238.9 1.4 add_select_fusion
  240.3 3.1 collective-permute-start.9
  244.2 3.1 slice.235
  247.3 2.3 fusion.19
  251.7 1.7 fusion.27
  255.1 1.3 fusion.33
  256.4 1.0 fusion.107
  258.2 1.1 convolution_bitcast_fusion.4
  259.3 3.8 %fusion.29 = (f32[8,256]{1,0:T(8,128)}, f32[8,256]{1,0:T(8,128)}, f32[256,256]{1,0:T(8,128)S(1)}) fusion(f32[8,256]{1,0:T(8,128)} %add_bitcast_fusion.1, f32[256,256]{1,0:T(8,128)} %fusion.107, pred[256,256]{1,0:T(8,128)(4,1)} %bitcast.328, f32[256,8,64]{0,2,1:T(8,128)S(1)} %bitcast.317, f32[256,8]{0,1:T(8,128)S(1)} %get-tuple-element.181, ...), kind=kOutput, calls=%fused_computation.34 | convolution fusion | flops 207155200 | bytes 1671168 | tf_op jit(solution)/shard_map/transpose(jvp())/while/body/eval_jaxpr/checkpoint/hts,shp->thp/dot_general | solution.py:108
  263.1 2.7 multiply_reduce_fusion.1
  267.5 2.5 reduce-window.44
  271.0 1.2 fusion.58
  272.2 3.3 fusion
  275.5 2.8 reshape.520
  278.4 1.5 copy.195
  281.5 3.7 gather_fusion.1
  285.2 2.1 gather_fusion
  287.3 2.0 bitcast_select_fusion
  289.4 1.1 select_bitcast_fusion.1
  290.5 4.0 %collective-permute-start.10 = (f32[256,4,256]{2,0,1:T(8,128)}, f32[256,4,256]{2,0,1:T(8,128)S(1)}, u32[]{:S(2)}, u32[]{:S(2)}) collective-permute-start(f32[256,4,256]{2,0,1:T(8,128)} %select_bitcast_fusion.1), channel_id=1, source_target_pairs={{0,1},{1,0},{2,3},{3,2},{4,5},{5,4},{6,7},{7,6},{8,11},{9,10},{10,... | collective-permute-start | bytes 3145736 | tf_op jit(solution)/shard_map/ppermute | solution.py:85
  295.2 1.2 select_bitcast_fusion
  296.4 2.8 collective-permute-start.13
  299.2 8.4 %collective-permute-done.10 = f32[256,4,256]{2,0,1:T(8,128)S(1)} collective-permute-done((f32[256,4,256]{2,0,1:T(8,128)}, f32[256,4,256]{2,0,1:T(8,128)S(1)}, u32[]{:S(2)}, u32[]{:S(2)}) %collective-permute-start.10) | collective-permute-done | bytes 1048608 | tf_op jit(solution)/shard_map/ppermute | solution.py:85
  307.6 1.7 bitcast_add_fusion.1
  309.3 1.0 select_bitcast_fusion.3
  310.3 3.0 collective-permute-start.11
  313.3 8.1 %collective-permute-done.13 = f32[256,4,256]{2,0,1:T(8,128)} collective-permute-done((f32[256,4,256]{2,0,1:T(8,128)}, f32[256,4,256]{2,0,1:T(8,128)}, u32[]{:S(2)}, u32[]{:S(2)}) %collective-permute-start.13) | collective-permute-done | bytes 1048608 | tf_op jit(solution)/shard_map/ppermute | solution.py:85
  321.3 1.4 bitcast_add_fusion
  322.9 2.8 collective-permute-start.14
  325.7 2.3 collective-permute-done.11
  328.0 1.1 fusion.54
  329.2 15.4 %collective-permute-start.12 = (f32[256,1,256]{2,0,1:T(8,128)S(1)}, f32[256,1,256]{2,0,1:T(8,128)S(1)}, u32[]{:S(2)}, u32[]{:S(2)}) collective-permute-start(f32[256,1,256]{2,0,1:T(8,128)S(1)} %select_bitcast_fusion.6), channel_id=1, source_target_pairs={{0,4},{1,5},{2,6},{3,7},{4,0},{5,1},{6,2},{7,3},{8,12},{9,13},{10,... | collective-permute-start | bytes 786440 | tf_op jit(solution)/shard_map/ppermute | solution.py:85
  344.6 1.1 fusion.55
  345.8 6.1 %collective-permute-start.15 = (f32[256,1,256]{2,0,1:T(8,128)S(1)}, f32[256,1,256]{2,0,1:T(8,128)S(1)}, u32[]{:S(2)}, u32[]{:S(2)}) collective-permute-start(f32[256,1,256]{2,0,1:T(8,128)S(1)} %select_bitcast_fusion.4), channel_id=1, source_target_pairs={{0,4},{1,5},{2,6},{3,7},{4,0},{5,1},{6,2},{7,3},{8,12},{9,13},{10,... | collective-permute-start | bytes 786440 | tf_op jit(solution)/shard_map/ppermute | solution.py:85
  351.9 8.1 %collective-permute-done.12 = f32[256,1,256]{2,0,1:T(8,128)S(1)} collective-permute-done((f32[256,1,256]{2,0,1:T(8,128)S(1)}, f32[256,1,256]{2,0,1:T(8,128)S(1)}, u32[]{:S(2)}, u32[]{:S(2)}) %collective-permute-start.12) | collective-permute-done | bytes 262176 | tf_op jit(solution)/shard_map/ppermute | solution.py:85
  360.6 5.3 %collective-permute-done.15 = f32[256,1,256]{2,0,1:T(8,128)S(1)} collective-permute-done((f32[256,1,256]{2,0,1:T(8,128)S(1)}, f32[256,1,256]{2,0,1:T(8,128)S(1)}, u32[]{:S(2)}, u32[]{:S(2)}) %collective-permute-start.15) | collective-permute-done | bytes 262176 | tf_op jit(solution)/shard_map/ppermute | solution.py:85
  (172 shorter events, 33.3 us)
Async XLA Ops:
  7.2 132.0 %all-gather.2.cloned.1.call-start = ((), (), s32[]{:S(2)}) async-start(), calls=%async_computation | async-start | bytes 5857280 | tf_op jit(solution)/shard_map/all_gather | solution.py:202
  11.3 16.8 %collective-permute-start = (bf16[256,512]{1,0:T(8,128)(2,1)S(1)}, bf16[256,512]{1,0:T(8,128)(2,1)S(1)}, u32[]{:S(2)}, u32[]{:S(2)}) collective-permute-start(bf16[256,512]{1,0:T(8,128)(2,1)S(1)} %constant_dynamic-update-slice_fusion), channel_id=1, source_target_pairs={{0,4},{1,5},{2,6},{3,7},{4,0},{5,1},{6,2},{7,3},{8,12},{9,13},{10,... | collective-permute-start | bytes 786440 | tf_op jit(solution)/shard_map/ppermute | solution.py:180
  28.3 11.4 %collective-permute-start.1 = (bf16[512,512]{1,0:T(8,128)(2,1)S(1)}, bf16[512,512]{1,0:T(8,128)(2,1)S(1)}, u32[]{:S(2)}, u32[]{:S(2)}) collective-permute-start(bf16[512,512]{1,0:T(8,128)(2,1)S(1)} %maximum_select_fusion.2), channel_id=1, source_target_pairs={{0,2},{1,3},{2,0},{3,1},{4,6},{5,7},{6,4},{7,5},{8,10},{9,11},{10,... | collective-permute-start | bytes 1572872 | tf_op jit(solution)/shard_map/ppermute | solution.py:180
  40.2 26.0 %collective-permute-start.2 = (bf16[1024,512]{1,0:T(8,128)(2,1)S(1)}, bf16[1024,512]{1,0:T(8,128)(2,1)S(1)}, u32[]{:S(2)}, u32[]{:S(2)}) collective-permute-start(bf16[1024,512]{1,0:T(8,128)(2,1)S(1)} %maximum_select_fusion.1), channel_id=1, source_target_pairs={{0,1},{1,0},{2,3},{3,2},{4,5},{5,4},{6,7},{7,6},{8,9},{9,8},{10,11... | collective-permute-start | bytes 3145736 | tf_op jit(solution)/shard_map/ppermute | solution.py:180
  141.7 3.6 copy-start.17
  141.7 3.6 copy-start.34
  145.3 1.0 copy-start.36
  145.5 2.3 copy-start.28
  146.9 0.6 copy-start.9
  147.1 0.6 copy-start.16
  147.2 1.2 copy-start.10
  150.0 4.0 %collective-permute-start.3 = (f32[8,16512]{1,0:T(8,128)}, f32[8,16512]{1,0:T(8,128)S(1)}, u32[]{:S(2)}, u32[]{:S(2)}) collective-permute-start(f32[8,16512]{1,0:T(8,128)} %pad_maximum_fusion), channel_id=1, source_target_pairs={{0,8},{8,0},{16,24},{24,16},{32,40},{40,32},{48,56},{56,48},{64,72... | collective-permute-start | bytes 1585160 | tf_op jit(solution)/shard_map/ppermute | solution.py:23
  154.7 0.6 copy-start.24
  154.7 11.3 %copy-start.26 = (f32[8]{0:T(128)}, f32[8]{0:T(128)S(1)}, u32[]{:S(2)}) copy-start(f32[8]{0:T(128)S(1)} %get-tuple-element.216) | copy-start | bytes 100
  154.7 12.8 %copy-start.30 = (f32[8]{0:T(128)}, f32[8]{0:T(128)S(1)}, u32[]{:S(2)}) copy-start(f32[8]{0:T(128)S(1)} %get-tuple-element.215) | copy-start | bytes 100
  156.1 9.9 %collective-permute-start.4 = (f32[8,8320]{1,0:T(8,128)}, f32[8,8320]{1,0:T(8,128)}, u32[]{:S(2)}, u32[]{:S(2)}) collective-permute-start(f32[8,8320]{1,0:T(8,128)} %pad_maximum_fusion.1), channel_id=1, source_target_pairs={{0,16},{8,24},{16,0},{24,8},{32,48},{40,56},{48,32},{56,40},{64,80... | collective-permute-start | bytes 798728 | tf_op jit(solution)/shard_map/ppermute | solution.py:41
  166.8 0.7 copy-start.22
  167.5 1.9 copy-start.29
  169.4 16.2 %collective-permute-start.5 = (f32[8,8320]{1,0:T(8,128)}, f32[8,8320]{1,0:T(8,128)}, u32[]{:S(2)}, u32[]{:S(2)}) collective-permute-start(f32[8,8320]{1,0:T(8,128)} %pad_maximum_fusion.2), channel_id=1, source_target_pairs={{0,32},{8,40},{16,48},{24,56},{32,0},{40,8},{48,16},{56,24},{64,96... | collective-permute-start | bytes 798728 | tf_op jit(solution)/shard_map/ppermute | solution.py:41
  186.4 0.7 copy-start.31
  187.0 1.9 copy-start.35
  188.9 15.8 %collective-permute-start.6 = (f32[8,8320]{1,0:T(8,128)}, f32[8,8320]{1,0:T(8,128)}, u32[]{:S(2)}, u32[]{:S(2)}) collective-permute-start(f32[8,8320]{1,0:T(8,128)} %pad_maximum_fusion.3), channel_id=1, source_target_pairs={{0,64},{8,72},{16,80},{24,88},{32,96},{40,104},{48,112},{56,120},{... | collective-permute-start | bytes 798728 | tf_op jit(solution)/shard_map/ppermute | solution.py:41
  205.5 0.7 copy-start.23
  206.1 1.9 copy-start.32
  208.0 11.9 %collective-permute-start.7 = (f32[8,8320]{1,0:T(8,128)}, f32[8,8320]{1,0:T(8,128)}, u32[]{:S(2)}, u32[]{:S(2)}) collective-permute-start(f32[8,8320]{1,0:T(8,128)} %pad_maximum_fusion.4), channel_id=1, source_target_pairs={{0,128},{8,136},{16,144},{24,152},{32,160},{40,168},{48,176},{56,1... | collective-permute-start | bytes 798728 | tf_op jit(solution)/shard_map/ppermute | solution.py:41
  220.7 0.7 copy-start.33
  222.6 16.3 %collective-permute-start.8 = (f32[8,8320]{1,0:T(8,128)S(1)}, f32[8,8320]{1,0:T(8,128)S(1)}, u32[]{:S(2)}, u32[]{:S(2)}) collective-permute-start(f32[8,8320]{1,0:T(8,128)S(1)} %pad_maximum_fusion.5), channel_id=1, source_target_pairs={{0,256},{8,264},{16,272},{24,280},{32,288},{40,296},{48,304},{56,3... | collective-permute-start | bytes 798728 | tf_op jit(solution)/shard_map/ppermute | solution.py:41
  240.3 9.3 %collective-permute-start.9 = (f32[8,8192]{1,0:T(8,128)S(1)}, f32[8,8192]{1,0:T(8,128)S(1)}, u32[]{:S(2)}, u32[]{:S(2)}) collective-permute-start(f32[8,8192]{1,0:T(8,128)S(1)} %add_select_fusion), channel_id=1, source_target_pairs={{0,8},{8,0},{16,24},{24,16},{32,40},{40,32},{48,56},{56,48},{64,72... | collective-permute-start | bytes 786440 | tf_op jit(solution)/shard_map/ppermute | solution.py:50
  244.2 3.1 copy-start.13
  247.3 2.3 copy-start.25
  247.3 2.3 copy-start.27
  247.3 2.7 copy-start.18
  247.3 4.4 %copy-start.11 = (f32[256,8]{0,1:T(8,128)S(1)}, f32[256,8]{0,1:T(8,128)}, u32[]{:S(2)}) copy-start(f32[256,8]{0,1:T(8,128)} %copy-done.10) | copy-start | bytes 24580
  251.7 2.9 copy-start.7
  253.9 0.7 copy-start.19
  259.3 3.8 %copy-start.6 = (f32[256,256]{1,0:T(8,128)S(1)}, f32[256,256]{1,0:T(8,128)}, u32[]{:S(2)}) copy-start(f32[256,256]{1,0:T(8,128)} %fusion.107) | copy-start | bytes 786436
  259.3 3.8 %copy-start.12 = (pred[1,256,256]{2,1,0:T(8,128)(4,1)S(1)}, pred[1,256,256]{2,1,0:T(8,128)(4,1)}, u32[]{:S(2)}) copy-start(pred[1,256,256]{2,1,0:T(8,128)(4,1)} %iota_compare_fusion) | copy-start | bytes 196612
  259.3 3.8 %copy-start.14 = (f32[256,8]{0,1:T(8,128)S(1)}, f32[256,8]{0,1:T(8,128)}, u32[]{:S(2)}) copy-start(f32[256,8]{0,1:T(8,128)} %subtract_exponential_fusion) | copy-start | bytes 24580
  259.3 3.8 %copy-start.21 = (f32[8,256]{1,0:T(8,128)S(1)}, f32[8,256]{1,0:T(8,128)}, u32[]{:S(2)}) copy-start(f32[8,256]{1,0:T(8,128)} %add_bitcast_fusion.1) | copy-start | bytes 24580
  263.1 3.3 copy-start.8
  263.1 3.3 copy-start.20
  265.8 0.7 copy-start.15
  278.4 2.3 copy-start.5
  287.3 7.2 %copy-start.4 = (f32[8,256,256]{2,1,0:T(8,128)S(1)}, f32[8,256,256]{2,1,0:T(8,128)}, u32[]{:S(2)}) copy-start(f32[8,256,256]{2,1,0:T(8,128)} %gather_fusion.1) | copy-start | bytes 6291460
  289.3 5.9 %copy-start = (f32[256,8,256]{2,0,1:T(8,128)}, f32[256,8,256]{2,0,1:T(8,128)S(1)}, u32[]{:S(2)}) copy-start(f32[256,8,256]{2,0,1:T(8,128)S(1)} %bitcast_select_fusion) | copy-start | bytes 6291460
  289.3 5.2 %copy-start.3 = (f32[256,4,2,256]{3,2,1,0:T(2,128)S(1)}, f32[256,4,2,256]{3,2,1,0:T(2,128)}, u32[]{:S(2)}) copy-start(f32[256,4,2,256]{3,2,1,0:T(2,128)} %reshape.520) | copy-start | bytes 6291460
  290.5 17.1 %collective-permute-start.10 = (f32[256,4,256]{2,0,1:T(8,128)}, f32[256,4,256]{2,0,1:T(8,128)S(1)}, u32[]{:S(2)}, u32[]{:S(2)}) collective-permute-start(f32[256,4,256]{2,0,1:T(8,128)} %select_bitcast_fusion.1), channel_id=1, source_target_pairs={{0,1},{1,0},{2,3},{3,2},{4,5},{5,4},{6,7},{7,6},{8,11},{9,10},{10,... | collective-permute-start | bytes 3145736 | tf_op jit(solution)/shard_map/ppermute | solution.py:85
  296.4 24.9 %collective-permute-start.13 = (f32[256,4,256]{2,0,1:T(8,128)}, f32[256,4,256]{2,0,1:T(8,128)}, u32[]{:S(2)}, u32[]{:S(2)}) collective-permute-start(f32[256,4,256]{2,0,1:T(8,128)} %select_bitcast_fusion), channel_id=1, source_target_pairs={{0,1},{1,0},{2,3},{3,2},{4,5},{5,4},{6,7},{7,6},{8,11},{9,10},{10,... | collective-permute-start | bytes 3145736 | tf_op jit(solution)/shard_map/ppermute | solution.py:85
  309.3 13.5 %copy-start.1 = (f32[256,4,256]{2,0,1:T(8,128)}, f32[256,4,256]{2,0,1:T(8,128)S(1)}, u32[]{:S(2)}) copy-start(f32[256,4,256]{2,0,1:T(8,128)S(1)} %bitcast_add_fusion.1) | copy-start | bytes 3145732
  310.3 17.7 %collective-permute-start.11 = (f32[256,2,256]{2,0,1:T(8,128)}, f32[256,2,256]{2,0,1:T(8,128)}, u32[]{:S(2)}, u32[]{:S(2)}) collective-permute-start(f32[256,2,256]{2,0,1:T(8,128)} %select_bitcast_fusion.3), channel_id=1, source_target_pairs={{0,2},{1,3},{2,0},{3,1},{4,6},{5,7},{6,4},{7,5},{8,10},{9,11},{10,... | collective-permute-start | bytes 1572872 | tf_op jit(solution)/shard_map/ppermute | solution.py:85
  322.8 5.2 %copy-start.2 = (f32[256,4,256]{2,0,1:T(8,128)S(1)}, f32[256,4,256]{2,0,1:T(8,128)}, u32[]{:S(2)}) copy-start(f32[256,4,256]{2,0,1:T(8,128)} %copy-done.1) | copy-start | bytes 3145732
  322.9 21.7 %collective-permute-start.14 = (f32[256,2,256]{2,0,1:T(8,128)S(1)}, f32[256,2,256]{2,0,1:T(8,128)}, u32[]{:S(2)}, u32[]{:S(2)}) collective-permute-start(f32[256,2,256]{2,0,1:T(8,128)S(1)} %select_bitcast_fusion.2), channel_id=1, source_target_pairs={{0,2},{1,3},{2,0},{3,1},{4,6},{5,7},{6,4},{7,5},{8,10},{9,11},{10,... | collective-permute-start | bytes 1572872 | tf_op jit(solution)/shard_map/ppermute | solution.py:85
  329.2 30.8 %collective-permute-start.12 = (f32[256,1,256]{2,0,1:T(8,128)S(1)}, f32[256,1,256]{2,0,1:T(8,128)S(1)}, u32[]{:S(2)}, u32[]{:S(2)}) collective-permute-start(f32[256,1,256]{2,0,1:T(8,128)S(1)} %select_bitcast_fusion.6), channel_id=1, source_target_pairs={{0,4},{1,5},{2,6},{3,7},{4,0},{5,1},{6,2},{7,3},{8,12},{9,13},{10,... | collective-permute-start | bytes 786440 | tf_op jit(solution)/shard_map/ppermute | solution.py:85
  345.8 20.1 %collective-permute-start.15 = (f32[256,1,256]{2,0,1:T(8,128)S(1)}, f32[256,1,256]{2,0,1:T(8,128)S(1)}, u32[]{:S(2)}, u32[]{:S(2)}) collective-permute-start(f32[256,1,256]{2,0,1:T(8,128)S(1)} %select_bitcast_fusion.4), channel_id=1, source_target_pairs={{0,4},{1,5},{2,6},{3,7},{4,0},{5,1},{6,2},{7,3},{8,12},{9,13},{10,... | collective-permute-start | bytes 786440 | tf_op jit(solution)/shard_map/ppermute | solution.py:85
Sparse Core Ops, SparseCore 0:
  10.7 128.4 all-gather.1

commit v14 on v11

--- a/solution.py
+++ b/solution.py
@@ -37,6 +37,14 @@
     before_m = jnp.zeros_like(total_m)
     bit = 2
     while bit < devices:
+        if 2 * bit >= devices:
+            wanted = [
+                (i, i ^ bit) for i in range(devices) if ((i & bit) != 0) == ((i & 1) != 0)
+            ]
+            got_m = lax.ppermute(total_m, axis, wanted)
+            flag = ((position & bit) != 0) != second
+            before_m = jnp.where(flag, before_a * got_m + before_m, before_m)
+            break
         message = jnp.concatenate([total_m, jnp.broadcast_to(total_a, (heads, 128))], axis=1)
         got = lax.ppermute(message, axis, [(i, i ^ bit) for i in range(devices)])
         got_m = got[:, :size]

time: 371 us -> 368 us (level)
    ppermute x5 -> x4, waiting for transfers between devices: 42.9 us -> 30.9 us  [both_carries(): got = lax.ppermute(message, axis, [(i, i ^ bit) for i in range(devices)])]
    ppermute x0 -> x1, waiting for transfers between devices: none -> 9.49 us  [both_carries(): got_m = lax.ppermute(total_m, axis, wanted)]
    ppermute x5 -> x4, starting transfers between devices: 25.4 us -> 20.7 us  [both_carries(): got = lax.ppermute(message, axis, [(i, i ^ bit) for i in range(devices)])]
where the time goes in v14:
time: 368 us; the launch traced here: 363 us
  waiting for transfers between devices  176 us (48%)
  starting transfers between devices  81.8 us (22%)
  matrix products  35.3 us (10%)
  other arithmetic  32.3 us (9%)
  local copies, waits for them, and re-layouts  22.1 us (6%)
  between operations  15 us (4%)
    all_gather x1, waiting for transfers between devices, per_device(): lax.all_gather(jnp.concatenate([w_out.T, w_in, w_bc, w_dt], axis=1), 'ctx...  72.3 us
    ppermute x6, starting transfers between devices, scattered_sum(): blocks = keep + lax.ppermute(send, (rows_axis, axis), pairs)  37 us
    ppermute x3, waiting for transfers between devices, doubled_rows(): other = lax.ppermute(x, axis, [(i, i ^ bit) for i in range(devices)])  36 us
    ppermute x4, waiting for transfers between devices, both_carries(): got = lax.ppermute(message, axis, [(i, i ^ bit) for i in range(devices)])  30.9 us
    ppermute x6, waiting for transfers between devices, scattered_sum(): blocks = keep + lax.ppermute(send, (rows_axis, axis), pairs)  25.6 us
    ppermute x4, starting transfers between devices, both_carries(): got = lax.ppermute(message, axis, [(i, i ^ bit) for i in range(devices)])  20.7 us
    ppermute x3, starting transfers between devices, doubled_rows(): other = lax.ppermute(x, axis, [(i, i ^ bit) for i in range(devices)])  18.1 us
    dot_general x8, matrix products, per_device(): jnp.dot(piece[:, width:], block[:, :out_cols], preferred_element_type=jnp...  10.3 us
  transfers between devices with their start and end apart: 17, of which 13 were waited for; matrix products, arithmetic and copies ran while one was open for 4% of the time, Pallas kernels for 0%

profile of v14, /device:TPU:1, one launch (start us, length us, event | category | flops | bytes accessed | tf_op | source)
XLA Modules:
  0.0 362.6 jit_solution(14436932147277387907)
XLA Ops:
  8.0 1.4 pad_maximum_fusion.6
  11.3 8.3 %collective-permute-start = (bf16[256,512]{1,0:T(8,128)(2,1)S(1)}, bf16[256,512]{1,0:T(8,128)(2,1)S(1)}, u32[]{:S(2)}, u32[]{:S(2)}) collective-permute-start(bf16[256,512]{1,0:T(8,128)(2,1)S(1)} %constant_dynamic-update-slice_fusion), channel_id=1, source_target_pairs={{0,4},{1,5},{2,6},{3,7},{4,0},{5,1},{6,2},{7,3},{8,12},{9,13},{10,... | collective-permute-start | bytes 786440 | tf_op jit(solution)/shard_map/ppermute | solution.py:188
  19.6 8.5 %collective-permute-done = bf16[256,512]{1,0:T(8,128)(2,1)S(1)} collective-permute-done((bf16[256,512]{1,0:T(8,128)(2,1)S(1)}, bf16[256,512]{1,0:T(8,128)(2,1)S(1)}, u32[]{:S(2)}, u32[]{:S(2)}) %collective-permute-start) | collective-permute-done | bytes 262176 | tf_op jit(solution)/shard_map/ppermute | solution.py:188
  28.3 3.7 %collective-permute-start.1 = (bf16[512,512]{1,0:T(8,128)(2,1)S(1)}, bf16[512,512]{1,0:T(8,128)(2,1)S(1)}, u32[]{:S(2)}, u32[]{:S(2)}) collective-permute-start(bf16[512,512]{1,0:T(8,128)(2,1)S(1)} %maximum_select_fusion.2), channel_id=1, source_target_pairs={{0,2},{1,3},{2,0},{3,1},{4,6},{5,7},{6,4},{7,5},{8,10},{9,11},{10,... | collective-permute-start | bytes 1572872 | tf_op jit(solution)/shard_map/ppermute | solution.py:188
  32.0 7.7 %collective-permute-done.1 = bf16[512,512]{1,0:T(8,128)(2,1)S(1)} collective-permute-done((bf16[512,512]{1,0:T(8,128)(2,1)S(1)}, bf16[512,512]{1,0:T(8,128)(2,1)S(1)}, u32[]{:S(2)}, u32[]{:S(2)}) %collective-permute-start.1) | collective-permute-done | bytes 524320 | tf_op jit(solution)/shard_map/ppermute | solution.py:188
  40.2 6.1 %collective-permute-start.2 = (bf16[1024,512]{1,0:T(8,128)(2,1)S(1)}, bf16[1024,512]{1,0:T(8,128)(2,1)S(1)}, u32[]{:S(2)}, u32[]{:S(2)}) collective-permute-start(bf16[1024,512]{1,0:T(8,128)(2,1)S(1)} %maximum_select_fusion.1), channel_id=1, source_target_pairs={{0,1},{1,0},{2,3},{3,2},{4,5},{5,4},{6,7},{7,6},{8,9},{9,8},{10,11... | collective-permute-start | bytes 3145736 | tf_op jit(solution)/shard_map/ppermute | solution.py:188
  46.3 19.8 %collective-permute-done.2 = bf16[1024,512]{1,0:T(8,128)(2,1)S(1)} collective-permute-done((bf16[1024,512]{1,0:T(8,128)(2,1)S(1)}, bf16[1024,512]{1,0:T(8,128)(2,1)S(1)}, u32[]{:S(2)}, u32[]{:S(2)}) %collective-permute-start.2) | collective-permute-done | bytes 1048608 | tf_op jit(solution)/shard_map/ppermute | solution.py:188
  66.9 72.3 %all-gather.2.cloned.1.call-done = bf16[2048,1288]{1,0:T(8,128)(2,1)} async-done(((bf16[32,1288]{1,0:T(8,128)(2,1)}), bf16[2048,1288]{1,0:T(8,128)(2,1)}) %all-gather.2.cloned.1.call-update) | async-done | bytes 5275664 | tf_op jit(solution)/shard_map/all_gather | solution.py:210
  139.2 1.3 fusion.72
  140.5 1.5 convolution_add_fusion.6
  142.0 1.7 convolution_add_fusion.5
  143.7 1.3 convolution_add_fusion.4
  145.7 1.3 convolution_add_fusion.1
  147.1 1.2 fusion.145
  152.3 1.4 fusion.86
  153.7 1.3 convolution_add_fusion.13
  155.0 1.3 convolution_add_fusion.12
  156.3 1.3 convolution_add_fusion.11
  157.6 1.3 convolution_add_fusion.10
  158.9 1.3 convolution_add_fusion.9
  160.3 1.2 convolution_add_fusion.8
  161.4 1.2 convolution_add_fusion.7
  164.6 2.1 collective-permute-start.3
  166.8 1.8 collective-permute-done.3
  169.9 3.1 collective-permute-start.4
  173.0 6.8 %collective-permute-done.4 = f32[8,8320]{1,0:T(8,128)S(1)} collective-permute-done((f32[8,8320]{1,0:T(8,128)}, f32[8,8320]{1,0:T(8,128)S(1)}, u32[]{:S(2)}, u32[]{:S(2)}) %collective-permute-start.4) | collective-permute-done | bytes 266272 | tf_op jit(solution)/shard_map/ppermute | solution.py:49
  180.9 3.9 %collective-permute-start.5 = (f32[8,8320]{1,0:T(8,128)}, f32[8,8320]{1,0:T(8,128)}, u32[]{:S(2)}, u32[]{:S(2)}) collective-permute-start(f32[8,8320]{1,0:T(8,128)} %pad_maximum_fusion.2), channel_id=1, source_target_pairs={{0,32},{8,40},{16,48},{24,56},{32,0},{40,8},{48,16},{56,24},{64,96... | collective-permute-start | bytes 798728 | tf_op jit(solution)/shard_map/ppermute | solution.py:49
  184.8 12.3 %collective-permute-done.5 = f32[8,8320]{1,0:T(8,128)} collective-permute-done((f32[8,8320]{1,0:T(8,128)}, f32[8,8320]{1,0:T(8,128)}, u32[]{:S(2)}, u32[]{:S(2)}) %collective-permute-start.5) | collective-permute-done | bytes 266272 | tf_op jit(solution)/shard_map/ppermute | solution.py:49
  197.9 1.1 add_select_fusion.6
  199.7 6.8 %collective-permute-start.6 = (f32[8,8320]{1,0:T(8,128)}, f32[8,8320]{1,0:T(8,128)}, u32[]{:S(2)}, u32[]{:S(2)}) collective-permute-start(f32[8,8320]{1,0:T(8,128)} %pad_maximum_fusion.3), channel_id=1, source_target_pairs={{0,64},{8,72},{16,80},{24,88},{32,96},{40,104},{48,112},{56,120},{... | collective-permute-start | bytes 798728 | tf_op jit(solution)/shard_map/ppermute | solution.py:49
  207.3 8.3 %collective-permute-done.6 = f32[8,8320]{1,0:T(8,128)} collective-permute-done((f32[8,8320]{1,0:T(8,128)}, f32[8,8320]{1,0:T(8,128)}, u32[]{:S(2)}, u32[]{:S(2)}) %collective-permute-start.6) | collective-permute-done | bytes 266272 | tf_op jit(solution)/shard_map/ppermute | solution.py:49
  216.3 1.1 add_select_fusion.5
  218.2 6.8 %collective-permute-start.7 = (f32[8,8320]{1,0:T(8,128)}, f32[8,8320]{1,0:T(8,128)}, u32[]{:S(2)}, u32[]{:S(2)}) collective-permute-start(f32[8,8320]{1,0:T(8,128)} %pad_maximum_fusion.4), channel_id=1, source_target_pairs={{0,128},{8,136},{16,144},{24,152},{32,160},{40,168},{48,176},{56,1... | collective-permute-start | bytes 798728 | tf_op jit(solution)/shard_map/ppermute | solution.py:49
  226.5 3.5 collective-permute-done.7
  230.8 1.1 add_select_fusion.4
  231.9 1.3 collective-permute-start.8
  233.2 9.5 %collective-permute-done.8 = f32[8,8192]{1,0:T(8,128)S(1)} collective-permute-done((f32[8,8192]{1,0:T(8,128)S(1)}, f32[8,8192]{1,0:T(8,128)S(1)}, u32[]{:S(2)}, u32[]{:S(2)}) %collective-permute-start.8) | collective-permute-done | bytes 262176 | tf_op jit(solution)/shard_map/ppermute | solution.py:44
  242.7 1.3 add_select_fusion
  244.0 2.5 collective-permute-start.9
  246.6 2.2 fusion.12
  250.4 1.7 fusion.20
  255.3 2.2 fusion.22
  257.6 1.9 multiply_reduce_fusion.1
  260.4 2.5 reduce-window.44
  264.7 3.3 fusion
  268.0 2.8 reshape.520
  270.8 1.6 copy.209
  273.9 3.7 %gather_fusion.1 = f32[8,256,256]{2,1,0:T(8,128)} fusion(f32[256,8,256]{2,0,1:T(8,128)} %bitcast.319, s32[1024]{0:T(1024)} %pad_clamp_fusion), kind=kCustom, calls=%fused_computation.1 | custom fusion | bytes 4194336 | tf_op jit(solution)/shard_map/gather | solution.py:80
  277.6 2.1 gather_fusion
  279.8 2.0 bitcast_select_fusion
  281.8 1.2 select_bitcast_fusion.1
  283.0 3.8 %collective-permute-start.10 = (f32[256,4,256]{2,0,1:T(8,128)}, f32[256,4,256]{2,0,1:T(8,128)}, u32[]{:S(2)}, u32[]{:S(2)}) collective-permute-start(f32[256,4,256]{2,0,1:T(8,128)} %select_bitcast_fusion.1), channel_id=1, source_target_pairs={{0,1},{1,0},{2,3},{3,2},{4,5},{5,4},{6,7},{7,6},{8,11},{9,10},{10,... | collective-permute-start | bytes 3145736 | tf_op jit(solution)/shard_map/ppermute | solution.py:93
  287.6 1.1 select_bitcast_fusion
  288.7 3.0 collective-permute-start.13
  291.7 8.5 %collective-permute-done.10 = f32[256,4,256]{2,0,1:T(8,128)} collective-permute-done((f32[256,4,256]{2,0,1:T(8,128)}, f32[256,4,256]{2,0,1:T(8,128)}, u32[]{:S(2)}, u32[]{:S(2)}) %collective-permute-start.10) | collective-permute-done | bytes 1048608 | tf_op jit(solution)/shard_map/ppermute | solution.py:93
  300.2 2.1 bitcast_add_fusion.1
  302.4 2.6 collective-permute-start.11
  305.0 9.5 %collective-permute-done.13 = f32[256,4,256]{2,0,1:T(8,128)} collective-permute-done((f32[256,4,256]{2,0,1:T(8,128)}, f32[256,4,256]{2,0,1:T(8,128)}, u32[]{:S(2)}, u32[]{:S(2)}) %collective-permute-start.13) | collective-permute-done | bytes 1048608 | tf_op jit(solution)/shard_map/ppermute | solution.py:93
  314.6 1.4 bitcast_add_fusion
  317.9 2.5 collective-permute-start.14
  320.5 17.1 %collective-permute-start.12 = (f32[256,1,256]{2,0,1:T(8,128)S(1)}, f32[256,1,256]{2,0,1:T(8,128)S(1)}, u32[]{:S(2)}, u32[]{:S(2)}) collective-permute-start(f32[256,1,256]{2,0,1:T(8,128)S(1)} %select_bitcast_fusion.6), channel_id=1, source_target_pairs={{0,4},{1,5},{2,6},{3,7},{4,0},{5,1},{6,2},{7,3},{8,12},{9,13},{10,... | collective-permute-start | bytes 786440 | tf_op jit(solution)/shard_map/ppermute | solution.py:93
  337.7 1.1 fusion.46
  338.9 8.0 %collective-permute-start.15 = (f32[256,1,256]{2,0,1:T(8,128)S(1)}, f32[256,1,256]{2,0,1:T(8,128)S(1)}, u32[]{:S(2)}, u32[]{:S(2)}) collective-permute-start(f32[256,1,256]{2,0,1:T(8,128)S(1)} %select_bitcast_fusion.4), channel_id=1, source_target_pairs={{0,4},{1,5},{2,6},{3,7},{4,0},{5,1},{6,2},{7,3},{8,12},{9,13},{10,... | collective-permute-start | bytes 786440 | tf_op jit(solution)/shard_map/ppermute | solution.py:93
  347.6 7.5 %collective-permute-done.15 = f32[256,1,256]{2,0,1:T(8,128)S(1)} collective-permute-done((f32[256,1,256]{2,0,1:T(8,128)S(1)}, f32[256,1,256]{2,0,1:T(8,128)S(1)}, u32[]{:S(2)}, u32[]{:S(2)}) %collective-permute-start.15) | collective-permute-done | bytes 262176 | tf_op jit(solution)/shard_map/ppermute | solution.py:93
  (178 shorter events, 32.1 us)
Async XLA Ops:
  7.2 132.0 %all-gather.2.cloned.1.call-start = ((), (), s32[]{:S(2)}) async-start(), calls=%async_computation | async-start | bytes 5857280 | tf_op jit(solution)/shard_map/all_gather | solution.py:210
  11.3 16.8 %collective-permute-start = (bf16[256,512]{1,0:T(8,128)(2,1)S(1)}, bf16[256,512]{1,0:T(8,128)(2,1)S(1)}, u32[]{:S(2)}, u32[]{:S(2)}) collective-permute-start(bf16[256,512]{1,0:T(8,128)(2,1)S(1)} %constant_dynamic-update-slice_fusion), channel_id=1, source_target_pairs={{0,4},{1,5},{2,6},{3,7},{4,0},{5,1},{6,2},{7,3},{8,12},{9,13},{10,... | collective-permute-start | bytes 786440 | tf_op jit(solution)/shard_map/ppermute | solution.py:188
  28.3 11.4 %collective-permute-start.1 = (bf16[512,512]{1,0:T(8,128)(2,1)S(1)}, bf16[512,512]{1,0:T(8,128)(2,1)S(1)}, u32[]{:S(2)}, u32[]{:S(2)}) collective-permute-start(bf16[512,512]{1,0:T(8,128)(2,1)S(1)} %maximum_select_fusion.2), channel_id=1, source_target_pairs={{0,2},{1,3},{2,0},{3,1},{4,6},{5,7},{6,4},{7,5},{8,10},{9,11},{10,... | collective-permute-start | bytes 1572872 | tf_op jit(solution)/shard_map/ppermute | solution.py:188
  40.2 26.0 %collective-permute-start.2 = (bf16[1024,512]{1,0:T(8,128)(2,1)S(1)}, bf16[1024,512]{1,0:T(8,128)(2,1)S(1)}, u32[]{:S(2)}, u32[]{:S(2)}) collective-permute-start(bf16[1024,512]{1,0:T(8,128)(2,1)S(1)} %maximum_select_fusion.1), channel_id=1, source_target_pairs={{0,1},{1,0},{2,3},{3,2},{4,5},{5,4},{6,7},{7,6},{8,9},{9,8},{10,11... | collective-permute-start | bytes 3145736 | tf_op jit(solution)/shard_map/ppermute | solution.py:188
  66.9 78.5 %copy-start.6 = (bf16[2,2,2,256,512]{4,3,2,1,0:T(8,128)(2,1)}, bf16[2,2,2,256,512]{4,3,2,1,0:T(8,128)(2,1)S(1)}, u32[]{:S(2)}) copy-start(bf16[2,2,2,256,512]{4,3,2,1,0:T(8,128)(2,1)S(1)} %copy.125) | copy-start | bytes 6291460
  140.5 4.5 %copy-start.1 = (bf16[2048,1288]{1,0:T(8,128)(2,1)S(1)}, bf16[2048,1288]{1,0:T(8,128)(2,1)}, u32[]{:S(2)}) copy-start(bf16[2048,1288]{1,0:T(8,128)(2,1)} %all-gather.2.cloned.1.call-done) | copy-start | bytes 15826948
  145.7 3.6 copy-start.23
  145.7 3.6 copy-start.28
  145.7 14.5 %slice-start = ((s8[5767168]{0:T(1024)(128)(4,1)}), s8[1572864]{0:T(1024)(128)(4,1)S(1)}, s32[]{:S(2)}) async-start(s8[5767168]{0:T(1024)(128)(4,1)} %bitcast.294), calls=%async_computation.1 | async-start | bytes 3145728
  148.3 1.0 copy-start.15
  149.5 5.6 %copy-start.26 = (f32[8]{0:T(128)}, f32[8]{0:T(128)S(1)}, u32[]{:S(2)}) copy-start(f32[8]{0:T(128)S(1)} %get-tuple-element.201) | copy-start | bytes 100
  150.1 1.0 copy-start.16
  150.3 0.6 copy-start.21
  150.4 12.3 %copy-start.18 = (f32[256,8]{0,1:T(8,128)}, f32[256,8]{0,1:T(8,128)S(1)}, u32[]{:S(2)}) copy-start(f32[256,8]{0,1:T(8,128)S(1)} %get-tuple-element.199) | copy-start | bytes 24580
  151.2 1.0 copy-start.11
  152.1 10.5 %copy-start.13 = (f32[256,128]{1,0:T(8,128)}, f32[256,128]{1,0:T(8,128)S(1)}, u32[]{:S(2)}) copy-start(f32[256,128]{1,0:T(8,128)S(1)} %copy.136) | copy-start | bytes 393220
  152.2 8.0 %slice-start.1 = ((s8[5767168]{0:T(1024)(128)(4,1)}), s8[4194304]{0:T(1024)(128)(4,1)S(1)}, s32[]{:S(2)}) async-start(s8[5767168]{0:T(1024)(128)(4,1)} %bitcast.294), calls=%async_computation.2 | async-start | bytes 8388608
  162.6 6.1 %copy-start.27 = (f32[8]{0:T(128)S(1)}, f32[8]{0:T(128)}, u32[]{:S(2)}) copy-start(f32[8]{0:T(128)} %copy-done.26) | copy-start | bytes 100
  164.6 4.0 %collective-permute-start.3 = (f32[8,16512]{1,0:T(8,128)}, f32[8,16512]{1,0:T(8,128)S(1)}, u32[]{:S(2)}, u32[]{:S(2)}) collective-permute-start(f32[8,16512]{1,0:T(8,128)} %pad_maximum_fusion), channel_id=1, source_target_pairs={{0,8},{8,0},{16,24},{24,16},{32,40},{40,32},{48,56},{56,48},{64,72... | collective-permute-start | bytes 1585160 | tf_op jit(solution)/shard_map/ppermute | solution.py:23
  169.9 55.1 %copy-start.30 = (s32[8]{0:T(128)S(1)}, s32[8]{0:T(128)}, u32[]{:S(2)}) copy-start(s32[8]{0:T(128)} %constant.154) | copy-start | bytes 100
  169.9 10.0 %collective-permute-start.4 = (f32[8,8320]{1,0:T(8,128)}, f32[8,8320]{1,0:T(8,128)S(1)}, u32[]{:S(2)}, u32[]{:S(2)}) collective-permute-start(f32[8,8320]{1,0:T(8,128)} %pad_maximum_fusion.1), channel_id=1, source_target_pairs={{0,16},{8,24},{16,0},{24,8},{32,48},{40,56},{48,32},{56,40},{64,80... | collective-permute-start | bytes 798728 | tf_op jit(solution)/shard_map/ppermute | solution.py:49
  180.0 45.6 %copy-start.29 = (f32[8]{0:T(128)S(1)}, f32[8]{0:T(128)}, u32[]{:S(2)}) copy-start(f32[8]{0:T(128)} %param.17) | copy-start | bytes 100
  180.0 46.4 %copy-start.12 = (bf16[256,256]{0,1:T(8,128)(2,1)S(1)}, bf16[256,256]{0,1:T(8,128)(2,1)}, u32[]{:S(2)}) copy-start(bf16[256,256]{0,1:T(8,128)(2,1)} %copy-done.11) | copy-start | bytes 393220
  180.9 16.2 %collective-permute-start.5 = (f32[8,8320]{1,0:T(8,128)}, f32[8,8320]{1,0:T(8,128)}, u32[]{:S(2)}, u32[]{:S(2)}) collective-permute-start(f32[8,8320]{1,0:T(8,128)} %pad_maximum_fusion.2), channel_id=1, source_target_pairs={{0,32},{8,40},{16,48},{24,56},{32,0},{40,8},{48,16},{56,24},{64,96... | collective-permute-start | bytes 798728 | tf_op jit(solution)/shard_map/ppermute | solution.py:49
  199.7 15.8 %collective-permute-start.6 = (f32[8,8320]{1,0:T(8,128)}, f32[8,8320]{1,0:T(8,128)}, u32[]{:S(2)}, u32[]{:S(2)}) collective-permute-start(f32[8,8320]{1,0:T(8,128)} %pad_maximum_fusion.3), channel_id=1, source_target_pairs={{0,64},{8,72},{16,80},{24,88},{32,96},{40,104},{48,112},{56,120},{... | collective-permute-start | bytes 798728 | tf_op jit(solution)/shard_map/ppermute | solution.py:49
  216.3 30.2 %copy-start.17 = (f32[8,2,128]{2,0,1:T(8,128)S(1)}, f32[8,2,128]{2,0,1:T(8,128)}, u32[]{:S(2)}) copy-start(f32[8,2,128]{2,0,1:T(8,128)} %copy-done.16) | copy-start | bytes 24580
  216.3 30.2 %copy-start.22 = (f32[8,2]{0,1:T(2,128)S(1)}, f32[8,2]{0,1:T(2,128)}, u32[]{:S(2)}) copy-start(f32[8,2]{0,1:T(2,128)} %copy-done.21) | copy-start | bytes 196
  218.2 11.9 %collective-permute-start.7 = (f32[8,8320]{1,0:T(8,128)}, f32[8,8320]{1,0:T(8,128)}, u32[]{:S(2)}, u32[]{:S(2)}) collective-permute-start(f32[8,8320]{1,0:T(8,128)} %pad_maximum_fusion.4), channel_id=1, source_target_pairs={{0,128},{8,136},{16,144},{24,152},{32,160},{40,168},{48,176},{56,1... | collective-permute-start | bytes 798728 | tf_op jit(solution)/shard_map/ppermute | solution.py:49
  231.9 10.8 %collective-permute-start.8 = (f32[8,8192]{1,0:T(8,128)S(1)}, f32[8,8192]{1,0:T(8,128)S(1)}, u32[]{:S(2)}, u32[]{:S(2)}) collective-permute-start(f32[8,8192]{1,0:T(8,128)S(1)} %add_select_fusion.4), channel_id=1, source_target_pairs={{0,256},{16,272},{32,288},{48,304},{64,320},{80,336},{96,352},{112... | collective-permute-start | bytes 786440 | tf_op jit(solution)/shard_map/ppermute | solution.py:44
  244.0 4.8 %collective-permute-start.9 = (f32[8,8192]{1,0:T(8,128)S(1)}, f32[8,8192]{1,0:T(8,128)S(1)}, u32[]{:S(2)}, u32[]{:S(2)}) collective-permute-start(f32[8,8192]{1,0:T(8,128)S(1)} %add_select_fusion), channel_id=1, source_target_pairs={{0,8},{8,0},{16,24},{24,16},{32,40},{40,32},{48,56},{56,48},{64,72... | collective-permute-start | bytes 786440 | tf_op jit(solution)/shard_map/ppermute | solution.py:58
  246.6 2.6 copy-start.24
  246.6 3.8 %copy-start.14 = (f32[256,128]{1,0:T(8,128)S(1)}, f32[256,128]{1,0:T(8,128)}, u32[]{:S(2)}) copy-start(f32[256,128]{1,0:T(8,128)} %copy-done.13) | copy-start | bytes 393220
  246.6 3.8 %copy-start.19 = (f32[256,8]{0,1:T(8,128)S(1)}, f32[256,8]{0,1:T(8,128)}, u32[]{:S(2)}) copy-start(f32[256,8]{0,1:T(8,128)} %copy-done.18) | copy-start | bytes 24580
  248.8 3.8 %copy-start.9 = (f32[256,1,128]{0,2,1:T(8,128)S(1)}, f32[256,1,128]{0,2,1:T(8,128)}, u32[]{:S(2)}) copy-start(f32[256,1,128]{0,2,1:T(8,128)} %get-tuple-element.186) | copy-start | bytes 393220
  250.0 3.8 %copy-start.10 = (f32[256,1,128]{0,2,1:T(8,128)S(1)}, f32[256,1,128]{0,2,1:T(8,128)}, u32[]{:S(2)}) copy-start(f32[256,1,128]{0,2,1:T(8,128)} %get-tuple-element.184) | copy-start | bytes 393220
  252.7 2.6 copy-start.20
  257.6 5.4 %copy-start.25 = (f32[8]{0:T(128)S(1)}, f32[8]{0:T(128)}, u32[]{:S(2)}) copy-start(f32[8]{0:T(128)} %param.16) | copy-start | bytes 100
  270.8 2.3 slice-start.2
  279.8 7.1 %copy-start.8 = (f32[8,256,256]{2,1,0:T(8,128)S(1)}, f32[8,256,256]{2,1,0:T(8,128)}, u32[]{:S(2)}) copy-start(f32[8,256,256]{2,1,0:T(8,128)} %gather_fusion.1) | copy-start | bytes 6291460
  281.8 5.8 %copy-start = (f32[256,8,256]{2,0,1:T(8,128)}, f32[256,8,256]{2,0,1:T(8,128)S(1)}, u32[]{:S(2)}) copy-start(f32[256,8,256]{2,0,1:T(8,128)S(1)} %bitcast_select_fusion) | copy-start | bytes 6291460
  281.8 5.0 %copy-start.7 = (f32[256,4,2,256]{3,2,1,0:T(2,128)S(1)}, f32[256,4,2,256]{3,2,1,0:T(2,128)}, u32[]{:S(2)}) copy-start(f32[256,4,2,256]{3,2,1,0:T(2,128)} %reshape.520) | copy-start | bytes 6291460
  283.0 17.2 %collective-permute-start.10 = (f32[256,4,256]{2,0,1:T(8,128)}, f32[256,4,256]{2,0,1:T(8,128)}, u32[]{:S(2)}, u32[]{:S(2)}) collective-permute-start(f32[256,4,256]{2,0,1:T(8,128)} %select_bitcast_fusion.1), channel_id=1, source_target_pairs={{0,1},{1,0},{2,3},{3,2},{4,5},{5,4},{6,7},{7,6},{8,11},{9,10},{10,... | collective-permute-start | bytes 3145736 | tf_op jit(solution)/shard_map/ppermute | solution.py:93
  288.7 25.9 %collective-permute-start.13 = (f32[256,4,256]{2,0,1:T(8,128)}, f32[256,4,256]{2,0,1:T(8,128)}, u32[]{:S(2)}, u32[]{:S(2)}) collective-permute-start(f32[256,4,256]{2,0,1:T(8,128)} %select_bitcast_fusion), channel_id=1, source_target_pairs={{0,1},{1,0},{2,3},{3,2},{4,5},{5,4},{6,7},{7,6},{8,11},{9,10},{10,... | collective-permute-start | bytes 3145736 | tf_op jit(solution)/shard_map/ppermute | solution.py:93
  302.3 2.7 copy-start.4
  302.4 18.0 %collective-permute-start.11 = (f32[256,2,256]{2,0,1:T(8,128)S(1)}, f32[256,2,256]{2,0,1:T(8,128)S(1)}, u32[]{:S(2)}, u32[]{:S(2)}) collective-permute-start(f32[256,2,256]{2,0,1:T(8,128)S(1)} %select_bitcast_fusion.3), channel_id=1, source_target_pairs={{0,2},{1,3},{2,0},{3,1},{4,6},{5,7},{6,4},{7,5},{8,10},{9,11},{10,... | collective-permute-start | bytes 1572872 | tf_op jit(solution)/shard_map/ppermute | solution.py:93
  316.0 1.0 copy-start.2
  316.0 4.4 %copy-start.5 = (f32[256,4,256]{2,0,1:T(8,128)S(1)}, f32[256,4,256]{2,0,1:T(8,128)}, u32[]{:S(2)}) copy-start(f32[256,4,256]{2,0,1:T(8,128)} %copy-done.4) | copy-start | bytes 3145732
  317.9 19.8 %copy-start.3 = (f32[256,4,256]{2,0,1:T(8,128)S(1)}, f32[256,4,256]{2,0,1:T(8,128)}, u32[]{:S(2)}) copy-start(f32[256,4,256]{2,0,1:T(8,128)} %copy-done.2) | copy-start | bytes 3145732
  317.9 19.8 %collective-permute-start.14 = (f32[256,2,256]{2,0,1:T(8,128)}, f32[256,2,256]{2,0,1:T(8,128)}, u32[]{:S(2)}, u32[]{:S(2)}) collective-permute-start(f32[256,2,256]{2,0,1:T(8,128)} %select_bitcast_fusion.2), channel_id=1, source_target_pairs={{0,2},{1,3},{2,0},{3,1},{4,6},{5,7},{6,4},{7,5},{8,10},{9,11},{10,... | collective-permute-start | bytes 1572872 | tf_op jit(solution)/shard_map/ppermute | solution.py:93
  320.5 26.3 %collective-permute-start.12 = (f32[256,1,256]{2,0,1:T(8,128)S(1)}, f32[256,1,256]{2,0,1:T(8,128)S(1)}, u32[]{:S(2)}, u32[]{:S(2)}) collective-permute-start(f32[256,1,256]{2,0,1:T(8,128)S(1)} %select_bitcast_fusion.6), channel_id=1, source_target_pairs={{0,4},{1,5},{2,6},{3,7},{4,0},{5,1},{6,2},{7,3},{8,12},{9,13},{10,... | collective-permute-start | bytes 786440 | tf_op jit(solution)/shard_map/ppermute | solution.py:93
  338.9 16.2 %collective-permute-start.15 = (f32[256,1,256]{2,0,1:T(8,128)S(1)}, f32[256,1,256]{2,0,1:T(8,128)S(1)}, u32[]{:S(2)}, u32[]{:S(2)}) collective-permute-start(f32[256,1,256]{2,0,1:T(8,128)S(1)} %select_bitcast_fusion.4), channel_id=1, source_target_pairs={{0,4},{1,5},{2,6},{3,7},{4,0},{5,1},{6,2},{7,3},{8,12},{9,13},{10,... | collective-permute-start | bytes 786440 | tf_op jit(solution)/shard_map/ppermute | solution.py:93
Sparse Core Ops, SparseCore 0:
  10.7 128.4 all-gather.1
